TPU v7x, 32 devices: a whole 2x2x4 slice. The times are simulated.
32 devices in a mesh: row: 8 (over y, x, core), col: 4 (over z).
Axes of the slice: x: 2, y: 2, z: 4, core: 2. Of those that a mesh axis runs over, the one named last changes fastest.
Arguments:
- emb_in: float32 [16384, 128], P(('row', 'col')), may hold values from -2.5 to 2.5
- ctx_in: float32 [16384, 128], P(('row', 'col')), may hold values from -2.5 to 2.5
- pos_weight: bfloat16 [8, 4, 64, 256, 256], P('row', 'col'), may hold values from 0.049804688 to 3
- neg_weight: bfloat16 [8, 4, 64, 256, 256], P('row', 'col'), may hold values from 0.049804688 to 1
- tile_row: int32 [8, 4, 64], P('row', 'col'), may hold values from 0 to 7, as said below
- tile_col: int32 [8, 4, 64], P('row', 'col'), may hold values from 0 to 15, as said below
- tile_count: int32 [8, 4], P('row', 'col'), may hold values from 8 to 64, as said below
Outputs:
- emb_out: float32 [16384, 128], P(('row', 'col'))
- ctx_out: float32 [16384, 128], P(('row', 'col'))
Inputs may be any that keep to these rules, and one draw needn't show every extreme that they name: `tile_row`: on each block the 64 slots name distinct tiles. `tile_col`: on each block the 64 slots name distinct tiles. `tile_count`: some block has all 64 slots live.
All inputs are finite; a program needn't handle non-finite values.
Results may differ from a plain program's by a relative error of at most 0.02.
Values may be sent and summed in bfloat16 or wider, within the bound.
No kernel may reach another device: no remote copies, remote signals or barrier semaphores. Data moves between devices by JAX's collectives and lax.ppermute only.
A program may use at most 128 MiB of HBM per device.

v0:
```python
import jax
import jax.numpy as jnp
from jax import lax
from jax.sharding import PartitionSpec as P

ITERS = 2


def tile_sweep(pos, neg, rows, cols, count, emb_low, ctx_low):
    tile_size = pos.shape[-1]

    def visit(slot_index, totals):
        grad_emb, grad_ctx = totals
        row_start = rows[slot_index] * tile_size
        col_start = cols[slot_index] * tile_size
        emb_rows = lax.dynamic_slice_in_dim(emb_low, row_start, tile_size, 0)
        ctx_rows = lax.dynamic_slice_in_dim(ctx_low, col_start, tile_size, 0)
        score = lax.dot_general(
            emb_rows, ctx_rows, (((1,), (1,)), ((), ())), preferred_element_type=jnp.float32
        )
        squashed = jax.nn.sigmoid(score)
        positive = lax.dynamic_index_in_dim(pos, slot_index, 0, keepdims=False).astype(jnp.float32)
        negative = lax.dynamic_index_in_dim(neg, slot_index, 0, keepdims=False).astype(jnp.float32)
        coeff_tile = (positive * (1.0 - squashed) - negative * squashed).astype(jnp.bfloat16)
        emb_step = jnp.dot(coeff_tile, ctx_rows, preferred_element_type=jnp.float32)
        ctx_step = lax.dot_general(
            coeff_tile, emb_rows, (((0,), (0,)), ((), ())), preferred_element_type=jnp.float32
        )
        grad_emb = lax.dynamic_update_slice_in_dim(
            grad_emb,
            lax.dynamic_slice_in_dim(grad_emb, row_start, tile_size, 0) + emb_step,
            row_start,
            0,
        )
        grad_ctx = lax.dynamic_update_slice_in_dim(
            grad_ctx,
            lax.dynamic_slice_in_dim(grad_ctx, col_start, tile_size, 0) + ctx_step,
            col_start,
            0,
        )
        return (grad_emb, grad_ctx)

    start = (jnp.zeros(emb_low.shape, jnp.float32), jnp.zeros(ctx_low.shape, jnp.float32))
    grad_emb, grad_ctx = lax.fori_loop(jnp.int32(0), count, visit, start)
    return (grad_emb.astype(jnp.bfloat16), grad_ctx.astype(jnp.bfloat16))


def body(emb_in, ctx_in, pos_weight, neg_weight, tile_row, tile_col, tile_count):
    pos = pos_weight[0, 0]
    neg = neg_weight[0, 0]
    rows = tile_row[0, 0]
    cols = tile_col[0, 0]
    count = tile_count[0, 0]
    emb = emb_in
    ctx = ctx_in
    for iteration in range(ITERS):
        emb_low = lax.all_gather(emb.astype(jnp.bfloat16), "col", axis=0, tiled=True)
        ctx_low = lax.all_gather(ctx.astype(jnp.bfloat16), "row", axis=0, tiled=True)
        grad_emb, grad_ctx = tile_sweep(pos, neg, rows, cols, count, emb_low, ctx_low)
        emb = emb + 0.05 * lax.psum_scatter(
            grad_emb, "col", scatter_dimension=0, tiled=True
        ).astype(jnp.float32)
        ctx = ctx + 0.05 * lax.psum_scatter(
            grad_ctx, "row", scatter_dimension=0, tiled=True
        ).astype(jnp.float32)
    return (emb, ctx)


def solution(mesh):
    in_specs = (
        P(("row", "col"), None),
        P(("row", "col"), None),
        P("row", "col", None, None, None),
        P("row", "col", None, None, None),
        P("row", "col", None),
        P("row", "col", None),
        P("row", "col"),
    )
    out_specs = (P(("row", "col"), None), P(("row", "col"), None))
    return jax.shard_map(body, mesh=mesh, in_specs=in_specs, out_specs=out_specs, check_vma=False)
```

profile of v0, /device:TPU:0, one launch (start us, length us, event | category | flops | bytes accessed | tf_op | source)
XLA Modules:
  0.0 1033.9 jit_solution(3363487664062064386)
XLA Ops:
  7.2 1.6 convert_element_type.67
  9.9 18.0 %all_gather.12 = bf16[2048,128]{1,0:T(8,128)(2,1)} all-gather(bf16[512,128]{1,0:T(8,128)(2,1)S(1)} %convert_element_type.66), channel_id=1, replica_groups=mesh['row'=8,'col'=4] {'col'}, dimensions={0}, use_global_device_ids=true | all-gather | bytes 655360 | tf_op jit(solution)/shard_map/all_gather | solution.py:57
  27.9 8.8 all-gather.3.cloned.1.call-done
  36.9 276.9 %while.24 = (s32[]{:T(128)}, f32[2048,128]{1,0:T(8,128)S(1)}, f32[4096,128]{1,0:T(8,128)S(1)}, s32[]{:T(128)}, s32[64]{0:T(128)S(1)}, /*index=5*/bf16[64,256,256...) while((s32[]{:T(128)}, f32[2048,128]{1,0:T(8,128)S(1)}, ...), condition=%wide.region_1.2_spmd, body=%wide.region_0.1_spmd.sunk | while | flops 51052556 | bytes 1442119 | solution.py:44
  40.1 1.3 fusion.58
  53.2 1.3 fusion.58
  66.4 1.3 fusion.58
  79.5 1.3 fusion.58
  92.7 1.3 fusion.58
  105.8 1.3 fusion.58
  119.0 1.3 fusion.58
  132.2 1.3 fusion.58
  145.3 1.3 fusion.58
  158.5 1.3 fusion.58
  171.6 1.3 fusion.58
  250.5 1.3 fusion.58
  315.9 179.7 %reduce-scatter.7.cloned.1.call-done = bf16[512,128]{1,0:T(8,128)(2,1)} async-done(((bf16[4096,128]{1,0:T(8,128)(2,1)}), bf16[512,128]{1,0:T(8,128)(2,1)}) %reduce-scatter.7.cloned.1.call-update) | async-done | bytes 131088 | tf_op jit(solution)/shard_map/reduce_scatter | solution.py:63
  495.6 1.6 fusion.29
  497.3 22.2 %reduce-scatter.5.cloned.1.call-done = bf16[512,128]{1,0:T(8,128)(2,1)} async-done(((bf16[2048,128]{1,0:T(8,128)(2,1)}), bf16[512,128]{1,0:T(8,128)(2,1)}) %reduce-scatter.5.cloned.1.call-update) | async-done | bytes 131088 | tf_op jit(solution)/shard_map/reduce_scatter | solution.py:60
  520.5 16.6 %all_gather.14 = bf16[2048,128]{1,0:T(8,128)(2,1)} all-gather(bf16[512,128]{1,0:T(8,128)(2,1)S(1)} %fusion.28), channel_id=1, replica_groups=mesh['row'=8,'col'=4] {'col'}, dimensions={0}, use_global_device_ids=true | all-gather | bytes 655360 | tf_op jit(solution)/shard_map/all_gather | solution.py:57
  537.1 6.6 all-gather.5.cloned.1.call-done
  543.9 276.9 %while.25 = (s32[]{:T(128)}, f32[2048,128]{1,0:T(8,128)S(1)}, f32[4096,128]{1,0:T(8,128)S(1)}, s32[]{:T(128)}, s32[64]{0:T(128)S(1)}, /*index=5*/bf16[64,256,256...) while((s32[]{:T(128)}, f32[2048,128]{1,0:T(8,128)S(1)}, ...), condition=%wide.region_5.6_spmd, body=%wide.region_4.5_spmd.sunk | while | flops 51052556 | bytes 1442119 | solution.py:44
  553.6 1.3 fusion.67
  612.8 1.3 fusion.67
  639.1 1.3 fusion.67
  672.0 1.3 fusion.67
  698.3 1.3 fusion.67
  757.5 1.3 fusion.67
  822.8 165.1 %reduce-scatter.9.cloned.1.call-done = bf16[512,128]{1,0:T(8,128)(2,1)} async-done(((bf16[2048,128]{1,0:T(8,128)(2,1)}), bf16[512,128]{1,0:T(8,128)(2,1)}) %reduce-scatter.9.cloned.1.call-update) | async-done | bytes 131088 | tf_op jit(solution)/shard_map/reduce_scatter | solution.py:60
  988.0 1.7 multiply_add_fusion.1
  989.6 35.8 %reduce-scatter.11.cloned.1.call-done = bf16[512,128]{1,0:T(8,128)(2,1)} async-done(((bf16[4096,128]{1,0:T(8,128)(2,1)}), bf16[512,128]{1,0:T(8,128)(2,1)}) %reduce-scatter.11.cloned.1.call-update) | async-done | bytes 131088 | tf_op jit(solution)/shard_map/reduce_scatter | solution.py:63
  1025.4 1.7 multiply_add_fusion
  (438 shorter events, 367.1 us)
Async XLA Ops:
  7.2 29.5 %all-gather.3.cloned.1.call-start = ((), (), s32[]{:S(2)}) async-start(), calls=%async_computation.4 | async-start | bytes 1179648 | tf_op jit(solution)/shard_map/all_gather | solution.py:58
  8.9 28.0 %copy-start.5 = (s32[1,1,64]{2,1,0:T(1,128)S(1)}, s32[1,1,64]{2,1,0:T(1,128)}, u32[]{:S(2)}) copy-start(s32[1,1,64]{2,1,0:T(1,128)} %param.15) | copy-start | bytes 772
  8.9 28.0 %copy-start.6 = (s32[1,1,64]{2,1,0:T(1,128)S(1)}, s32[1,1,64]{2,1,0:T(1,128)}, u32[]{:S(2)}) copy-start(s32[1,1,64]{2,1,0:T(1,128)} %param.16) | copy-start | bytes 772
  8.9 486.8 %reduce-scatter.7.cloned.1.call-start = ((), (), s32[]{:S(2)}) async-start(), calls=%async_computation.6 | async-start | bytes 1179648 | tf_op jit(solution)/shard_map/reduce_scatter | solution.py:63
  314.9 180.7 %copy-start.1 = (f32[512,128]{1,0:T(8,128)S(1)}, f32[512,128]{1,0:T(8,128)}, u32[]{:S(2)}) copy-start(f32[512,128]{1,0:T(8,128)} %param.12) | copy-start | bytes 786436
  314.9 204.7 %copy-start = (f32[512,128]{1,0:T(8,128)S(1)}, f32[512,128]{1,0:T(8,128)}, u32[]{:S(2)}) copy-start(f32[512,128]{1,0:T(8,128)} %param.11) | copy-start | bytes 786436
  314.9 204.6 %reduce-scatter.5.cloned.1.call-start = ((), (), s32[]{:S(2)}) async-start(), calls=%async_computation.5 | async-start | bytes 655360 | tf_op jit(solution)/shard_map/reduce_scatter | solution.py:60
  315.9 227.8 %all-gather.5.cloned.1.call-start = ((), (), s32[]{:S(2)}) async-start(), calls=%async_computation.7 | async-start | bytes 1179648 | tf_op jit(solution)/shard_map/all_gather | solution.py:58
  497.3 490.7 %reduce-scatter.9.cloned.1.call-start = ((), (), s32[]{:S(2)}) async-start(), calls=%async_computation.8 | async-start | bytes 655360 | tf_op jit(solution)/shard_map/reduce_scatter | solution.py:60
  821.7 203.7 %reduce-scatter.11.cloned.1.call-start = ((), (), s32[]{:S(2)}) async-start(), calls=%async_computation.9 | async-start | bytes 1179648 | tf_op jit(solution)/shard_map/reduce_scatter | solution.py:63
  821.7 166.3 %copy-start.4 = (bf16[512,128]{1,0:T(8,128)(2,1)S(1)}, bf16[512,128]{1,0:T(8,128)(2,1)}, u32[]{:S(2)}) copy-start(bf16[512,128]{1,0:T(8,128)(2,1)} %reduce-scatter.5.cloned.1.call-done) | copy-start | bytes 393220
  821.7 203.7 %copy-start.2 = (f32[512,128]{1,0:T(8,128)S(1)}, f32[512,128]{1,0:T(8,128)}, u32[]{:S(2)}) copy-start(f32[512,128]{1,0:T(8,128)} %param.12) | copy-start | bytes 786436
  821.7 203.7 %copy-start.3 = (bf16[512,128]{1,0:T(8,128)(2,1)S(1)}, bf16[512,128]{1,0:T(8,128)(2,1)}, u32[]{:S(2)}) copy-start(bf16[512,128]{1,0:T(8,128)(2,1)} %reduce-scatter.7.cloned.1.call-done) | copy-start | bytes 393220
Sparse Core Ops, SparseCore 0:
  10.5 26.1 all-gather.2
  315.0 180.5 reduce-scatter.6
  497.9 21.5 reduce-scatter.4
  521.9 21.7 all-gather.4
  821.8 166.1 reduce-scatter.8
  991.0 34.3 reduce-scatter.10
where the time goes:
time: 1050 us; the launch traced here: 1030 us
  waiting for transfers between devices  418 us (40%)
  matrix products  285 us (27%)
  loops' own time  170 us (16%)
  local copies, waits for them, and re-layouts  99.2 us (9%)
  blocking collectives  34.6 us (3%)
  between operations  14.2 us (1%)
  other arithmetic  12.4 us (1%)
    reduce_scatter x2, waiting for transfers between devices, body(): lax.psum_scatter(grad_ctx, 'row', scatter_dimension=0, tiled=True)  215 us
    reduce_scatter x2, waiting for transfers between devices, body(): lax.psum_scatter(grad_emb, 'col', scatter_dimension=0, tiled=True)  187 us
    another operation x2, loops' own time, tile_sweep(): grad_emb, grad_ctx = lax.fori_loop(jnp.int32(0), count, visit, start)  170 us
    dot_general x84, matrix products, visit(): lax.dot_general(emb_rows, ctx_rows, (((1,), (1,)), ((), ())), preferred_e...  110 us
    dot_general x84, matrix products, visit(): lax.dot_general(coeff_tile, emb_rows, (((0,), (0,)), ((), ())), preferred...  89.9 us
    dot_general x84, matrix products, visit(): emb_step = jnp.dot(coeff_tile, ctx_rows, preferred_element_type=jnp.float32)  85.2 us
    dynamic_slice x84, local copies, waits for them, and re-layouts, visit(): row_start = rows[slot_index] * tile_size  49.4 us
    dynamic_slice x84, local copies, waits for them, and re-layouts, visit(): col_start = cols[slot_index] * tile_size  49.3 us
  transfers between devices with their start and end apart: 6, of which 6 were waited for; matrix products, arithmetic and copies ran while one was open for 1% of the time, Pallas kernels for 0%

commit v1 on v0

v1 whole, which is shorter than its diff:
```python
import functools

import jax
import jax.numpy as jnp
from jax import lax
from jax.experimental import pallas as pl
from jax.experimental.pallas import tpu as pltpu
from jax.sharding import PartitionSpec as P

ITERS = 2


def sweep_kernel(tile, rows_ref, cols_ref, count_ref, emb_ref, ctx_ref, pos_ref, neg_ref,
                 gemb_ref, gctx_ref, acc_e, acc_c):
    k = pl.program_id(0)
    n = count_ref[0]

    @pl.when(k == 0)
    def _():
        acc_e[...] = jnp.zeros_like(acc_e)
        acc_c[...] = jnp.zeros_like(acc_c)

    @pl.when(k < n)
    def _():
        r0 = pl.multiple_of(rows_ref[k] * tile, tile)
        c0 = pl.multiple_of(cols_ref[k] * tile, tile)
        e = emb_ref[pl.ds(r0, tile), :]
        c = ctx_ref[pl.ds(c0, tile), :]
        score = lax.dot_general(e, c, (((1,), (1,)), ((), ())), preferred_element_type=jnp.float32)
        squashed = jax.nn.sigmoid(score)
        positive = pos_ref[0].astype(jnp.float32)
        negative = neg_ref[0].astype(jnp.float32)
        coeff = (positive * (1.0 - squashed) - negative * squashed).astype(jnp.bfloat16)
        acc_e[pl.ds(r0, tile), :] += jnp.dot(coeff, c, preferred_element_type=jnp.float32)
        acc_c[pl.ds(c0, tile), :] += lax.dot_general(
            coeff, e, (((0,), (0,)), ((), ())), preferred_element_type=jnp.float32
        )

    @pl.when(k == pl.num_programs(0) - 1)
    def _():
        gemb_ref[...] = acc_e[...].astype(gemb_ref.dtype)
        gctx_ref[...] = acc_c[...].astype(gctx_ref.dtype)


def tile_sweep(pos, neg, rows, cols, count, emb_low, ctx_low):
    cap, tile, _ = pos.shape
    ne, dim = emb_low.shape
    nc = ctx_low.shape[0]

    def slot(k, rows_ref, cols_ref, count_ref):
        return (jnp.minimum(k, jnp.maximum(count_ref[0] - 1, 0)), 0, 0)

    grid_spec = pltpu.PrefetchScalarGridSpec(
        num_scalar_prefetch=3,
        grid=(cap,),
        in_specs=[
            pl.BlockSpec((ne, dim), lambda k, *_: (0, 0)),
            pl.BlockSpec((nc, dim), lambda k, *_: (0, 0)),
            pl.BlockSpec((1, tile, tile), slot),
            pl.BlockSpec((1, tile, tile), slot),
        ],
        out_specs=[
            pl.BlockSpec((ne, dim), lambda k, *_: (0, 0)),
            pl.BlockSpec((nc, dim), lambda k, *_: (0, 0)),
        ],
        scratch_shapes=[
            pltpu.VMEM((ne, dim), jnp.float32),
            pltpu.VMEM((nc, dim), jnp.float32),
        ],
    )
    flops = cap * 3 * 2 * tile * tile * dim
    return pl.pallas_call(
        functools.partial(sweep_kernel, tile),
        grid_spec=grid_spec,
        out_shape=(
            jax.ShapeDtypeStruct((ne, dim), jnp.bfloat16),
            jax.ShapeDtypeStruct((nc, dim), jnp.bfloat16),
        ),
        compiler_params=pltpu.CompilerParams(dimension_semantics=("arbitrary",)),
        cost_estimate=pl.CostEstimate(
            flops=flops,
            transcendentals=cap * tile * tile,
            bytes_accessed=2 * cap * tile * tile * 2 + 3 * (ne + nc) * dim * 2,
        ),
    )(rows, cols, count.reshape(1), emb_low, ctx_low, pos, neg)


def body(emb_in, ctx_in, pos_weight, neg_weight, tile_row, tile_col, tile_count):
    pos = pos_weight[0, 0]
    neg = neg_weight[0, 0]
    rows = tile_row[0, 0]
    cols = tile_col[0, 0]
    count = tile_count[0, 0]
    emb = emb_in
    ctx = ctx_in
    for iteration in range(ITERS):
        emb_low = lax.all_gather(emb.astype(jnp.bfloat16), "col", axis=0, tiled=True)
        ctx_low = lax.all_gather(ctx.astype(jnp.bfloat16), "row", axis=0, tiled=True)
        grad_emb, grad_ctx = tile_sweep(pos, neg, rows, cols, count, emb_low, ctx_low)
        emb = emb + 0.05 * lax.psum_scatter(
            grad_emb, "col", scatter_dimension=0, tiled=True
        ).astype(jnp.float32)
        ctx = ctx + 0.05 * lax.psum_scatter(
            grad_ctx, "row", scatter_dimension=0, tiled=True
        ).astype(jnp.float32)
    return (emb, ctx)


def solution(mesh):
    in_specs = (
        P(("row", "col"), None),
        P(("row", "col"), None),
        P("row", "col", None, None, None),
        P("row", "col", None, None, None),
        P("row", "col", None),
        P("row", "col", None),
        P("row", "col"),
    )
    out_specs = (P(("row", "col"), None), P(("row", "col"), None))
    return jax.shard_map(body, mesh=mesh, in_specs=in_specs, out_specs=out_specs, check_vma=False)
```

time: 1050 us -> 288 us (0.27); the launches traced: 1030 us -> 286 us
  matrix products: 285 us -> 0 us
  waiting for transfers between devices: 418 us -> 161 us
  loops' own time: 170 us -> 0 us
  local copies, waits for them, and re-layouts: 99.2 us -> 0.01 us
  Pallas kernels: 0 us -> 67.1 us
    dot_general x252 -> x0, matrix products: 285 us -> none  [the longest x84 110 us: visit(): lax.dot_general(emb_rows, ctx_rows, (((1,), (1,)), ((), ())), preferred_e...]
    another operation x2 -> x0, loops' own time: 170 us -> none  [tile_sweep(): grad_emb, grad_ctx = lax.fori_loop(jnp.int32(0), count, visit, start)]
    reduce_scatter x2, waiting for transfers between devices: 215 us -> 86.2 us  [body(): lax.psum_scatter(grad_ctx, 'row', scatter_dimension=0, tiled=True)]
    reduce_scatter x2, waiting for transfers between devices: 187 us -> 58.6 us  [body(): lax.psum_scatter(grad_emb, 'col', scatter_dimension=0, tiled=True)]
    dynamic_slice x168 -> x0, local copies, waits for them, and re-layouts: 98.7 us -> none  [the longest x84 49.4 us: visit(): row_start = rows[slot_index] * tile_size]
    pallas_call x0 -> x2, Pallas kernels: none -> 67.1 us  [tile_sweep(): pl.pallas_call(functools.partial(sweep_kernel, tile), grid_spec=grid_spec...]
  transfers between devices with their start and end apart: 6 -> 6, of which waited for: 6 -> 6; matrix products, arithmetic and copies ran while one was open for 1% -> 2% of each run, Pallas kernels for 0% -> 0%
where the time goes in v1:
time: 288 us; the launch traced here: 286 us
  waiting for transfers between devices  161 us (56%)
  Pallas kernels  67.1 us (23%)
  blocking collectives  34.6 us (12%)
  between operations  14.8 us (5%)
  other arithmetic  8.44 us (3%)
    reduce_scatter x2, waiting for transfers between devices, body(): lax.psum_scatter(grad_ctx, 'row', scatter_dimension=0, tiled=True)  86.2 us
    pallas_call x2, Pallas kernels, tile_sweep(): pl.pallas_call(functools.partial(sweep_kernel, tile), grid_spec=grid_spec...  67.1 us
    reduce_scatter x2, waiting for transfers between devices, body(): lax.psum_scatter(grad_emb, 'col', scatter_dimension=0, tiled=True)  58.6 us
    all_gather x2, blocking collectives, body(): lax.all_gather(emb.astype(jnp.bfloat16), 'col', axis=0, tiled=True)  34.6 us
    all_gather x2, waiting for transfers between devices, body(): lax.all_gather(ctx.astype(jnp.bfloat16), 'row', axis=0, tiled=True)  14.7 us
  transfers between devices with their start and end apart: 6, of which 6 were waited for; matrix products, arithmetic and copies ran while one was open for 2% of the time, Pallas kernels for 0%

profile of v1, /device:TPU:0, one launch (start us, length us, event | category | flops | bytes accessed | tf_op | source)
XLA Modules:
  0.0 286.0 jit_solution(8668287248760497541)
XLA Ops:
  7.2 0.0 all-gather.3.cloned.1.call-start
  7.2 1.6 convert_element_type.25
  8.8 0.0 all-gather.3.cloned.1.call-update
  8.9 0.0 reduce-scatter.7.cloned.1.call-start
  9.6 1.0 convert_element_type.24
  10.5 18.0 %all_gather.12.emb_ref = bf16[2048,128]{1,0:T(8,128)(2,1)} all-gather(bf16[512,128]{1,0:T(8,128)(2,1)S(1)} %convert_element_type.24), channel_id=1, replica_groups=mesh['row'=8,'col'=4] {'col'}, dimensions={0}, use_global_device_ids=true | all-gather | bytes 655360 | tf_op jit(solution)/shard_map/all_gather | solution.py:97
  28.5 8.2 %all-gather.3.cloned.1.call-done.ctx_ref = bf16[4096,128]{1,0:T(8,128)(2,1)} async-done(((bf16[512,128]{1,0:T(8,128)(2,1)}), bf16[4096,128]{1,0:T(8,128)(2,1)}) %all-gather.3.cloned.1.call-update) | async-done | bytes 1048592 | tf_op jit(solution)/shard_map/all_gather | solution.py:98
  36.7 33.6 %shard_map.86 = (bf16[2048,128]{1,0:T(8,128)(2,1)}, bf16[4096,128]{1,0:T(8,128)(2,1)}) custom-call(s32[64]{0:T(128)} %bitcast.11, s32[64]{0:T(128)} %bitcast.13, s32[1]{0:T(128)} %bitcast.5.count_ref, bf16[2048,128]{1,0:T(8,128)(2,1)} %all_gather.12.emb_ref, bf16[4096,128]{1,0:T(8,128)(2,1)} %all-gather.3.cloned.1.call-done.ctx_ref, ...), custom_call_target="tpu_custom_call" | custom-call | flops 3221225472 | bytes 21495808 | tf_op jit(solution)/shard_map/pallas_call | solution.py:72
  70.3 0.0 reduce-scatter.7.cloned.1.call-update
  70.3 0.0 reduce-scatter.5.cloned.1.call-start
  70.3 0.7 reduce-scatter.5.cloned.1.call-update
  71.0 0.0 all-gather.5.cloned.1.call-start
  71.1 50.5 %reduce-scatter.7.cloned.1.call-done = bf16[512,128]{1,0:T(8,128)(2,1)} async-done(((bf16[4096,128]{1,0:T(8,128)(2,1)}), bf16[512,128]{1,0:T(8,128)(2,1)}) %reduce-scatter.7.cloned.1.call-update) | async-done | bytes 131088 | tf_op jit(solution)/shard_map/reduce_scatter | solution.py:103
  121.5 0.0 copy-done.1
  121.5 1.6 fusion.1
  123.1 0.0 all-gather.5.cloned.1.call-update
  123.1 0.0 reduce-scatter.9.cloned.1.call-start
  123.2 22.3 %reduce-scatter.5.cloned.1.call-done = bf16[512,128]{1,0:T(8,128)(2,1)} async-done(((bf16[2048,128]{1,0:T(8,128)(2,1)}), bf16[512,128]{1,0:T(8,128)(2,1)}) %reduce-scatter.5.cloned.1.call-update) | async-done | bytes 131088 | tf_op jit(solution)/shard_map/reduce_scatter | solution.py:100
  145.5 0.0 copy-done
  145.5 0.9 fusion
  146.4 16.6 %all_gather.14.emb_ref = bf16[2048,128]{1,0:T(8,128)(2,1)} all-gather(bf16[512,128]{1,0:T(8,128)(2,1)S(1)} %fusion), channel_id=1, replica_groups=mesh['row'=8,'col'=4] {'col'}, dimensions={0}, use_global_device_ids=true | all-gather | bytes 655360 | tf_op jit(solution)/shard_map/all_gather | solution.py:97
  163.1 6.6 %all-gather.5.cloned.1.call-done.ctx_ref = bf16[4096,128]{1,0:T(8,128)(2,1)} async-done(((bf16[512,128]{1,0:T(8,128)(2,1)}), bf16[4096,128]{1,0:T(8,128)(2,1)}) %all-gather.5.cloned.1.call-update) | async-done | bytes 1048592 | tf_op jit(solution)/shard_map/all_gather | solution.py:98
  169.6 33.6 %shard_map.87 = (bf16[2048,128]{1,0:T(8,128)(2,1)}, bf16[4096,128]{1,0:T(8,128)(2,1)}) custom-call(s32[64]{0:T(128)} %bitcast.12, s32[64]{0:T(128)} %bitcast.14, s32[1]{0:T(128)} %bitcast.6.count_ref, bf16[2048,128]{1,0:T(8,128)(2,1)} %all_gather.14.emb_ref, bf16[4096,128]{1,0:T(8,128)(2,1)} %all-gather.5.cloned.1.call-done.ctx_ref, ...), custom_call_target="tpu_custom_call" | custom-call | flops 3221225472 | bytes 21495808 | tf_op jit(solution)/shard_map/pallas_call | solution.py:72
  203.2 0.0 reduce-scatter.9.cloned.1.call-update
  203.2 0.0 reduce-scatter.11.cloned.1.call-start
  203.3 0.5 reduce-scatter.11.cloned.1.call-update
  203.8 36.3 %reduce-scatter.9.cloned.1.call-done = bf16[512,128]{1,0:T(8,128)(2,1)} async-done(((bf16[2048,128]{1,0:T(8,128)(2,1)}), bf16[512,128]{1,0:T(8,128)(2,1)}) %reduce-scatter.9.cloned.1.call-update) | async-done | bytes 131088 | tf_op jit(solution)/shard_map/reduce_scatter | solution.py:100
  240.1 0.0 copy-done.3
  240.1 1.7 multiply_add_fusion.1
  241.8 35.7 %reduce-scatter.11.cloned.1.call-done = bf16[512,128]{1,0:T(8,128)(2,1)} async-done(((bf16[4096,128]{1,0:T(8,128)(2,1)}), bf16[512,128]{1,0:T(8,128)(2,1)}) %reduce-scatter.11.cloned.1.call-update) | async-done | bytes 131088 | tf_op jit(solution)/shard_map/reduce_scatter | solution.py:103
  277.5 0.0 copy-done.2
  277.5 1.7 multiply_add_fusion
  (4 shorter events, 0.0 us)
Async XLA Ops:
  7.2 29.5 %all-gather.3.cloned.1.call-start = ((), (), s32[]{:S(2)}) async-start(), calls=%async_computation.4 | async-start | bytes 1179648 | tf_op jit(solution)/shard_map/all_gather | solution.py:98
  8.9 112.7 %reduce-scatter.7.cloned.1.call-start = ((), (), s32[]{:S(2)}) async-start(), calls=%async_computation.6 | async-start | bytes 1179648 | tf_op jit(solution)/shard_map/reduce_scatter | solution.py:103
  36.7 84.8 %copy-start.1 = (f32[512,128]{1,0:T(8,128)S(1)}, f32[512,128]{1,0:T(8,128)}, u32[]{:S(2)}) copy-start(f32[512,128]{1,0:T(8,128)} %param.8) | copy-start | bytes 786436
  36.7 108.8 %copy-start = (f32[512,128]{1,0:T(8,128)S(1)}, f32[512,128]{1,0:T(8,128)}, u32[]{:S(2)}) copy-start(f32[512,128]{1,0:T(8,128)} %param.7) | copy-start | bytes 786436
  70.3 75.2 %reduce-scatter.5.cloned.1.call-start = ((), (), s32[]{:S(2)}) async-start(), calls=%async_computation.5 | async-start | bytes 655360 | tf_op jit(solution)/shard_map/reduce_scatter | solution.py:100
  71.0 98.6 %all-gather.5.cloned.1.call-start = ((), (), s32[]{:S(2)}) async-start(), calls=%async_computation.7 | async-start | bytes 1179648 | tf_op jit(solution)/shard_map/all_gather | solution.py:98
  123.1 116.9 %reduce-scatter.9.cloned.1.call-start = ((), (), s32[]{:S(2)}) async-start(), calls=%async_computation.8 | async-start | bytes 655360 | tf_op jit(solution)/shard_map/reduce_scatter | solution.py:100
  169.6 70.5 %copy-start.3 = (bf16[512,128]{1,0:T(8,128)(2,1)S(1)}, bf16[512,128]{1,0:T(8,128)(2,1)}, u32[]{:S(2)}) copy-start(bf16[512,128]{1,0:T(8,128)(2,1)} %reduce-scatter.5.cloned.1.call-done) | copy-start | bytes 393220
  169.6 107.9 %copy-start.2 = (bf16[512,128]{1,0:T(8,128)(2,1)S(1)}, bf16[512,128]{1,0:T(8,128)(2,1)}, u32[]{:S(2)}) copy-start(bf16[512,128]{1,0:T(8,128)(2,1)} %reduce-scatter.7.cloned.1.call-done) | copy-start | bytes 393220
  203.2 74.3 %reduce-scatter.11.cloned.1.call-start = ((), (), s32[]{:S(2)}) async-start(), calls=%async_computation.9 | async-start | bytes 1179648 | tf_op jit(solution)/shard_map/reduce_scatter | solution.py:103
Sparse Core Ops, SparseCore 0:
  10.5 26.1 all-gather.2
  70.4 51.0 reduce-scatter.6
  123.8 21.6 reduce-scatter.4
  147.8 21.8 all-gather.4
  203.3 36.7 reduce-scatter.8
  243.1 34.3 reduce-scatter.10

commit v2 on v1

--- a/solution.py
+++ b/solution.py
@@ -85,24 +85,47 @@
     )(rows, cols, count.reshape(1), emb_low, ctx_low, pos, neg)
 
 
+def gather_rotated(x, axis, n):
+    pieces = [x]
+    for s in range(1, n):
+        pieces.append(lax.ppermute(x, axis, [(i, (i + s) % n) for i in range(n)]))
+    return jnp.concatenate(pieces, axis=0)
+
+
+def scatter_rotated(g, axis, n):
+    chunks = g.reshape(n, -1, g.shape[-1])
+    total = chunks[0].astype(jnp.float32)
+    for s in range(1, n):
+        got = lax.ppermute(chunks[(n - s) % n], axis, [(i, (i + s) % n) for i in range(n)])
+        total = total + got.astype(jnp.float32)
+    return total
+
+
+def rotate_index(index, me, n, per_run):
+    run = index // per_run
+    return ((me - run) % n) * per_run + index % per_run
+
+
 def body(emb_in, ctx_in, pos_weight, neg_weight, tile_row, tile_col, tile_count):
+    n_row = lax.axis_size("row")
+    n_col = lax.axis_size("col")
+    me_row = lax.axis_index("row")
+    me_col = lax.axis_index("col")
     pos = pos_weight[0, 0]
     neg = neg_weight[0, 0]
-    rows = tile_row[0, 0]
-    cols = tile_col[0, 0]
+    tile = pos.shape[-1]
+    per_run = emb_in.shape[0] // tile
+    rows = rotate_index(tile_row[0, 0], me_col, n_col, per_run)
+    cols = rotate_index(tile_col[0, 0], me_row, n_row, per_run)
     count = tile_count[0, 0]
     emb = emb_in
     ctx = ctx_in
     for iteration in range(ITERS):
-        emb_low = lax.all_gather(emb.astype(jnp.bfloat16), "col", axis=0, tiled=True)
-        ctx_low = lax.all_gather(ctx.astype(jnp.bfloat16), "row", axis=0, tiled=True)
+        emb_low = gather_rotated(emb.astype(jnp.bfloat16), "col", n_col)
+        ctx_low = gather_rotated(ctx.astype(jnp.bfloat16), "row", n_row)
         grad_emb, grad_ctx = tile_sweep(pos, neg, rows, cols, count, emb_low, ctx_low)
-        emb = emb + 0.05 * lax.psum_scatter(
-            grad_emb, "col", scatter_dimension=0, tiled=True
-        ).astype(jnp.float32)
-        ctx = ctx + 0.05 * lax.psum_scatter(
-            grad_ctx, "row", scatter_dimension=0, tiled=True
-        ).astype(jnp.float32)
+        emb = emb + 0.05 * scatter_rotated(grad_emb, "col", n_col)
+        ctx = ctx + 0.05 * scatter_rotated(grad_ctx, "row", n_row)
     return (emb, ctx)
 
 

time: 288 us -> 201 us (0.70)
  waiting for transfers between devices: 161 us -> 28.9 us
  starting transfers between devices: 0.24 us -> 116 us
  blocking collectives: 34.6 us -> 0 us
  Pallas kernels: 67.1 us -> 36.9 us
  between operations: 14.8 us -> 1.53 us
  local copies, waits for them, and re-layouts: 0.01 us -> 4.99 us
    reduce_scatter x4 -> x0, waiting for transfers between devices: 145 us -> none  [the longest x2 86.2 us: body(): lax.psum_scatter(grad_ctx, 'row', scatter_dimension=0, tiled=True)]
    ppermute x0 -> x40, starting transfers between devices: none -> 116 us  [the longest x20 87 us: scatter_rotated(): lax.ppermute(chunks[(n - s) % n], axis, [(i, (i + s) % n) for i in range(...]
    all_gather x2 -> x0, blocking collectives: 34.6 us -> none  [body(): lax.all_gather(emb.astype(jnp.bfloat16), 'col', axis=0, tiled=True)]
    pallas_call x2, Pallas kernels: 67.1 us -> 36.9 us  [tile_sweep(): pl.pallas_call(functools.partial(sweep_kernel, tile), grid_spec=grid_spec...]
    ppermute x0 -> x40, waiting for transfers between devices: none -> 28.9 us  [the longest x20 18.3 us: gather_rotated(): pieces.append(lax.ppermute(x, axis, [(i, (i + s) % n) for i in range(n)]))]
    all_gather x2 -> x0, waiting for transfers between devices: 14.7 us -> none  [body(): lax.all_gather(ctx.astype(jnp.bfloat16), 'row', axis=0, tiled=True)]
    slice x0 -> x4, local copies, waits for them, and re-layouts: none -> 4.72 us  [scatter_rotated(): chunks[(n - s) % n]]
    convert_element_type x4 -> x2, other arithmetic: 5.12 us -> 1.96 us  [body(): emb_low = gather_rotated(emb.astype(jnp.bfloat16), 'col', n_col)]
  transfers between devices with their start and end apart: 6 -> 40, of which waited for: 6 -> 16; matrix products, arithmetic and copies ran while one was open for 2% -> 4% of each run, Pallas kernels for 0% -> 0%
where the time goes in v2:
time: 201 us; the launch traced here: 198 us
  starting transfers between devices  116 us (58%)
  Pallas kernels  36.9 us (18%)
  waiting for transfers between devices  28.9 us (14%)
  other arithmetic  10.5 us (5%)
  local copies, waits for them, and re-layouts  4.99 us (2%)
    ppermute x20, starting transfers between devices, scatter_rotated(): lax.ppermute(chunks[(n - s) % n], axis, [(i, (i + s) % n) for i in range(...  87 us
    pallas_call x2, Pallas kernels, tile_sweep(): pl.pallas_call(functools.partial(sweep_kernel, tile), grid_spec=grid_spec...  36.9 us
    ppermute x20, starting transfers between devices, gather_rotated(): pieces.append(lax.ppermute(x, axis, [(i, (i + s) % n) for i in range(n)]))  28.6 us
    ppermute x20, waiting for transfers between devices, gather_rotated(): pieces.append(lax.ppermute(x, axis, [(i, (i + s) % n) for i in range(n)]))  18.3 us
    ppermute x20, waiting for transfers between devices, scatter_rotated(): lax.ppermute(chunks[(n - s) % n], axis, [(i, (i + s) % n) for i in range(...  10.6 us
    slice x4, local copies, waits for them, and re-layouts, scatter_rotated(): chunks[(n - s) % n]  4.72 us
  transfers between devices with their start and end apart: 40, of which 16 were waited for; matrix products, arithmetic and copies ran while one was open for 4% of the time, Pallas kernels for 0%

profile of v2, /device:TPU:0, one launch (start us, length us, event | category | flops | bytes accessed | tf_op | source)
XLA Modules:
  0.0 198.4 jit_solution(5268095121260506368)
XLA Ops:
  2.1 2.6 %collective-permute-start.4 = (bf16[512,128]{1,0:T(8,128)(2,1)S(1)}, bf16[512,128]{1,0:T(8,128)(2,1)S(1)}, u32[]{:S(2)}, u32[]{:S(2)}) collective-permute-start(bf16[512,128]{1,0:T(8,128)(2,1)S(1)} %get-tuple-element.14), channel_id=1, source_target_pairs={{0,8},{4,12},{8,16},{12,20},{16,24},{20,28},{24,0},{28,4},{1,9},{5... | collective-permute-start | bytes 393224 | tf_op jit(solution)/shard_map/ppermute | solution.py:91
  4.7 2.4 %collective-permute-start.5 = (bf16[512,128]{1,0:T(8,128)(2,1)S(1)}, bf16[512,128]{1,0:T(8,128)(2,1)S(1)}, u32[]{:S(2)}, u32[]{:S(2)}) collective-permute-start(bf16[512,128]{1,0:T(8,128)(2,1)S(1)} %get-tuple-element.14), channel_id=1, source_target_pairs={{0,12},{4,16},{8,20},{12,24},{16,28},{20,0},{24,4},{28,8},{1,13},{... | collective-permute-start | bytes 393224 | tf_op jit(solution)/shard_map/ppermute | solution.py:91
  10.5 1.5 collective-permute-start.8
  12.0 2.4 %collective-permute-start.9 = (bf16[512,128]{1,0:T(8,128)(2,1)S(1)}, bf16[512,128]{1,0:T(8,128)(2,1)S(1)}, u32[]{:S(2)}, u32[]{:S(2)}) collective-permute-start(bf16[512,128]{1,0:T(8,128)(2,1)S(1)} %get-tuple-element.14), channel_id=1, source_target_pairs={{0,28},{4,0},{8,4},{12,8},{16,12},{20,16},{24,20},{28,24},{1,29},{... | collective-permute-start | bytes 393224 | tf_op jit(solution)/shard_map/ppermute | solution.py:91
  14.6 2.3 %collective-permute-start = (bf16[512,128]{1,0:T(8,128)(2,1)S(1)}, bf16[512,128]{1,0:T(8,128)(2,1)S(1)}, u32[]{:S(2)}, u32[]{:S(2)}) collective-permute-start(bf16[512,128]{1,0:T(8,128)(2,1)S(1)} %convert_element_type.84), channel_id=1, source_target_pairs={{0,1},{1,2},{2,3},{3,0},{4,5},{5,6},{6,7},{7,4},{8,9},{9,10},{10,1... | collective-permute-start | bytes 393224 | tf_op jit(solution)/shard_map/ppermute | solution.py:91
  16.9 2.7 %collective-permute-start.1 = (bf16[512,128]{1,0:T(8,128)(2,1)S(1)}, bf16[512,128]{1,0:T(8,128)(2,1)S(1)}, u32[]{:S(2)}, u32[]{:S(2)}) collective-permute-start(bf16[512,128]{1,0:T(8,128)(2,1)S(1)} %convert_element_type.84), channel_id=1, source_target_pairs={{0,2},{1,3},{2,0},{3,1},{4,6},{5,7},{6,4},{7,5},{8,10},{9,11},{10,... | collective-permute-start | bytes 393224 | tf_op jit(solution)/shard_map/ppermute | solution.py:91
  21.9 5.7 %collective-permute-done.1 = bf16[512,128]{1,0:T(8,128)(2,1)S(1)} collective-permute-done((bf16[512,128]{1,0:T(8,128)(2,1)S(1)}, bf16[512,128]{1,0:T(8,128)(2,1)S(1)}, u32[]{:S(2)}, u32[]{:S(2)}) %collective-permute-start.1) | collective-permute-done | bytes 131104 | tf_op jit(solution)/shard_map/ppermute | solution.py:91
  28.7 18.5 %shard_map.86 = (bf16[2048,128]{1,0:T(8,128)(2,1)}, bf16[4096,128]{1,0:T(8,128)(2,1)}) custom-call(s32[64]{0:T(128)} %get-tuple-element.35.rows_ref, s32[64]{0:T(128)} %get-tuple-element.36.cols_ref, s32[1]{0:T(128)} %bitcast.29.count_ref, bf16[2048,128]{1,0:T(8,128)(2,1)} %pad_maximum_fusion.emb_ref, bf16[4096,128]{1,0:T(8,128)(2,1)} %copy-done.2, ...), custom_call_target="tpu_custom_call" | custom-call | flops 3221225472 | bytes 21495808 | tf_op jit(solution)/shard_map/pallas_call | solution.py:72
  48.5 10.8 %collective-permute-start.16 = (bf16[512,128]{1,0:T(8,128)(2,1)S(1)}, bf16[512,128]{1,0:T(8,128)(2,1)S(1)}, u32[]{:S(2)}, u32[]{:S(2)}) collective-permute-start(bf16[512,128]{1,0:T(8,128)(2,1)S(1)} %get-tuple-element.22), channel_id=1, source_target_pairs={{0,4},{4,8},{8,12},{12,16},{16,20},{20,24},{24,28},{28,0},{1,5},{5... | collective-permute-start | bytes 393224 | tf_op jit(solution)/shard_map/ppermute | solution.py:99
  59.3 22.5 %collective-permute-start.18 = (bf16[512,128]{1,0:T(8,128)(2,1)S(1)}, bf16[512,128]{1,0:T(8,128)(2,1)S(1)}, u32[]{:S(2)}, u32[]{:S(2)}) collective-permute-start(bf16[512,128]{1,0:T(8,128)(2,1)S(1)} %get-tuple-element.27), channel_id=1, source_target_pairs={{0,12},{4,16},{8,20},{12,24},{16,28},{20,0},{24,4},{28,8},{1,13},{... | collective-permute-start | bytes 393224 | tf_op jit(solution)/shard_map/ppermute | solution.py:99
  82.4 3.0 %collective-permute-start.21 = (bf16[512,128]{1,0:T(8,128)(2,1)S(1)}, bf16[512,128]{1,0:T(8,128)(2,1)S(1)}, u32[]{:S(2)}, u32[]{:S(2)}) collective-permute-start(bf16[512,128]{1,0:T(8,128)(2,1)S(1)} %get-tuple-element.24), channel_id=1, source_target_pairs={{0,24},{4,28},{8,0},{12,4},{16,8},{20,12},{24,16},{28,20},{1,25},{... | collective-permute-start | bytes 393224 | tf_op jit(solution)/shard_map/ppermute | solution.py:99
  85.4 2.5 %collective-permute-start.22 = (bf16[512,128]{1,0:T(8,128)(2,1)S(1)}, bf16[512,128]{1,0:T(8,128)(2,1)S(1)}, u32[]{:S(2)}, u32[]{:S(2)}) collective-permute-start(bf16[512,128]{1,0:T(8,128)(2,1)S(1)} %get-tuple-element.23), channel_id=1, source_target_pairs={{0,28},{4,0},{8,4},{12,8},{16,12},{20,16},{24,20},{28,24},{1,29},{... | collective-permute-start | bytes 393224 | tf_op jit(solution)/shard_map/ppermute | solution.py:99
  89.1 4.9 %collective-permute-start.11 = (bf16[512,128]{1,0:T(8,128)(2,1)S(1)}, bf16[512,128]{1,0:T(8,128)(2,1)S(1)}, u32[]{:S(2)}, u32[]{:S(2)}) collective-permute-start(bf16[512,128]{1,0:T(8,128)(2,1)S(1)} %get-tuple-element.34), channel_id=1, source_target_pairs={{0,2},{1,3},{2,0},{3,1},{4,6},{5,7},{6,4},{7,5},{8,10},{9,11},{10,... | collective-permute-start | bytes 393224 | tf_op jit(solution)/shard_map/ppermute | solution.py:99
  94.0 1.6 collective-permute-start.12
  96.7 2.0 collective-permute-start.23
  98.6 2.6 %collective-permute-start.24 = (bf16[512,128]{1,0:T(8,128)(2,1)S(1)}, bf16[512,128]{1,0:T(8,128)(2,1)S(1)}, u32[]{:S(2)}, u32[]{:S(2)}) collective-permute-start(bf16[512,128]{1,0:T(8,128)(2,1)S(1)} %get-tuple-element.11), channel_id=1, source_target_pairs={{0,8},{4,12},{8,16},{12,20},{16,24},{20,28},{24,0},{28,4},{1,9},{5... | collective-permute-start | bytes 393224 | tf_op jit(solution)/shard_map/ppermute | solution.py:91
  101.8 1.7 collective-permute-done.11
  108.1 4.0 %collective-permute-done.25 = bf16[512,128]{1,0:T(8,128)(2,1)S(1)} collective-permute-done((bf16[512,128]{1,0:T(8,128)(2,1)S(1)}, bf16[512,128]{1,0:T(8,128)(2,1)S(1)}, u32[]{:S(2)}, u32[]{:S(2)}) %collective-permute-start.25) | collective-permute-done | bytes 131104 | tf_op jit(solution)/shard_map/ppermute | solution.py:91
  113.6 2.9 %collective-permute-start.15 = (bf16[512,128]{1,0:T(8,128)(2,1)S(1)}, bf16[512,128]{1,0:T(8,128)(2,1)S(1)}, u32[]{:S(2)}, u32[]{:S(2)}) collective-permute-start(bf16[512,128]{1,0:T(8,128)(2,1)S(1)} %fusion.6), channel_id=1, source_target_pairs={{0,3},{1,0},{2,1},{3,2},{4,7},{5,4},{6,5},{7,6},{8,11},{9,8},{10,9... | collective-permute-start | bytes 393224 | tf_op jit(solution)/shard_map/ppermute | solution.py:91
  116.5 3.6 %collective-permute-done.13 = bf16[512,128]{1,0:T(8,128)(2,1)S(1)} collective-permute-done((bf16[512,128]{1,0:T(8,128)(2,1)S(1)}, bf16[512,128]{1,0:T(8,128)(2,1)S(1)}, u32[]{:S(2)}, u32[]{:S(2)}) %collective-permute-start.13) | collective-permute-done | bytes 131104 | tf_op jit(solution)/shard_map/ppermute | solution.py:91
  120.2 2.8 %collective-permute-done.14 = bf16[512,128]{1,0:T(8,128)(2,1)S(1)} collective-permute-done((bf16[512,128]{1,0:T(8,128)(2,1)S(1)}, bf16[512,128]{1,0:T(8,128)(2,1)S(1)}, u32[]{:S(2)}, u32[]{:S(2)}) %collective-permute-start.14) | collective-permute-done | bytes 131104 | tf_op jit(solution)/shard_map/ppermute | solution.py:91
  124.1 18.4 %shard_map.87 = (bf16[2048,128]{1,0:T(8,128)(2,1)}, bf16[4096,128]{1,0:T(8,128)(2,1)}) custom-call(s32[64]{0:T(128)} %get-tuple-element.35.rows_ref, s32[64]{0:T(128)} %get-tuple-element.36.cols_ref, s32[1]{0:T(128)} %bitcast.30.count_ref, bf16[2048,128]{1,0:T(8,128)(2,1)} %pad_maximum_fusion.1.emb_ref, bf16[4096,128]{1,0:T(8,128)(2,1)} %copy-done.1, ...), custom_call_target="tpu_custom_call" | custom-call | flops 3221225472 | bytes 21495808 | tf_op jit(solution)/shard_map/pallas_call | solution.py:72
  143.7 12.3 %collective-permute-start.33 = (bf16[512,128]{1,0:T(8,128)(2,1)S(1)}, bf16[512,128]{1,0:T(8,128)(2,1)S(1)}, u32[]{:S(2)}, u32[]{:S(2)}) collective-permute-start(bf16[512,128]{1,0:T(8,128)(2,1)S(1)} %get-tuple-element.15), channel_id=1, source_target_pairs={{0,4},{4,8},{8,12},{12,16},{16,20},{20,24},{24,28},{28,0},{1,5},{5... | collective-permute-start | bytes 393224 | tf_op jit(solution)/shard_map/ppermute | solution.py:99
  157.1 18.6 %collective-permute-start.30 = (bf16[512,128]{1,0:T(8,128)(2,1)S(1)}, bf16[512,128]{1,0:T(8,128)(2,1)S(1)}, u32[]{:S(2)}, u32[]{:S(2)}) collective-permute-start(bf16[512,128]{1,0:T(8,128)(2,1)S(1)} %get-tuple-element.29), channel_id=1, source_target_pairs={{0,1},{1,2},{2,3},{3,0},{4,5},{5,6},{6,7},{7,4},{8,9},{9,10},{10,1... | collective-permute-start | bytes 393224 | tf_op jit(solution)/shard_map/ppermute | solution.py:99
  175.7 5.2 %collective-permute-start.31 = (bf16[512,128]{1,0:T(8,128)(2,1)S(1)}, bf16[512,128]{1,0:T(8,128)(2,1)S(1)}, u32[]{:S(2)}, u32[]{:S(2)}) collective-permute-start(bf16[512,128]{1,0:T(8,128)(2,1)S(1)} %get-tuple-element.31), channel_id=1, source_target_pairs={{0,2},{1,3},{2,0},{3,1},{4,6},{5,7},{6,4},{7,5},{8,10},{9,11},{10,... | collective-permute-start | bytes 393224 | tf_op jit(solution)/shard_map/ppermute | solution.py:99
  181.1 2.1 %collective-permute-start.36 = (bf16[512,128]{1,0:T(8,128)(2,1)S(1)}, bf16[512,128]{1,0:T(8,128)(2,1)S(1)}, u32[]{:S(2)}, u32[]{:S(2)}) collective-permute-start(bf16[512,128]{1,0:T(8,128)(2,1)S(1)} %get-tuple-element.19), channel_id=1, source_target_pairs={{0,16},{4,20},{8,24},{12,28},{16,0},{20,4},{24,8},{28,12},{1,17},{... | collective-permute-start | bytes 393224 | tf_op jit(solution)/shard_map/ppermute | solution.py:99
  183.2 1.5 collective-permute-done.30
  184.7 5.0 %collective-permute-done.31 = bf16[512,128]{1,0:T(8,128)(2,1)S(1)} collective-permute-done((bf16[512,128]{1,0:T(8,128)(2,1)S(1)}, bf16[512,128]{1,0:T(8,128)(2,1)S(1)}, u32[]{:S(2)}, u32[]{:S(2)}) %collective-permute-start.31) | collective-permute-done | bytes 131104 | tf_op jit(solution)/shard_map/ppermute | solution.py:99
  189.7 2.6 %collective-permute-start.38 = (bf16[512,128]{1,0:T(8,128)(2,1)S(1)}, bf16[512,128]{1,0:T(8,128)(2,1)S(1)}, u32[]{:S(2)}, u32[]{:S(2)}) collective-permute-start(bf16[512,128]{1,0:T(8,128)(2,1)S(1)} %get-tuple-element.17), channel_id=1, source_target_pairs={{0,24},{4,28},{8,0},{12,4},{16,8},{20,12},{24,16},{28,20},{1,25},{... | collective-permute-start | bytes 393224 | tf_op jit(solution)/shard_map/ppermute | solution.py:99
  192.4 1.8 multiply_add_fusion.1
  195.2 1.4 collective-permute-done.39
  196.6 1.8 multiply_add_fusion
  (85 shorter events, 23.4 us)
Async XLA Ops:
  1.6 8.9 %collective-permute-start.3 = (bf16[512,128]{1,0:T(8,128)(2,1)S(1)}, bf16[512,128]{1,0:T(8,128)(2,1)S(1)}, u32[]{:S(2)}, u32[]{:S(2)}) collective-permute-start(bf16[512,128]{1,0:T(8,128)(2,1)S(1)} %get-tuple-element.14), channel_id=1, source_target_pairs={{0,4},{4,8},{8,12},{12,16},{16,20},{20,24},{24,28},{28,0},{1,5},{5... | collective-permute-start | bytes 393224 | tf_op jit(solution)/shard_map/ppermute | solution.py:91
  2.1 9.9 %collective-permute-start.4 = (bf16[512,128]{1,0:T(8,128)(2,1)S(1)}, bf16[512,128]{1,0:T(8,128)(2,1)S(1)}, u32[]{:S(2)}, u32[]{:S(2)}) collective-permute-start(bf16[512,128]{1,0:T(8,128)(2,1)S(1)} %get-tuple-element.14), channel_id=1, source_target_pairs={{0,8},{4,12},{8,16},{12,20},{16,24},{20,28},{24,0},{28,4},{1,9},{5... | collective-permute-start | bytes 393224 | tf_op jit(solution)/shard_map/ppermute | solution.py:91
  4.7 9.9 %collective-permute-start.5 = (bf16[512,128]{1,0:T(8,128)(2,1)S(1)}, bf16[512,128]{1,0:T(8,128)(2,1)S(1)}, u32[]{:S(2)}, u32[]{:S(2)}) collective-permute-start(bf16[512,128]{1,0:T(8,128)(2,1)S(1)} %get-tuple-element.14), channel_id=1, source_target_pairs={{0,12},{4,16},{8,20},{12,24},{16,28},{20,0},{24,4},{28,8},{1,13},{... | collective-permute-start | bytes 393224 | tf_op jit(solution)/shard_map/ppermute | solution.py:91
  7.0 9.9 %collective-permute-start.6 = (bf16[512,128]{1,0:T(8,128)(2,1)S(1)}, bf16[512,128]{1,0:T(8,128)(2,1)S(1)}, u32[]{:S(2)}, u32[]{:S(2)}) collective-permute-start(bf16[512,128]{1,0:T(8,128)(2,1)S(1)} %get-tuple-element.14), channel_id=1, source_target_pairs={{0,16},{4,20},{8,24},{12,28},{16,0},{20,4},{24,8},{28,12},{1,17},{... | collective-permute-start | bytes 393224 | tf_op jit(solution)/shard_map/ppermute | solution.py:91
  7.5 12.1 %collective-permute-start.7 = (bf16[512,128]{1,0:T(8,128)(2,1)S(1)}, bf16[512,128]{1,0:T(8,128)(2,1)S(1)}, u32[]{:S(2)}, u32[]{:S(2)}) collective-permute-start(bf16[512,128]{1,0:T(8,128)(2,1)S(1)} %get-tuple-element.14), channel_id=1, source_target_pairs={{0,20},{4,24},{8,28},{12,0},{16,4},{20,8},{24,12},{28,16},{1,21},{... | collective-permute-start | bytes 393224 | tf_op jit(solution)/shard_map/ppermute | solution.py:91
  10.5 10.6 %collective-permute-start.8 = (bf16[512,128]{1,0:T(8,128)(2,1)S(1)}, bf16[512,128]{1,0:T(8,128)(2,1)S(1)}, u32[]{:S(2)}, u32[]{:S(2)}) collective-permute-start(bf16[512,128]{1,0:T(8,128)(2,1)S(1)} %get-tuple-element.14), channel_id=1, source_target_pairs={{0,24},{4,28},{8,0},{12,4},{16,8},{20,12},{24,16},{28,20},{1,25},{... | collective-permute-start | bytes 393224 | tf_op jit(solution)/shard_map/ppermute | solution.py:91
  12.0 9.1 %collective-permute-start.9 = (bf16[512,128]{1,0:T(8,128)(2,1)S(1)}, bf16[512,128]{1,0:T(8,128)(2,1)S(1)}, u32[]{:S(2)}, u32[]{:S(2)}) collective-permute-start(bf16[512,128]{1,0:T(8,128)(2,1)S(1)} %get-tuple-element.14), channel_id=1, source_target_pairs={{0,28},{4,0},{8,4},{12,8},{16,12},{20,16},{24,20},{28,24},{1,29},{... | collective-permute-start | bytes 393224 | tf_op jit(solution)/shard_map/ppermute | solution.py:91
  16.9 10.7 %collective-permute-start.1 = (bf16[512,128]{1,0:T(8,128)(2,1)S(1)}, bf16[512,128]{1,0:T(8,128)(2,1)S(1)}, u32[]{:S(2)}, u32[]{:S(2)}) collective-permute-start(bf16[512,128]{1,0:T(8,128)(2,1)S(1)} %convert_element_type.84), channel_id=1, source_target_pairs={{0,2},{1,3},{2,0},{3,1},{4,6},{5,7},{6,4},{7,5},{8,10},{9,11},{10,... | collective-permute-start | bytes 393224 | tf_op jit(solution)/shard_map/ppermute | solution.py:91
  48.5 33.9 %collective-permute-start.16 = (bf16[512,128]{1,0:T(8,128)(2,1)S(1)}, bf16[512,128]{1,0:T(8,128)(2,1)S(1)}, u32[]{:S(2)}, u32[]{:S(2)}) collective-permute-start(bf16[512,128]{1,0:T(8,128)(2,1)S(1)} %get-tuple-element.22), channel_id=1, source_target_pairs={{0,4},{4,8},{8,12},{12,16},{16,20},{20,24},{24,28},{28,0},{1,5},{5... | collective-permute-start | bytes 393224 | tf_op jit(solution)/shard_map/ppermute | solution.py:99
  59.3 26.1 %collective-permute-start.17 = (bf16[512,128]{1,0:T(8,128)(2,1)S(1)}, bf16[512,128]{1,0:T(8,128)(2,1)S(1)}, u32[]{:S(2)}, u32[]{:S(2)}) collective-permute-start(bf16[512,128]{1,0:T(8,128)(2,1)S(1)} %get-tuple-element.28), channel_id=1, source_target_pairs={{0,8},{4,12},{8,16},{12,20},{16,24},{20,28},{24,0},{28,4},{1,9},{5... | collective-permute-start | bytes 393224 | tf_op jit(solution)/shard_map/ppermute | solution.py:99
  59.3 29.7 %collective-permute-start.18 = (bf16[512,128]{1,0:T(8,128)(2,1)S(1)}, bf16[512,128]{1,0:T(8,128)(2,1)S(1)}, u32[]{:S(2)}, u32[]{:S(2)}) collective-permute-start(bf16[512,128]{1,0:T(8,128)(2,1)S(1)} %get-tuple-element.27), channel_id=1, source_target_pairs={{0,12},{4,16},{8,20},{12,24},{16,28},{20,0},{24,4},{28,8},{1,13},{... | collective-permute-start | bytes 393224 | tf_op jit(solution)/shard_map/ppermute | solution.py:99
  81.8 12.2 %collective-permute-start.20 = (bf16[512,128]{1,0:T(8,128)(2,1)S(1)}, bf16[512,128]{1,0:T(8,128)(2,1)S(1)}, u32[]{:S(2)}, u32[]{:S(2)}) collective-permute-start(bf16[512,128]{1,0:T(8,128)(2,1)S(1)} %get-tuple-element.25), channel_id=1, source_target_pairs={{0,20},{4,24},{8,28},{12,0},{16,4},{20,8},{24,12},{28,16},{1,21},{... | collective-permute-start | bytes 393224 | tf_op jit(solution)/shard_map/ppermute | solution.py:99
  82.4 13.2 %collective-permute-start.21 = (bf16[512,128]{1,0:T(8,128)(2,1)S(1)}, bf16[512,128]{1,0:T(8,128)(2,1)S(1)}, u32[]{:S(2)}, u32[]{:S(2)}) collective-permute-start(bf16[512,128]{1,0:T(8,128)(2,1)S(1)} %get-tuple-element.24), channel_id=1, source_target_pairs={{0,24},{4,28},{8,0},{12,4},{16,8},{20,12},{24,16},{28,20},{1,25},{... | collective-permute-start | bytes 393224 | tf_op jit(solution)/shard_map/ppermute | solution.py:99
  85.4 10.2 %collective-permute-start.22 = (bf16[512,128]{1,0:T(8,128)(2,1)S(1)}, bf16[512,128]{1,0:T(8,128)(2,1)S(1)}, u32[]{:S(2)}, u32[]{:S(2)}) collective-permute-start(bf16[512,128]{1,0:T(8,128)(2,1)S(1)} %get-tuple-element.23), channel_id=1, source_target_pairs={{0,28},{4,0},{8,4},{12,8},{16,12},{20,16},{24,20},{28,24},{1,29},{... | collective-permute-start | bytes 393224 | tf_op jit(solution)/shard_map/ppermute | solution.py:99
  89.0 12.3 %collective-permute-start.10 = (bf16[512,128]{1,0:T(8,128)(2,1)S(1)}, bf16[512,128]{1,0:T(8,128)(2,1)S(1)}, u32[]{:S(2)}, u32[]{:S(2)}) collective-permute-start(bf16[512,128]{1,0:T(8,128)(2,1)S(1)} %get-tuple-element.32), channel_id=1, source_target_pairs={{0,1},{1,2},{2,3},{3,0},{4,5},{5,6},{6,7},{7,4},{8,9},{9,10},{10,1... | collective-permute-start | bytes 393224 | tf_op jit(solution)/shard_map/ppermute | solution.py:99
  89.1 14.4 %collective-permute-start.11 = (bf16[512,128]{1,0:T(8,128)(2,1)S(1)}, bf16[512,128]{1,0:T(8,128)(2,1)S(1)}, u32[]{:S(2)}, u32[]{:S(2)}) collective-permute-start(bf16[512,128]{1,0:T(8,128)(2,1)S(1)} %get-tuple-element.34), channel_id=1, source_target_pairs={{0,2},{1,3},{2,0},{3,1},{4,6},{5,7},{6,4},{7,5},{8,10},{9,11},{10,... | collective-permute-start | bytes 393224 | tf_op jit(solution)/shard_map/ppermute | solution.py:99
  94.0 10.1 %collective-permute-start.12 = (bf16[512,128]{1,0:T(8,128)(2,1)S(1)}, bf16[512,128]{1,0:T(8,128)(2,1)S(1)}, u32[]{:S(2)}, u32[]{:S(2)}) collective-permute-start(bf16[512,128]{1,0:T(8,128)(2,1)S(1)} %get-tuple-element.33), channel_id=1, source_target_pairs={{0,3},{1,0},{2,1},{3,2},{4,7},{5,4},{6,5},{7,6},{8,11},{9,8},{10,9... | collective-permute-start | bytes 393224 | tf_op jit(solution)/shard_map/ppermute | solution.py:99
  96.7 9.4 %collective-permute-start.23 = (bf16[512,128]{1,0:T(8,128)(2,1)S(1)}, bf16[512,128]{1,0:T(8,128)(2,1)S(1)}, u32[]{:S(2)}, u32[]{:S(2)}) collective-permute-start(bf16[512,128]{1,0:T(8,128)(2,1)S(1)} %get-tuple-element.11), channel_id=1, source_target_pairs={{0,4},{4,8},{8,12},{12,16},{16,20},{20,24},{24,28},{28,0},{1,5},{5... | collective-permute-start | bytes 393224 | tf_op jit(solution)/shard_map/ppermute | solution.py:91
  101.3 10.9 %collective-permute-start.25 = (bf16[512,128]{1,0:T(8,128)(2,1)S(1)}, bf16[512,128]{1,0:T(8,128)(2,1)S(1)}, u32[]{:S(2)}, u32[]{:S(2)}) collective-permute-start(bf16[512,128]{1,0:T(8,128)(2,1)S(1)} %get-tuple-element.11), channel_id=1, source_target_pairs={{0,12},{4,16},{8,20},{12,24},{16,28},{20,0},{24,4},{28,8},{1,13},{... | collective-permute-start | bytes 393224 | tf_op jit(solution)/shard_map/ppermute | solution.py:91
  104.1 9.4 %collective-permute-start.27 = (bf16[512,128]{1,0:T(8,128)(2,1)S(1)}, bf16[512,128]{1,0:T(8,128)(2,1)S(1)}, u32[]{:S(2)}, u32[]{:S(2)}) collective-permute-start(bf16[512,128]{1,0:T(8,128)(2,1)S(1)} %get-tuple-element.11), channel_id=1, source_target_pairs={{0,20},{4,24},{8,28},{12,0},{16,4},{20,8},{24,12},{28,16},{1,21},{... | collective-permute-start | bytes 393224 | tf_op jit(solution)/shard_map/ppermute | solution.py:91
  106.1 10.4 %collective-permute-start.28 = (bf16[512,128]{1,0:T(8,128)(2,1)S(1)}, bf16[512,128]{1,0:T(8,128)(2,1)S(1)}, u32[]{:S(2)}, u32[]{:S(2)}) collective-permute-start(bf16[512,128]{1,0:T(8,128)(2,1)S(1)} %get-tuple-element.11), channel_id=1, source_target_pairs={{0,24},{4,28},{8,0},{12,4},{16,8},{20,12},{24,16},{28,20},{1,25},{... | collective-permute-start | bytes 393224 | tf_op jit(solution)/shard_map/ppermute | solution.py:91
  107.4 9.1 %collective-permute-start.29 = (bf16[512,128]{1,0:T(8,128)(2,1)S(1)}, bf16[512,128]{1,0:T(8,128)(2,1)S(1)}, u32[]{:S(2)}, u32[]{:S(2)}) collective-permute-start(bf16[512,128]{1,0:T(8,128)(2,1)S(1)} %get-tuple-element.11), channel_id=1, source_target_pairs={{0,28},{4,0},{8,4},{12,8},{16,12},{20,16},{24,20},{28,24},{1,29},{... | collective-permute-start | bytes 393224 | tf_op jit(solution)/shard_map/ppermute | solution.py:91
  112.3 10.6 %collective-permute-start.14 = (bf16[512,128]{1,0:T(8,128)(2,1)S(1)}, bf16[512,128]{1,0:T(8,128)(2,1)S(1)}, u32[]{:S(2)}, u32[]{:S(2)}) collective-permute-start(bf16[512,128]{1,0:T(8,128)(2,1)S(1)} %fusion.6), channel_id=1, source_target_pairs={{0,2},{1,3},{2,0},{3,1},{4,6},{5,7},{6,4},{7,5},{8,10},{9,11},{10,... | collective-permute-start | bytes 393224 | tf_op jit(solution)/shard_map/ppermute | solution.py:91
  113.6 9.7 %collective-permute-start.15 = (bf16[512,128]{1,0:T(8,128)(2,1)S(1)}, bf16[512,128]{1,0:T(8,128)(2,1)S(1)}, u32[]{:S(2)}, u32[]{:S(2)}) collective-permute-start(bf16[512,128]{1,0:T(8,128)(2,1)S(1)} %fusion.6), channel_id=1, source_target_pairs={{0,3},{1,0},{2,1},{3,2},{4,7},{5,4},{6,5},{7,6},{8,11},{9,8},{10,9... | collective-permute-start | bytes 393224 | tf_op jit(solution)/shard_map/ppermute | solution.py:91
  143.7 37.1 %collective-permute-start.33 = (bf16[512,128]{1,0:T(8,128)(2,1)S(1)}, bf16[512,128]{1,0:T(8,128)(2,1)S(1)}, u32[]{:S(2)}, u32[]{:S(2)}) collective-permute-start(bf16[512,128]{1,0:T(8,128)(2,1)S(1)} %get-tuple-element.15), channel_id=1, source_target_pairs={{0,4},{4,8},{8,12},{12,16},{16,20},{20,24},{24,28},{28,0},{1,5},{5... | collective-permute-start | bytes 393224 | tf_op jit(solution)/shard_map/ppermute | solution.py:99
  156.0 25.1 %collective-permute-start.34 = (bf16[512,128]{1,0:T(8,128)(2,1)S(1)}, bf16[512,128]{1,0:T(8,128)(2,1)S(1)}, u32[]{:S(2)}, u32[]{:S(2)}) collective-permute-start(bf16[512,128]{1,0:T(8,128)(2,1)S(1)} %get-tuple-element.21), channel_id=1, source_target_pairs={{0,8},{4,12},{8,16},{12,20},{16,24},{20,28},{24,0},{28,4},{1,9},{5... | collective-permute-start | bytes 393224 | tf_op jit(solution)/shard_map/ppermute | solution.py:99
  157.1 27.6 %collective-permute-start.30 = (bf16[512,128]{1,0:T(8,128)(2,1)S(1)}, bf16[512,128]{1,0:T(8,128)(2,1)S(1)}, u32[]{:S(2)}, u32[]{:S(2)}) collective-permute-start(bf16[512,128]{1,0:T(8,128)(2,1)S(1)} %get-tuple-element.29), channel_id=1, source_target_pairs={{0,1},{1,2},{2,3},{3,0},{4,5},{5,6},{6,7},{7,4},{8,9},{9,10},{10,1... | collective-permute-start | bytes 393224 | tf_op jit(solution)/shard_map/ppermute | solution.py:99
  175.7 14.0 %collective-permute-start.31 = (bf16[512,128]{1,0:T(8,128)(2,1)S(1)}, bf16[512,128]{1,0:T(8,128)(2,1)S(1)}, u32[]{:S(2)}, u32[]{:S(2)}) collective-permute-start(bf16[512,128]{1,0:T(8,128)(2,1)S(1)} %get-tuple-element.31), channel_id=1, source_target_pairs={{0,2},{1,3},{2,0},{3,1},{4,6},{5,7},{6,4},{7,5},{8,10},{9,11},{10,... | collective-permute-start | bytes 393224 | tf_op jit(solution)/shard_map/ppermute | solution.py:99
  180.9 11.5 %collective-permute-start.32 = (bf16[512,128]{1,0:T(8,128)(2,1)S(1)}, bf16[512,128]{1,0:T(8,128)(2,1)S(1)}, u32[]{:S(2)}, u32[]{:S(2)}) collective-permute-start(bf16[512,128]{1,0:T(8,128)(2,1)S(1)} %get-tuple-element.30), channel_id=1, source_target_pairs={{0,3},{1,0},{2,1},{3,2},{4,7},{5,4},{6,5},{7,6},{8,11},{9,8},{10,9... | collective-permute-start | bytes 393224 | tf_op jit(solution)/shard_map/ppermute | solution.py:99
  180.9 13.4 %collective-permute-start.35 = (bf16[512,128]{1,0:T(8,128)(2,1)S(1)}, bf16[512,128]{1,0:T(8,128)(2,1)S(1)}, u32[]{:S(2)}, u32[]{:S(2)}) collective-permute-start(bf16[512,128]{1,0:T(8,128)(2,1)S(1)} %get-tuple-element.20), channel_id=1, source_target_pairs={{0,12},{4,16},{8,20},{12,24},{16,28},{20,0},{24,4},{28,8},{1,13},{... | collective-permute-start | bytes 393224 | tf_op jit(solution)/shard_map/ppermute | solution.py:99
  181.1 13.1 %collective-permute-start.36 = (bf16[512,128]{1,0:T(8,128)(2,1)S(1)}, bf16[512,128]{1,0:T(8,128)(2,1)S(1)}, u32[]{:S(2)}, u32[]{:S(2)}) collective-permute-start(bf16[512,128]{1,0:T(8,128)(2,1)S(1)} %get-tuple-element.19), channel_id=1, source_target_pairs={{0,16},{4,20},{8,24},{12,28},{16,0},{20,4},{24,8},{28,12},{1,17},{... | collective-permute-start | bytes 393224 | tf_op jit(solution)/shard_map/ppermute | solution.py:99
  184.7 9.5 %collective-permute-start.37 = (bf16[512,128]{1,0:T(8,128)(2,1)S(1)}, bf16[512,128]{1,0:T(8,128)(2,1)S(1)}, u32[]{:S(2)}, u32[]{:S(2)}) collective-permute-start(bf16[512,128]{1,0:T(8,128)(2,1)S(1)} %get-tuple-element.18), channel_id=1, source_target_pairs={{0,20},{4,24},{8,28},{12,0},{16,4},{20,8},{24,12},{28,16},{1,21},{... | collective-permute-start | bytes 393224 | tf_op jit(solution)/shard_map/ppermute | solution.py:99
  (12 other events, 216.5 us)

commit v3 on v2

v3 whole, which is shorter than its diff:
```python
import functools

import jax
import jax.numpy as jnp
from jax import lax
from jax.experimental import pallas as pl
from jax.experimental.pallas import tpu as pltpu
from jax.sharding import PartitionSpec as P

ITERS = 2


def sweep_kernel(tile, group, rows_ref, cols_ref, count_ref, emb_ref, embt_ref, ctx_ref, pos_ref, neg_ref,
                 gemb_ref, gctxt_ref, acc_e, acc_ct):
    k = pl.program_id(0)
    n = count_ref[0]

    @pl.when(k == 0)
    def _():
        acc_e[...] = jnp.zeros_like(acc_e)
        acc_ct[...] = jnp.zeros_like(acc_ct)

    def visit(j):
        slot = k * group + j
        r0 = pl.multiple_of(rows_ref[slot] * tile, tile)
        c0 = pl.multiple_of(cols_ref[slot] * tile, tile)
        e = emb_ref[pl.ds(r0, tile), :]
        c = ctx_ref[pl.ds(c0, tile), :]
        score = lax.dot_general(e, c, (((1,), (1,)), ((), ())), preferred_element_type=jnp.float32)
        positive = pos_ref[j].astype(jnp.float32)
        negative = neg_ref[j].astype(jnp.float32)
        t = jnp.tanh(score * 0.5)
        coeff = (0.5 * ((positive - negative) - (positive + negative) * t)).astype(jnp.bfloat16)
        acc_e[pl.ds(r0, tile), :] += jnp.dot(coeff, c, preferred_element_type=jnp.float32)
        acc_ct[:, pl.ds(c0, tile)] += jnp.dot(
            embt_ref[:, pl.ds(r0, tile)], coeff, preferred_element_type=jnp.float32
        )

    full = (k + 1) * group <= n

    @pl.when(full)
    def _():
        for j in range(group):
            visit(j)

    @pl.when(jnp.logical_not(full))
    def _():
        for j in range(group):
            pl.when(k * group + j < n)(functools.partial(visit, j))

    @pl.when(k == pl.num_programs(0) - 1)
    def _():
        gemb_ref[...] = acc_e[...].astype(gemb_ref.dtype)
        gctxt_ref[...] = acc_ct[...].astype(gctxt_ref.dtype)


def tile_sweep(pos, neg, rows, cols, count, emb_low, ctx_low):
    cap, tile, _ = pos.shape
    ne, dim = emb_low.shape
    nc = ctx_low.shape[0]
    group = next(g for g in (8, 4, 2, 1) if cap % g == 0)

    def slot(k, rows_ref, cols_ref, count_ref):
        last = jnp.maximum((count_ref[0] + group - 1) // group - 1, 0)
        return (jnp.minimum(k, last), 0, 0)

    grid_spec = pltpu.PrefetchScalarGridSpec(
        num_scalar_prefetch=3,
        grid=(cap // group,),
        in_specs=[
            pl.BlockSpec((ne, dim), lambda k, *_: (0, 0)),
            pl.BlockSpec((dim, ne), lambda k, *_: (0, 0)),
            pl.BlockSpec((nc, dim), lambda k, *_: (0, 0)),
            pl.BlockSpec((group, tile, tile), slot),
            pl.BlockSpec((group, tile, tile), slot),
        ],
        out_specs=[
            pl.BlockSpec((ne, dim), lambda k, *_: (0, 0)),
            pl.BlockSpec((dim, nc), lambda k, *_: (0, 0)),
        ],
        scratch_shapes=[
            pltpu.VMEM((ne, dim), jnp.float32),
            pltpu.VMEM((dim, nc), jnp.float32),
        ],
    )
    flops = cap * 3 * 2 * tile * tile * dim
    return pl.pallas_call(
        functools.partial(sweep_kernel, tile, group),
        grid_spec=grid_spec,
        out_shape=(
            jax.ShapeDtypeStruct((ne, dim), jnp.bfloat16),
            jax.ShapeDtypeStruct((dim, nc), jnp.bfloat16),
        ),
        compiler_params=pltpu.CompilerParams(dimension_semantics=("arbitrary",)),
        cost_estimate=pl.CostEstimate(
            flops=flops,
            transcendentals=cap * tile * tile,
            bytes_accessed=2 * cap * tile * tile * 2 + 3 * (ne + nc) * dim * 2,
        ),
    )(rows, cols, count.reshape(1), emb_low, emb_low.T, ctx_low, pos, neg)


def gather_rotated(x, axis, n):
    pieces = [x]
    for s in range(1, n):
        pieces.append(lax.ppermute(x, axis, [(i, (i + s) % n) for i in range(n)]))
    return jnp.concatenate(pieces, axis=0)


def scatter_rotated(g, axis, n):
    chunks = g.reshape(n, -1, g.shape[-1])
    total = chunks[0].astype(jnp.float32)
    for s in range(1, n):
        got = lax.ppermute(chunks[(n - s) % n], axis, [(i, (i + s) % n) for i in range(n)])
        total = total + got.astype(jnp.float32)
    return total


def scatter_rotated_t(gt, axis, n):
    width = gt.shape[1] // n
    chunk = lambda s: gt[:, s * width:(s + 1) * width]
    total = chunk(0).astype(jnp.float32)
    for s in range(1, n):
        got = lax.ppermute(chunk((n - s) % n), axis, [(i, (i + s) % n) for i in range(n)])
        total = total + got.astype(jnp.float32)
    return total.T


def rotate_index(index, me, n, per_run):
    run = index // per_run
    return ((me - run) % n) * per_run + index % per_run


def body(emb_in, ctx_in, pos_weight, neg_weight, tile_row, tile_col, tile_count):
    n_row = lax.axis_size("row")
    n_col = lax.axis_size("col")
    me_row = lax.axis_index("row")
    me_col = lax.axis_index("col")
    pos = pos_weight[0, 0]
    neg = neg_weight[0, 0]
    tile = pos.shape[-1]
    per_run = emb_in.shape[0] // tile
    rows = rotate_index(tile_row[0, 0], me_col, n_col, per_run)
    cols = rotate_index(tile_col[0, 0], me_row, n_row, per_run)
    count = tile_count[0, 0]
    emb = emb_in
    ctx = ctx_in
    for iteration in range(ITERS):
        emb_low = gather_rotated(emb.astype(jnp.bfloat16), "col", n_col)
        ctx_low = gather_rotated(ctx.astype(jnp.bfloat16), "row", n_row)
        grad_emb, grad_ctx_t = tile_sweep(pos, neg, rows, cols, count, emb_low, ctx_low)
        emb = emb + 0.05 * scatter_rotated(grad_emb, "col", n_col)
        ctx = ctx + 0.05 * scatter_rotated_t(grad_ctx_t, "row", n_row)
    return (emb, ctx)


def solution(mesh):
    in_specs = (
        P(("row", "col"), None),
        P(("row", "col"), None),
        P("row", "col", None, None, None),
        P("row", "col", None, None, None),
        P("row", "col", None),
        P("row", "col", None),
        P("row", "col"),
    )
    out_specs = (P(("row", "col"), None), P(("row", "col"), None))
    return jax.shard_map(body, mesh=mesh, in_specs=in_specs, out_specs=out_specs, check_vma=False)
```

time: 201 us -> 142 us (0.71)
  starting transfers between devices: 116 us -> 72 us
  Pallas kernels: 36.9 us -> 13.7 us
  local copies, waits for them, and re-layouts: 4.99 us -> 13.4 us
  waiting for transfers between devices: 28.9 us -> 31 us
    ppermute x20 -> x6, starting transfers between devices: 87 us -> 15.9 us  [scatter_rotated(): lax.ppermute(chunks[(n - s) % n], axis, [(i, (i + s) % n) for i in range(...]
    ppermute x0 -> x14, starting transfers between devices: none -> 29.1 us  [scatter_rotated_t(): lax.ppermute(chunk((n - s) % n), axis, [(i, (i + s) % n) for i in range(n)])]
    pallas_call x2, Pallas kernels: 36.9 us -> 13.7 us  [tile_sweep(): pl.pallas_call(functools.partial(sweep_kernel, tile, group), grid_spec=gr...]
    pallas_call x0 -> x4, local copies, waits for them, and re-layouts: none -> 5.71 us  [tile_sweep(): pl.pallas_call(functools.partial(sweep_kernel, tile, group), grid_spec=gr...]
    slice x4 -> x2, local copies, waits for them, and re-layouts: 4.72 us -> 0.06 us  [scatter_rotated(): chunks[(n - s) % n]]
    unnamed x20 -> x28, local copies, waits for them, and re-layouts: 0.24 us -> 4.16 us
    ppermute x20, waiting for transfers between devices: 18.3 us -> 14.5 us  [gather_rotated(): pieces.append(lax.ppermute(x, axis, [(i, (i + s) % n) for i in range(n)]))]
    ppermute x0 -> x14, waiting for transfers between devices: none -> 3.45 us  [scatter_rotated_t(): lax.ppermute(chunk((n - s) % n), axis, [(i, (i + s) % n) for i in range(n)])]
  transfers between devices with their start and end apart: 40 -> 40, of which waited for: 16 -> 15; matrix products, arithmetic and copies ran while one was open for 4% -> 9% of each run, Pallas kernels for 0% -> 0%
where the time goes in v3:
time: 142 us; the launch traced here: 141 us
  starting transfers between devices  72 us (51%)
  waiting for transfers between devices  31 us (22%)
  Pallas kernels  13.7 us (10%)
  local copies, waits for them, and re-layouts  13.4 us (9%)
  other arithmetic  9.22 us (6%)
  between operations  1.62 us (1%)
    ppermute x14, starting transfers between devices, scatter_rotated_t(): lax.ppermute(chunk((n - s) % n), axis, [(i, (i + s) % n) for i in range(n)])  29.1 us
    ppermute x20, starting transfers between devices, gather_rotated(): pieces.append(lax.ppermute(x, axis, [(i, (i + s) % n) for i in range(n)]))  27 us
    ppermute x6, starting transfers between devices, scatter_rotated(): lax.ppermute(chunks[(n - s) % n], axis, [(i, (i + s) % n) for i in range(...  15.9 us
    ppermute x20, waiting for transfers between devices, gather_rotated(): pieces.append(lax.ppermute(x, axis, [(i, (i + s) % n) for i in range(n)]))  14.5 us
    pallas_call x2, Pallas kernels, tile_sweep(): pl.pallas_call(functools.partial(sweep_kernel, tile, group), grid_spec=gr...  13.7 us
    ppermute x6, waiting for transfers between devices, scatter_rotated(): lax.ppermute(chunks[(n - s) % n], axis, [(i, (i + s) % n) for i in range(...  13 us
    pallas_call x4, local copies, waits for them, and re-layouts, tile_sweep(): pl.pallas_call(functools.partial(sweep_kernel, tile, group), grid_spec=gr...  5.71 us
    unnamed x28, local copies, waits for them, and re-layouts  4.16 us
  transfers between devices with their start and end apart: 40, of which 15 were waited for; matrix products, arithmetic and copies ran while one was open for 9% of the time, Pallas kernels for 0%

profile of v3, /device:TPU:0, one launch (start us, length us, event | category | flops | bytes accessed | tf_op | source)
XLA Modules:
  0.0 140.9 jit_solution(1554885559023631754)
XLA Ops:
  2.1 2.6 %collective-permute-start.4 = (bf16[512,128]{1,0:T(8,128)(2,1)S(1)}, bf16[512,128]{1,0:T(8,128)(2,1)S(1)}, u32[]{:S(2)}, u32[]{:S(2)}) collective-permute-start(bf16[512,128]{1,0:T(8,128)(2,1)S(1)} %get-tuple-element.16), channel_id=1, source_target_pairs={{0,8},{4,12},{8,16},{12,20},{16,24},{20,28},{24,0},{28,4},{1,9},{5... | collective-permute-start | bytes 393224 | tf_op jit(solution)/shard_map/ppermute | solution.py:106
  5.8 1.6 %collective-permute-start = (bf16[512,128]{0,1:T(8,128)(2,1)S(1)}, bf16[512,128]{0,1:T(8,128)(2,1)S(1)}, u32[]{:S(2)}, u32[]{:S(2)}) collective-permute-start(bf16[512,128]{0,1:T(8,128)(2,1)S(1)} %convert_element_type.84), channel_id=1, source_target_pairs={{0,1},{1,2},{2,3},{3,0},{4,5},{5,6},{6,7},{7,4},{8,9},{9,10},{10,1... | collective-permute-start | bytes 393224 | tf_op jit(solution)/shard_map/ppermute | solution.py:106
  7.4 2.6 %collective-permute-start.1 = (bf16[512,128]{0,1:T(8,128)(2,1)S(1)}, bf16[512,128]{0,1:T(8,128)(2,1)S(1)}, u32[]{:S(2)}, u32[]{:S(2)}) collective-permute-start(bf16[512,128]{0,1:T(8,128)(2,1)S(1)} %convert_element_type.84), channel_id=1, source_target_pairs={{0,2},{1,3},{2,0},{3,1},{4,6},{5,7},{6,4},{7,5},{8,10},{9,11},{10,... | collective-permute-start | bytes 393224 | tf_op jit(solution)/shard_map/ppermute | solution.py:106
  15.3 4.3 %collective-permute-done.1 = bf16[512,128]{0,1:T(8,128)(2,1)S(1)} collective-permute-done((bf16[512,128]{0,1:T(8,128)(2,1)S(1)}, bf16[512,128]{0,1:T(8,128)(2,1)S(1)}, u32[]{:S(2)}, u32[]{:S(2)}) %collective-permute-start.1) | collective-permute-done | bytes 131104 | tf_op jit(solution)/shard_map/ppermute | solution.py:106
  22.0 1.5 %collective-permute-start.8 = (bf16[512,128]{1,0:T(8,128)(2,1)S(1)}, bf16[512,128]{1,0:T(8,128)(2,1)S(1)}, u32[]{:S(2)}, u32[]{:S(2)}) collective-permute-start(bf16[512,128]{1,0:T(8,128)(2,1)S(1)} %get-tuple-element.16), channel_id=1, source_target_pairs={{0,24},{4,28},{8,0},{12,4},{16,8},{20,12},{24,16},{28,20},{1,25},{... | collective-permute-start | bytes 393224 | tf_op jit(solution)/shard_map/ppermute | solution.py:106
  26.2 1.6 %collective-permute-done.8 = bf16[512,128]{1,0:T(8,128)(2,1)S(1)} collective-permute-done((bf16[512,128]{1,0:T(8,128)(2,1)S(1)}, bf16[512,128]{1,0:T(8,128)(2,1)S(1)}, u32[]{:S(2)}, u32[]{:S(2)}) %collective-permute-start.8) | collective-permute-done | bytes 131104 | tf_op jit(solution)/shard_map/ppermute | solution.py:106
  29.8 6.9 %shard_map.86 = (bf16[2048,128]{1,0:T(8,128)(2,1)}, bf16[128,4096]{1,0:T(8,128)(2,1)}) custom-call(s32[64]{0:T(128)} %get-tuple-element.41.rows_ref, s32[64]{0:T(128)} %get-tuple-element.42.cols_ref, s32[1]{0:T(128)} %bitcast.38.count_ref, bf16[2048,128]{1,0:T(8,128)(2,1)} %copy.10.emb_ref, bf16[128,2048]{1,0:T(8,128)(2,1)} %get-tuple-element.39.embt_ref, ...), custom_call_target="tpu_custom_call" | custom-call | flops 3221225472 | bytes 21495808 | tf_op jit(solution)/shard_map/pallas_call | solution.py:87
  36.7 1.6 %copy.16 = bf16[128,4096]{0,1:T(8,128)(2,1)S(1)} copy(bf16[128,4096]{1,0:T(8,128)(2,1)} %get-tuple-element.7) | data formatting | bytes 2097152 | tf_op jit(solution)/shard_map/pallas_call | solution.py:87
  39.0 5.3 %collective-permute-start.16 = (bf16[128,512]{0,1:T(8,128)(2,1)}, bf16[128,512]{0,1:T(8,128)(2,1)S(1)}, u32[]{:S(2)}, u32[]{:S(2)}) collective-permute-start(bf16[128,512]{0,1:T(8,128)(2,1)} %get-tuple-element.24), channel_id=1, source_target_pairs={{0,4},{4,8},{8,12},{12,16},{16,20},{20,24},{24,28},{28,0},{1,5},{5... | collective-permute-start | bytes 393224 | tf_op jit(solution)/shard_map/ppermute | solution.py:124
  44.3 7.3 %collective-permute-start.17 = (bf16[128,512]{0,1:T(8,128)(2,1)S(1)}, bf16[128,512]{0,1:T(8,128)(2,1)S(1)}, u32[]{:S(2)}, u32[]{:S(2)}) collective-permute-start(bf16[128,512]{0,1:T(8,128)(2,1)S(1)} %get-tuple-element.30), channel_id=1, source_target_pairs={{0,8},{4,12},{8,16},{12,20},{16,24},{20,28},{24,0},{28,4},{1,9},{5... | collective-permute-start | bytes 393224 | tf_op jit(solution)/shard_map/ppermute | solution.py:124
  52.9 1.4 collective-permute-start.10
  54.3 7.2 %collective-permute-start.11 = (bf16[512,128]{0,1:T(8,128)(2,1)S(1)}, bf16[512,128]{0,1:T(8,128)(2,1)S(1)}, u32[]{:S(2)}, u32[]{:S(2)}) collective-permute-start(bf16[512,128]{0,1:T(8,128)(2,1)S(1)} %get-tuple-element.38), channel_id=1, source_target_pairs={{0,2},{1,3},{2,0},{3,1},{4,6},{5,7},{6,4},{7,5},{8,10},{9,11},{10,... | collective-permute-start | bytes 393224 | tf_op jit(solution)/shard_map/ppermute | solution.py:114
  61.6 2.0 %collective-permute-start.19 = (bf16[128,512]{0,1:T(8,128)(2,1)S(1)}, bf16[128,512]{0,1:T(8,128)(2,1)S(1)}, u32[]{:S(2)}, u32[]{:S(2)}) collective-permute-start(bf16[128,512]{0,1:T(8,128)(2,1)S(1)} %get-tuple-element.28), channel_id=1, source_target_pairs={{0,16},{4,20},{8,24},{12,28},{16,0},{20,4},{24,8},{28,12},{1,17},{... | collective-permute-start | bytes 393224 | tf_op jit(solution)/shard_map/ppermute | solution.py:124
  63.7 1.7 %collective-permute-done.10 = bf16[512,128]{0,1:T(8,128)(2,1)S(1)} collective-permute-done((bf16[512,128]{0,1:T(8,128)(2,1)S(1)}, bf16[512,128]{0,1:T(8,128)(2,1)S(1)}, u32[]{:S(2)}, u32[]{:S(2)}) %collective-permute-start.10) | collective-permute-done | bytes 131104 | tf_op jit(solution)/shard_map/ppermute | solution.py:114
  65.4 4.8 %collective-permute-done.11 = bf16[512,128]{0,1:T(8,128)(2,1)S(1)} collective-permute-done((bf16[512,128]{0,1:T(8,128)(2,1)S(1)}, bf16[512,128]{0,1:T(8,128)(2,1)S(1)}, u32[]{:S(2)}, u32[]{:S(2)}) %collective-permute-start.11) | collective-permute-done | bytes 131104 | tf_op jit(solution)/shard_map/ppermute | solution.py:114
  70.4 3.2 %collective-permute-start.13 = (bf16[512,128]{0,1:T(8,128)(2,1)S(1)}, bf16[512,128]{0,1:T(8,128)(2,1)S(1)}, u32[]{:S(2)}, u32[]{:S(2)}) collective-permute-start(bf16[512,128]{0,1:T(8,128)(2,1)S(1)} %fusion.6), channel_id=1, source_target_pairs={{0,1},{1,2},{2,3},{3,0},{4,5},{5,6},{6,7},{7,4},{8,9},{9,10},{10,1... | collective-permute-start | bytes 393224 | tf_op jit(solution)/shard_map/ppermute | solution.py:106
  73.7 2.4 %collective-permute-start.15 = (bf16[512,128]{0,1:T(8,128)(2,1)S(1)}, bf16[512,128]{0,1:T(8,128)(2,1)S(1)}, u32[]{:S(2)}, u32[]{:S(2)}) collective-permute-start(bf16[512,128]{0,1:T(8,128)(2,1)S(1)} %fusion.6), channel_id=1, source_target_pairs={{0,3},{1,0},{2,1},{3,2},{4,7},{5,4},{6,5},{7,6},{8,11},{9,8},{10,9... | collective-permute-start | bytes 393224 | tf_op jit(solution)/shard_map/ppermute | solution.py:106
  76.1 1.8 %constant_dynamic-update-slice_fusion.15 = (bf16[4096,128]{1,0:T(8,128)(2,1)S(1)}, bf16[512,128]{1,0:T(8,128)(2,1)}, f32[512,128]{1,0:T(8,128)S(1)}) fusion(f32[512,128]{1,0:T(8,128)S(1)} %copy-done.2, bf16[128,512]{0,1:T(8,128)(2,1)S(1)} %collective-permute-done.22, bf16[128,512]{0,1:T(8,128)(2,1)S(1)} %collective-permute-done.21, ...), kind=kLoop, calls=%fused_computation.21 | loop fusion | flops 1179647 | bytes 1835008
  80.4 3.4 %collective-permute-done.14 = bf16[512,128]{0,1:T(8,128)(2,1)S(1)} collective-permute-done((bf16[512,128]{0,1:T(8,128)(2,1)S(1)}, bf16[512,128]{0,1:T(8,128)(2,1)S(1)}, u32[]{:S(2)}, u32[]{:S(2)}) %collective-permute-start.14) | collective-permute-done | bytes 131104 | tf_op jit(solution)/shard_map/ppermute | solution.py:106
  83.8 1.7 %collective-permute-start.26 = (bf16[512,128]{1,0:T(8,128)(2,1)}, bf16[512,128]{1,0:T(8,128)(2,1)S(1)}, u32[]{:S(2)}, u32[]{:S(2)}) collective-permute-start(bf16[512,128]{1,0:T(8,128)(2,1)} %get-tuple-element.13), channel_id=1, source_target_pairs={{0,16},{4,20},{8,24},{12,28},{16,0},{20,4},{24,8},{28,12},{1,17},{... | collective-permute-start | bytes 393224 | tf_op jit(solution)/shard_map/ppermute | solution.py:106
  86.4 1.8 %collective-permute-start.28 = (bf16[512,128]{1,0:T(8,128)(2,1)}, bf16[512,128]{1,0:T(8,128)(2,1)S(1)}, u32[]{:S(2)}, u32[]{:S(2)}) collective-permute-start(bf16[512,128]{1,0:T(8,128)(2,1)} %get-tuple-element.13), channel_id=1, source_target_pairs={{0,24},{4,28},{8,0},{12,4},{16,8},{20,12},{24,16},{28,20},{1,25},{... | collective-permute-start | bytes 393224 | tf_op jit(solution)/shard_map/ppermute | solution.py:106
  90.5 1.6 %collective-permute-done.27 = bf16[512,128]{1,0:T(8,128)(2,1)S(1)} collective-permute-done((bf16[512,128]{1,0:T(8,128)(2,1)}, bf16[512,128]{1,0:T(8,128)(2,1)S(1)}, u32[]{:S(2)}, u32[]{:S(2)}) %collective-permute-start.27) | collective-permute-done | bytes 131104 | tf_op jit(solution)/shard_map/ppermute | solution.py:106
  94.8 6.8 %shard_map.87 = (bf16[2048,128]{1,0:T(8,128)(2,1)}, bf16[128,4096]{1,0:T(8,128)(2,1)}) custom-call(s32[64]{0:T(128)} %get-tuple-element.41.rows_ref, s32[64]{0:T(128)} %get-tuple-element.42.cols_ref, s32[1]{0:T(128)} %bitcast.39.count_ref, bf16[2048,128]{1,0:T(8,128)(2,1)} %copy.24.emb_ref, bf16[128,2048]{1,0:T(8,128)(2,1)} %get-tuple-element.34.embt_ref, ...), custom_call_target="tpu_custom_call" | custom-call | flops 3221225472 | bytes 21495808 | tf_op jit(solution)/shard_map/pallas_call | solution.py:87
  101.6 1.6 %copy.29 = bf16[128,4096]{0,1:T(8,128)(2,1)S(1)} copy(bf16[128,4096]{1,0:T(8,128)(2,1)} %get-tuple-element.9) | data formatting | bytes 2097152 | tf_op jit(solution)/shard_map/pallas_call | solution.py:87
  103.9 4.9 %collective-permute-start.33 = (bf16[128,512]{0,1:T(8,128)(2,1)S(1)}, bf16[128,512]{0,1:T(8,128)(2,1)}, u32[]{:S(2)}, u32[]{:S(2)}) collective-permute-start(bf16[128,512]{0,1:T(8,128)(2,1)S(1)} %get-tuple-element.17), channel_id=1, source_target_pairs={{0,4},{4,8},{8,12},{12,16},{16,20},{20,24},{24,28},{28,0},{1,5},{5... | collective-permute-start | bytes 393224 | tf_op jit(solution)/shard_map/ppermute | solution.py:124
  108.8 7.4 %collective-permute-start.34 = (bf16[128,512]{0,1:T(8,128)(2,1)S(1)}, bf16[128,512]{0,1:T(8,128)(2,1)}, u32[]{:S(2)}, u32[]{:S(2)}) collective-permute-start(bf16[128,512]{0,1:T(8,128)(2,1)S(1)} %get-tuple-element.23), channel_id=1, source_target_pairs={{0,8},{4,12},{8,16},{12,20},{16,24},{20,28},{24,0},{28,4},{1,9},{5... | collective-permute-start | bytes 393224 | tf_op jit(solution)/shard_map/ppermute | solution.py:124
  118.3 6.4 %collective-permute-start.31 = (bf16[512,128]{0,1:T(8,128)(2,1)S(1)}, bf16[512,128]{0,1:T(8,128)(2,1)S(1)}, u32[]{:S(2)}, u32[]{:S(2)}) collective-permute-start(bf16[512,128]{0,1:T(8,128)(2,1)S(1)} %get-tuple-element.33), channel_id=1, source_target_pairs={{0,2},{1,3},{2,0},{3,1},{4,6},{5,7},{6,4},{7,5},{8,10},{9,11},{10,... | collective-permute-start | bytes 393224 | tf_op jit(solution)/shard_map/ppermute | solution.py:114
  124.8 2.1 %collective-permute-start.36 = (bf16[128,512]{0,1:T(8,128)(2,1)S(1)}, bf16[128,512]{0,1:T(8,128)(2,1)}, u32[]{:S(2)}, u32[]{:S(2)}) collective-permute-start(bf16[128,512]{0,1:T(8,128)(2,1)S(1)} %get-tuple-element.21), channel_id=1, source_target_pairs={{0,16},{4,20},{8,24},{12,28},{16,0},{20,4},{24,8},{28,12},{1,17},{... | collective-permute-start | bytes 393224 | tf_op jit(solution)/shard_map/ppermute | solution.py:124
  126.8 1.8 %collective-permute-done.30 = bf16[512,128]{0,1:T(8,128)(2,1)S(1)} collective-permute-done((bf16[512,128]{0,1:T(8,128)(2,1)S(1)}, bf16[512,128]{0,1:T(8,128)(2,1)S(1)}, u32[]{:S(2)}, u32[]{:S(2)}) %collective-permute-start.30) | collective-permute-done | bytes 131104 | tf_op jit(solution)/shard_map/ppermute | solution.py:114
  128.6 4.8 %collective-permute-done.31 = bf16[512,128]{0,1:T(8,128)(2,1)S(1)} collective-permute-done((bf16[512,128]{0,1:T(8,128)(2,1)S(1)}, bf16[512,128]{0,1:T(8,128)(2,1)S(1)}, u32[]{:S(2)}, u32[]{:S(2)}) %collective-permute-start.31) | collective-permute-done | bytes 131104 | tf_op jit(solution)/shard_map/ppermute | solution.py:114
  135.4 3.4 %collective-permute-done.38 = bf16[128,512]{0,1:T(8,128)(2,1)} collective-permute-done((bf16[128,512]{0,1:T(8,128)(2,1)S(1)}, bf16[128,512]{0,1:T(8,128)(2,1)}, u32[]{:S(2)}, u32[]{:S(2)}) %collective-permute-start.38) | collective-permute-done | bytes 131104 | tf_op jit(solution)/shard_map/ppermute | solution.py:124
  138.8 2.1 %bitcast_add_fusion = f32[512,128]{1,0:T(8,128)} fusion(f32[512,128]{1,0:T(8,128)S(1)} %get-tuple-element.14, bf16[128,512]{0,1:T(8,128)(2,1)} %collective-permute-done.39, bf16[128,512]{0,1:T(8,128)(2,1)} %collective-permute-done.38, bf16[128,512]{0,1:T(8,128)(2,1)} %collective-permute-done.37, bf16[128,512]{0,1:T(8,128)(2,1)} %collective-permute-done.36, ...), kind=kLoop, calls=%fused_computation.2 | loop fusion | flops 1114112 | bytes 1572864 | tf_op jit(solution)/shard_map/add | solution.py:153
  (99 shorter events, 29.7 us)
Async XLA Ops:
  1.6 20.4 %collective-permute-start.3 = (bf16[512,128]{1,0:T(8,128)(2,1)S(1)}, bf16[512,128]{1,0:T(8,128)(2,1)S(1)}, u32[]{:S(2)}, u32[]{:S(2)}) collective-permute-start(bf16[512,128]{1,0:T(8,128)(2,1)S(1)} %get-tuple-element.16), channel_id=1, source_target_pairs={{0,4},{4,8},{8,12},{12,16},{16,20},{20,24},{24,28},{28,0},{1,5},{5... | collective-permute-start | bytes 393224 | tf_op jit(solution)/shard_map/ppermute | solution.py:106
  2.1 21.4 %collective-permute-start.4 = (bf16[512,128]{1,0:T(8,128)(2,1)S(1)}, bf16[512,128]{1,0:T(8,128)(2,1)S(1)}, u32[]{:S(2)}, u32[]{:S(2)}) collective-permute-start(bf16[512,128]{1,0:T(8,128)(2,1)S(1)} %get-tuple-element.16), channel_id=1, source_target_pairs={{0,8},{4,12},{8,16},{12,20},{16,24},{20,28},{24,0},{28,4},{1,9},{5... | collective-permute-start | bytes 393224 | tf_op jit(solution)/shard_map/ppermute | solution.py:106
  5.8 8.1 %collective-permute-start = (bf16[512,128]{0,1:T(8,128)(2,1)S(1)}, bf16[512,128]{0,1:T(8,128)(2,1)S(1)}, u32[]{:S(2)}, u32[]{:S(2)}) collective-permute-start(bf16[512,128]{0,1:T(8,128)(2,1)S(1)} %convert_element_type.84), channel_id=1, source_target_pairs={{0,1},{1,2},{2,3},{3,0},{4,5},{5,6},{6,7},{7,4},{8,9},{9,10},{10,1... | collective-permute-start | bytes 393224 | tf_op jit(solution)/shard_map/ppermute | solution.py:106
  7.4 12.2 %collective-permute-start.1 = (bf16[512,128]{0,1:T(8,128)(2,1)S(1)}, bf16[512,128]{0,1:T(8,128)(2,1)S(1)}, u32[]{:S(2)}, u32[]{:S(2)}) collective-permute-start(bf16[512,128]{0,1:T(8,128)(2,1)S(1)} %convert_element_type.84), channel_id=1, source_target_pairs={{0,2},{1,3},{2,0},{3,1},{4,6},{5,7},{6,4},{7,5},{8,10},{9,11},{10,... | collective-permute-start | bytes 393224 | tf_op jit(solution)/shard_map/ppermute | solution.py:106
  10.0 10.6 %collective-permute-start.2 = (bf16[512,128]{0,1:T(8,128)(2,1)S(1)}, bf16[512,128]{0,1:T(8,128)(2,1)S(1)}, u32[]{:S(2)}, u32[]{:S(2)}) collective-permute-start(bf16[512,128]{0,1:T(8,128)(2,1)S(1)} %convert_element_type.84), channel_id=1, source_target_pairs={{0,3},{1,0},{2,1},{3,2},{4,7},{5,4},{6,5},{7,6},{8,11},{9,8},{10,9... | collective-permute-start | bytes 393224 | tf_op jit(solution)/shard_map/ppermute | solution.py:106
  13.9 10.9 %collective-permute-start.5 = (bf16[512,128]{1,0:T(8,128)(2,1)S(1)}, bf16[512,128]{1,0:T(8,128)(2,1)S(1)}, u32[]{:S(2)}, u32[]{:S(2)}) collective-permute-start(bf16[512,128]{1,0:T(8,128)(2,1)S(1)} %get-tuple-element.16), channel_id=1, source_target_pairs={{0,12},{4,16},{8,20},{12,24},{16,28},{20,0},{24,4},{28,8},{1,13},{... | collective-permute-start | bytes 393224 | tf_op jit(solution)/shard_map/ppermute | solution.py:106
  39.0 22.5 %collective-permute-start.16 = (bf16[128,512]{0,1:T(8,128)(2,1)}, bf16[128,512]{0,1:T(8,128)(2,1)S(1)}, u32[]{:S(2)}, u32[]{:S(2)}) collective-permute-start(bf16[128,512]{0,1:T(8,128)(2,1)} %get-tuple-element.24), channel_id=1, source_target_pairs={{0,4},{4,8},{8,12},{12,16},{16,20},{20,24},{24,28},{28,0},{1,5},{5... | collective-permute-start | bytes 393224 | tf_op jit(solution)/shard_map/ppermute | solution.py:124
  44.3 17.3 %collective-permute-start.17 = (bf16[128,512]{0,1:T(8,128)(2,1)S(1)}, bf16[128,512]{0,1:T(8,128)(2,1)S(1)}, u32[]{:S(2)}, u32[]{:S(2)}) collective-permute-start(bf16[128,512]{0,1:T(8,128)(2,1)S(1)} %get-tuple-element.30), channel_id=1, source_target_pairs={{0,8},{4,12},{8,16},{12,20},{16,24},{20,28},{24,0},{28,4},{1,9},{5... | collective-permute-start | bytes 393224 | tf_op jit(solution)/shard_map/ppermute | solution.py:124
  52.9 12.5 %collective-permute-start.10 = (bf16[512,128]{0,1:T(8,128)(2,1)S(1)}, bf16[512,128]{0,1:T(8,128)(2,1)S(1)}, u32[]{:S(2)}, u32[]{:S(2)}) collective-permute-start(bf16[512,128]{0,1:T(8,128)(2,1)S(1)} %get-tuple-element.36), channel_id=1, source_target_pairs={{0,1},{1,2},{2,3},{3,0},{4,5},{5,6},{6,7},{7,4},{8,9},{9,10},{10,1... | collective-permute-start | bytes 393224 | tf_op jit(solution)/shard_map/ppermute | solution.py:114
  54.3 15.9 %collective-permute-start.11 = (bf16[512,128]{0,1:T(8,128)(2,1)S(1)}, bf16[512,128]{0,1:T(8,128)(2,1)S(1)}, u32[]{:S(2)}, u32[]{:S(2)}) collective-permute-start(bf16[512,128]{0,1:T(8,128)(2,1)S(1)} %get-tuple-element.38), channel_id=1, source_target_pairs={{0,2},{1,3},{2,0},{3,1},{4,6},{5,7},{6,4},{7,5},{8,10},{9,11},{10,... | collective-permute-start | bytes 393224 | tf_op jit(solution)/shard_map/ppermute | solution.py:114
  61.5 8.6 %collective-permute-start.12 = (bf16[512,128]{0,1:T(8,128)(2,1)S(1)}, bf16[512,128]{0,1:T(8,128)(2,1)S(1)}, u32[]{:S(2)}, u32[]{:S(2)}) collective-permute-start(bf16[512,128]{0,1:T(8,128)(2,1)S(1)} %get-tuple-element.37), channel_id=1, source_target_pairs={{0,3},{1,0},{2,1},{3,2},{4,7},{5,4},{6,5},{7,6},{8,11},{9,8},{10,9... | collective-permute-start | bytes 393224 | tf_op jit(solution)/shard_map/ppermute | solution.py:114
  61.6 8.8 %collective-permute-start.18 = (bf16[128,512]{0,1:T(8,128)(2,1)S(1)}, bf16[128,512]{0,1:T(8,128)(2,1)S(1)}, u32[]{:S(2)}, u32[]{:S(2)}) collective-permute-start(bf16[128,512]{0,1:T(8,128)(2,1)S(1)} %get-tuple-element.29), channel_id=1, source_target_pairs={{0,12},{4,16},{8,20},{12,24},{16,28},{20,0},{24,4},{28,8},{1,13},{... | collective-permute-start | bytes 393224 | tf_op jit(solution)/shard_map/ppermute | solution.py:124
  61.6 12.0 %collective-permute-start.19 = (bf16[128,512]{0,1:T(8,128)(2,1)S(1)}, bf16[128,512]{0,1:T(8,128)(2,1)S(1)}, u32[]{:S(2)}, u32[]{:S(2)}) collective-permute-start(bf16[128,512]{0,1:T(8,128)(2,1)S(1)} %get-tuple-element.28), channel_id=1, source_target_pairs={{0,16},{4,20},{8,24},{12,28},{16,0},{20,4},{24,8},{28,12},{1,17},{... | collective-permute-start | bytes 393224 | tf_op jit(solution)/shard_map/ppermute | solution.py:124
  65.4 8.3 %collective-permute-start.20 = (bf16[128,512]{0,1:T(8,128)(2,1)S(1)}, bf16[128,512]{0,1:T(8,128)(2,1)S(1)}, u32[]{:S(2)}, u32[]{:S(2)}) collective-permute-start(bf16[128,512]{0,1:T(8,128)(2,1)S(1)} %get-tuple-element.27), channel_id=1, source_target_pairs={{0,20},{4,24},{8,28},{12,0},{16,4},{20,8},{24,12},{28,16},{1,21},{... | collective-permute-start | bytes 393224 | tf_op jit(solution)/shard_map/ppermute | solution.py:124
  70.2 5.9 %collective-permute-start.22 = (bf16[128,512]{0,1:T(8,128)(2,1)S(1)}, bf16[128,512]{0,1:T(8,128)(2,1)S(1)}, u32[]{:S(2)}, u32[]{:S(2)}) collective-permute-start(bf16[128,512]{0,1:T(8,128)(2,1)S(1)} %get-tuple-element.25), channel_id=1, source_target_pairs={{0,28},{4,0},{8,4},{12,8},{16,12},{20,16},{24,20},{28,24},{1,29},{... | collective-permute-start | bytes 393224 | tf_op jit(solution)/shard_map/ppermute | solution.py:124
  70.4 9.5 %collective-permute-start.13 = (bf16[512,128]{0,1:T(8,128)(2,1)S(1)}, bf16[512,128]{0,1:T(8,128)(2,1)S(1)}, u32[]{:S(2)}, u32[]{:S(2)}) collective-permute-start(bf16[512,128]{0,1:T(8,128)(2,1)S(1)} %fusion.6), channel_id=1, source_target_pairs={{0,1},{1,2},{2,3},{3,0},{4,5},{5,6},{6,7},{7,4},{8,9},{9,10},{10,1... | collective-permute-start | bytes 393224 | tf_op jit(solution)/shard_map/ppermute | solution.py:106
  73.6 10.2 %collective-permute-start.14 = (bf16[512,128]{0,1:T(8,128)(2,1)S(1)}, bf16[512,128]{0,1:T(8,128)(2,1)S(1)}, u32[]{:S(2)}, u32[]{:S(2)}) collective-permute-start(bf16[512,128]{0,1:T(8,128)(2,1)S(1)} %fusion.6), channel_id=1, source_target_pairs={{0,2},{1,3},{2,0},{3,1},{4,6},{5,7},{6,4},{7,5},{8,10},{9,11},{10,... | collective-permute-start | bytes 393224 | tf_op jit(solution)/shard_map/ppermute | solution.py:106
  73.7 11.8 %collective-permute-start.15 = (bf16[512,128]{0,1:T(8,128)(2,1)S(1)}, bf16[512,128]{0,1:T(8,128)(2,1)S(1)}, u32[]{:S(2)}, u32[]{:S(2)}) collective-permute-start(bf16[512,128]{0,1:T(8,128)(2,1)S(1)} %fusion.6), channel_id=1, source_target_pairs={{0,3},{1,0},{2,1},{3,2},{4,7},{5,4},{6,5},{7,6},{8,11},{9,8},{10,9... | collective-permute-start | bytes 393224 | tf_op jit(solution)/shard_map/ppermute | solution.py:106
  77.9 8.5 %collective-permute-start.23 = (bf16[512,128]{1,0:T(8,128)(2,1)}, bf16[512,128]{1,0:T(8,128)(2,1)S(1)}, u32[]{:S(2)}, u32[]{:S(2)}) collective-permute-start(bf16[512,128]{1,0:T(8,128)(2,1)} %get-tuple-element.13), channel_id=1, source_target_pairs={{0,4},{4,8},{8,12},{12,16},{16,20},{20,24},{24,28},{28,0},{1,5},{5... | collective-permute-start | bytes 393224 | tf_op jit(solution)/shard_map/ppermute | solution.py:106
  78.8 9.4 %collective-permute-start.24 = (bf16[512,128]{1,0:T(8,128)(2,1)}, bf16[512,128]{1,0:T(8,128)(2,1)S(1)}, u32[]{:S(2)}, u32[]{:S(2)}) collective-permute-start(bf16[512,128]{1,0:T(8,128)(2,1)} %get-tuple-element.13), channel_id=1, source_target_pairs={{0,8},{4,12},{8,16},{12,20},{16,24},{20,28},{24,0},{28,4},{1,9},{5... | collective-permute-start | bytes 393224 | tf_op jit(solution)/shard_map/ppermute | solution.py:106
  79.9 10.4 %collective-permute-start.25 = (bf16[512,128]{1,0:T(8,128)(2,1)}, bf16[512,128]{1,0:T(8,128)(2,1)S(1)}, u32[]{:S(2)}, u32[]{:S(2)}) collective-permute-start(bf16[512,128]{1,0:T(8,128)(2,1)} %get-tuple-element.13), channel_id=1, source_target_pairs={{0,12},{4,16},{8,20},{12,24},{16,28},{20,0},{24,4},{28,8},{1,13},{... | collective-permute-start | bytes 393224 | tf_op jit(solution)/shard_map/ppermute | solution.py:106
  83.8 6.7 %collective-permute-start.26 = (bf16[512,128]{1,0:T(8,128)(2,1)}, bf16[512,128]{1,0:T(8,128)(2,1)S(1)}, u32[]{:S(2)}, u32[]{:S(2)}) collective-permute-start(bf16[512,128]{1,0:T(8,128)(2,1)} %get-tuple-element.13), channel_id=1, source_target_pairs={{0,16},{4,20},{8,24},{12,28},{16,0},{20,4},{24,8},{28,12},{1,17},{... | collective-permute-start | bytes 393224 | tf_op jit(solution)/shard_map/ppermute | solution.py:106
  85.5 6.7 %collective-permute-start.27 = (bf16[512,128]{1,0:T(8,128)(2,1)}, bf16[512,128]{1,0:T(8,128)(2,1)S(1)}, u32[]{:S(2)}, u32[]{:S(2)}) collective-permute-start(bf16[512,128]{1,0:T(8,128)(2,1)} %get-tuple-element.13), channel_id=1, source_target_pairs={{0,20},{4,24},{8,28},{12,0},{16,4},{20,8},{24,12},{28,16},{1,21},{... | collective-permute-start | bytes 393224 | tf_op jit(solution)/shard_map/ppermute | solution.py:106
  86.4 6.8 %collective-permute-start.28 = (bf16[512,128]{1,0:T(8,128)(2,1)}, bf16[512,128]{1,0:T(8,128)(2,1)S(1)}, u32[]{:S(2)}, u32[]{:S(2)}) collective-permute-start(bf16[512,128]{1,0:T(8,128)(2,1)} %get-tuple-element.13), channel_id=1, source_target_pairs={{0,24},{4,28},{8,0},{12,4},{16,8},{20,12},{24,16},{28,20},{1,25},{... | collective-permute-start | bytes 393224 | tf_op jit(solution)/shard_map/ppermute | solution.py:106
  103.9 20.8 %collective-permute-start.33 = (bf16[128,512]{0,1:T(8,128)(2,1)S(1)}, bf16[128,512]{0,1:T(8,128)(2,1)}, u32[]{:S(2)}, u32[]{:S(2)}) collective-permute-start(bf16[128,512]{0,1:T(8,128)(2,1)S(1)} %get-tuple-element.17), channel_id=1, source_target_pairs={{0,4},{4,8},{8,12},{12,16},{16,20},{20,24},{24,28},{28,0},{1,5},{5... | collective-permute-start | bytes 393224 | tf_op jit(solution)/shard_map/ppermute | solution.py:124
  108.8 16.0 %collective-permute-start.34 = (bf16[128,512]{0,1:T(8,128)(2,1)S(1)}, bf16[128,512]{0,1:T(8,128)(2,1)}, u32[]{:S(2)}, u32[]{:S(2)}) collective-permute-start(bf16[128,512]{0,1:T(8,128)(2,1)S(1)} %get-tuple-element.23), channel_id=1, source_target_pairs={{0,8},{4,12},{8,16},{12,20},{16,24},{20,28},{24,0},{28,4},{1,9},{5... | collective-permute-start | bytes 393224 | tf_op jit(solution)/shard_map/ppermute | solution.py:124
  117.5 11.1 %collective-permute-start.30 = (bf16[512,128]{0,1:T(8,128)(2,1)S(1)}, bf16[512,128]{0,1:T(8,128)(2,1)S(1)}, u32[]{:S(2)}, u32[]{:S(2)}) collective-permute-start(bf16[512,128]{0,1:T(8,128)(2,1)S(1)} %get-tuple-element.31), channel_id=1, source_target_pairs={{0,1},{1,2},{2,3},{3,0},{4,5},{5,6},{6,7},{7,4},{8,9},{9,10},{10,1... | collective-permute-start | bytes 393224 | tf_op jit(solution)/shard_map/ppermute | solution.py:114
  118.3 15.1 %collective-permute-start.31 = (bf16[512,128]{0,1:T(8,128)(2,1)S(1)}, bf16[512,128]{0,1:T(8,128)(2,1)S(1)}, u32[]{:S(2)}, u32[]{:S(2)}) collective-permute-start(bf16[512,128]{0,1:T(8,128)(2,1)S(1)} %get-tuple-element.33), channel_id=1, source_target_pairs={{0,2},{1,3},{2,0},{3,1},{4,6},{5,7},{6,4},{7,5},{8,10},{9,11},{10,... | collective-permute-start | bytes 393224 | tf_op jit(solution)/shard_map/ppermute | solution.py:114
  124.7 8.6 %collective-permute-start.32 = (bf16[512,128]{0,1:T(8,128)(2,1)S(1)}, bf16[512,128]{0,1:T(8,128)(2,1)S(1)}, u32[]{:S(2)}, u32[]{:S(2)}) collective-permute-start(bf16[512,128]{0,1:T(8,128)(2,1)S(1)} %get-tuple-element.32), channel_id=1, source_target_pairs={{0,3},{1,0},{2,1},{3,2},{4,7},{5,4},{6,5},{7,6},{8,11},{9,8},{10,9... | collective-permute-start | bytes 393224 | tf_op jit(solution)/shard_map/ppermute | solution.py:114
  124.7 10.6 %collective-permute-start.35 = (bf16[128,512]{0,1:T(8,128)(2,1)}, bf16[128,512]{0,1:T(8,128)(2,1)}, u32[]{:S(2)}, u32[]{:S(2)}) collective-permute-start(bf16[128,512]{0,1:T(8,128)(2,1)} %get-tuple-element.22), channel_id=1, source_target_pairs={{0,12},{4,16},{8,20},{12,24},{16,28},{20,0},{24,4},{28,8},{1,13},{... | collective-permute-start | bytes 393224 | tf_op jit(solution)/shard_map/ppermute | solution.py:124
  124.8 10.6 %collective-permute-start.36 = (bf16[128,512]{0,1:T(8,128)(2,1)S(1)}, bf16[128,512]{0,1:T(8,128)(2,1)}, u32[]{:S(2)}, u32[]{:S(2)}) collective-permute-start(bf16[128,512]{0,1:T(8,128)(2,1)S(1)} %get-tuple-element.21), channel_id=1, source_target_pairs={{0,16},{4,20},{8,24},{12,28},{16,0},{20,4},{24,8},{28,12},{1,17},{... | collective-permute-start | bytes 393224 | tf_op jit(solution)/shard_map/ppermute | solution.py:124
  128.6 6.8 %collective-permute-start.37 = (bf16[128,512]{0,1:T(8,128)(2,1)S(1)}, bf16[128,512]{0,1:T(8,128)(2,1)}, u32[]{:S(2)}, u32[]{:S(2)}) collective-permute-start(bf16[128,512]{0,1:T(8,128)(2,1)S(1)} %get-tuple-element.20), channel_id=1, source_target_pairs={{0,20},{4,24},{8,28},{12,0},{16,4},{20,8},{24,12},{28,16},{1,21},{... | collective-permute-start | bytes 393224 | tf_op jit(solution)/shard_map/ppermute | solution.py:124
  (15 other events, 132.5 us)

commit v4 on v3

--- a/solution.py
+++ b/solution.py
@@ -126,6 +126,34 @@
     return total.T
 
 
+def paired(n):
+    return n % 2 == 0 and n & (n - 1) == 0
+
+
+def gather_paired(x, axis, n):
+    pair = jnp.concatenate([x, lax.ppermute(x, axis, [(i, i ^ 1) for i in range(n)])], axis=0)
+    blocks = [pair]
+    for b in range(1, n // 2):
+        blocks.append(lax.ppermute(pair, axis, [(i, i ^ (2 * b)) for i in range(n)]))
+    return jnp.concatenate(blocks, axis=0)
+
+
+def scatter_paired_t(gt, axis, n):
+    width = gt.shape[1] // n
+    total = gt[:, : 2 * width].astype(jnp.float32)
+    for b in range(1, n // 2):
+        got = lax.ppermute(
+            gt[:, 2 * b * width : (2 * b + 2) * width], axis, [(i, i ^ (2 * b)) for i in range(n)]
+        )
+        total = total + got.astype(jnp.float32)
+    got = lax.ppermute(total[:, width:], axis, [(i, i ^ 1) for i in range(n)])
+    return (total[:, :width] + got).T
+
+
+def pair_index(index, me, per_run):
+    return (me ^ (index // per_run)) * per_run + index % per_run
+
+
 def rotate_index(index, me, n, per_run):
     run = index // per_run
     return ((me - run) % n) * per_run + index % per_run
@@ -141,16 +169,21 @@
     tile = pos.shape[-1]
     per_run = emb_in.shape[0] // tile
     rows = rotate_index(tile_row[0, 0], me_col, n_col, per_run)
-    cols = rotate_index(tile_col[0, 0], me_row, n_row, per_run)
+    if paired(n_row):
+        cols = pair_index(tile_col[0, 0], me_row, per_run)
+        gather_row, scatter_row = gather_paired, scatter_paired_t
+    else:
+        cols = rotate_index(tile_col[0, 0], me_row, n_row, per_run)
+        gather_row, scatter_row = gather_rotated, scatter_rotated_t
     count = tile_count[0, 0]
     emb = emb_in
     ctx = ctx_in
     for iteration in range(ITERS):
         emb_low = gather_rotated(emb.astype(jnp.bfloat16), "col", n_col)
-        ctx_low = gather_rotated(ctx.astype(jnp.bfloat16), "row", n_row)
+        ctx_low = gather_row(ctx.astype(jnp.bfloat16), "row", n_row)
         grad_emb, grad_ctx_t = tile_sweep(pos, neg, rows, cols, count, emb_low, ctx_low)
         emb = emb + 0.05 * scatter_rotated(grad_emb, "col", n_col)
-        ctx = ctx + 0.05 * scatter_rotated_t(grad_ctx_t, "row", n_row)
+        ctx = ctx + 0.05 * scatter_row(grad_ctx_t, "row", n_row)
     return (emb, ctx)
 
 

time: 142 us -> 143 us (level)
  starting transfers between devices: 72 us -> 52 us
  waiting for transfers between devices: 31 us -> 42 us
  Pallas kernels: 13.7 us -> 20.8 us
  local copies, waits for them, and re-layouts: 13.4 us -> 16.5 us
    ppermute x14 -> x16, waiting for transfers between devices: 3.45 us -> 26.2 us  [the longest x6 14.5 us: gather_paired(): blocks.append(lax.ppermute(pair, axis, [(i, i ^ 2 * b) for i in range(n)]))]
    ppermute x20 -> x6, starting transfers between devices: 27 us -> 13.4 us  [gather_rotated(): pieces.append(lax.ppermute(x, axis, [(i, (i + s) % n) for i in range(n)]))]
    ppermute x20 -> x6, waiting for transfers between devices: 14.5 us -> 6.97 us  [gather_rotated(): pieces.append(lax.ppermute(x, axis, [(i, (i + s) % n) for i in range(n)]))]
    pallas_call x2, Pallas kernels: 13.7 us -> 20.8 us  [tile_sweep(): pl.pallas_call(functools.partial(sweep_kernel, tile, group), grid_spec=gr...]
    ppermute x14 -> x16, starting transfers between devices: 29.1 us -> 22.6 us  [the longest x6 15.5 us: scatter_paired_t(): lax.ppermute(gt[:, 2 * b * width:(2 * b + 2) * width], axis, [(i, i ^ 2 *...]
    ppermute x6, waiting for transfers between devices: 13 us -> 8.9 us  [scatter_rotated(): lax.ppermute(chunks[(n - s) % n], axis, [(i, (i + s) % n) for i in range(...]
    unnamed x28 -> x22, local copies, waits for them, and re-layouts: 4.16 us -> 7.68 us
    unnamed x2, other arithmetic: 2.78 us -> 1.04 us
  transfers between devices with their start and end apart: 40 -> 28, of which waited for: 15 -> 11; matrix products, arithmetic and copies ran while one was open for 9% -> 11% of each run, Pallas kernels for 0% -> 0%
where the time goes in v4:
time: 143 us; the launch traced here: 142 us
  starting transfers between devices  52 us (36%)
  waiting for transfers between devices  42 us (29%)
  Pallas kernels  20.8 us (15%)
  local copies, waits for them, and re-layouts  16.5 us (12%)
  other arithmetic  9.29 us (6%)
  between operations  1.55 us (1%)
    pallas_call x2, Pallas kernels, tile_sweep(): pl.pallas_call(functools.partial(sweep_kernel, tile, group), grid_spec=gr...  20.8 us
    ppermute x6, starting transfers between devices, scatter_rotated(): lax.ppermute(chunks[(n - s) % n], axis, [(i, (i + s) % n) for i in range(...  16 us
    ppermute x6, starting transfers between devices, scatter_paired_t(): lax.ppermute(gt[:, 2 * b * width:(2 * b + 2) * width], axis, [(i, i ^ 2 *...  15.5 us
    ppermute x6, waiting for transfers between devices, gather_paired(): blocks.append(lax.ppermute(pair, axis, [(i, i ^ 2 * b) for i in range(n)]))  14.5 us
    ppermute x6, starting transfers between devices, gather_rotated(): pieces.append(lax.ppermute(x, axis, [(i, (i + s) % n) for i in range(n)]))  13.4 us
    ppermute x6, waiting for transfers between devices, scatter_paired_t(): lax.ppermute(gt[:, 2 * b * width:(2 * b + 2) * width], axis, [(i, i ^ 2 *...  11.7 us
    ppermute x6, waiting for transfers between devices, scatter_rotated(): lax.ppermute(chunks[(n - s) % n], axis, [(i, (i + s) % n) for i in range(...  8.9 us
    unnamed x22, local copies, waits for them, and re-layouts  7.68 us
  transfers between devices with their start and end apart: 28, of which 11 were waited for; matrix products, arithmetic and copies ran while one was open for 11% of the time, Pallas kernels for 0%

profile of v4, /device:TPU:0, one launch (start us, length us, event | category | flops | bytes accessed | tf_op | source)
XLA Modules:
  0.0 142.2 jit_solution(8397064504362133809)
XLA Ops:
  1.7 3.1 %collective-permute-start = (bf16[512,128]{0,1:T(8,128)(2,1)S(1)}, bf16[512,128]{0,1:T(8,128)(2,1)S(1)}, u32[]{:S(2)}, u32[]{:S(2)}) collective-permute-start(bf16[512,128]{0,1:T(8,128)(2,1)S(1)} %convert_element_type.60), channel_id=1, source_target_pairs={{0,1},{1,2},{2,3},{3,0},{4,5},{5,6},{6,7},{7,4},{8,9},{9,10},{10,1... | collective-permute-start | bytes 393224 | tf_op jit(solution)/shard_map/ppermute | solution.py:106
  4.8 2.6 %collective-permute-start.1 = (bf16[512,128]{0,1:T(8,128)(2,1)S(1)}, bf16[512,128]{0,1:T(8,128)(2,1)S(1)}, u32[]{:S(2)}, u32[]{:S(2)}) collective-permute-start(bf16[512,128]{0,1:T(8,128)(2,1)S(1)} %convert_element_type.60), channel_id=1, source_target_pairs={{0,2},{1,3},{2,0},{3,1},{4,6},{5,7},{6,4},{7,5},{8,10},{9,11},{10,... | collective-permute-start | bytes 393224 | tf_op jit(solution)/shard_map/ppermute | solution.py:106
  7.4 1.3 collective-permute-start.2
  9.8 1.3 fusion.6
  11.8 1.6 %collective-permute-start.4 = (bf16[1024,128]{1,0:T(8,128)(2,1)S(1)}, bf16[1024,128]{1,0:T(8,128)(2,1)S(1)}, u32[]{:S(2)}, u32[]{:S(2)}) collective-permute-start(bf16[1024,128]{1,0:T(8,128)(2,1)S(1)} %pad_maximum_fusion.2), channel_id=1, source_target_pairs={{0,8},{4,12},{8,0},{12,4},{16,24},{20,28},{24,16},{28,20},{1,9},{5... | collective-permute-start | bytes 786440 | tf_op jit(solution)/shard_map/ppermute | solution.py:137
  13.3 1.5 %collective-permute-start.5 = (bf16[1024,128]{1,0:T(8,128)(2,1)S(1)}, bf16[1024,128]{1,0:T(8,128)(2,1)S(1)}, u32[]{:S(2)}, u32[]{:S(2)}) collective-permute-start(bf16[1024,128]{1,0:T(8,128)(2,1)S(1)} %pad_maximum_fusion.2), channel_id=1, source_target_pairs={{0,16},{4,20},{8,24},{12,28},{16,0},{20,4},{24,8},{28,12},{1,17},{... | collective-permute-start | bytes 786440 | tf_op jit(solution)/shard_map/ppermute | solution.py:137
  18.0 2.9 %collective-permute-done.4 = bf16[1024,128]{1,0:T(8,128)(2,1)S(1)} collective-permute-done((bf16[1024,128]{1,0:T(8,128)(2,1)S(1)}, bf16[1024,128]{1,0:T(8,128)(2,1)S(1)}, u32[]{:S(2)}, u32[]{:S(2)}) %collective-permute-start.4) | collective-permute-done | bytes 262176 | tf_op jit(solution)/shard_map/ppermute | solution.py:137
  21.0 6.4 %collective-permute-done.5 = bf16[1024,128]{1,0:T(8,128)(2,1)S(1)} collective-permute-done((bf16[1024,128]{1,0:T(8,128)(2,1)S(1)}, bf16[1024,128]{1,0:T(8,128)(2,1)S(1)}, u32[]{:S(2)}, u32[]{:S(2)}) %collective-permute-start.5) | collective-permute-done | bytes 262176 | tf_op jit(solution)/shard_map/ppermute | solution.py:137
  28.5 10.4 %shard_map.86 = (bf16[2048,128]{1,0:T(8,128)(2,1)}, bf16[128,4096]{1,0:T(8,128)(2,1)}) custom-call(s32[64]{0:T(128)} %get-tuple-element.32.rows_ref, s32[64]{0:T(128)} %get-tuple-element.33.cols_ref, s32[1]{0:T(128)} %bitcast.46.count_ref, bf16[2048,128]{1,0:T(8,128)(2,1)} %copy.10.emb_ref, bf16[128,2048]{1,0:T(8,128)(2,1)} %get-tuple-element.30.embt_ref, ...), custom_call_target="tpu_custom_call" | custom-call | flops 3221225472 | bytes 21495808 | tf_op jit(solution)/shard_map/pallas_call | solution.py:87
  38.9 1.6 %copy.16 = bf16[128,4096]{0,1:T(8,128)(2,1)S(1)} copy(bf16[128,4096]{1,0:T(8,128)(2,1)} %get-tuple-element.7) | data formatting | bytes 2097152 | tf_op jit(solution)/shard_map/pallas_call | solution.py:87
  40.7 6.5 %collective-permute-start.14 = (bf16[128,1024]{0,1:T(8,128)(2,1)S(1)}, bf16[128,1024]{0,1:T(8,128)(2,1)S(1)}, u32[]{:S(2)}, u32[]{:S(2)}) collective-permute-start(bf16[128,1024]{0,1:T(8,128)(2,1)S(1)} %get-tuple-element.21), channel_id=1, source_target_pairs={{0,16},{4,20},{8,24},{12,28},{16,0},{20,4},{24,8},{28,12},{1,17},{... | collective-permute-start | bytes 786440 | tf_op jit(solution)/shard_map/ppermute | solution.py:145
  47.2 1.4 collective-permute-start.15
  48.6 10.9 %collective-permute-done.14 = bf16[128,1024]{0,1:T(8,128)(2,1)S(1)} collective-permute-done((bf16[128,1024]{0,1:T(8,128)(2,1)S(1)}, bf16[128,1024]{0,1:T(8,128)(2,1)S(1)}, u32[]{:S(2)}, u32[]{:S(2)}) %collective-permute-start.14) | collective-permute-done | bytes 262176 | tf_op jit(solution)/shard_map/ppermute | solution.py:145
  60.0 1.2 copy.11
  61.3 4.0 %collective-permute-start.7 = (bf16[512,128]{0,1:T(8,128)(2,1)S(1)}, bf16[512,128]{0,1:T(8,128)(2,1)S(1)}, u32[]{:S(2)}, u32[]{:S(2)}) collective-permute-start(bf16[512,128]{0,1:T(8,128)(2,1)S(1)} %get-tuple-element.27), channel_id=1, source_target_pairs={{0,1},{1,2},{2,3},{3,0},{4,5},{5,6},{6,7},{7,4},{8,9},{9,10},{10,1... | collective-permute-start | bytes 393224 | tf_op jit(solution)/shard_map/ppermute | solution.py:114
  65.4 2.4 %collective-permute-start.9 = (bf16[512,128]{0,1:T(8,128)(2,1)S(1)}, bf16[512,128]{0,1:T(8,128)(2,1)S(1)}, u32[]{:S(2)}, u32[]{:S(2)}) collective-permute-start(bf16[512,128]{0,1:T(8,128)(2,1)S(1)} %get-tuple-element.28), channel_id=1, source_target_pairs={{0,3},{1,0},{2,1},{3,2},{4,7},{5,4},{6,5},{7,6},{8,11},{9,8},{10,9... | collective-permute-start | bytes 393224 | tf_op jit(solution)/shard_map/ppermute | solution.py:114
  69.2 5.4 %collective-permute-done.8 = bf16[512,128]{0,1:T(8,128)(2,1)S(1)} collective-permute-done((bf16[512,128]{0,1:T(8,128)(2,1)S(1)}, bf16[512,128]{0,1:T(8,128)(2,1)S(1)}, u32[]{:S(2)}, u32[]{:S(2)}) %collective-permute-start.8) | collective-permute-done | bytes 131104 | tf_op jit(solution)/shard_map/ppermute | solution.py:114
  74.6 3.4 %collective-permute-start.10 = (bf16[512,128]{0,1:T(8,128)(2,1)S(1)}, bf16[512,128]{0,1:T(8,128)(2,1)S(1)}, u32[]{:S(2)}, u32[]{:S(2)}) collective-permute-start(bf16[512,128]{0,1:T(8,128)(2,1)S(1)} %fusion.11), channel_id=1, source_target_pairs={{0,1},{1,2},{2,3},{3,0},{4,5},{5,6},{6,7},{7,4},{8,9},{9,10},{10,1... | collective-permute-start | bytes 393224 | tf_op jit(solution)/shard_map/ppermute | solution.py:106
  78.0 3.0 %collective-permute-start.11 = (bf16[512,128]{0,1:T(8,128)(2,1)S(1)}, bf16[512,128]{0,1:T(8,128)(2,1)S(1)}, u32[]{:S(2)}, u32[]{:S(2)}) collective-permute-start(bf16[512,128]{0,1:T(8,128)(2,1)S(1)} %fusion.11), channel_id=1, source_target_pairs={{0,2},{1,3},{2,0},{3,1},{4,6},{5,7},{6,4},{7,5},{8,10},{9,11},{10,... | collective-permute-start | bytes 393224 | tf_op jit(solution)/shard_map/ppermute | solution.py:106
  83.5 1.4 collective-permute-done.10
  84.9 4.9 %collective-permute-done.11 = bf16[512,128]{0,1:T(8,128)(2,1)S(1)} collective-permute-done((bf16[512,128]{0,1:T(8,128)(2,1)S(1)}, bf16[512,128]{0,1:T(8,128)(2,1)S(1)}, u32[]{:S(2)}, u32[]{:S(2)}) %collective-permute-start.11) | collective-permute-done | bytes 131104 | tf_op jit(solution)/shard_map/ppermute | solution.py:106
  95.8 5.2 %collective-permute-done.20 = bf16[1024,128]{1,0:T(8,128)(2,1)S(1)} collective-permute-done((bf16[1024,128]{1,0:T(8,128)(2,1)}, bf16[1024,128]{1,0:T(8,128)(2,1)S(1)}, u32[]{:S(2)}, u32[]{:S(2)}) %collective-permute-start.20) | collective-permute-done | bytes 262176 | tf_op jit(solution)/shard_map/ppermute | solution.py:137
  102.0 10.3 %shard_map.87 = (bf16[2048,128]{1,0:T(8,128)(2,1)}, bf16[128,4096]{1,0:T(8,128)(2,1)}) custom-call(s32[64]{0:T(128)} %get-tuple-element.32.rows_ref, s32[64]{0:T(128)} %get-tuple-element.33.cols_ref, s32[1]{0:T(128)} %bitcast.47.count_ref, bf16[2048,128]{1,0:T(8,128)(2,1)} %copy.20.emb_ref, bf16[128,2048]{1,0:T(8,128)(2,1)} %get-tuple-element.25.embt_ref, ...), custom_call_target="tpu_custom_call" | custom-call | flops 3221225472 | bytes 21495808 | tf_op jit(solution)/shard_map/pallas_call | solution.py:87
  112.3 1.6 %copy.25 = bf16[128,4096]{0,1:T(8,128)(2,1)S(1)} copy(bf16[128,4096]{1,0:T(8,128)(2,1)} %get-tuple-element.9) | data formatting | bytes 2097152 | tf_op jit(solution)/shard_map/pallas_call | solution.py:87
  114.8 6.1 %collective-permute-start.25 = (bf16[128,1024]{0,1:T(8,128)(2,1)}, bf16[128,1024]{0,1:T(8,128)(2,1)}, u32[]{:S(2)}, u32[]{:S(2)}) collective-permute-start(bf16[128,1024]{0,1:T(8,128)(2,1)} %get-tuple-element.18), channel_id=1, source_target_pairs={{0,16},{4,20},{8,24},{12,28},{16,0},{20,4},{24,8},{28,12},{1,17},{... | collective-permute-start | bytes 786440 | tf_op jit(solution)/shard_map/ppermute | solution.py:145
  120.9 1.5 %collective-permute-start.26 = (bf16[128,1024]{0,1:T(8,128)(2,1)}, bf16[128,1024]{0,1:T(8,128)(2,1)}, u32[]{:S(2)}, u32[]{:S(2)}) collective-permute-start(bf16[128,1024]{0,1:T(8,128)(2,1)} %get-tuple-element.17), channel_id=1, source_target_pairs={{0,24},{4,28},{8,16},{12,20},{16,8},{20,12},{24,0},{28,4},{1,25},{... | collective-permute-start | bytes 786440 | tf_op jit(solution)/shard_map/ppermute | solution.py:145
  122.4 1.2 copy.21
  123.7 7.1 %collective-permute-start.21 = (bf16[512,128]{0,1:T(8,128)(2,1)S(1)}, bf16[512,128]{0,1:T(8,128)(2,1)S(1)}, u32[]{:S(2)}, u32[]{:S(2)}) collective-permute-start(bf16[512,128]{0,1:T(8,128)(2,1)S(1)} %get-tuple-element.22), channel_id=1, source_target_pairs={{0,1},{1,2},{2,3},{3,0},{4,5},{5,6},{6,7},{7,4},{8,9},{9,10},{10,1... | collective-permute-start | bytes 393224 | tf_op jit(solution)/shard_map/ppermute | solution.py:114
  130.7 2.4 %collective-permute-start.23 = (bf16[512,128]{0,1:T(8,128)(2,1)S(1)}, bf16[512,128]{0,1:T(8,128)(2,1)S(1)}, u32[]{:S(2)}, u32[]{:S(2)}) collective-permute-start(bf16[512,128]{0,1:T(8,128)(2,1)S(1)} %get-tuple-element.23), channel_id=1, source_target_pairs={{0,3},{1,0},{2,1},{3,2},{4,7},{5,4},{6,5},{7,6},{8,11},{9,8},{10,9... | collective-permute-start | bytes 393224 | tf_op jit(solution)/shard_map/ppermute | solution.py:114
  133.9 1.2 convert_add_fusion
  136.2 2.3 %collective-permute-done.22 = bf16[512,128]{0,1:T(8,128)(2,1)S(1)} collective-permute-done((bf16[512,128]{0,1:T(8,128)(2,1)S(1)}, bf16[512,128]{0,1:T(8,128)(2,1)S(1)}, u32[]{:S(2)}, u32[]{:S(2)}) %collective-permute-start.22) | collective-permute-done | bytes 131104 | tf_op jit(solution)/shard_map/ppermute | solution.py:114
  140.4 1.7 %fusion.2 = f32[512,128]{1,0:T(8,128)} fusion(f32[128,512]{0,1:T(8,128)S(1)} %collective-permute-done.27, f32[128,1024]{0,1:T(8,128)} %copy-done.1, f32[512,128]{1,0:T(8,128)S(1)} %copy-done, f32[128,512]{0,1:T(8,128)S(1)} %collective-permute-done.16, f32[128,1024]{0,1:T(8,128)S(1)} %convert_add_fusion.1), kind=kLoop, calls=%fused_computation.7 | loop fusion | flops 393216 | bytes 1572864 | tf_op jit(solution)/shard_map/add | solution.py:186
  (75 shorter events, 22.7 us)
Async XLA Ops:
  1.7 13.1 %collective-permute-start = (bf16[512,128]{0,1:T(8,128)(2,1)S(1)}, bf16[512,128]{0,1:T(8,128)(2,1)S(1)}, u32[]{:S(2)}, u32[]{:S(2)}) collective-permute-start(bf16[512,128]{0,1:T(8,128)(2,1)S(1)} %convert_element_type.60), channel_id=1, source_target_pairs={{0,1},{1,2},{2,3},{3,0},{4,5},{5,6},{6,7},{7,4},{8,9},{9,10},{10,1... | collective-permute-start | bytes 393224 | tf_op jit(solution)/shard_map/ppermute | solution.py:106
  4.8 11.2 %collective-permute-start.1 = (bf16[512,128]{0,1:T(8,128)(2,1)S(1)}, bf16[512,128]{0,1:T(8,128)(2,1)S(1)}, u32[]{:S(2)}, u32[]{:S(2)}) collective-permute-start(bf16[512,128]{0,1:T(8,128)(2,1)S(1)} %convert_element_type.60), channel_id=1, source_target_pairs={{0,2},{1,3},{2,0},{3,1},{4,6},{5,7},{6,4},{7,5},{8,10},{9,11},{10,... | collective-permute-start | bytes 393224 | tf_op jit(solution)/shard_map/ppermute | solution.py:106
  7.4 8.6 %collective-permute-start.2 = (bf16[512,128]{0,1:T(8,128)(2,1)S(1)}, bf16[512,128]{0,1:T(8,128)(2,1)S(1)}, u32[]{:S(2)}, u32[]{:S(2)}) collective-permute-start(bf16[512,128]{0,1:T(8,128)(2,1)S(1)} %convert_element_type.60), channel_id=1, source_target_pairs={{0,3},{1,0},{2,1},{3,2},{4,7},{5,4},{6,5},{7,6},{8,11},{9,8},{10,9... | collective-permute-start | bytes 393224 | tf_op jit(solution)/shard_map/ppermute | solution.py:106
  9.7 2.0 %collective-permute-start.3 = (bf16[512,128]{1,0:T(8,128)(2,1)S(1)}, bf16[512,128]{1,0:T(8,128)(2,1)S(1)}, u32[]{:S(2)}, u32[]{:S(2)}) collective-permute-start(bf16[512,128]{1,0:T(8,128)(2,1)S(1)} %get-tuple-element.15), channel_id=1, source_target_pairs={{0,4},{4,0},{8,12},{12,8},{16,20},{20,16},{24,28},{28,24},{1,5},{5... | collective-permute-start | bytes 393224 | tf_op jit(solution)/shard_map/ppermute | solution.py:134
  11.8 9.2 %collective-permute-start.4 = (bf16[1024,128]{1,0:T(8,128)(2,1)S(1)}, bf16[1024,128]{1,0:T(8,128)(2,1)S(1)}, u32[]{:S(2)}, u32[]{:S(2)}) collective-permute-start(bf16[1024,128]{1,0:T(8,128)(2,1)S(1)} %pad_maximum_fusion.2), channel_id=1, source_target_pairs={{0,8},{4,12},{8,0},{12,4},{16,24},{20,28},{24,16},{28,20},{1,9},{5... | collective-permute-start | bytes 786440 | tf_op jit(solution)/shard_map/ppermute | solution.py:137
  13.3 14.0 %collective-permute-start.5 = (bf16[1024,128]{1,0:T(8,128)(2,1)S(1)}, bf16[1024,128]{1,0:T(8,128)(2,1)S(1)}, u32[]{:S(2)}, u32[]{:S(2)}) collective-permute-start(bf16[1024,128]{1,0:T(8,128)(2,1)S(1)} %pad_maximum_fusion.2), channel_id=1, source_target_pairs={{0,16},{4,20},{8,24},{12,28},{16,0},{20,4},{24,8},{28,12},{1,17},{... | collective-permute-start | bytes 786440 | tf_op jit(solution)/shard_map/ppermute | solution.py:137
  14.9 12.6 %collective-permute-start.6 = (bf16[1024,128]{1,0:T(8,128)(2,1)S(1)}, bf16[1024,128]{1,0:T(8,128)(2,1)S(1)}, u32[]{:S(2)}, u32[]{:S(2)}) collective-permute-start(bf16[1024,128]{1,0:T(8,128)(2,1)S(1)} %pad_maximum_fusion.2), channel_id=1, source_target_pairs={{0,24},{4,28},{8,16},{12,20},{16,8},{20,12},{24,0},{28,4},{1,25},{... | collective-permute-start | bytes 786440 | tf_op jit(solution)/shard_map/ppermute | solution.py:137
  28.5 39.3 %copy-start = (f32[512,128]{1,0:T(8,128)S(1)}, f32[512,128]{1,0:T(8,128)}, u32[]{:S(2)}) copy-start(f32[512,128]{1,0:T(8,128)} %param.8) | copy-start | bytes 786436
  40.6 8.0 %collective-permute-start.13 = (bf16[128,1024]{0,1:T(8,128)(2,1)S(1)}, bf16[128,1024]{0,1:T(8,128)(2,1)S(1)}, u32[]{:S(2)}, u32[]{:S(2)}) collective-permute-start(bf16[128,1024]{0,1:T(8,128)(2,1)S(1)} %get-tuple-element.19), channel_id=1, source_target_pairs={{0,8},{4,12},{8,0},{12,4},{16,24},{20,28},{24,16},{28,20},{1,9},{5... | collective-permute-start | bytes 786440 | tf_op jit(solution)/shard_map/ppermute | solution.py:145
  40.7 18.8 %collective-permute-start.14 = (bf16[128,1024]{0,1:T(8,128)(2,1)S(1)}, bf16[128,1024]{0,1:T(8,128)(2,1)S(1)}, u32[]{:S(2)}, u32[]{:S(2)}) collective-permute-start(bf16[128,1024]{0,1:T(8,128)(2,1)S(1)} %get-tuple-element.21), channel_id=1, source_target_pairs={{0,16},{4,20},{8,24},{12,28},{16,0},{20,4},{24,8},{28,12},{1,17},{... | collective-permute-start | bytes 786440 | tf_op jit(solution)/shard_map/ppermute | solution.py:145
  47.2 12.3 %collective-permute-start.15 = (bf16[128,1024]{0,1:T(8,128)(2,1)S(1)}, bf16[128,1024]{0,1:T(8,128)(2,1)S(1)}, u32[]{:S(2)}, u32[]{:S(2)}) collective-permute-start(bf16[128,1024]{0,1:T(8,128)(2,1)S(1)} %get-tuple-element.20), channel_id=1, source_target_pairs={{0,24},{4,28},{8,16},{12,20},{16,8},{20,12},{24,0},{28,4},{1,25},{... | collective-permute-start | bytes 786440 | tf_op jit(solution)/shard_map/ppermute | solution.py:145
  59.6 8.2 %collective-permute-start.16 = (f32[128,512]{0,1:T(8,128)S(1)}, f32[128,512]{0,1:T(8,128)S(1)}, u32[]{:S(2)}, u32[]{:S(2)}) collective-permute-start(f32[128,512]{0,1:T(8,128)S(1)} %slice.97), channel_id=1, source_target_pairs={{0,4},{4,0},{8,12},{12,8},{16,20},{20,16},{24,28},{28,24},{1,5},{5... | collective-permute-start | bytes 786440 | tf_op jit(solution)/shard_map/ppermute | solution.py:149
  61.3 7.8 %collective-permute-start.7 = (bf16[512,128]{0,1:T(8,128)(2,1)S(1)}, bf16[512,128]{0,1:T(8,128)(2,1)S(1)}, u32[]{:S(2)}, u32[]{:S(2)}) collective-permute-start(bf16[512,128]{0,1:T(8,128)(2,1)S(1)} %get-tuple-element.27), channel_id=1, source_target_pairs={{0,1},{1,2},{2,3},{3,0},{4,5},{5,6},{6,7},{7,4},{8,9},{9,10},{10,1... | collective-permute-start | bytes 393224 | tf_op jit(solution)/shard_map/ppermute | solution.py:114
  65.4 9.2 %collective-permute-start.8 = (bf16[512,128]{0,1:T(8,128)(2,1)S(1)}, bf16[512,128]{0,1:T(8,128)(2,1)S(1)}, u32[]{:S(2)}, u32[]{:S(2)}) collective-permute-start(bf16[512,128]{0,1:T(8,128)(2,1)S(1)} %get-tuple-element.29), channel_id=1, source_target_pairs={{0,2},{1,3},{2,0},{3,1},{4,6},{5,7},{6,4},{7,5},{8,10},{9,11},{10,... | collective-permute-start | bytes 393224 | tf_op jit(solution)/shard_map/ppermute | solution.py:114
  65.4 9.2 %collective-permute-start.9 = (bf16[512,128]{0,1:T(8,128)(2,1)S(1)}, bf16[512,128]{0,1:T(8,128)(2,1)S(1)}, u32[]{:S(2)}, u32[]{:S(2)}) collective-permute-start(bf16[512,128]{0,1:T(8,128)(2,1)S(1)} %get-tuple-element.28), channel_id=1, source_target_pairs={{0,3},{1,0},{2,1},{3,2},{4,7},{5,4},{6,5},{7,6},{8,11},{9,8},{10,9... | collective-permute-start | bytes 393224 | tf_op jit(solution)/shard_map/ppermute | solution.py:114
  67.9 13.2 %collective-permute-start.17 = (bf16[512,128]{1,0:T(8,128)(2,1)S(1)}, bf16[512,128]{1,0:T(8,128)(2,1)S(1)}, u32[]{:S(2)}, u32[]{:S(2)}) collective-permute-start(bf16[512,128]{1,0:T(8,128)(2,1)S(1)} %get-tuple-element.13), channel_id=1, source_target_pairs={{0,4},{4,0},{8,12},{12,8},{16,20},{20,16},{24,28},{28,24},{1,5},{5... | collective-permute-start | bytes 393224 | tf_op jit(solution)/shard_map/ppermute | solution.py:134
  74.5 15.2 %copy-start.4 = (bf16[512,128]{0,1:T(8,128)(2,1)}, bf16[512,128]{0,1:T(8,128)(2,1)S(1)}, u32[]{:S(2)}) copy-start(bf16[512,128]{0,1:T(8,128)(2,1)S(1)} %collective-permute-done.8) | copy-start | bytes 393220
  74.5 15.2 %copy-start.5 = (bf16[512,128]{0,1:T(8,128)(2,1)}, bf16[512,128]{0,1:T(8,128)(2,1)S(1)}, u32[]{:S(2)}) copy-start(bf16[512,128]{0,1:T(8,128)(2,1)S(1)} %collective-permute-done.9) | copy-start | bytes 393220
  74.6 10.2 %collective-permute-start.10 = (bf16[512,128]{0,1:T(8,128)(2,1)S(1)}, bf16[512,128]{0,1:T(8,128)(2,1)S(1)}, u32[]{:S(2)}, u32[]{:S(2)}) collective-permute-start(bf16[512,128]{0,1:T(8,128)(2,1)S(1)} %fusion.11), channel_id=1, source_target_pairs={{0,1},{1,2},{2,3},{3,0},{4,5},{5,6},{6,7},{7,4},{8,9},{9,10},{10,1... | collective-permute-start | bytes 393224 | tf_op jit(solution)/shard_map/ppermute | solution.py:106
  78.0 11.7 %collective-permute-start.11 = (bf16[512,128]{0,1:T(8,128)(2,1)S(1)}, bf16[512,128]{0,1:T(8,128)(2,1)S(1)}, u32[]{:S(2)}, u32[]{:S(2)}) collective-permute-start(bf16[512,128]{0,1:T(8,128)(2,1)S(1)} %fusion.11), channel_id=1, source_target_pairs={{0,2},{1,3},{2,0},{3,1},{4,6},{5,7},{6,4},{7,5},{8,10},{9,11},{10,... | collective-permute-start | bytes 393224 | tf_op jit(solution)/shard_map/ppermute | solution.py:106
  81.0 8.7 %collective-permute-start.12 = (bf16[512,128]{0,1:T(8,128)(2,1)S(1)}, bf16[512,128]{0,1:T(8,128)(2,1)S(1)}, u32[]{:S(2)}, u32[]{:S(2)}) collective-permute-start(bf16[512,128]{0,1:T(8,128)(2,1)S(1)} %fusion.11), channel_id=1, source_target_pairs={{0,3},{1,0},{2,1},{3,2},{4,7},{5,4},{6,5},{7,6},{8,11},{9,8},{10,9... | collective-permute-start | bytes 393224 | tf_op jit(solution)/shard_map/ppermute | solution.py:106
  81.0 8.7 %copy-start.6 = (bf16[512,128]{1,0:T(8,128)(2,1)}, bf16[512,128]{1,0:T(8,128)(2,1)S(1)}, u32[]{:S(2)}) copy-start(bf16[512,128]{1,0:T(8,128)(2,1)S(1)} %collective-permute-done.17) | copy-start | bytes 393220
  81.8 12.0 %collective-permute-start.18 = (bf16[1024,128]{1,0:T(8,128)(2,1)}, bf16[1024,128]{1,0:T(8,128)(2,1)}, u32[]{:S(2)}, u32[]{:S(2)}) collective-permute-start(bf16[1024,128]{1,0:T(8,128)(2,1)} %pad_maximum_fusion.3), channel_id=1, source_target_pairs={{0,8},{4,12},{8,0},{12,4},{16,24},{20,28},{24,16},{28,20},{1,9},{5... | collective-permute-start | bytes 786440 | tf_op jit(solution)/shard_map/ppermute | solution.py:137
  83.0 11.8 %collective-permute-start.19 = (bf16[1024,128]{1,0:T(8,128)(2,1)}, bf16[1024,128]{1,0:T(8,128)(2,1)}, u32[]{:S(2)}, u32[]{:S(2)}) collective-permute-start(bf16[1024,128]{1,0:T(8,128)(2,1)} %pad_maximum_fusion.3), channel_id=1, source_target_pairs={{0,16},{4,20},{8,24},{12,28},{16,0},{20,4},{24,8},{28,12},{1,17},{... | collective-permute-start | bytes 786440 | tf_op jit(solution)/shard_map/ppermute | solution.py:137
  91.7 9.2 %collective-permute-start.20 = (bf16[1024,128]{1,0:T(8,128)(2,1)}, bf16[1024,128]{1,0:T(8,128)(2,1)S(1)}, u32[]{:S(2)}, u32[]{:S(2)}) collective-permute-start(bf16[1024,128]{1,0:T(8,128)(2,1)} %pad_maximum_fusion.3), channel_id=1, source_target_pairs={{0,24},{4,28},{8,16},{12,20},{16,8},{20,12},{24,0},{28,4},{1,25},{... | collective-permute-start | bytes 786440 | tf_op jit(solution)/shard_map/ppermute | solution.py:137
  114.8 15.9 %collective-permute-start.24 = (bf16[128,1024]{0,1:T(8,128)(2,1)}, bf16[128,1024]{0,1:T(8,128)(2,1)}, u32[]{:S(2)}, u32[]{:S(2)}) collective-permute-start(bf16[128,1024]{0,1:T(8,128)(2,1)} %get-tuple-element.16), channel_id=1, source_target_pairs={{0,8},{4,12},{8,0},{12,4},{16,24},{20,28},{24,16},{28,20},{1,9},{5... | collective-permute-start | bytes 786440 | tf_op jit(solution)/shard_map/ppermute | solution.py:145
  114.8 19.1 %collective-permute-start.25 = (bf16[128,1024]{0,1:T(8,128)(2,1)}, bf16[128,1024]{0,1:T(8,128)(2,1)}, u32[]{:S(2)}, u32[]{:S(2)}) collective-permute-start(bf16[128,1024]{0,1:T(8,128)(2,1)} %get-tuple-element.18), channel_id=1, source_target_pairs={{0,16},{4,20},{8,24},{12,28},{16,0},{20,4},{24,8},{28,12},{1,17},{... | collective-permute-start | bytes 786440 | tf_op jit(solution)/shard_map/ppermute | solution.py:145
  120.9 13.0 %collective-permute-start.26 = (bf16[128,1024]{0,1:T(8,128)(2,1)}, bf16[128,1024]{0,1:T(8,128)(2,1)}, u32[]{:S(2)}, u32[]{:S(2)}) collective-permute-start(bf16[128,1024]{0,1:T(8,128)(2,1)} %get-tuple-element.17), channel_id=1, source_target_pairs={{0,24},{4,28},{8,16},{12,20},{16,8},{20,12},{24,0},{28,4},{1,25},{... | collective-permute-start | bytes 786440 | tf_op jit(solution)/shard_map/ppermute | solution.py:145
  123.7 12.5 %collective-permute-start.21 = (bf16[512,128]{0,1:T(8,128)(2,1)S(1)}, bf16[512,128]{0,1:T(8,128)(2,1)S(1)}, u32[]{:S(2)}, u32[]{:S(2)}) collective-permute-start(bf16[512,128]{0,1:T(8,128)(2,1)S(1)} %get-tuple-element.22), channel_id=1, source_target_pairs={{0,1},{1,2},{2,3},{3,0},{4,5},{5,6},{6,7},{7,4},{8,9},{9,10},{10,1... | collective-permute-start | bytes 393224 | tf_op jit(solution)/shard_map/ppermute | solution.py:114
  130.7 7.7 %collective-permute-start.22 = (bf16[512,128]{0,1:T(8,128)(2,1)S(1)}, bf16[512,128]{0,1:T(8,128)(2,1)S(1)}, u32[]{:S(2)}, u32[]{:S(2)}) collective-permute-start(bf16[512,128]{0,1:T(8,128)(2,1)S(1)} %get-tuple-element.24), channel_id=1, source_target_pairs={{0,2},{1,3},{2,0},{3,1},{4,6},{5,7},{6,4},{7,5},{8,10},{9,11},{10,... | collective-permute-start | bytes 393224 | tf_op jit(solution)/shard_map/ppermute | solution.py:114
  130.7 7.7 %collective-permute-start.23 = (bf16[512,128]{0,1:T(8,128)(2,1)S(1)}, bf16[512,128]{0,1:T(8,128)(2,1)S(1)}, u32[]{:S(2)}, u32[]{:S(2)}) collective-permute-start(bf16[512,128]{0,1:T(8,128)(2,1)S(1)} %get-tuple-element.23), channel_id=1, source_target_pairs={{0,3},{1,0},{2,1},{3,2},{4,7},{5,4},{6,5},{7,6},{8,11},{9,8},{10,9... | collective-permute-start | bytes 393224 | tf_op jit(solution)/shard_map/ppermute | solution.py:114
  136.0 4.5 %collective-permute-start.27 = (f32[128,512]{0,1:T(8,128)S(1)}, f32[128,512]{0,1:T(8,128)S(1)}, u32[]{:S(2)}, u32[]{:S(2)}) collective-permute-start(f32[128,512]{0,1:T(8,128)S(1)} %slice.107), channel_id=1, source_target_pairs={{0,4},{4,0},{8,12},{12,8},{16,20},{20,16},{24,28},{28,24},{1,5},{5... | collective-permute-start | bytes 786440 | tf_op jit(solution)/shard_map/ppermute | solution.py:149
  (3 other events, 2.8 us)

commit v5 on v4

--- a/solution.py
+++ b/solution.py
@@ -150,6 +150,22 @@
     return (total[:, :width] + got).T
 
 
+def gather_xor(x, axis, n):
+    pieces = [x]
+    for p in range(1, n):
+        pieces.append(lax.ppermute(x, axis, [(i, i ^ p) for i in range(n)]))
+    return jnp.concatenate(pieces, axis=0)
+
+
+def scatter_xor_t(gt, axis, n):
+    width = gt.shape[1] // n
+    total = gt[:, :width].astype(jnp.float32)
+    for p in range(1, n):
+        got = lax.ppermute(gt[:, p * width : (p + 1) * width], axis, [(i, i ^ p) for i in range(n)])
+        total = total + got.astype(jnp.float32)
+    return total.T
+
+
 def pair_index(index, me, per_run):
     return (me ^ (index // per_run)) * per_run + index % per_run
 
@@ -171,19 +187,22 @@
     rows = rotate_index(tile_row[0, 0], me_col, n_col, per_run)
     if paired(n_row):
         cols = pair_index(tile_col[0, 0], me_row, per_run)
-        gather_row, scatter_row = gather_paired, scatter_paired_t
+        gathers = (gather_paired, gather_xor)
+        scatters = (scatter_xor_t, scatter_paired_t)
     else:
         cols = rotate_index(tile_col[0, 0], me_row, n_row, per_run)
-        gather_row, scatter_row = gather_rotated, scatter_rotated_t
+        gathers = (gather_rotated, gather_rotated)
+        scatters = (scatter_rotated_t, scatter_rotated_t)
     count = tile_count[0, 0]
     emb = emb_in
     ctx = ctx_in
     for iteration in range(ITERS):
         emb_low = gather_rotated(emb.astype(jnp.bfloat16), "col", n_col)
-        ctx_low = gather_row(ctx.astype(jnp.bfloat16), "row", n_row)
+        first, last = iteration == 0, iteration == ITERS - 1
+        ctx_low = gathers[0 if first else 1](ctx.astype(jnp.bfloat16), "row", n_row)
         grad_emb, grad_ctx_t = tile_sweep(pos, neg, rows, cols, count, emb_low, ctx_low)
         emb = emb + 0.05 * scatter_rotated(grad_emb, "col", n_col)
-        ctx = ctx + 0.05 * scatter_row(grad_ctx_t, "row", n_row)
+        ctx = ctx + 0.05 * scatters[1 if last else 0](grad_ctx_t, "row", n_row)
     return (emb, ctx)
 
 

time: 143 us -> 133 us (0.930)
  Pallas kernels: 20.8 us -> 31.6 us
  waiting for transfers between devices: 42 us -> 32.6 us
  starting transfers between devices: 52 us -> 43.9 us
  local copies, waits for them, and re-layouts: 16.5 us -> 13.6 us
    ppermute x0 -> x14, starting transfers between devices: none -> 15.1 us  [the longest x7 8.77 us: scatter_xor_t(): lax.ppermute(gt[:, p * width:(p + 1) * width], axis, [(i, i ^ p) for i in...]
    ppermute x6 -> x3, starting transfers between devices: 15.5 us -> 3.94 us  [scatter_paired_t(): lax.ppermute(gt[:, 2 * b * width:(2 * b + 2) * width], axis, [(i, i ^ 2 *...]
    pallas_call x2, Pallas kernels: 20.8 us -> 31.6 us  [tile_sweep(): pl.pallas_call(functools.partial(sweep_kernel, tile, group), grid_spec=gr...]
    ppermute x6 -> x3, waiting for transfers between devices: 11.7 us -> 1.76 us  [scatter_paired_t(): lax.ppermute(gt[:, 2 * b * width:(2 * b + 2) * width], axis, [(i, i ^ 2 *...]
    ppermute x0 -> x14, waiting for transfers between devices: none -> 9.3 us  [the longest x7 7.8 us: gather_xor(): pieces.append(lax.ppermute(x, axis, [(i, i ^ p) for i in range(n)]))]
    ppermute x6 -> x3, waiting for transfers between devices: 14.5 us -> 8.4 us  [gather_paired(): blocks.append(lax.ppermute(pair, axis, [(i, i ^ 2 * b) for i in range(n)]))]
    ppermute x6, starting transfers between devices: 16 us -> 10.1 us  [scatter_rotated(): lax.ppermute(chunks[(n - s) % n], axis, [(i, (i + s) % n) for i in range(...]
    unnamed x22 -> x27, local copies, waits for them, and re-layouts: 7.68 us -> 4.82 us
  transfers between devices with their start and end apart: 28 -> 34, of which waited for: 11 -> 13; matrix products, arithmetic and copies ran while one was open for 11% -> 11% of each run, Pallas kernels for 0% -> 0%
where the time goes in v5:
time: 133 us
  starting transfers between devices  43.9 us (33%)
  waiting for transfers between devices  32.6 us (25%)
  Pallas kernels  31.6 us (24%)
  local copies, waits for them, and re-layouts  13.6 us (10%)
  other arithmetic  9.89 us (7%)
  between operations  1.59 us (1%)
    pallas_call x2, Pallas kernels, tile_sweep(): pl.pallas_call(functools.partial(sweep_kernel, tile, group), grid_spec=gr...  31.6 us
    ppermute x6, starting transfers between devices, gather_rotated(): pieces.append(lax.ppermute(x, axis, [(i, (i + s) % n) for i in range(n)]))  11.1 us
    ppermute x6, starting transfers between devices, scatter_rotated(): lax.ppermute(chunks[(n - s) % n], axis, [(i, (i + s) % n) for i in range(...  10.1 us
    ppermute x7, starting transfers between devices, scatter_xor_t(): lax.ppermute(gt[:, p * width:(p + 1) * width], axis, [(i, i ^ p) for i in...  8.77 us
    ppermute x6, waiting for transfers between devices, scatter_rotated(): lax.ppermute(chunks[(n - s) % n], axis, [(i, (i + s) % n) for i in range(...  8.51 us
    ppermute x3, waiting for transfers between devices, gather_paired(): blocks.append(lax.ppermute(pair, axis, [(i, i ^ 2 * b) for i in range(n)]))  8.4 us
    ppermute x7, waiting for transfers between devices, gather_xor(): pieces.append(lax.ppermute(x, axis, [(i, i ^ p) for i in range(n)]))  7.8 us
    ppermute x7, starting transfers between devices, gather_xor(): pieces.append(lax.ppermute(x, axis, [(i, i ^ p) for i in range(n)]))  6.29 us
  transfers between devices with their start and end apart: 34, of which 13 were waited for; matrix products, arithmetic and copies ran while one was open for 11% of the time, Pallas kernels for 0%

profile of v5, /device:TPU:0, one launch (start us, length us, event | category | flops | bytes accessed | tf_op | source)
XLA Modules:
  0.0 133.2 jit_solution(9699958042025168668)
XLA Ops:
  1.7 3.1 %collective-permute-start = (bf16[512,128]{0,1:T(8,128)(2,1)S(1)}, bf16[512,128]{0,1:T(8,128)(2,1)S(1)}, u32[]{:S(2)}, u32[]{:S(2)}) collective-permute-start(bf16[512,128]{0,1:T(8,128)(2,1)S(1)} %convert_element_type.72), channel_id=1, source_target_pairs={{0,1},{1,2},{2,3},{3,0},{4,5},{5,6},{6,7},{7,4},{8,9},{9,10},{10,1... | collective-permute-start | bytes 393224 | tf_op jit(solution)/shard_map/ppermute | solution.py:106
  4.8 2.6 %collective-permute-start.1 = (bf16[512,128]{0,1:T(8,128)(2,1)S(1)}, bf16[512,128]{0,1:T(8,128)(2,1)S(1)}, u32[]{:S(2)}, u32[]{:S(2)}) collective-permute-start(bf16[512,128]{0,1:T(8,128)(2,1)S(1)} %convert_element_type.72), channel_id=1, source_target_pairs={{0,2},{1,3},{2,0},{3,1},{4,6},{5,7},{6,4},{7,5},{8,10},{9,11},{10,... | collective-permute-start | bytes 393224 | tf_op jit(solution)/shard_map/ppermute | solution.py:106
  7.4 1.3 %collective-permute-start.2 = (bf16[512,128]{0,1:T(8,128)(2,1)S(1)}, bf16[512,128]{0,1:T(8,128)(2,1)}, u32[]{:S(2)}, u32[]{:S(2)}) collective-permute-start(bf16[512,128]{0,1:T(8,128)(2,1)S(1)} %convert_element_type.72), channel_id=1, source_target_pairs={{0,3},{1,0},{2,1},{3,2},{4,7},{5,4},{6,5},{7,6},{8,11},{9,8},{10,9... | collective-permute-start | bytes 393224 | tf_op jit(solution)/shard_map/ppermute | solution.py:106
  11.7 1.6 %collective-permute-start.4 = (bf16[1024,128]{1,0:T(8,128)(2,1)S(1)}, bf16[1024,128]{1,0:T(8,128)(2,1)S(1)}, u32[]{:S(2)}, u32[]{:S(2)}) collective-permute-start(bf16[1024,128]{1,0:T(8,128)(2,1)S(1)} %pad_maximum_fusion.2), channel_id=1, source_target_pairs={{0,8},{4,12},{8,0},{12,4},{16,24},{20,28},{24,16},{28,20},{1,9},{5... | collective-permute-start | bytes 786440 | tf_op jit(solution)/shard_map/ppermute | solution.py:137
  13.3 1.5 %collective-permute-start.5 = (bf16[1024,128]{1,0:T(8,128)(2,1)S(1)}, bf16[1024,128]{1,0:T(8,128)(2,1)S(1)}, u32[]{:S(2)}, u32[]{:S(2)}) collective-permute-start(bf16[1024,128]{1,0:T(8,128)(2,1)S(1)} %pad_maximum_fusion.2), channel_id=1, source_target_pairs={{0,16},{4,20},{8,24},{12,28},{16,0},{20,4},{24,8},{28,12},{1,17},{... | collective-permute-start | bytes 786440 | tf_op jit(solution)/shard_map/ppermute | solution.py:137
  16.1 1.8 %fusion.9 = (bf16[128,2048]{1,0:T(8,128)(2,1)}, bf16[2048,128]{0,1:T(8,128)(2,1)S(1)}) fusion(bf16[512,128]{0,1:T(8,128)(2,1)} %collective-permute-done.2, bf16[512,128]{0,1:T(8,128)(2,1)S(1)} %collective-permute-done.1, bf16[512,128]{0,1:T(8,128)(2,1)S(1)} %collective-permute-done, bf16[512,128]{0,1:T(8,128)(2,1)S(1)} %convert_element_type.72), kind=kLoop, calls=%fused_computation.45 | loop fusion | flops 2097152 | bytes 1572864 | tf_op jit(solution)/shard_map/transpose | solution.py:100
  18.9 2.0 %collective-permute-done.4 = bf16[1024,128]{1,0:T(8,128)(2,1)S(1)} collective-permute-done((bf16[1024,128]{1,0:T(8,128)(2,1)S(1)}, bf16[1024,128]{1,0:T(8,128)(2,1)S(1)}, u32[]{:S(2)}, u32[]{:S(2)}) %collective-permute-start.4) | collective-permute-done | bytes 262176 | tf_op jit(solution)/shard_map/ppermute | solution.py:137
  20.9 6.4 %collective-permute-done.5 = bf16[1024,128]{1,0:T(8,128)(2,1)S(1)} collective-permute-done((bf16[1024,128]{1,0:T(8,128)(2,1)S(1)}, bf16[1024,128]{1,0:T(8,128)(2,1)S(1)}, u32[]{:S(2)}, u32[]{:S(2)}) %collective-permute-start.5) | collective-permute-done | bytes 262176 | tf_op jit(solution)/shard_map/ppermute | solution.py:137
  28.4 15.9 %shard_map.86 = (bf16[2048,128]{1,0:T(8,128)(2,1)}, bf16[128,4096]{1,0:T(8,128)(2,1)}) custom-call(s32[64]{0:T(128)} %get-tuple-element.37.rows_ref, s32[64]{0:T(128)} %get-tuple-element.38.cols_ref, s32[1]{0:T(128)} %bitcast.40.count_ref, bf16[2048,128]{1,0:T(8,128)(2,1)} %copy.10.emb_ref, bf16[128,2048]{1,0:T(8,128)(2,1)} %get-tuple-element.35.embt_ref, ...), custom_call_target="tpu_custom_call" | custom-call | flops 3221225472 | bytes 21495808 | tf_op jit(solution)/shard_map/pallas_call | solution.py:87
  44.3 1.6 %copy.16 = bf16[128,4096]{0,1:T(8,128)(2,1)S(1)} copy(bf16[128,4096]{1,0:T(8,128)(2,1)} %get-tuple-element.7) | data formatting | bytes 2097152 | tf_op jit(solution)/shard_map/pallas_call | solution.py:87
  46.2 1.2 copy.11
  47.5 3.2 %collective-permute-start.7 = (bf16[512,128]{0,1:T(8,128)(2,1)S(1)}, bf16[512,128]{0,1:T(8,128)(2,1)S(1)}, u32[]{:S(2)}, u32[]{:S(2)}) collective-permute-start(bf16[512,128]{0,1:T(8,128)(2,1)S(1)} %get-tuple-element.32), channel_id=1, source_target_pairs={{0,1},{1,2},{2,3},{3,0},{4,5},{5,6},{6,7},{7,4},{8,9},{9,10},{10,1... | collective-permute-start | bytes 393224 | tf_op jit(solution)/shard_map/ppermute | solution.py:114
  50.7 2.4 %collective-permute-start.9 = (bf16[512,128]{0,1:T(8,128)(2,1)S(1)}, bf16[512,128]{0,1:T(8,128)(2,1)S(1)}, u32[]{:S(2)}, u32[]{:S(2)}) collective-permute-start(bf16[512,128]{0,1:T(8,128)(2,1)S(1)} %get-tuple-element.33), channel_id=1, source_target_pairs={{0,3},{1,0},{2,1},{3,2},{4,7},{5,4},{6,5},{7,6},{8,11},{9,8},{10,9... | collective-permute-start | bytes 393224 | tf_op jit(solution)/shard_map/ppermute | solution.py:114
  54.0 1.7 %collective-permute-start.16 = (bf16[128,512]{0,1:T(8,128)(2,1)S(1)}, bf16[128,512]{0,1:T(8,128)(2,1)S(1)}, u32[]{:S(2)}, u32[]{:S(2)}) collective-permute-start(bf16[128,512]{0,1:T(8,128)(2,1)S(1)} %get-tuple-element.24), channel_id=1, source_target_pairs={{0,16},{4,20},{8,24},{12,28},{16,0},{20,4},{24,8},{28,12},{1,17},{... | collective-permute-start | bytes 393224 | tf_op jit(solution)/shard_map/ppermute | solution.py:164
  55.7 1.8 %collective-permute-start.17 = (bf16[128,512]{0,1:T(8,128)(2,1)S(1)}, bf16[128,512]{0,1:T(8,128)(2,1)S(1)}, u32[]{:S(2)}, u32[]{:S(2)}) collective-permute-start(bf16[128,512]{0,1:T(8,128)(2,1)S(1)} %get-tuple-element.23), channel_id=1, source_target_pairs={{0,20},{4,16},{8,28},{12,24},{16,4},{20,0},{24,12},{28,8},{1,21},{... | collective-permute-start | bytes 393224 | tf_op jit(solution)/shard_map/ppermute | solution.py:164
  57.6 3.3 %collective-permute-done.8 = bf16[512,128]{0,1:T(8,128)(2,1)S(1)} collective-permute-done((bf16[512,128]{0,1:T(8,128)(2,1)S(1)}, bf16[512,128]{0,1:T(8,128)(2,1)S(1)}, u32[]{:S(2)}, u32[]{:S(2)}) %collective-permute-start.8) | collective-permute-done | bytes 131104 | tf_op jit(solution)/shard_map/ppermute | solution.py:114
  60.9 4.2 %collective-permute-start.18 = (bf16[128,512]{0,1:T(8,128)(2,1)S(1)}, bf16[128,512]{0,1:T(8,128)(2,1)S(1)}, u32[]{:S(2)}, u32[]{:S(2)}) collective-permute-start(bf16[128,512]{0,1:T(8,128)(2,1)S(1)} %get-tuple-element.22), channel_id=1, source_target_pairs={{0,24},{4,28},{8,16},{12,20},{16,8},{20,12},{24,0},{28,4},{1,25},{... | collective-permute-start | bytes 393224 | tf_op jit(solution)/shard_map/ppermute | solution.py:164
  65.2 1.6 %collective-permute-start.10 = (bf16[512,128]{0,1:T(8,128)(2,1)S(1)}, bf16[512,128]{0,1:T(8,128)(2,1)S(1)}, u32[]{:S(2)}, u32[]{:S(2)}) collective-permute-start(bf16[512,128]{0,1:T(8,128)(2,1)S(1)} %fusion.7), channel_id=1, source_target_pairs={{0,1},{1,2},{2,3},{3,0},{4,5},{5,6},{6,7},{7,4},{8,9},{9,10},{10,1... | collective-permute-start | bytes 393224 | tf_op jit(solution)/shard_map/ppermute | solution.py:106
  66.8 1.7 %collective-permute-start.11 = (bf16[512,128]{0,1:T(8,128)(2,1)S(1)}, bf16[512,128]{0,1:T(8,128)(2,1)S(1)}, u32[]{:S(2)}, u32[]{:S(2)}) collective-permute-start(bf16[512,128]{0,1:T(8,128)(2,1)S(1)} %fusion.7), channel_id=1, source_target_pairs={{0,2},{1,3},{2,0},{3,1},{4,6},{5,7},{6,4},{7,5},{8,10},{9,11},{10,... | collective-permute-start | bytes 393224 | tf_op jit(solution)/shard_map/ppermute | solution.py:106
  69.3 1.5 %collective-permute-done.19 = bf16[128,512]{0,1:T(8,128)(2,1)S(1)} collective-permute-done((bf16[128,512]{0,1:T(8,128)(2,1)S(1)}, bf16[128,512]{0,1:T(8,128)(2,1)S(1)}, u32[]{:S(2)}, u32[]{:S(2)}) %collective-permute-start.19) | collective-permute-done | bytes 131104 | tf_op jit(solution)/shard_map/ppermute | solution.py:164
  70.8 1.8 %constant_dynamic-update-slice_fusion.12 = (bf16[4096,128]{1,0:T(8,128)(2,1)S(1)}, bf16[512,128]{1,0:T(8,128)(2,1)}, f32[512,128]{1,0:T(8,128)S(1)}) fusion(f32[512,128]{1,0:T(8,128)S(1)} %copy-done.2, bf16[128,512]{0,1:T(8,128)(2,1)S(1)} %collective-permute-done.19, bf16[128,512]{0,1:T(8,128)(2,1)S(1)} %collective-permute-done.18, ...), kind=kLoop, calls=%fused_computation.23 | loop fusion | flops 1179647 | bytes 1835008
  74.5 3.8 %collective-permute-done.11 = bf16[512,128]{0,1:T(8,128)(2,1)S(1)} collective-permute-done((bf16[512,128]{0,1:T(8,128)(2,1)S(1)}, bf16[512,128]{0,1:T(8,128)(2,1)S(1)}, u32[]{:S(2)}, u32[]{:S(2)}) %collective-permute-start.11) | collective-permute-done | bytes 131104 | tf_op jit(solution)/shard_map/ppermute | solution.py:106
  80.6 1.6 %collective-permute-start.25 = (bf16[512,128]{1,0:T(8,128)(2,1)}, bf16[512,128]{1,0:T(8,128)(2,1)S(1)}, u32[]{:S(2)}, u32[]{:S(2)}) collective-permute-start(bf16[512,128]{1,0:T(8,128)(2,1)} %get-tuple-element.13), channel_id=1, source_target_pairs={{0,24},{4,28},{8,16},{12,20},{16,8},{20,12},{24,0},{28,4},{1,25},{... | collective-permute-start | bytes 393224 | tf_op jit(solution)/shard_map/ppermute | solution.py:156
  82.3 1.4 %collective-permute-start.26 = (bf16[512,128]{1,0:T(8,128)(2,1)}, bf16[512,128]{1,0:T(8,128)(2,1)S(1)}, u32[]{:S(2)}, u32[]{:S(2)}) collective-permute-start(bf16[512,128]{1,0:T(8,128)(2,1)} %get-tuple-element.13), channel_id=1, source_target_pairs={{0,28},{4,24},{8,20},{12,16},{16,12},{20,8},{24,4},{28,0},{1,29},{... | collective-permute-start | bytes 393224 | tf_op jit(solution)/shard_map/ppermute | solution.py:156
  84.8 6.7 %collective-permute-done.24 = bf16[512,128]{1,0:T(8,128)(2,1)S(1)} collective-permute-done((bf16[512,128]{1,0:T(8,128)(2,1)}, bf16[512,128]{1,0:T(8,128)(2,1)S(1)}, u32[]{:S(2)}, u32[]{:S(2)}) %collective-permute-start.24) | collective-permute-done | bytes 131104 | tf_op jit(solution)/shard_map/ppermute | solution.py:156
  93.6 15.8 %shard_map.87 = (bf16[2048,128]{1,0:T(8,128)(2,1)}, bf16[128,4096]{1,0:T(8,128)(2,1)}) custom-call(s32[64]{0:T(128)} %get-tuple-element.37.rows_ref, s32[64]{0:T(128)} %get-tuple-element.38.cols_ref, s32[1]{0:T(128)} %bitcast.41.count_ref, bf16[2048,128]{1,0:T(8,128)(2,1)} %copy.24.emb_ref, bf16[128,2048]{1,0:T(8,128)(2,1)} %get-tuple-element.30.embt_ref, ...), custom_call_target="tpu_custom_call" | custom-call | flops 3221225472 | bytes 21495808 | tf_op jit(solution)/shard_map/pallas_call | solution.py:87
  109.4 1.6 %copy.29 = bf16[128,4096]{0,1:T(8,128)(2,1)S(1)} copy(bf16[128,4096]{1,0:T(8,128)(2,1)} %get-tuple-element.9) | data formatting | bytes 2097152 | tf_op jit(solution)/shard_map/pallas_call | solution.py:87
  111.9 2.5 %collective-permute-start.31 = (bf16[128,1024]{0,1:T(8,128)(2,1)}, bf16[128,1024]{0,1:T(8,128)(2,1)S(1)}, u32[]{:S(2)}, u32[]{:S(2)}) collective-permute-start(bf16[128,1024]{0,1:T(8,128)(2,1)} %get-tuple-element.19), channel_id=1, source_target_pairs={{0,16},{4,20},{8,24},{12,28},{16,0},{20,4},{24,8},{28,12},{1,17},{... | collective-permute-start | bytes 786440 | tf_op jit(solution)/shard_map/ppermute | solution.py:145
  114.3 1.5 %collective-permute-start.32 = (bf16[128,1024]{0,1:T(8,128)(2,1)S(1)}, bf16[128,1024]{0,1:T(8,128)(2,1)}, u32[]{:S(2)}, u32[]{:S(2)}) collective-permute-start(bf16[128,1024]{0,1:T(8,128)(2,1)S(1)} %get-tuple-element.18), channel_id=1, source_target_pairs={{0,24},{4,28},{8,16},{12,20},{16,8},{20,12},{24,0},{28,4},{1,25},{... | collective-permute-start | bytes 786440 | tf_op jit(solution)/shard_map/ppermute | solution.py:145
  117.5 4.0 %collective-permute-start.28 = (bf16[512,128]{0,1:T(8,128)(2,1)S(1)}, bf16[512,128]{0,1:T(8,128)(2,1)S(1)}, u32[]{:S(2)}, u32[]{:S(2)}) collective-permute-start(bf16[512,128]{0,1:T(8,128)(2,1)S(1)} %get-tuple-element.29), channel_id=1, source_target_pairs={{0,2},{1,3},{2,0},{3,1},{4,6},{5,7},{6,4},{7,5},{8,10},{9,11},{10,... | collective-permute-start | bytes 393224 | tf_op jit(solution)/shard_map/ppermute | solution.py:114
  121.5 1.8 %collective-permute-done.31 = bf16[128,1024]{0,1:T(8,128)(2,1)S(1)} collective-permute-done((bf16[128,1024]{0,1:T(8,128)(2,1)}, bf16[128,1024]{0,1:T(8,128)(2,1)S(1)}, u32[]{:S(2)}, u32[]{:S(2)}) %collective-permute-start.31) | collective-permute-done | bytes 262176 | tf_op jit(solution)/shard_map/ppermute | solution.py:145
  125.4 4.9 %collective-permute-done.28 = bf16[512,128]{0,1:T(8,128)(2,1)S(1)} collective-permute-done((bf16[512,128]{0,1:T(8,128)(2,1)S(1)}, bf16[512,128]{0,1:T(8,128)(2,1)S(1)}, u32[]{:S(2)}, u32[]{:S(2)}) %collective-permute-start.28) | collective-permute-done | bytes 131104 | tf_op jit(solution)/shard_map/ppermute | solution.py:114
  (89 shorter events, 23.7 us)
Async XLA Ops:
  1.7 13.1 %collective-permute-start = (bf16[512,128]{0,1:T(8,128)(2,1)S(1)}, bf16[512,128]{0,1:T(8,128)(2,1)S(1)}, u32[]{:S(2)}, u32[]{:S(2)}) collective-permute-start(bf16[512,128]{0,1:T(8,128)(2,1)S(1)} %convert_element_type.72), channel_id=1, source_target_pairs={{0,1},{1,2},{2,3},{3,0},{4,5},{5,6},{6,7},{7,4},{8,9},{9,10},{10,1... | collective-permute-start | bytes 393224 | tf_op jit(solution)/shard_map/ppermute | solution.py:106
  4.8 11.2 %collective-permute-start.1 = (bf16[512,128]{0,1:T(8,128)(2,1)S(1)}, bf16[512,128]{0,1:T(8,128)(2,1)S(1)}, u32[]{:S(2)}, u32[]{:S(2)}) collective-permute-start(bf16[512,128]{0,1:T(8,128)(2,1)S(1)} %convert_element_type.72), channel_id=1, source_target_pairs={{0,2},{1,3},{2,0},{3,1},{4,6},{5,7},{6,4},{7,5},{8,10},{9,11},{10,... | collective-permute-start | bytes 393224 | tf_op jit(solution)/shard_map/ppermute | solution.py:106
  7.4 8.6 %collective-permute-start.2 = (bf16[512,128]{0,1:T(8,128)(2,1)S(1)}, bf16[512,128]{0,1:T(8,128)(2,1)}, u32[]{:S(2)}, u32[]{:S(2)}) collective-permute-start(bf16[512,128]{0,1:T(8,128)(2,1)S(1)} %convert_element_type.72), channel_id=1, source_target_pairs={{0,3},{1,0},{2,1},{3,2},{4,7},{5,4},{6,5},{7,6},{8,11},{9,8},{10,9... | collective-permute-start | bytes 393224 | tf_op jit(solution)/shard_map/ppermute | solution.py:106
  11.7 9.2 %collective-permute-start.4 = (bf16[1024,128]{1,0:T(8,128)(2,1)S(1)}, bf16[1024,128]{1,0:T(8,128)(2,1)S(1)}, u32[]{:S(2)}, u32[]{:S(2)}) collective-permute-start(bf16[1024,128]{1,0:T(8,128)(2,1)S(1)} %pad_maximum_fusion.2), channel_id=1, source_target_pairs={{0,8},{4,12},{8,0},{12,4},{16,24},{20,28},{24,16},{28,20},{1,9},{5... | collective-permute-start | bytes 786440 | tf_op jit(solution)/shard_map/ppermute | solution.py:137
  13.3 14.0 %collective-permute-start.5 = (bf16[1024,128]{1,0:T(8,128)(2,1)S(1)}, bf16[1024,128]{1,0:T(8,128)(2,1)S(1)}, u32[]{:S(2)}, u32[]{:S(2)}) collective-permute-start(bf16[1024,128]{1,0:T(8,128)(2,1)S(1)} %pad_maximum_fusion.2), channel_id=1, source_target_pairs={{0,16},{4,20},{8,24},{12,28},{16,0},{20,4},{24,8},{28,12},{1,17},{... | collective-permute-start | bytes 786440 | tf_op jit(solution)/shard_map/ppermute | solution.py:137
  14.8 12.6 %collective-permute-start.6 = (bf16[1024,128]{1,0:T(8,128)(2,1)S(1)}, bf16[1024,128]{1,0:T(8,128)(2,1)S(1)}, u32[]{:S(2)}, u32[]{:S(2)}) collective-permute-start(bf16[1024,128]{1,0:T(8,128)(2,1)S(1)} %pad_maximum_fusion.2), channel_id=1, source_target_pairs={{0,24},{4,28},{8,16},{12,20},{16,8},{20,12},{24,0},{28,4},{1,25},{... | collective-permute-start | bytes 786440 | tf_op jit(solution)/shard_map/ppermute | solution.py:137
  46.0 7.1 %collective-permute-start.13 = (bf16[128,512]{0,1:T(8,128)(2,1)S(1)}, bf16[128,512]{0,1:T(8,128)(2,1)S(1)}, u32[]{:S(2)}, u32[]{:S(2)}) collective-permute-start(bf16[128,512]{0,1:T(8,128)(2,1)S(1)} %get-tuple-element.20), channel_id=1, source_target_pairs={{0,4},{4,0},{8,12},{12,8},{16,20},{20,16},{24,28},{28,24},{1,5},{5... | collective-permute-start | bytes 393224 | tf_op jit(solution)/shard_map/ppermute | solution.py:164
  46.1 7.9 %collective-permute-start.14 = (bf16[128,512]{0,1:T(8,128)(2,1)S(1)}, bf16[128,512]{0,1:T(8,128)(2,1)S(1)}, u32[]{:S(2)}, u32[]{:S(2)}) collective-permute-start(bf16[128,512]{0,1:T(8,128)(2,1)S(1)} %get-tuple-element.26), channel_id=1, source_target_pairs={{0,8},{4,12},{8,0},{12,4},{16,24},{20,28},{24,16},{28,20},{1,9},{5... | collective-permute-start | bytes 393224 | tf_op jit(solution)/shard_map/ppermute | solution.py:164
  47.5 8.3 %collective-permute-start.7 = (bf16[512,128]{0,1:T(8,128)(2,1)S(1)}, bf16[512,128]{0,1:T(8,128)(2,1)S(1)}, u32[]{:S(2)}, u32[]{:S(2)}) collective-permute-start(bf16[512,128]{0,1:T(8,128)(2,1)S(1)} %get-tuple-element.32), channel_id=1, source_target_pairs={{0,1},{1,2},{2,3},{3,0},{4,5},{5,6},{6,7},{7,4},{8,9},{9,10},{10,1... | collective-permute-start | bytes 393224 | tf_op jit(solution)/shard_map/ppermute | solution.py:114
  50.7 10.2 %collective-permute-start.8 = (bf16[512,128]{0,1:T(8,128)(2,1)S(1)}, bf16[512,128]{0,1:T(8,128)(2,1)S(1)}, u32[]{:S(2)}, u32[]{:S(2)}) collective-permute-start(bf16[512,128]{0,1:T(8,128)(2,1)S(1)} %get-tuple-element.34), channel_id=1, source_target_pairs={{0,2},{1,3},{2,0},{3,1},{4,6},{5,7},{6,4},{7,5},{8,10},{9,11},{10,... | collective-permute-start | bytes 393224 | tf_op jit(solution)/shard_map/ppermute | solution.py:114
  50.7 14.4 %collective-permute-start.9 = (bf16[512,128]{0,1:T(8,128)(2,1)S(1)}, bf16[512,128]{0,1:T(8,128)(2,1)S(1)}, u32[]{:S(2)}, u32[]{:S(2)}) collective-permute-start(bf16[512,128]{0,1:T(8,128)(2,1)S(1)} %get-tuple-element.33), channel_id=1, source_target_pairs={{0,3},{1,0},{2,1},{3,2},{4,7},{5,4},{6,5},{7,6},{8,11},{9,8},{10,9... | collective-permute-start | bytes 393224 | tf_op jit(solution)/shard_map/ppermute | solution.py:114
  53.1 12.1 %collective-permute-start.15 = (bf16[128,512]{0,1:T(8,128)(2,1)S(1)}, bf16[128,512]{0,1:T(8,128)(2,1)S(1)}, u32[]{:S(2)}, u32[]{:S(2)}) collective-permute-start(bf16[128,512]{0,1:T(8,128)(2,1)S(1)} %get-tuple-element.25), channel_id=1, source_target_pairs={{0,12},{4,8},{8,4},{12,0},{16,28},{20,24},{24,20},{28,16},{1,13},{... | collective-permute-start | bytes 393224 | tf_op jit(solution)/shard_map/ppermute | solution.py:164
  54.0 12.8 %collective-permute-start.16 = (bf16[128,512]{0,1:T(8,128)(2,1)S(1)}, bf16[128,512]{0,1:T(8,128)(2,1)S(1)}, u32[]{:S(2)}, u32[]{:S(2)}) collective-permute-start(bf16[128,512]{0,1:T(8,128)(2,1)S(1)} %get-tuple-element.24), channel_id=1, source_target_pairs={{0,16},{4,20},{8,24},{12,28},{16,0},{20,4},{24,8},{28,12},{1,17},{... | collective-permute-start | bytes 393224 | tf_op jit(solution)/shard_map/ppermute | solution.py:164
  55.7 12.7 %collective-permute-start.17 = (bf16[128,512]{0,1:T(8,128)(2,1)S(1)}, bf16[128,512]{0,1:T(8,128)(2,1)S(1)}, u32[]{:S(2)}, u32[]{:S(2)}) collective-permute-start(bf16[128,512]{0,1:T(8,128)(2,1)S(1)} %get-tuple-element.23), channel_id=1, source_target_pairs={{0,20},{4,16},{8,28},{12,24},{16,4},{20,0},{24,12},{28,8},{1,21},{... | collective-permute-start | bytes 393224 | tf_op jit(solution)/shard_map/ppermute | solution.py:164
  60.9 8.4 %collective-permute-start.18 = (bf16[128,512]{0,1:T(8,128)(2,1)S(1)}, bf16[128,512]{0,1:T(8,128)(2,1)S(1)}, u32[]{:S(2)}, u32[]{:S(2)}) collective-permute-start(bf16[128,512]{0,1:T(8,128)(2,1)S(1)} %get-tuple-element.22), channel_id=1, source_target_pairs={{0,24},{4,28},{8,16},{12,20},{16,8},{20,12},{24,0},{28,4},{1,25},{... | collective-permute-start | bytes 393224 | tf_op jit(solution)/shard_map/ppermute | solution.py:164
  65.2 8.3 %collective-permute-start.10 = (bf16[512,128]{0,1:T(8,128)(2,1)S(1)}, bf16[512,128]{0,1:T(8,128)(2,1)S(1)}, u32[]{:S(2)}, u32[]{:S(2)}) collective-permute-start(bf16[512,128]{0,1:T(8,128)(2,1)S(1)} %fusion.7), channel_id=1, source_target_pairs={{0,1},{1,2},{2,3},{3,0},{4,5},{5,6},{6,7},{7,4},{8,9},{9,10},{10,1... | collective-permute-start | bytes 393224 | tf_op jit(solution)/shard_map/ppermute | solution.py:106
  66.8 11.5 %collective-permute-start.11 = (bf16[512,128]{0,1:T(8,128)(2,1)S(1)}, bf16[512,128]{0,1:T(8,128)(2,1)S(1)}, u32[]{:S(2)}, u32[]{:S(2)}) collective-permute-start(bf16[512,128]{0,1:T(8,128)(2,1)S(1)} %fusion.7), channel_id=1, source_target_pairs={{0,2},{1,3},{2,0},{3,1},{4,6},{5,7},{6,4},{7,5},{8,10},{9,11},{10,... | collective-permute-start | bytes 393224 | tf_op jit(solution)/shard_map/ppermute | solution.py:106
  68.5 10.9 %collective-permute-start.12 = (bf16[512,128]{0,1:T(8,128)(2,1)S(1)}, bf16[512,128]{0,1:T(8,128)(2,1)S(1)}, u32[]{:S(2)}, u32[]{:S(2)}) collective-permute-start(bf16[512,128]{0,1:T(8,128)(2,1)S(1)} %fusion.7), channel_id=1, source_target_pairs={{0,3},{1,0},{2,1},{3,2},{4,7},{5,4},{6,5},{7,6},{8,11},{9,8},{10,9... | collective-permute-start | bytes 393224 | tf_op jit(solution)/shard_map/ppermute | solution.py:106
  72.6 8.0 %collective-permute-start.20 = (bf16[512,128]{1,0:T(8,128)(2,1)}, bf16[512,128]{1,0:T(8,128)(2,1)S(1)}, u32[]{:S(2)}, u32[]{:S(2)}) collective-permute-start(bf16[512,128]{1,0:T(8,128)(2,1)} %get-tuple-element.13), channel_id=1, source_target_pairs={{0,4},{4,0},{8,12},{12,8},{16,20},{20,16},{24,28},{28,24},{1,5},{5... | collective-permute-start | bytes 393224 | tf_op jit(solution)/shard_map/ppermute | solution.py:156
  72.6 9.7 %collective-permute-start.21 = (bf16[512,128]{1,0:T(8,128)(2,1)}, bf16[512,128]{1,0:T(8,128)(2,1)S(1)}, u32[]{:S(2)}, u32[]{:S(2)}) collective-permute-start(bf16[512,128]{1,0:T(8,128)(2,1)} %get-tuple-element.13), channel_id=1, source_target_pairs={{0,8},{4,12},{8,0},{12,4},{16,24},{20,28},{24,16},{28,20},{1,9},{5... | collective-permute-start | bytes 393224 | tf_op jit(solution)/shard_map/ppermute | solution.py:156
  73.5 10.2 %collective-permute-start.22 = (bf16[512,128]{1,0:T(8,128)(2,1)}, bf16[512,128]{1,0:T(8,128)(2,1)S(1)}, u32[]{:S(2)}, u32[]{:S(2)}) collective-permute-start(bf16[512,128]{1,0:T(8,128)(2,1)} %get-tuple-element.13), channel_id=1, source_target_pairs={{0,12},{4,8},{8,4},{12,0},{16,28},{20,24},{24,20},{28,16},{1,13},{... | collective-permute-start | bytes 393224 | tf_op jit(solution)/shard_map/ppermute | solution.py:156
  78.2 6.6 %collective-permute-start.23 = (bf16[512,128]{1,0:T(8,128)(2,1)}, bf16[512,128]{1,0:T(8,128)(2,1)S(1)}, u32[]{:S(2)}, u32[]{:S(2)}) collective-permute-start(bf16[512,128]{1,0:T(8,128)(2,1)} %get-tuple-element.13), channel_id=1, source_target_pairs={{0,16},{4,20},{8,24},{12,28},{16,0},{20,4},{24,8},{28,12},{1,17},{... | collective-permute-start | bytes 393224 | tf_op jit(solution)/shard_map/ppermute | solution.py:156
  79.4 12.2 %collective-permute-start.24 = (bf16[512,128]{1,0:T(8,128)(2,1)}, bf16[512,128]{1,0:T(8,128)(2,1)S(1)}, u32[]{:S(2)}, u32[]{:S(2)}) collective-permute-start(bf16[512,128]{1,0:T(8,128)(2,1)} %get-tuple-element.13), channel_id=1, source_target_pairs={{0,20},{4,16},{8,28},{12,24},{16,4},{20,0},{24,12},{28,8},{1,21},{... | collective-permute-start | bytes 393224 | tf_op jit(solution)/shard_map/ppermute | solution.py:156
  80.6 11.9 %collective-permute-start.25 = (bf16[512,128]{1,0:T(8,128)(2,1)}, bf16[512,128]{1,0:T(8,128)(2,1)S(1)}, u32[]{:S(2)}, u32[]{:S(2)}) collective-permute-start(bf16[512,128]{1,0:T(8,128)(2,1)} %get-tuple-element.13), channel_id=1, source_target_pairs={{0,24},{4,28},{8,16},{12,20},{16,8},{20,12},{24,0},{28,4},{1,25},{... | collective-permute-start | bytes 393224 | tf_op jit(solution)/shard_map/ppermute | solution.py:156
  82.3 10.3 %collective-permute-start.26 = (bf16[512,128]{1,0:T(8,128)(2,1)}, bf16[512,128]{1,0:T(8,128)(2,1)S(1)}, u32[]{:S(2)}, u32[]{:S(2)}) collective-permute-start(bf16[512,128]{1,0:T(8,128)(2,1)} %get-tuple-element.13), channel_id=1, source_target_pairs={{0,28},{4,24},{8,20},{12,16},{16,12},{20,8},{24,4},{28,0},{1,29},{... | collective-permute-start | bytes 393224 | tf_op jit(solution)/shard_map/ppermute | solution.py:156
  111.9 9.7 %collective-permute-start.30 = (bf16[128,1024]{0,1:T(8,128)(2,1)}, bf16[128,1024]{0,1:T(8,128)(2,1)S(1)}, u32[]{:S(2)}, u32[]{:S(2)}) collective-permute-start(bf16[128,1024]{0,1:T(8,128)(2,1)} %get-tuple-element.17), channel_id=1, source_target_pairs={{0,8},{4,12},{8,0},{12,4},{16,24},{20,28},{24,16},{28,20},{1,9},{5... | collective-permute-start | bytes 786440 | tf_op jit(solution)/shard_map/ppermute | solution.py:145
  111.9 11.4 %collective-permute-start.31 = (bf16[128,1024]{0,1:T(8,128)(2,1)}, bf16[128,1024]{0,1:T(8,128)(2,1)S(1)}, u32[]{:S(2)}, u32[]{:S(2)}) collective-permute-start(bf16[128,1024]{0,1:T(8,128)(2,1)} %get-tuple-element.19), channel_id=1, source_target_pairs={{0,16},{4,20},{8,24},{12,28},{16,0},{20,4},{24,8},{28,12},{1,17},{... | collective-permute-start | bytes 786440 | tf_op jit(solution)/shard_map/ppermute | solution.py:145
  114.3 9.7 %collective-permute-start.32 = (bf16[128,1024]{0,1:T(8,128)(2,1)S(1)}, bf16[128,1024]{0,1:T(8,128)(2,1)}, u32[]{:S(2)}, u32[]{:S(2)}) collective-permute-start(bf16[128,1024]{0,1:T(8,128)(2,1)S(1)} %get-tuple-element.18), channel_id=1, source_target_pairs={{0,24},{4,28},{8,16},{12,20},{16,8},{20,12},{24,0},{28,4},{1,25},{... | collective-permute-start | bytes 786440 | tf_op jit(solution)/shard_map/ppermute | solution.py:145
  117.1 8.3 %collective-permute-start.27 = (bf16[512,128]{0,1:T(8,128)(2,1)S(1)}, bf16[512,128]{0,1:T(8,128)(2,1)S(1)}, u32[]{:S(2)}, u32[]{:S(2)}) collective-permute-start(bf16[512,128]{0,1:T(8,128)(2,1)S(1)} %get-tuple-element.27), channel_id=1, source_target_pairs={{0,1},{1,2},{2,3},{3,0},{4,5},{5,6},{6,7},{7,4},{8,9},{9,10},{10,1... | collective-permute-start | bytes 393224 | tf_op jit(solution)/shard_map/ppermute | solution.py:114
  117.5 12.8 %collective-permute-start.28 = (bf16[512,128]{0,1:T(8,128)(2,1)S(1)}, bf16[512,128]{0,1:T(8,128)(2,1)S(1)}, u32[]{:S(2)}, u32[]{:S(2)}) collective-permute-start(bf16[512,128]{0,1:T(8,128)(2,1)S(1)} %get-tuple-element.29), channel_id=1, source_target_pairs={{0,2},{1,3},{2,0},{3,1},{4,6},{5,7},{6,4},{7,5},{8,10},{9,11},{10,... | collective-permute-start | bytes 393224 | tf_op jit(solution)/shard_map/ppermute | solution.py:114
  121.5 8.9 %collective-permute-start.29 = (bf16[512,128]{0,1:T(8,128)(2,1)S(1)}, bf16[512,128]{0,1:T(8,128)(2,1)S(1)}, u32[]{:S(2)}, u32[]{:S(2)}) collective-permute-start(bf16[512,128]{0,1:T(8,128)(2,1)S(1)} %get-tuple-element.28), channel_id=1, source_target_pairs={{0,3},{1,0},{2,1},{3,2},{4,7},{5,4},{6,5},{7,6},{8,11},{9,8},{10,9... | collective-permute-start | bytes 393224 | tf_op jit(solution)/shard_map/ppermute | solution.py:114
  125.2 7.2 %collective-permute-start.33 = (f32[128,512]{0,1:T(8,128)S(1)}, f32[128,512]{0,1:T(8,128)S(1)}, u32[]{:S(2)}, u32[]{:S(2)}) collective-permute-start(f32[128,512]{0,1:T(8,128)S(1)} %slice.117), channel_id=1, source_target_pairs={{0,4},{4,0},{8,12},{12,8},{16,20},{20,16},{24,28},{28,24},{1,5},{5... | collective-permute-start | bytes 786440 | tf_op jit(solution)/shard_map/ppermute | solution.py:149
  (10 other events, 97.1 us)

commit v6 on v5

--- a/solution.py
+++ b/solution.py
@@ -10,15 +10,15 @@
 ITERS = 2
 
 
-def sweep_kernel(tile, group, rows_ref, cols_ref, count_ref, emb_ref, embt_ref, ctx_ref, pos_ref, neg_ref,
-                 gemb_ref, gctxt_ref, acc_e, acc_ct):
+def sweep_kernel(tile, group, rows_ref, cols_ref, count_ref, emb_ref, ctx_ref, pos_ref, neg_ref,
+                 gemb_ref, gctx_ref, acc_e, acc_c):
     k = pl.program_id(0)
     n = count_ref[0]
 
     @pl.when(k == 0)
     def _():
         acc_e[...] = jnp.zeros_like(acc_e)
-        acc_ct[...] = jnp.zeros_like(acc_ct)
+        acc_c[...] = jnp.zeros_like(acc_c)
 
     def visit(j):
         slot = k * group + j
@@ -32,8 +32,8 @@
         t = jnp.tanh(score * 0.5)
         coeff = (0.5 * ((positive - negative) - (positive + negative) * t)).astype(jnp.bfloat16)
         acc_e[pl.ds(r0, tile), :] += jnp.dot(coeff, c, preferred_element_type=jnp.float32)
-        acc_ct[:, pl.ds(c0, tile)] += jnp.dot(
-            embt_ref[:, pl.ds(r0, tile)], coeff, preferred_element_type=jnp.float32
+        acc_c[pl.ds(c0, tile), :] += lax.dot_general(
+            coeff, e, (((0,), (0,)), ((), ())), preferred_element_type=jnp.float32
         )
 
     full = (k + 1) * group <= n
@@ -51,7 +51,7 @@
     @pl.when(k == pl.num_programs(0) - 1)
     def _():
         gemb_ref[...] = acc_e[...].astype(gemb_ref.dtype)
-        gctxt_ref[...] = acc_ct[...].astype(gctxt_ref.dtype)
+        gctx_ref[...] = acc_c[...].astype(gctx_ref.dtype)
 
 
 def tile_sweep(pos, neg, rows, cols, count, emb_low, ctx_low):
@@ -69,18 +69,17 @@
         grid=(cap // group,),
         in_specs=[
             pl.BlockSpec((ne, dim), lambda k, *_: (0, 0)),
-            pl.BlockSpec((dim, ne), lambda k, *_: (0, 0)),
             pl.BlockSpec((nc, dim), lambda k, *_: (0, 0)),
             pl.BlockSpec((group, tile, tile), slot),
             pl.BlockSpec((group, tile, tile), slot),
         ],
         out_specs=[
             pl.BlockSpec((ne, dim), lambda k, *_: (0, 0)),
-            pl.BlockSpec((dim, nc), lambda k, *_: (0, 0)),
+            pl.BlockSpec((nc, dim), lambda k, *_: (0, 0)),
         ],
         scratch_shapes=[
             pltpu.VMEM((ne, dim), jnp.float32),
-            pltpu.VMEM((dim, nc), jnp.float32),
+            pltpu.VMEM((nc, dim), jnp.float32),
         ],
     )
     flops = cap * 3 * 2 * tile * tile * dim
@@ -89,7 +88,7 @@
         grid_spec=grid_spec,
         out_shape=(
             jax.ShapeDtypeStruct((ne, dim), jnp.bfloat16),
-            jax.ShapeDtypeStruct((dim, nc), jnp.bfloat16),
+            jax.ShapeDtypeStruct((nc, dim), jnp.bfloat16),
         ),
         compiler_params=pltpu.CompilerParams(dimension_semantics=("arbitrary",)),
         cost_estimate=pl.CostEstimate(
@@ -97,7 +96,7 @@
             transcendentals=cap * tile * tile,
             bytes_accessed=2 * cap * tile * tile * 2 + 3 * (ne + nc) * dim * 2,
         ),
-    )(rows, cols, count.reshape(1), emb_low, emb_low.T, ctx_low, pos, neg)
+    )(rows, cols, count.reshape(1), emb_low, ctx_low, pos, neg)
 
 
 def gather_rotated(x, axis, n):
@@ -116,16 +115,6 @@
     return total
 
 
-def scatter_rotated_t(gt, axis, n):
-    width = gt.shape[1] // n
-    chunk = lambda s: gt[:, s * width:(s + 1) * width]
-    total = chunk(0).astype(jnp.float32)
-    for s in range(1, n):
-        got = lax.ppermute(chunk((n - s) % n), axis, [(i, (i + s) % n) for i in range(n)])
-        total = total + got.astype(jnp.float32)
-    return total.T
-
-
 def paired(n):
     return n % 2 == 0 and n & (n - 1) == 0
 
@@ -138,16 +127,14 @@
     return jnp.concatenate(blocks, axis=0)
 
 
-def scatter_paired_t(gt, axis, n):
-    width = gt.shape[1] // n
-    total = gt[:, : 2 * width].astype(jnp.float32)
+def scatter_paired(g, axis, n):
+    width = g.shape[0] // n
+    total = g[: 2 * width].astype(jnp.float32)
     for b in range(1, n // 2):
-        got = lax.ppermute(
-            gt[:, 2 * b * width : (2 * b + 2) * width], axis, [(i, i ^ (2 * b)) for i in range(n)]
-        )
+        got = lax.ppermute(g[2 * b * width : (2 * b + 2) * width], axis, [(i, i ^ (2 * b)) for i in range(n)])
         total = total + got.astype(jnp.float32)
-    got = lax.ppermute(total[:, width:], axis, [(i, i ^ 1) for i in range(n)])
-    return (total[:, :width] + got).T
+    got = lax.ppermute(total[width:], axis, [(i, i ^ 1) for i in range(n)])
+    return total[:width] + got
 
 
 def gather_xor(x, axis, n):
@@ -157,13 +144,13 @@
     return jnp.concatenate(pieces, axis=0)
 
 
-def scatter_xor_t(gt, axis, n):
-    width = gt.shape[1] // n
-    total = gt[:, :width].astype(jnp.float32)
+def scatter_xor(g, axis, n):
+    width = g.shape[0] // n
+    total = g[:width].astype(jnp.float32)
     for p in range(1, n):
-        got = lax.ppermute(gt[:, p * width : (p + 1) * width], axis, [(i, i ^ p) for i in range(n)])
+        got = lax.ppermute(g[p * width : (p + 1) * width], axis, [(i, i ^ p) for i in range(n)])
         total = total + got.astype(jnp.float32)
-    return total.T
+    return total
 
 
 def pair_index(index, me, per_run):
@@ -188,11 +175,11 @@
     if paired(n_row):
         cols = pair_index(tile_col[0, 0], me_row, per_run)
         gathers = (gather_paired, gather_xor)
-        scatters = (scatter_xor_t, scatter_paired_t)
+        scatters = (scatter_xor, scatter_paired)
     else:
         cols = rotate_index(tile_col[0, 0], me_row, n_row, per_run)
         gathers = (gather_rotated, gather_rotated)
-        scatters = (scatter_rotated_t, scatter_rotated_t)
+        scatters = (scatter_rotated, scatter_rotated)
     count = tile_count[0, 0]
     emb = emb_in
     ctx = ctx_in
@@ -200,9 +187,9 @@
         emb_low = gather_rotated(emb.astype(jnp.bfloat16), "col", n_col)
         first, last = iteration == 0, iteration == ITERS - 1
         ctx_low = gathers[0 if first else 1](ctx.astype(jnp.bfloat16), "row", n_row)
-        grad_emb, grad_ctx_t = tile_sweep(pos, neg, rows, cols, count, emb_low, ctx_low)
+        grad_emb, grad_ctx = tile_sweep(pos, neg, rows, cols, count, emb_low, ctx_low)
         emb = emb + 0.05 * scatter_rotated(grad_emb, "col", n_col)
-        ctx = ctx + 0.05 * scatters[1 if last else 0](grad_ctx_t, "row", n_row)
+        ctx = ctx + 0.05 * scatters[1 if last else 0](grad_ctx, "row", n_row)
     return (emb, ctx)
 
 

time: 133 us -> 129 us (0.970)
  starting transfers between devices: 43.9 us -> 63.5 us
  Pallas kernels: 31.6 us -> 15.4 us
  local copies, waits for them, and re-layouts: 13.6 us -> 5.86 us
    ppermute x11, starting transfers between devices: 12.8 us -> 33.2 us  [the longest x7 18.3 us: scatter_xor(): lax.ppermute(g[p * width:(p + 1) * width], axis, [(i, i ^ p) for i in ran...]
    pallas_call x2, Pallas kernels: 31.6 us -> 15.4 us  [tile_sweep(): pl.pallas_call(functools.partial(sweep_kernel, tile, group), grid_spec=gr...]
    pallas_call x4 -> x0, local copies, waits for them, and re-layouts: 5.71 us -> none  [tile_sweep(): pl.pallas_call(functools.partial(sweep_kernel, tile, group), grid_spec=gr...]
    ppermute x7, waiting for transfers between devices: 7.8 us -> 2.55 us  [gather_xor(): pieces.append(lax.ppermute(x, axis, [(i, i ^ p) for i in range(n)]))]
    ppermute x6, starting transfers between devices: 10.1 us -> 5.29 us  [scatter_rotated(): lax.ppermute(chunks[(n - s) % n], axis, [(i, (i + s) % n) for i in range(...]
    ppermute x11, waiting for transfers between devices: 3.26 us -> 7.35 us  [the longest x7 5.02 us: scatter_xor(): lax.ppermute(g[p * width:(p + 1) * width], axis, [(i, i ^ p) for i in ran...]
    unnamed x27 -> x17, local copies, waits for them, and re-layouts: 4.82 us -> 1.22 us
    ppermute x6, starting transfers between devices: 11.1 us -> 14.5 us  [gather_rotated(): pieces.append(lax.ppermute(x, axis, [(i, (i + s) % n) for i in range(n)]))]
  transfers between devices with their start and end apart: 34 -> 34, of which waited for: 13 -> 12; matrix products, arithmetic and copies ran while one was open for 11% -> 8% of each run, Pallas kernels for 0% -> 0%
where the time goes in v6:
time: 129 us
  starting transfers between devices  63.5 us (49%)
  waiting for transfers between devices  31.7 us (25%)
  Pallas kernels  15.4 us (12%)
  other arithmetic  10.6 us (8%)
  local copies, waits for them, and re-layouts  5.86 us (5%)
  between operations  1.55 us (1%)
    ppermute x7, starting transfers between devices, scatter_xor(): lax.ppermute(g[p * width:(p + 1) * width], axis, [(i, i ^ p) for i in ran...  18.3 us
    pallas_call x2, Pallas kernels, tile_sweep(): pl.pallas_call(functools.partial(sweep_kernel, tile, group), grid_spec=gr...  15.4 us
    ppermute x3, starting transfers between devices, scatter_paired(): lax.ppermute(g[2 * b * width:(2 * b + 2) * width], axis, [(i, i ^ 2 * b)...  14.9 us
    ppermute x6, starting transfers between devices, gather_rotated(): pieces.append(lax.ppermute(x, axis, [(i, (i + s) % n) for i in range(n)]))  14.5 us
    ppermute x3, waiting for transfers between devices, gather_paired(): blocks.append(lax.ppermute(pair, axis, [(i, i ^ 2 * b) for i in range(n)]))  10.4 us
    ppermute x7, starting transfers between devices, gather_xor(): pieces.append(lax.ppermute(x, axis, [(i, i ^ p) for i in range(n)]))  6.91 us
    ppermute x6, waiting for transfers between devices, scatter_rotated(): lax.ppermute(chunks[(n - s) % n], axis, [(i, (i + s) % n) for i in range(...  6.14 us
    ppermute x6, starting transfers between devices, scatter_rotated(): lax.ppermute(chunks[(n - s) % n], axis, [(i, (i + s) % n) for i in range(...  5.29 us
  transfers between devices with their start and end apart: 34, of which 12 were waited for; matrix products, arithmetic and copies ran while one was open for 8% of the time, Pallas kernels for 0%

profile of v6, /device:TPU:0, one launch (start us, length us, event | category | flops | bytes accessed | tf_op | source)
XLA Modules:
  0.0 128.6 jit_solution(6484014902546700015)
XLA Ops:
  1.6 3.1 %collective-permute-start = (bf16[512,128]{1,0:T(8,128)(2,1)S(1)}, bf16[512,128]{1,0:T(8,128)(2,1)S(1)}, u32[]{:S(2)}, u32[]{:S(2)}) collective-permute-start(bf16[512,128]{1,0:T(8,128)(2,1)S(1)} %convert_element_type.72), channel_id=1, source_target_pairs={{0,1},{1,2},{2,3},{3,0},{4,5},{5,6},{6,7},{7,4},{8,9},{9,10},{10,1... | collective-permute-start | bytes 393224 | tf_op jit(solution)/shard_map/ppermute | solution.py:105
  4.7 2.6 %collective-permute-start.1 = (bf16[512,128]{1,0:T(8,128)(2,1)S(1)}, bf16[512,128]{1,0:T(8,128)(2,1)S(1)}, u32[]{:S(2)}, u32[]{:S(2)}) collective-permute-start(bf16[512,128]{1,0:T(8,128)(2,1)S(1)} %convert_element_type.72), channel_id=1, source_target_pairs={{0,2},{1,3},{2,0},{3,1},{4,6},{5,7},{6,4},{7,5},{8,10},{9,11},{10,... | collective-permute-start | bytes 393224 | tf_op jit(solution)/shard_map/ppermute | solution.py:105
  7.3 1.3 %collective-permute-start.2 = (bf16[512,128]{1,0:T(8,128)(2,1)S(1)}, bf16[512,128]{1,0:T(8,128)(2,1)S(1)}, u32[]{:S(2)}, u32[]{:S(2)}) collective-permute-start(bf16[512,128]{1,0:T(8,128)(2,1)S(1)} %convert_element_type.72), channel_id=1, source_target_pairs={{0,3},{1,0},{2,1},{3,2},{4,7},{5,4},{6,5},{7,6},{8,11},{9,8},{10,9... | collective-permute-start | bytes 393224 | tf_op jit(solution)/shard_map/ppermute | solution.py:105
  11.6 1.6 %collective-permute-start.4 = (bf16[1024,128]{1,0:T(8,128)(2,1)S(1)}, bf16[1024,128]{1,0:T(8,128)(2,1)S(1)}, u32[]{:S(2)}, u32[]{:S(2)}) collective-permute-start(bf16[1024,128]{1,0:T(8,128)(2,1)S(1)} %pad_maximum_fusion.2), channel_id=1, source_target_pairs={{0,8},{4,12},{8,0},{12,4},{16,24},{20,28},{24,16},{28,20},{1,9},{5... | collective-permute-start | bytes 786440 | tf_op jit(solution)/shard_map/ppermute | solution.py:126
  13.1 1.5 %collective-permute-start.5 = (bf16[1024,128]{1,0:T(8,128)(2,1)S(1)}, bf16[1024,128]{1,0:T(8,128)(2,1)S(1)}, u32[]{:S(2)}, u32[]{:S(2)}) collective-permute-start(bf16[1024,128]{1,0:T(8,128)(2,1)S(1)} %pad_maximum_fusion.2), channel_id=1, source_target_pairs={{0,16},{4,20},{8,24},{12,28},{16,0},{20,4},{24,8},{28,12},{1,17},{... | collective-permute-start | bytes 786440 | tf_op jit(solution)/shard_map/ppermute | solution.py:126
  16.8 4.0 %collective-permute-done.4 = bf16[1024,128]{1,0:T(8,128)(2,1)S(1)} collective-permute-done((bf16[1024,128]{1,0:T(8,128)(2,1)S(1)}, bf16[1024,128]{1,0:T(8,128)(2,1)S(1)}, u32[]{:S(2)}, u32[]{:S(2)}) %collective-permute-start.4) | collective-permute-done | bytes 262176 | tf_op jit(solution)/shard_map/ppermute | solution.py:126
  20.8 6.4 %collective-permute-done.5 = bf16[1024,128]{1,0:T(8,128)(2,1)S(1)} collective-permute-done((bf16[1024,128]{1,0:T(8,128)(2,1)S(1)}, bf16[1024,128]{1,0:T(8,128)(2,1)S(1)}, u32[]{:S(2)}, u32[]{:S(2)}) %collective-permute-start.5) | collective-permute-done | bytes 262176 | tf_op jit(solution)/shard_map/ppermute | solution.py:126
  28.3 7.8 %shard_map.86 = (bf16[2048,128]{1,0:T(8,128)(2,1)}, bf16[4096,128]{1,0:T(8,128)(2,1)}) custom-call(s32[64]{0:T(128)} %get-tuple-element.31.rows_ref, s32[64]{0:T(128)} %get-tuple-element.32.cols_ref, s32[1]{0:T(128)} %bitcast.29.count_ref, bf16[2048,128]{1,0:T(8,128)(2,1)} %pad_maximum_fusion.emb_ref, bf16[4096,128]{1,0:T(8,128)(2,1)} %copy-done.2, ...), custom_call_target="tpu_custom_call" | custom-call | flops 3221225472 | bytes 21495808 | tf_op jit(solution)/shard_map/pallas_call | solution.py:86
  36.1 1.3 %fusion.8 = (bf16[512,128]{1,0:T(8,128)(2,1)S(1)}, bf16[512,128]{1,0:T(8,128)(2,1)S(1)}, bf16[512,128]{1,0:T(8,128)(2,1)S(1)}, bf16[512,128]{1,0:T(8,128)(2,1)S(...) fusion(bf16[4096,128]{1,0:T(8,128)(2,1)} %get-tuple-element.7), kind=kLoop, calls=%fused_computation.44 | loop fusion | bytes 1835008 | tf_op jit(solution)/shard_map/slice | solution.py:151
  37.4 3.1 %collective-permute-start.13 = (bf16[512,128]{1,0:T(8,128)(2,1)S(1)}, bf16[512,128]{1,0:T(8,128)(2,1)S(1)}, u32[]{:S(2)}, u32[]{:S(2)}) collective-permute-start(bf16[512,128]{1,0:T(8,128)(2,1)S(1)} %get-tuple-element.18), channel_id=1, source_target_pairs={{0,4},{4,0},{8,12},{12,8},{16,20},{20,16},{24,28},{28,24},{1,5},{5... | collective-permute-start | bytes 393224 | tf_op jit(solution)/shard_map/ppermute | solution.py:151
  40.4 1.4 %collective-permute-start.15 = (bf16[512,128]{1,0:T(8,128)(2,1)S(1)}, bf16[512,128]{1,0:T(8,128)(2,1)S(1)}, u32[]{:S(2)}, u32[]{:S(2)}) collective-permute-start(bf16[512,128]{1,0:T(8,128)(2,1)S(1)} %get-tuple-element.23), channel_id=1, source_target_pairs={{0,12},{4,8},{8,4},{12,0},{16,28},{20,24},{24,20},{28,16},{1,13},{... | collective-permute-start | bytes 393224 | tf_op jit(solution)/shard_map/ppermute | solution.py:151
  41.9 9.3 %collective-permute-start.16 = (bf16[512,128]{1,0:T(8,128)(2,1)S(1)}, bf16[512,128]{1,0:T(8,128)(2,1)S(1)}, u32[]{:S(2)}, u32[]{:S(2)}) collective-permute-start(bf16[512,128]{1,0:T(8,128)(2,1)S(1)} %get-tuple-element.22), channel_id=1, source_target_pairs={{0,16},{4,20},{8,24},{12,28},{16,0},{20,4},{24,8},{28,12},{1,17},{... | collective-permute-start | bytes 393224 | tf_op jit(solution)/shard_map/ppermute | solution.py:151
  51.2 2.9 %collective-permute-start.18 = (bf16[512,128]{1,0:T(8,128)(2,1)S(1)}, bf16[512,128]{1,0:T(8,128)(2,1)S(1)}, u32[]{:S(2)}, u32[]{:S(2)}) collective-permute-start(bf16[512,128]{1,0:T(8,128)(2,1)S(1)} %get-tuple-element.20), channel_id=1, source_target_pairs={{0,24},{4,28},{8,16},{12,20},{16,8},{20,12},{24,0},{28,4},{1,25},{... | collective-permute-start | bytes 393224 | tf_op jit(solution)/shard_map/ppermute | solution.py:151
  54.0 1.6 %collective-permute-start.19 = (bf16[512,128]{1,0:T(8,128)(2,1)S(1)}, bf16[512,128]{1,0:T(8,128)(2,1)S(1)}, u32[]{:S(2)}, u32[]{:S(2)}) collective-permute-start(bf16[512,128]{1,0:T(8,128)(2,1)S(1)} %get-tuple-element.19), channel_id=1, source_target_pairs={{0,28},{4,24},{8,20},{12,16},{16,12},{20,8},{24,4},{28,0},{1,29},{... | collective-permute-start | bytes 393224 | tf_op jit(solution)/shard_map/ppermute | solution.py:151
  56.8 3.7 %collective-permute-done.16 = bf16[512,128]{1,0:T(8,128)(2,1)S(1)} collective-permute-done((bf16[512,128]{1,0:T(8,128)(2,1)S(1)}, bf16[512,128]{1,0:T(8,128)(2,1)S(1)}, u32[]{:S(2)}, u32[]{:S(2)}) %collective-permute-start.16) | collective-permute-done | bytes 131104 | tf_op jit(solution)/shard_map/ppermute | solution.py:151
  61.4 1.3 collective-permute-done.17
  64.6 1.9 %collective-permute-start.21 = (bf16[512,128]{1,0:T(8,128)(2,1)S(1)}, bf16[512,128]{1,0:T(8,128)(2,1)S(1)}, u32[]{:S(2)}, u32[]{:S(2)}) collective-permute-start(bf16[512,128]{1,0:T(8,128)(2,1)S(1)} %get-tuple-element.11), channel_id=1, source_target_pairs={{0,8},{4,12},{8,0},{12,4},{16,24},{20,28},{24,16},{28,20},{1,9},{5... | collective-permute-start | bytes 393224 | tf_op jit(solution)/shard_map/ppermute | solution.py:143
  66.6 4.2 %collective-permute-done.8 = bf16[512,128]{1,0:T(8,128)(2,1)S(1)} collective-permute-done((bf16[512,128]{1,0:T(8,128)(2,1)S(1)}, bf16[512,128]{1,0:T(8,128)(2,1)S(1)}, u32[]{:S(2)}, u32[]{:S(2)}) %collective-permute-start.8) | collective-permute-done | bytes 131104 | tf_op jit(solution)/shard_map/ppermute | solution.py:113
  73.1 1.8 %collective-permute-start.25 = (bf16[512,128]{1,0:T(8,128)(2,1)S(1)}, bf16[512,128]{1,0:T(8,128)(2,1)S(1)}, u32[]{:S(2)}, u32[]{:S(2)}) collective-permute-start(bf16[512,128]{1,0:T(8,128)(2,1)S(1)} %get-tuple-element.11), channel_id=1, source_target_pairs={{0,24},{4,28},{8,16},{12,20},{16,8},{20,12},{24,0},{28,4},{1,25},{... | collective-permute-start | bytes 393224 | tf_op jit(solution)/shard_map/ppermute | solution.py:143
  75.0 1.3 %collective-permute-start.26 = (bf16[512,128]{1,0:T(8,128)(2,1)S(1)}, bf16[512,128]{1,0:T(8,128)(2,1)S(1)}, u32[]{:S(2)}, u32[]{:S(2)}) collective-permute-start(bf16[512,128]{1,0:T(8,128)(2,1)S(1)} %get-tuple-element.11), channel_id=1, source_target_pairs={{0,28},{4,24},{8,20},{12,16},{16,12},{20,8},{24,4},{28,0},{1,29},{... | collective-permute-start | bytes 393224 | tf_op jit(solution)/shard_map/ppermute | solution.py:143
  77.3 2.4 %collective-permute-start.11 = (bf16[512,128]{1,0:T(8,128)(2,1)S(1)}, bf16[512,128]{1,0:T(8,128)(2,1)S(1)}, u32[]{:S(2)}, u32[]{:S(2)}) collective-permute-start(bf16[512,128]{1,0:T(8,128)(2,1)S(1)} %fusion.6), channel_id=1, source_target_pairs={{0,2},{1,3},{2,0},{3,1},{4,6},{5,7},{6,4},{7,5},{8,10},{9,11},{10,... | collective-permute-start | bytes 393224 | tf_op jit(solution)/shard_map/ppermute | solution.py:105
  79.7 2.5 %collective-permute-done.24 = bf16[512,128]{1,0:T(8,128)(2,1)S(1)} collective-permute-done((bf16[512,128]{1,0:T(8,128)(2,1)S(1)}, bf16[512,128]{1,0:T(8,128)(2,1)S(1)}, u32[]{:S(2)}, u32[]{:S(2)}) %collective-permute-start.24) | collective-permute-done | bytes 131104 | tf_op jit(solution)/shard_map/ppermute | solution.py:143
  82.3 4.2 %collective-permute-start.12 = (bf16[512,128]{1,0:T(8,128)(2,1)S(1)}, bf16[512,128]{1,0:T(8,128)(2,1)S(1)}, u32[]{:S(2)}, u32[]{:S(2)}) collective-permute-start(bf16[512,128]{1,0:T(8,128)(2,1)S(1)} %fusion.6), channel_id=1, source_target_pairs={{0,3},{1,0},{2,1},{3,2},{4,7},{5,4},{6,5},{7,6},{8,11},{9,8},{10,9... | collective-permute-start | bytes 393224 | tf_op jit(solution)/shard_map/ppermute | solution.py:105
  86.6 2.8 %collective-permute-done.11 = bf16[512,128]{1,0:T(8,128)(2,1)S(1)} collective-permute-done((bf16[512,128]{1,0:T(8,128)(2,1)S(1)}, bf16[512,128]{1,0:T(8,128)(2,1)S(1)}, u32[]{:S(2)}, u32[]{:S(2)}) %collective-permute-start.11) | collective-permute-done | bytes 131104 | tf_op jit(solution)/shard_map/ppermute | solution.py:105
  89.4 1.7 %collective-permute-done.12 = bf16[512,128]{1,0:T(8,128)(2,1)S(1)} collective-permute-done((bf16[512,128]{1,0:T(8,128)(2,1)S(1)}, bf16[512,128]{1,0:T(8,128)(2,1)S(1)}, u32[]{:S(2)}, u32[]{:S(2)}) %collective-permute-start.12) | collective-permute-done | bytes 131104 | tf_op jit(solution)/shard_map/ppermute | solution.py:105
  91.9 7.6 %shard_map.87 = (bf16[2048,128]{1,0:T(8,128)(2,1)}, bf16[4096,128]{1,0:T(8,128)(2,1)}) custom-call(s32[64]{0:T(128)} %get-tuple-element.31.rows_ref, s32[64]{0:T(128)} %get-tuple-element.32.cols_ref, s32[1]{0:T(128)} %bitcast.30.count_ref, bf16[2048,128]{1,0:T(8,128)(2,1)} %pad_maximum_fusion.1.emb_ref, bf16[4096,128]{1,0:T(8,128)(2,1)} %copy-done.1, ...), custom_call_target="tpu_custom_call" | custom-call | flops 3221225472 | bytes 21495808 | tf_op jit(solution)/shard_map/pallas_call | solution.py:86
  101.8 13.8 %collective-permute-start.31 = (bf16[1024,128]{1,0:T(8,128)(2,1)S(1)}, bf16[1024,128]{1,0:T(8,128)(2,1)S(1)}, u32[]{:S(2)}, u32[]{:S(2)}) collective-permute-start(bf16[1024,128]{1,0:T(8,128)(2,1)S(1)} %get-tuple-element.17), channel_id=1, source_target_pairs={{0,16},{4,20},{8,24},{12,28},{16,0},{20,4},{24,8},{28,12},{1,17},{... | collective-permute-start | bytes 786440 | tf_op jit(solution)/shard_map/ppermute | solution.py:134
  116.7 1.6 %collective-permute-start.28 = (bf16[512,128]{1,0:T(8,128)(2,1)S(1)}, bf16[512,128]{1,0:T(8,128)(2,1)S(1)}, u32[]{:S(2)}, u32[]{:S(2)}) collective-permute-start(bf16[512,128]{1,0:T(8,128)(2,1)S(1)} %get-tuple-element.27), channel_id=1, source_target_pairs={{0,2},{1,3},{2,0},{3,1},{4,6},{5,7},{6,4},{7,5},{8,10},{9,11},{10,... | collective-permute-start | bytes 393224 | tf_op jit(solution)/shard_map/ppermute | solution.py:113
  118.3 2.2 %collective-permute-start.29 = (bf16[512,128]{1,0:T(8,128)(2,1)S(1)}, bf16[512,128]{1,0:T(8,128)(2,1)S(1)}, u32[]{:S(2)}, u32[]{:S(2)}) collective-permute-start(bf16[512,128]{1,0:T(8,128)(2,1)S(1)} %get-tuple-element.26), channel_id=1, source_target_pairs={{0,3},{1,0},{2,1},{3,2},{4,7},{5,4},{6,5},{7,6},{8,11},{9,8},{10,9... | collective-permute-start | bytes 393224 | tf_op jit(solution)/shard_map/ppermute | solution.py:113
  120.5 1.8 %collective-permute-done.31 = bf16[1024,128]{1,0:T(8,128)(2,1)S(1)} collective-permute-done((bf16[1024,128]{1,0:T(8,128)(2,1)S(1)}, bf16[1024,128]{1,0:T(8,128)(2,1)S(1)}, u32[]{:S(2)}, u32[]{:S(2)}) %collective-permute-start.31) | collective-permute-done | bytes 262176 | tf_op jit(solution)/shard_map/ppermute | solution.py:134
  124.0 2.0 %collective-permute-done.28 = bf16[512,128]{1,0:T(8,128)(2,1)S(1)} collective-permute-done((bf16[512,128]{1,0:T(8,128)(2,1)S(1)}, bf16[512,128]{1,0:T(8,128)(2,1)S(1)}, u32[]{:S(2)}, u32[]{:S(2)}) %collective-permute-start.28) | collective-permute-done | bytes 131104 | tf_op jit(solution)/shard_map/ppermute | solution.py:113
  126.0 1.8 %multiply_add_fusion = f32[512,128]{1,0:T(8,128)} fusion(bf16[512,128]{1,0:T(8,128)(2,1)S(1)} %collective-permute-done.29, bf16[512,128]{1,0:T(8,128)(2,1)S(1)} %collective-permute-done.28, bf16[512,128]{1,0:T(8,128)(2,1)S(1)} %collective-permute-done.27, bf16[2048,128]{1,0:T(8,128)(2,1)} %get-tuple-element.8, f32[512,128]{1,0:T(8,128)S(1)} %copy-done, ...), kind=kLoop, calls=%fused_computation.7 | loop fusion | flops 1179648 | bytes 1572864 | tf_op jit(solution)/shard_map/add | solution.py:191
  (73 shorter events, 20.6 us)
Async XLA Ops:
  1.6 13.1 %collective-permute-start = (bf16[512,128]{1,0:T(8,128)(2,1)S(1)}, bf16[512,128]{1,0:T(8,128)(2,1)S(1)}, u32[]{:S(2)}, u32[]{:S(2)}) collective-permute-start(bf16[512,128]{1,0:T(8,128)(2,1)S(1)} %convert_element_type.72), channel_id=1, source_target_pairs={{0,1},{1,2},{2,3},{3,0},{4,5},{5,6},{6,7},{7,4},{8,9},{9,10},{10,1... | collective-permute-start | bytes 393224 | tf_op jit(solution)/shard_map/ppermute | solution.py:105
  4.7 11.2 %collective-permute-start.1 = (bf16[512,128]{1,0:T(8,128)(2,1)S(1)}, bf16[512,128]{1,0:T(8,128)(2,1)S(1)}, u32[]{:S(2)}, u32[]{:S(2)}) collective-permute-start(bf16[512,128]{1,0:T(8,128)(2,1)S(1)} %convert_element_type.72), channel_id=1, source_target_pairs={{0,2},{1,3},{2,0},{3,1},{4,6},{5,7},{6,4},{7,5},{8,10},{9,11},{10,... | collective-permute-start | bytes 393224 | tf_op jit(solution)/shard_map/ppermute | solution.py:105
  7.3 8.6 %collective-permute-start.2 = (bf16[512,128]{1,0:T(8,128)(2,1)S(1)}, bf16[512,128]{1,0:T(8,128)(2,1)S(1)}, u32[]{:S(2)}, u32[]{:S(2)}) collective-permute-start(bf16[512,128]{1,0:T(8,128)(2,1)S(1)} %convert_element_type.72), channel_id=1, source_target_pairs={{0,3},{1,0},{2,1},{3,2},{4,7},{5,4},{6,5},{7,6},{8,11},{9,8},{10,9... | collective-permute-start | bytes 393224 | tf_op jit(solution)/shard_map/ppermute | solution.py:105
  11.6 9.2 %collective-permute-start.4 = (bf16[1024,128]{1,0:T(8,128)(2,1)S(1)}, bf16[1024,128]{1,0:T(8,128)(2,1)S(1)}, u32[]{:S(2)}, u32[]{:S(2)}) collective-permute-start(bf16[1024,128]{1,0:T(8,128)(2,1)S(1)} %pad_maximum_fusion.2), channel_id=1, source_target_pairs={{0,8},{4,12},{8,0},{12,4},{16,24},{20,28},{24,16},{28,20},{1,9},{5... | collective-permute-start | bytes 786440 | tf_op jit(solution)/shard_map/ppermute | solution.py:126
  13.1 14.0 %collective-permute-start.5 = (bf16[1024,128]{1,0:T(8,128)(2,1)S(1)}, bf16[1024,128]{1,0:T(8,128)(2,1)S(1)}, u32[]{:S(2)}, u32[]{:S(2)}) collective-permute-start(bf16[1024,128]{1,0:T(8,128)(2,1)S(1)} %pad_maximum_fusion.2), channel_id=1, source_target_pairs={{0,16},{4,20},{8,24},{12,28},{16,0},{20,4},{24,8},{28,12},{1,17},{... | collective-permute-start | bytes 786440 | tf_op jit(solution)/shard_map/ppermute | solution.py:126
  14.7 12.6 %collective-permute-start.6 = (bf16[1024,128]{1,0:T(8,128)(2,1)S(1)}, bf16[1024,128]{1,0:T(8,128)(2,1)S(1)}, u32[]{:S(2)}, u32[]{:S(2)}) collective-permute-start(bf16[1024,128]{1,0:T(8,128)(2,1)S(1)} %pad_maximum_fusion.2), channel_id=1, source_target_pairs={{0,24},{4,28},{8,16},{12,20},{16,8},{20,12},{24,0},{28,4},{1,25},{... | collective-permute-start | bytes 786440 | tf_op jit(solution)/shard_map/ppermute | solution.py:126
  37.4 13.8 %collective-permute-start.13 = (bf16[512,128]{1,0:T(8,128)(2,1)S(1)}, bf16[512,128]{1,0:T(8,128)(2,1)S(1)}, u32[]{:S(2)}, u32[]{:S(2)}) collective-permute-start(bf16[512,128]{1,0:T(8,128)(2,1)S(1)} %get-tuple-element.18), channel_id=1, source_target_pairs={{0,4},{4,0},{8,12},{12,8},{16,20},{20,16},{24,28},{28,24},{1,5},{5... | collective-permute-start | bytes 393224 | tf_op jit(solution)/shard_map/ppermute | solution.py:151
  40.4 13.6 %collective-permute-start.14 = (bf16[512,128]{1,0:T(8,128)(2,1)S(1)}, bf16[512,128]{1,0:T(8,128)(2,1)S(1)}, u32[]{:S(2)}, u32[]{:S(2)}) collective-permute-start(bf16[512,128]{1,0:T(8,128)(2,1)S(1)} %get-tuple-element.24), channel_id=1, source_target_pairs={{0,8},{4,12},{8,0},{12,4},{16,24},{20,28},{24,16},{28,20},{1,9},{5... | collective-permute-start | bytes 393224 | tf_op jit(solution)/shard_map/ppermute | solution.py:151
  40.4 16.3 %collective-permute-start.15 = (bf16[512,128]{1,0:T(8,128)(2,1)S(1)}, bf16[512,128]{1,0:T(8,128)(2,1)S(1)}, u32[]{:S(2)}, u32[]{:S(2)}) collective-permute-start(bf16[512,128]{1,0:T(8,128)(2,1)S(1)} %get-tuple-element.23), channel_id=1, source_target_pairs={{0,12},{4,8},{8,4},{12,0},{16,28},{20,24},{24,20},{28,16},{1,13},{... | collective-permute-start | bytes 393224 | tf_op jit(solution)/shard_map/ppermute | solution.py:151
  41.9 18.6 %collective-permute-start.16 = (bf16[512,128]{1,0:T(8,128)(2,1)S(1)}, bf16[512,128]{1,0:T(8,128)(2,1)S(1)}, u32[]{:S(2)}, u32[]{:S(2)}) collective-permute-start(bf16[512,128]{1,0:T(8,128)(2,1)S(1)} %get-tuple-element.22), channel_id=1, source_target_pairs={{0,16},{4,20},{8,24},{12,28},{16,0},{20,4},{24,8},{28,12},{1,17},{... | collective-permute-start | bytes 393224 | tf_op jit(solution)/shard_map/ppermute | solution.py:151
  51.1 11.5 %collective-permute-start.17 = (bf16[512,128]{1,0:T(8,128)(2,1)S(1)}, bf16[512,128]{1,0:T(8,128)(2,1)S(1)}, u32[]{:S(2)}, u32[]{:S(2)}) collective-permute-start(bf16[512,128]{1,0:T(8,128)(2,1)S(1)} %get-tuple-element.21), channel_id=1, source_target_pairs={{0,20},{4,16},{8,28},{12,24},{16,4},{20,0},{24,12},{28,8},{1,21},{... | collective-permute-start | bytes 393224 | tf_op jit(solution)/shard_map/ppermute | solution.py:151
  51.2 12.0 %collective-permute-start.18 = (bf16[512,128]{1,0:T(8,128)(2,1)S(1)}, bf16[512,128]{1,0:T(8,128)(2,1)S(1)}, u32[]{:S(2)}, u32[]{:S(2)}) collective-permute-start(bf16[512,128]{1,0:T(8,128)(2,1)S(1)} %get-tuple-element.20), channel_id=1, source_target_pairs={{0,24},{4,28},{8,16},{12,20},{16,8},{20,12},{24,0},{28,4},{1,25},{... | collective-permute-start | bytes 393224 | tf_op jit(solution)/shard_map/ppermute | solution.py:151
  54.0 9.1 %collective-permute-start.19 = (bf16[512,128]{1,0:T(8,128)(2,1)S(1)}, bf16[512,128]{1,0:T(8,128)(2,1)S(1)}, u32[]{:S(2)}, u32[]{:S(2)}) collective-permute-start(bf16[512,128]{1,0:T(8,128)(2,1)S(1)} %get-tuple-element.19), channel_id=1, source_target_pairs={{0,28},{4,24},{8,20},{12,16},{16,12},{20,8},{24,4},{28,0},{1,29},{... | collective-permute-start | bytes 393224 | tf_op jit(solution)/shard_map/ppermute | solution.py:151
  56.7 9.9 %collective-permute-start.7 = (bf16[512,128]{1,0:T(8,128)(2,1)S(1)}, bf16[512,128]{1,0:T(8,128)(2,1)S(1)}, u32[]{:S(2)}, u32[]{:S(2)}) collective-permute-start(bf16[512,128]{1,0:T(8,128)(2,1)S(1)} %get-tuple-element.28), channel_id=1, source_target_pairs={{0,1},{1,2},{2,3},{3,0},{4,5},{5,6},{6,7},{7,4},{8,9},{9,10},{10,1... | collective-permute-start | bytes 393224 | tf_op jit(solution)/shard_map/ppermute | solution.py:113
  60.5 10.3 %collective-permute-start.8 = (bf16[512,128]{1,0:T(8,128)(2,1)S(1)}, bf16[512,128]{1,0:T(8,128)(2,1)S(1)}, u32[]{:S(2)}, u32[]{:S(2)}) collective-permute-start(bf16[512,128]{1,0:T(8,128)(2,1)S(1)} %get-tuple-element.30), channel_id=1, source_target_pairs={{0,2},{1,3},{2,0},{3,1},{4,6},{5,7},{6,4},{7,5},{8,10},{9,11},{10,... | collective-permute-start | bytes 393224 | tf_op jit(solution)/shard_map/ppermute | solution.py:113
  62.6 8.7 %collective-permute-start.9 = (bf16[512,128]{1,0:T(8,128)(2,1)S(1)}, bf16[512,128]{1,0:T(8,128)(2,1)S(1)}, u32[]{:S(2)}, u32[]{:S(2)}) collective-permute-start(bf16[512,128]{1,0:T(8,128)(2,1)S(1)} %get-tuple-element.29), channel_id=1, source_target_pairs={{0,3},{1,0},{2,1},{3,2},{4,7},{5,4},{6,5},{7,6},{8,11},{9,8},{10,9... | collective-permute-start | bytes 393224 | tf_op jit(solution)/shard_map/ppermute | solution.py:113
  64.2 8.9 %collective-permute-start.20 = (bf16[512,128]{1,0:T(8,128)(2,1)S(1)}, bf16[512,128]{1,0:T(8,128)(2,1)S(1)}, u32[]{:S(2)}, u32[]{:S(2)}) collective-permute-start(bf16[512,128]{1,0:T(8,128)(2,1)S(1)} %get-tuple-element.11), channel_id=1, source_target_pairs={{0,4},{4,0},{8,12},{12,8},{16,20},{20,16},{24,28},{28,24},{1,5},{5... | collective-permute-start | bytes 393224 | tf_op jit(solution)/shard_map/ppermute | solution.py:143
  64.6 10.3 %collective-permute-start.21 = (bf16[512,128]{1,0:T(8,128)(2,1)S(1)}, bf16[512,128]{1,0:T(8,128)(2,1)S(1)}, u32[]{:S(2)}, u32[]{:S(2)}) collective-permute-start(bf16[512,128]{1,0:T(8,128)(2,1)S(1)} %get-tuple-element.11), channel_id=1, source_target_pairs={{0,8},{4,12},{8,0},{12,4},{16,24},{20,28},{24,16},{28,20},{1,9},{5... | collective-permute-start | bytes 393224 | tf_op jit(solution)/shard_map/ppermute | solution.py:143
  66.6 9.8 %collective-permute-start.22 = (bf16[512,128]{1,0:T(8,128)(2,1)S(1)}, bf16[512,128]{1,0:T(8,128)(2,1)S(1)}, u32[]{:S(2)}, u32[]{:S(2)}) collective-permute-start(bf16[512,128]{1,0:T(8,128)(2,1)S(1)} %get-tuple-element.11), channel_id=1, source_target_pairs={{0,12},{4,8},{8,4},{12,0},{16,28},{20,24},{24,20},{28,16},{1,13},{... | collective-permute-start | bytes 393224 | tf_op jit(solution)/shard_map/ppermute | solution.py:143
  70.7 6.6 %collective-permute-start.23 = (bf16[512,128]{1,0:T(8,128)(2,1)S(1)}, bf16[512,128]{1,0:T(8,128)(2,1)S(1)}, u32[]{:S(2)}, u32[]{:S(2)}) collective-permute-start(bf16[512,128]{1,0:T(8,128)(2,1)S(1)} %get-tuple-element.11), channel_id=1, source_target_pairs={{0,16},{4,20},{8,24},{12,28},{16,0},{20,4},{24,8},{28,12},{1,17},{... | collective-permute-start | bytes 393224 | tf_op jit(solution)/shard_map/ppermute | solution.py:143
  71.3 10.9 %collective-permute-start.24 = (bf16[512,128]{1,0:T(8,128)(2,1)S(1)}, bf16[512,128]{1,0:T(8,128)(2,1)S(1)}, u32[]{:S(2)}, u32[]{:S(2)}) collective-permute-start(bf16[512,128]{1,0:T(8,128)(2,1)S(1)} %get-tuple-element.11), channel_id=1, source_target_pairs={{0,20},{4,16},{8,28},{12,24},{16,4},{20,0},{24,12},{28,8},{1,21},{... | collective-permute-start | bytes 393224 | tf_op jit(solution)/shard_map/ppermute | solution.py:143
  73.1 13.4 %collective-permute-start.25 = (bf16[512,128]{1,0:T(8,128)(2,1)S(1)}, bf16[512,128]{1,0:T(8,128)(2,1)S(1)}, u32[]{:S(2)}, u32[]{:S(2)}) collective-permute-start(bf16[512,128]{1,0:T(8,128)(2,1)S(1)} %get-tuple-element.11), channel_id=1, source_target_pairs={{0,24},{4,28},{8,16},{12,20},{16,8},{20,12},{24,0},{28,4},{1,25},{... | collective-permute-start | bytes 393224 | tf_op jit(solution)/shard_map/ppermute | solution.py:143
  75.0 11.5 %collective-permute-start.26 = (bf16[512,128]{1,0:T(8,128)(2,1)S(1)}, bf16[512,128]{1,0:T(8,128)(2,1)S(1)}, u32[]{:S(2)}, u32[]{:S(2)}) collective-permute-start(bf16[512,128]{1,0:T(8,128)(2,1)S(1)} %get-tuple-element.11), channel_id=1, source_target_pairs={{0,28},{4,24},{8,20},{12,16},{16,12},{20,8},{24,4},{28,0},{1,29},{... | collective-permute-start | bytes 393224 | tf_op jit(solution)/shard_map/ppermute | solution.py:143
  76.4 10.2 %collective-permute-start.10 = (bf16[512,128]{1,0:T(8,128)(2,1)S(1)}, bf16[512,128]{1,0:T(8,128)(2,1)S(1)}, u32[]{:S(2)}, u32[]{:S(2)}) collective-permute-start(bf16[512,128]{1,0:T(8,128)(2,1)S(1)} %fusion.6), channel_id=1, source_target_pairs={{0,1},{1,2},{2,3},{3,0},{4,5},{5,6},{6,7},{7,4},{8,9},{9,10},{10,1... | collective-permute-start | bytes 393224 | tf_op jit(solution)/shard_map/ppermute | solution.py:105
  77.3 12.0 %collective-permute-start.11 = (bf16[512,128]{1,0:T(8,128)(2,1)S(1)}, bf16[512,128]{1,0:T(8,128)(2,1)S(1)}, u32[]{:S(2)}, u32[]{:S(2)}) collective-permute-start(bf16[512,128]{1,0:T(8,128)(2,1)S(1)} %fusion.6), channel_id=1, source_target_pairs={{0,2},{1,3},{2,0},{3,1},{4,6},{5,7},{6,4},{7,5},{8,10},{9,11},{10,... | collective-permute-start | bytes 393224 | tf_op jit(solution)/shard_map/ppermute | solution.py:105
  82.3 8.8 %collective-permute-start.12 = (bf16[512,128]{1,0:T(8,128)(2,1)S(1)}, bf16[512,128]{1,0:T(8,128)(2,1)S(1)}, u32[]{:S(2)}, u32[]{:S(2)}) collective-permute-start(bf16[512,128]{1,0:T(8,128)(2,1)S(1)} %fusion.6), channel_id=1, source_target_pairs={{0,3},{1,0},{2,1},{3,2},{4,7},{5,4},{6,5},{7,6},{8,11},{9,8},{10,9... | collective-permute-start | bytes 393224 | tf_op jit(solution)/shard_map/ppermute | solution.py:105
  100.7 17.6 %collective-permute-start.30 = (bf16[1024,128]{1,0:T(8,128)(2,1)S(1)}, bf16[1024,128]{1,0:T(8,128)(2,1)S(1)}, u32[]{:S(2)}, u32[]{:S(2)}) collective-permute-start(bf16[1024,128]{1,0:T(8,128)(2,1)S(1)} %get-tuple-element.15), channel_id=1, source_target_pairs={{0,8},{4,12},{8,0},{12,4},{16,24},{20,28},{24,16},{28,20},{1,9},{5... | collective-permute-start | bytes 786440 | tf_op jit(solution)/shard_map/ppermute | solution.py:134
  101.8 20.5 %collective-permute-start.31 = (bf16[1024,128]{1,0:T(8,128)(2,1)S(1)}, bf16[1024,128]{1,0:T(8,128)(2,1)S(1)}, u32[]{:S(2)}, u32[]{:S(2)}) collective-permute-start(bf16[1024,128]{1,0:T(8,128)(2,1)S(1)} %get-tuple-element.17), channel_id=1, source_target_pairs={{0,16},{4,20},{8,24},{12,28},{16,0},{20,4},{24,8},{28,12},{1,17},{... | collective-permute-start | bytes 786440 | tf_op jit(solution)/shard_map/ppermute | solution.py:134
  115.6 7.3 %collective-permute-start.32 = (bf16[1024,128]{1,0:T(8,128)(2,1)S(1)}, bf16[1024,128]{1,0:T(8,128)(2,1)S(1)}, u32[]{:S(2)}, u32[]{:S(2)}) collective-permute-start(bf16[1024,128]{1,0:T(8,128)(2,1)S(1)} %get-tuple-element.16), channel_id=1, source_target_pairs={{0,24},{4,28},{8,16},{12,20},{16,8},{20,12},{24,0},{28,4},{1,25},{... | collective-permute-start | bytes 786440 | tf_op jit(solution)/shard_map/ppermute | solution.py:134
  116.6 7.4 %collective-permute-start.27 = (bf16[512,128]{1,0:T(8,128)(2,1)S(1)}, bf16[512,128]{1,0:T(8,128)(2,1)S(1)}, u32[]{:S(2)}, u32[]{:S(2)}) collective-permute-start(bf16[512,128]{1,0:T(8,128)(2,1)S(1)} %get-tuple-element.25), channel_id=1, source_target_pairs={{0,1},{1,2},{2,3},{3,0},{4,5},{5,6},{6,7},{7,4},{8,9},{9,10},{10,1... | collective-permute-start | bytes 393224 | tf_op jit(solution)/shard_map/ppermute | solution.py:113
  116.7 9.3 %collective-permute-start.28 = (bf16[512,128]{1,0:T(8,128)(2,1)S(1)}, bf16[512,128]{1,0:T(8,128)(2,1)S(1)}, u32[]{:S(2)}, u32[]{:S(2)}) collective-permute-start(bf16[512,128]{1,0:T(8,128)(2,1)S(1)} %get-tuple-element.27), channel_id=1, source_target_pairs={{0,2},{1,3},{2,0},{3,1},{4,6},{5,7},{6,4},{7,5},{8,10},{9,11},{10,... | collective-permute-start | bytes 393224 | tf_op jit(solution)/shard_map/ppermute | solution.py:113
  118.3 7.7 %collective-permute-start.29 = (bf16[512,128]{1,0:T(8,128)(2,1)S(1)}, bf16[512,128]{1,0:T(8,128)(2,1)S(1)}, u32[]{:S(2)}, u32[]{:S(2)}) collective-permute-start(bf16[512,128]{1,0:T(8,128)(2,1)S(1)} %get-tuple-element.26), channel_id=1, source_target_pairs={{0,3},{1,0},{2,1},{3,2},{4,7},{5,4},{6,5},{7,6},{8,11},{9,8},{10,9... | collective-permute-start | bytes 393224 | tf_op jit(solution)/shard_map/ppermute | solution.py:113
  (6 other events, 90.9 us)

commit v7 on v6

--- a/solution.py
+++ b/solution.py
@@ -11,14 +11,15 @@
 
 
 def sweep_kernel(tile, group, rows_ref, cols_ref, count_ref, emb_ref, ctx_ref, pos_ref, neg_ref,
-                 gemb_ref, gctx_ref, acc_e, acc_c):
+                 gemb_ref, gctx_ref, acc_e, acc_ct, emb_t):
     k = pl.program_id(0)
     n = count_ref[0]
 
     @pl.when(k == 0)
     def _():
         acc_e[...] = jnp.zeros_like(acc_e)
-        acc_c[...] = jnp.zeros_like(acc_c)
+        acc_ct[...] = jnp.zeros_like(acc_ct)
+        emb_t[...] = emb_ref[...].astype(jnp.float32).T.astype(emb_t.dtype)
 
     def visit(j):
         slot = k * group + j
@@ -32,8 +33,8 @@
         t = jnp.tanh(score * 0.5)
         coeff = (0.5 * ((positive - negative) - (positive + negative) * t)).astype(jnp.bfloat16)
         acc_e[pl.ds(r0, tile), :] += jnp.dot(coeff, c, preferred_element_type=jnp.float32)
-        acc_c[pl.ds(c0, tile), :] += lax.dot_general(
-            coeff, e, (((0,), (0,)), ((), ())), preferred_element_type=jnp.float32
+        acc_ct[:, pl.ds(c0, tile)] += jnp.dot(
+            emb_t[:, pl.ds(r0, tile)], coeff, preferred_element_type=jnp.float32
         )
 
     full = (k + 1) * group <= n
@@ -51,7 +52,7 @@
     @pl.when(k == pl.num_programs(0) - 1)
     def _():
         gemb_ref[...] = acc_e[...].astype(gemb_ref.dtype)
-        gctx_ref[...] = acc_c[...].astype(gctx_ref.dtype)
+        gctx_ref[...] = acc_ct[...].T.astype(gctx_ref.dtype)
 
 
 def tile_sweep(pos, neg, rows, cols, count, emb_low, ctx_low):
@@ -79,7 +80,8 @@
         ],
         scratch_shapes=[
             pltpu.VMEM((ne, dim), jnp.float32),
-            pltpu.VMEM((nc, dim), jnp.float32),
+            pltpu.VMEM((dim, nc), jnp.float32),
+            pltpu.VMEM((dim, ne), jnp.bfloat16),
         ],
     )
     flops = cap * 3 * 2 * tile * tile * dim

time: 129 us -> 127 us (0.984)
  waiting for transfers between devices: 31.7 us -> 29.5 us
  starting transfers between devices: 63.5 us -> 65.5 us
  Pallas kernels: 15.4 us -> 14.1 us
    ppermute x6, starting transfers between devices: 5.29 us -> 12.3 us  [scatter_rotated(): lax.ppermute(chunks[(n - s) % n], axis, [(i, (i + s) % n) for i in range(...]
    ppermute x7, starting transfers between devices: 18.3 us -> 14.6 us  [scatter_xor(): lax.ppermute(g[p * width:(p + 1) * width], axis, [(i, i ^ p) for i in ran...]
    ppermute x3, starting transfers between devices: 14.9 us -> 12.4 us  [scatter_paired(): lax.ppermute(g[2 * b * width:(2 * b + 2) * width], axis, [(i, i ^ 2 * b)...]
    ppermute x6, waiting for transfers between devices: 6.14 us -> 4.11 us  [scatter_rotated(): lax.ppermute(chunks[(n - s) % n], axis, [(i, (i + s) % n) for i in range(...]
    pallas_call x2, Pallas kernels: 15.4 us -> 14.1 us  [tile_sweep(): pl.pallas_call(functools.partial(sweep_kernel, tile, group), grid_spec=gr...]
  transfers between devices with their start and end apart: 34 -> 34, of which waited for: 12 -> 13; matrix products, arithmetic and copies ran while one was open for 8% -> 8% of each run, Pallas kernels for 0% -> 0%
where the time goes in v7:
time: 127 us
  starting transfers between devices  65.5 us (52%)
  waiting for transfers between devices  29.5 us (23%)
  Pallas kernels  14.1 us (11%)
  other arithmetic  10.6 us (8%)
  local copies, waits for them, and re-layouts  5.86 us (5%)
  between operations  1.53 us (1%)
    ppermute x6, starting transfers between devices, gather_rotated(): pieces.append(lax.ppermute(x, axis, [(i, (i + s) % n) for i in range(n)]))  15.4 us
    ppermute x7, starting transfers between devices, scatter_xor(): lax.ppermute(g[p * width:(p + 1) * width], axis, [(i, i ^ p) for i in ran...  14.6 us
    pallas_call x2, Pallas kernels, tile_sweep(): pl.pallas_call(functools.partial(sweep_kernel, tile, group), grid_spec=gr...  14.1 us
    ppermute x3, starting transfers between devices, scatter_paired(): lax.ppermute(g[2 * b * width:(2 * b + 2) * width], axis, [(i, i ^ 2 * b)...  12.4 us
    ppermute x6, starting transfers between devices, scatter_rotated(): lax.ppermute(chunks[(n - s) % n], axis, [(i, (i + s) % n) for i in range(...  12.3 us
    ppermute x3, waiting for transfers between devices, gather_paired(): blocks.append(lax.ppermute(pair, axis, [(i, i ^ 2 * b) for i in range(n)]))  10.4 us
    ppermute x7, starting transfers between devices, gather_xor(): pieces.append(lax.ppermute(x, axis, [(i, i ^ p) for i in range(n)]))  7.28 us
    ppermute x7, waiting for transfers between devices, scatter_xor(): lax.ppermute(g[p * width:(p + 1) * width], axis, [(i, i ^ p) for i in ran...  5.25 us
  transfers between devices with their start and end apart: 34, of which 13 were waited for; matrix products, arithmetic and copies ran while one was open for 8% of the time, Pallas kernels for 0%

profile of v7, /device:TPU:0, one launch (start us, length us, event | category | flops | bytes accessed | tf_op | source)
XLA Modules:
  0.0 127.1 jit_solution(10312097539495194740)
XLA Ops:
  1.6 3.1 %collective-permute-start = (bf16[512,128]{1,0:T(8,128)(2,1)S(1)}, bf16[512,128]{1,0:T(8,128)(2,1)S(1)}, u32[]{:S(2)}, u32[]{:S(2)}) collective-permute-start(bf16[512,128]{1,0:T(8,128)(2,1)S(1)} %convert_element_type.72), channel_id=1, source_target_pairs={{0,1},{1,2},{2,3},{3,0},{4,5},{5,6},{6,7},{7,4},{8,9},{9,10},{10,1... | collective-permute-start | bytes 393224 | tf_op jit(solution)/shard_map/ppermute | solution.py:107
  4.7 2.6 %collective-permute-start.1 = (bf16[512,128]{1,0:T(8,128)(2,1)S(1)}, bf16[512,128]{1,0:T(8,128)(2,1)S(1)}, u32[]{:S(2)}, u32[]{:S(2)}) collective-permute-start(bf16[512,128]{1,0:T(8,128)(2,1)S(1)} %convert_element_type.72), channel_id=1, source_target_pairs={{0,2},{1,3},{2,0},{3,1},{4,6},{5,7},{6,4},{7,5},{8,10},{9,11},{10,... | collective-permute-start | bytes 393224 | tf_op jit(solution)/shard_map/ppermute | solution.py:107
  7.3 1.3 %collective-permute-start.2 = (bf16[512,128]{1,0:T(8,128)(2,1)S(1)}, bf16[512,128]{1,0:T(8,128)(2,1)S(1)}, u32[]{:S(2)}, u32[]{:S(2)}) collective-permute-start(bf16[512,128]{1,0:T(8,128)(2,1)S(1)} %convert_element_type.72), channel_id=1, source_target_pairs={{0,3},{1,0},{2,1},{3,2},{4,7},{5,4},{6,5},{7,6},{8,11},{9,8},{10,9... | collective-permute-start | bytes 393224 | tf_op jit(solution)/shard_map/ppermute | solution.py:107
  11.6 1.6 %collective-permute-start.4 = (bf16[1024,128]{1,0:T(8,128)(2,1)S(1)}, bf16[1024,128]{1,0:T(8,128)(2,1)S(1)}, u32[]{:S(2)}, u32[]{:S(2)}) collective-permute-start(bf16[1024,128]{1,0:T(8,128)(2,1)S(1)} %pad_maximum_fusion.2), channel_id=1, source_target_pairs={{0,8},{4,12},{8,0},{12,4},{16,24},{20,28},{24,16},{28,20},{1,9},{5... | collective-permute-start | bytes 786440 | tf_op jit(solution)/shard_map/ppermute | solution.py:128
  13.1 1.5 %collective-permute-start.5 = (bf16[1024,128]{1,0:T(8,128)(2,1)S(1)}, bf16[1024,128]{1,0:T(8,128)(2,1)S(1)}, u32[]{:S(2)}, u32[]{:S(2)}) collective-permute-start(bf16[1024,128]{1,0:T(8,128)(2,1)S(1)} %pad_maximum_fusion.2), channel_id=1, source_target_pairs={{0,16},{4,20},{8,24},{12,28},{16,0},{20,4},{24,8},{28,12},{1,17},{... | collective-permute-start | bytes 786440 | tf_op jit(solution)/shard_map/ppermute | solution.py:128
  16.8 4.0 %collective-permute-done.4 = bf16[1024,128]{1,0:T(8,128)(2,1)S(1)} collective-permute-done((bf16[1024,128]{1,0:T(8,128)(2,1)S(1)}, bf16[1024,128]{1,0:T(8,128)(2,1)S(1)}, u32[]{:S(2)}, u32[]{:S(2)}) %collective-permute-start.4) | collective-permute-done | bytes 262176 | tf_op jit(solution)/shard_map/ppermute | solution.py:128
  20.8 6.4 %collective-permute-done.5 = bf16[1024,128]{1,0:T(8,128)(2,1)S(1)} collective-permute-done((bf16[1024,128]{1,0:T(8,128)(2,1)S(1)}, bf16[1024,128]{1,0:T(8,128)(2,1)S(1)}, u32[]{:S(2)}, u32[]{:S(2)}) %collective-permute-start.5) | collective-permute-done | bytes 262176 | tf_op jit(solution)/shard_map/ppermute | solution.py:128
  28.3 7.1 %shard_map.86 = (bf16[2048,128]{1,0:T(8,128)(2,1)}, bf16[4096,128]{1,0:T(8,128)(2,1)}) custom-call(s32[64]{0:T(128)} %get-tuple-element.31.rows_ref, s32[64]{0:T(128)} %get-tuple-element.32.cols_ref, s32[1]{0:T(128)} %bitcast.29.count_ref, bf16[2048,128]{1,0:T(8,128)(2,1)} %pad_maximum_fusion.emb_ref, bf16[4096,128]{1,0:T(8,128)(2,1)} %copy-done.2, ...), custom_call_target="tpu_custom_call" | custom-call | flops 3221225472 | bytes 21495808 | tf_op jit(solution)/shard_map/pallas_call | solution.py:88
  36.7 6.3 %collective-permute-start.13 = (bf16[512,128]{1,0:T(8,128)(2,1)S(1)}, bf16[512,128]{1,0:T(8,128)(2,1)S(1)}, u32[]{:S(2)}, u32[]{:S(2)}) collective-permute-start(bf16[512,128]{1,0:T(8,128)(2,1)S(1)} %get-tuple-element.18), channel_id=1, source_target_pairs={{0,4},{4,0},{8,12},{12,8},{16,20},{20,16},{24,28},{28,24},{1,5},{5... | collective-permute-start | bytes 393224 | tf_op jit(solution)/shard_map/ppermute | solution.py:153
  43.0 4.8 %collective-permute-start.14 = (bf16[512,128]{1,0:T(8,128)(2,1)S(1)}, bf16[512,128]{1,0:T(8,128)(2,1)S(1)}, u32[]{:S(2)}, u32[]{:S(2)}) collective-permute-start(bf16[512,128]{1,0:T(8,128)(2,1)S(1)} %get-tuple-element.24), channel_id=1, source_target_pairs={{0,8},{4,12},{8,0},{12,4},{16,24},{20,28},{24,16},{28,20},{1,9},{5... | collective-permute-start | bytes 393224 | tf_op jit(solution)/shard_map/ppermute | solution.py:153
  47.9 1.5 %collective-permute-start.17 = (bf16[512,128]{1,0:T(8,128)(2,1)S(1)}, bf16[512,128]{1,0:T(8,128)(2,1)S(1)}, u32[]{:S(2)}, u32[]{:S(2)}) collective-permute-start(bf16[512,128]{1,0:T(8,128)(2,1)S(1)} %get-tuple-element.21), channel_id=1, source_target_pairs={{0,20},{4,16},{8,28},{12,24},{16,4},{20,0},{24,12},{28,8},{1,21},{... | collective-permute-start | bytes 393224 | tf_op jit(solution)/shard_map/ppermute | solution.py:153
  49.4 1.7 %collective-permute-start.18 = (bf16[512,128]{1,0:T(8,128)(2,1)S(1)}, bf16[512,128]{1,0:T(8,128)(2,1)S(1)}, u32[]{:S(2)}, u32[]{:S(2)}) collective-permute-start(bf16[512,128]{1,0:T(8,128)(2,1)S(1)} %get-tuple-element.20), channel_id=1, source_target_pairs={{0,24},{4,28},{8,16},{12,20},{16,8},{20,12},{24,0},{28,4},{1,25},{... | collective-permute-start | bytes 393224 | tf_op jit(solution)/shard_map/ppermute | solution.py:153
  54.5 2.3 %collective-permute-start.7 = (bf16[512,128]{1,0:T(8,128)(2,1)S(1)}, bf16[512,128]{1,0:T(8,128)(2,1)S(1)}, u32[]{:S(2)}, u32[]{:S(2)}) collective-permute-start(bf16[512,128]{1,0:T(8,128)(2,1)S(1)} %get-tuple-element.28), channel_id=1, source_target_pairs={{0,1},{1,2},{2,3},{3,0},{4,5},{5,6},{6,7},{7,4},{8,9},{9,10},{10,1... | collective-permute-start | bytes 393224 | tf_op jit(solution)/shard_map/ppermute | solution.py:115
  56.8 3.1 %collective-permute-done.16 = bf16[512,128]{1,0:T(8,128)(2,1)S(1)} collective-permute-done((bf16[512,128]{1,0:T(8,128)(2,1)S(1)}, bf16[512,128]{1,0:T(8,128)(2,1)S(1)}, u32[]{:S(2)}, u32[]{:S(2)}) %collective-permute-start.16) | collective-permute-done | bytes 131104 | tf_op jit(solution)/shard_map/ppermute | solution.py:153
  59.9 1.6 %collective-permute-start.8 = (bf16[512,128]{1,0:T(8,128)(2,1)S(1)}, bf16[512,128]{1,0:T(8,128)(2,1)S(1)}, u32[]{:S(2)}, u32[]{:S(2)}) collective-permute-start(bf16[512,128]{1,0:T(8,128)(2,1)S(1)} %get-tuple-element.30), channel_id=1, source_target_pairs={{0,2},{1,3},{2,0},{3,1},{4,6},{5,7},{6,4},{7,5},{8,10},{9,11},{10,... | collective-permute-start | bytes 393224 | tf_op jit(solution)/shard_map/ppermute | solution.py:115
  61.5 3.1 %collective-permute-start.9 = (bf16[512,128]{1,0:T(8,128)(2,1)S(1)}, bf16[512,128]{1,0:T(8,128)(2,1)S(1)}, u32[]{:S(2)}, u32[]{:S(2)}) collective-permute-start(bf16[512,128]{1,0:T(8,128)(2,1)S(1)} %get-tuple-element.29), channel_id=1, source_target_pairs={{0,3},{1,0},{2,1},{3,2},{4,7},{5,4},{6,5},{7,6},{8,11},{9,8},{10,9... | collective-permute-start | bytes 393224 | tf_op jit(solution)/shard_map/ppermute | solution.py:115
  65.7 1.8 %collective-permute-start.21 = (bf16[512,128]{1,0:T(8,128)(2,1)S(1)}, bf16[512,128]{1,0:T(8,128)(2,1)S(1)}, u32[]{:S(2)}, u32[]{:S(2)}) collective-permute-start(bf16[512,128]{1,0:T(8,128)(2,1)S(1)} %get-tuple-element.11), channel_id=1, source_target_pairs={{0,8},{4,12},{8,0},{12,4},{16,24},{20,28},{24,16},{28,20},{1,9},{5... | collective-permute-start | bytes 393224 | tf_op jit(solution)/shard_map/ppermute | solution.py:145
  67.8 1.6 %collective-permute-start.23 = (bf16[512,128]{1,0:T(8,128)(2,1)S(1)}, bf16[512,128]{1,0:T(8,128)(2,1)S(1)}, u32[]{:S(2)}, u32[]{:S(2)}) collective-permute-start(bf16[512,128]{1,0:T(8,128)(2,1)S(1)} %get-tuple-element.11), channel_id=1, source_target_pairs={{0,16},{4,20},{8,24},{12,28},{16,0},{20,4},{24,8},{28,12},{1,17},{... | collective-permute-start | bytes 393224 | tf_op jit(solution)/shard_map/ppermute | solution.py:145
  71.3 2.2 %collective-permute-start.25 = (bf16[512,128]{1,0:T(8,128)(2,1)S(1)}, bf16[512,128]{1,0:T(8,128)(2,1)S(1)}, u32[]{:S(2)}, u32[]{:S(2)}) collective-permute-start(bf16[512,128]{1,0:T(8,128)(2,1)S(1)} %get-tuple-element.11), channel_id=1, source_target_pairs={{0,24},{4,28},{8,16},{12,20},{16,8},{20,12},{24,0},{28,4},{1,25},{... | collective-permute-start | bytes 393224 | tf_op jit(solution)/shard_map/ppermute | solution.py:145
  74.3 2.1 %collective-permute-start.10 = (bf16[512,128]{1,0:T(8,128)(2,1)S(1)}, bf16[512,128]{1,0:T(8,128)(2,1)S(1)}, u32[]{:S(2)}, u32[]{:S(2)}) collective-permute-start(bf16[512,128]{1,0:T(8,128)(2,1)S(1)} %fusion.6), channel_id=1, source_target_pairs={{0,1},{1,2},{2,3},{3,0},{4,5},{5,6},{6,7},{7,4},{8,9},{9,10},{10,1... | collective-permute-start | bytes 393224 | tf_op jit(solution)/shard_map/ppermute | solution.py:107
  76.4 1.9 %collective-permute-start.11 = (bf16[512,128]{1,0:T(8,128)(2,1)S(1)}, bf16[512,128]{1,0:T(8,128)(2,1)S(1)}, u32[]{:S(2)}, u32[]{:S(2)}) collective-permute-start(bf16[512,128]{1,0:T(8,128)(2,1)S(1)} %fusion.6), channel_id=1, source_target_pairs={{0,2},{1,3},{2,0},{3,1},{4,6},{5,7},{6,4},{7,5},{8,10},{9,11},{10,... | collective-permute-start | bytes 393224 | tf_op jit(solution)/shard_map/ppermute | solution.py:107
  78.3 2.4 %collective-permute-done.24 = bf16[512,128]{1,0:T(8,128)(2,1)S(1)} collective-permute-done((bf16[512,128]{1,0:T(8,128)(2,1)S(1)}, bf16[512,128]{1,0:T(8,128)(2,1)S(1)}, u32[]{:S(2)}, u32[]{:S(2)}) %collective-permute-start.24) | collective-permute-done | bytes 131104 | tf_op jit(solution)/shard_map/ppermute | solution.py:145
  80.7 4.4 %collective-permute-start.12 = (bf16[512,128]{1,0:T(8,128)(2,1)S(1)}, bf16[512,128]{1,0:T(8,128)(2,1)S(1)}, u32[]{:S(2)}, u32[]{:S(2)}) collective-permute-start(bf16[512,128]{1,0:T(8,128)(2,1)S(1)} %fusion.6), channel_id=1, source_target_pairs={{0,3},{1,0},{2,1},{3,2},{4,7},{5,4},{6,5},{7,6},{8,11},{9,8},{10,9... | collective-permute-start | bytes 393224 | tf_op jit(solution)/shard_map/ppermute | solution.py:107
  85.2 2.3 %collective-permute-done.11 = bf16[512,128]{1,0:T(8,128)(2,1)S(1)} collective-permute-done((bf16[512,128]{1,0:T(8,128)(2,1)S(1)}, bf16[512,128]{1,0:T(8,128)(2,1)S(1)}, u32[]{:S(2)}, u32[]{:S(2)}) %collective-permute-start.11) | collective-permute-done | bytes 131104 | tf_op jit(solution)/shard_map/ppermute | solution.py:107
  87.5 2.0 %collective-permute-done.12 = bf16[512,128]{1,0:T(8,128)(2,1)S(1)} collective-permute-done((bf16[512,128]{1,0:T(8,128)(2,1)S(1)}, bf16[512,128]{1,0:T(8,128)(2,1)S(1)}, u32[]{:S(2)}, u32[]{:S(2)}) %collective-permute-start.12) | collective-permute-done | bytes 131104 | tf_op jit(solution)/shard_map/ppermute | solution.py:107
  90.4 7.0 %shard_map.87 = (bf16[2048,128]{1,0:T(8,128)(2,1)}, bf16[4096,128]{1,0:T(8,128)(2,1)}) custom-call(s32[64]{0:T(128)} %get-tuple-element.31.rows_ref, s32[64]{0:T(128)} %get-tuple-element.32.cols_ref, s32[1]{0:T(128)} %bitcast.30.count_ref, bf16[2048,128]{1,0:T(8,128)(2,1)} %pad_maximum_fusion.1.emb_ref, bf16[4096,128]{1,0:T(8,128)(2,1)} %copy-done.1, ...), custom_call_target="tpu_custom_call" | custom-call | flops 3221225472 | bytes 21495808 | tf_op jit(solution)/shard_map/pallas_call | solution.py:88
  98.5 10.8 %collective-permute-start.30 = (bf16[1024,128]{1,0:T(8,128)(2,1)S(1)}, bf16[1024,128]{1,0:T(8,128)(2,1)S(1)}, u32[]{:S(2)}, u32[]{:S(2)}) collective-permute-start(bf16[1024,128]{1,0:T(8,128)(2,1)S(1)} %get-tuple-element.15), channel_id=1, source_target_pairs={{0,8},{4,12},{8,0},{12,4},{16,24},{20,28},{24,16},{28,20},{1,9},{5... | collective-permute-start | bytes 786440 | tf_op jit(solution)/shard_map/ppermute | solution.py:136
  109.4 1.5 %collective-permute-start.32 = (bf16[1024,128]{1,0:T(8,128)(2,1)S(1)}, bf16[1024,128]{1,0:T(8,128)(2,1)S(1)}, u32[]{:S(2)}, u32[]{:S(2)}) collective-permute-start(bf16[1024,128]{1,0:T(8,128)(2,1)S(1)} %get-tuple-element.16), channel_id=1, source_target_pairs={{0,24},{4,28},{8,16},{12,20},{16,8},{20,12},{24,0},{28,4},{1,25},{... | collective-permute-start | bytes 786440 | tf_op jit(solution)/shard_map/ppermute | solution.py:136
  112.0 3.7 %collective-permute-start.27 = (bf16[512,128]{1,0:T(8,128)(2,1)S(1)}, bf16[512,128]{1,0:T(8,128)(2,1)S(1)}, u32[]{:S(2)}, u32[]{:S(2)}) collective-permute-start(bf16[512,128]{1,0:T(8,128)(2,1)S(1)} %get-tuple-element.25), channel_id=1, source_target_pairs={{0,1},{1,2},{2,3},{3,0},{4,5},{5,6},{6,7},{7,4},{8,9},{9,10},{10,1... | collective-permute-start | bytes 393224 | tf_op jit(solution)/shard_map/ppermute | solution.py:115
  116.5 1.6 %collective-permute-start.29 = (bf16[512,128]{1,0:T(8,128)(2,1)S(1)}, bf16[512,128]{1,0:T(8,128)(2,1)S(1)}, u32[]{:S(2)}, u32[]{:S(2)}) collective-permute-start(bf16[512,128]{1,0:T(8,128)(2,1)S(1)} %get-tuple-element.26), channel_id=1, source_target_pairs={{0,3},{1,0},{2,1},{3,2},{4,7},{5,4},{6,5},{7,6},{8,11},{9,8},{10,9... | collective-permute-start | bytes 393224 | tf_op jit(solution)/shard_map/ppermute | solution.py:115
  120.6 3.9 %collective-permute-done.28 = bf16[512,128]{1,0:T(8,128)(2,1)S(1)} collective-permute-done((bf16[512,128]{1,0:T(8,128)(2,1)S(1)}, bf16[512,128]{1,0:T(8,128)(2,1)S(1)}, u32[]{:S(2)}, u32[]{:S(2)}) %collective-permute-start.28) | collective-permute-done | bytes 131104 | tf_op jit(solution)/shard_map/ppermute | solution.py:115
  124.5 1.8 %multiply_add_fusion = f32[512,128]{1,0:T(8,128)} fusion(bf16[512,128]{1,0:T(8,128)(2,1)S(1)} %collective-permute-done.29, bf16[512,128]{1,0:T(8,128)(2,1)S(1)} %collective-permute-done.28, bf16[512,128]{1,0:T(8,128)(2,1)S(1)} %collective-permute-done.27, bf16[2048,128]{1,0:T(8,128)(2,1)} %get-tuple-element.8, f32[512,128]{1,0:T(8,128)S(1)} %copy-done, ...), kind=kLoop, calls=%fused_computation.7 | loop fusion | flops 1179648 | bytes 1572864 | tf_op jit(solution)/shard_map/add | solution.py:193
  (73 shorter events, 22.6 us)
Async XLA Ops:
  1.6 13.1 %collective-permute-start = (bf16[512,128]{1,0:T(8,128)(2,1)S(1)}, bf16[512,128]{1,0:T(8,128)(2,1)S(1)}, u32[]{:S(2)}, u32[]{:S(2)}) collective-permute-start(bf16[512,128]{1,0:T(8,128)(2,1)S(1)} %convert_element_type.72), channel_id=1, source_target_pairs={{0,1},{1,2},{2,3},{3,0},{4,5},{5,6},{6,7},{7,4},{8,9},{9,10},{10,1... | collective-permute-start | bytes 393224 | tf_op jit(solution)/shard_map/ppermute | solution.py:107
  4.7 11.2 %collective-permute-start.1 = (bf16[512,128]{1,0:T(8,128)(2,1)S(1)}, bf16[512,128]{1,0:T(8,128)(2,1)S(1)}, u32[]{:S(2)}, u32[]{:S(2)}) collective-permute-start(bf16[512,128]{1,0:T(8,128)(2,1)S(1)} %convert_element_type.72), channel_id=1, source_target_pairs={{0,2},{1,3},{2,0},{3,1},{4,6},{5,7},{6,4},{7,5},{8,10},{9,11},{10,... | collective-permute-start | bytes 393224 | tf_op jit(solution)/shard_map/ppermute | solution.py:107
  7.3 8.6 %collective-permute-start.2 = (bf16[512,128]{1,0:T(8,128)(2,1)S(1)}, bf16[512,128]{1,0:T(8,128)(2,1)S(1)}, u32[]{:S(2)}, u32[]{:S(2)}) collective-permute-start(bf16[512,128]{1,0:T(8,128)(2,1)S(1)} %convert_element_type.72), channel_id=1, source_target_pairs={{0,3},{1,0},{2,1},{3,2},{4,7},{5,4},{6,5},{7,6},{8,11},{9,8},{10,9... | collective-permute-start | bytes 393224 | tf_op jit(solution)/shard_map/ppermute | solution.py:107
  11.6 9.2 %collective-permute-start.4 = (bf16[1024,128]{1,0:T(8,128)(2,1)S(1)}, bf16[1024,128]{1,0:T(8,128)(2,1)S(1)}, u32[]{:S(2)}, u32[]{:S(2)}) collective-permute-start(bf16[1024,128]{1,0:T(8,128)(2,1)S(1)} %pad_maximum_fusion.2), channel_id=1, source_target_pairs={{0,8},{4,12},{8,0},{12,4},{16,24},{20,28},{24,16},{28,20},{1,9},{5... | collective-permute-start | bytes 786440 | tf_op jit(solution)/shard_map/ppermute | solution.py:128
  13.1 14.0 %collective-permute-start.5 = (bf16[1024,128]{1,0:T(8,128)(2,1)S(1)}, bf16[1024,128]{1,0:T(8,128)(2,1)S(1)}, u32[]{:S(2)}, u32[]{:S(2)}) collective-permute-start(bf16[1024,128]{1,0:T(8,128)(2,1)S(1)} %pad_maximum_fusion.2), channel_id=1, source_target_pairs={{0,16},{4,20},{8,24},{12,28},{16,0},{20,4},{24,8},{28,12},{1,17},{... | collective-permute-start | bytes 786440 | tf_op jit(solution)/shard_map/ppermute | solution.py:128
  14.7 12.6 %collective-permute-start.6 = (bf16[1024,128]{1,0:T(8,128)(2,1)S(1)}, bf16[1024,128]{1,0:T(8,128)(2,1)S(1)}, u32[]{:S(2)}, u32[]{:S(2)}) collective-permute-start(bf16[1024,128]{1,0:T(8,128)(2,1)S(1)} %pad_maximum_fusion.2), channel_id=1, source_target_pairs={{0,24},{4,28},{8,16},{12,20},{16,8},{20,12},{24,0},{28,4},{1,25},{... | collective-permute-start | bytes 786440 | tf_op jit(solution)/shard_map/ppermute | solution.py:128
  36.7 12.7 %collective-permute-start.13 = (bf16[512,128]{1,0:T(8,128)(2,1)S(1)}, bf16[512,128]{1,0:T(8,128)(2,1)S(1)}, u32[]{:S(2)}, u32[]{:S(2)}) collective-permute-start(bf16[512,128]{1,0:T(8,128)(2,1)S(1)} %get-tuple-element.18), channel_id=1, source_target_pairs={{0,4},{4,0},{8,12},{12,8},{16,20},{20,16},{24,28},{28,24},{1,5},{5... | collective-permute-start | bytes 393224 | tf_op jit(solution)/shard_map/ppermute | solution.py:153
  43.0 9.2 %collective-permute-start.14 = (bf16[512,128]{1,0:T(8,128)(2,1)S(1)}, bf16[512,128]{1,0:T(8,128)(2,1)S(1)}, u32[]{:S(2)}, u32[]{:S(2)}) collective-permute-start(bf16[512,128]{1,0:T(8,128)(2,1)S(1)} %get-tuple-element.24), channel_id=1, source_target_pairs={{0,8},{4,12},{8,0},{12,4},{16,24},{20,28},{24,16},{28,20},{1,9},{5... | collective-permute-start | bytes 393224 | tf_op jit(solution)/shard_map/ppermute | solution.py:153
  47.8 6.6 %collective-permute-start.15 = (bf16[512,128]{1,0:T(8,128)(2,1)S(1)}, bf16[512,128]{1,0:T(8,128)(2,1)S(1)}, u32[]{:S(2)}, u32[]{:S(2)}) collective-permute-start(bf16[512,128]{1,0:T(8,128)(2,1)S(1)} %get-tuple-element.23), channel_id=1, source_target_pairs={{0,12},{4,8},{8,4},{12,0},{16,28},{20,24},{24,20},{28,16},{1,13},{... | collective-permute-start | bytes 393224 | tf_op jit(solution)/shard_map/ppermute | solution.py:153
  47.9 12.0 %collective-permute-start.16 = (bf16[512,128]{1,0:T(8,128)(2,1)S(1)}, bf16[512,128]{1,0:T(8,128)(2,1)S(1)}, u32[]{:S(2)}, u32[]{:S(2)}) collective-permute-start(bf16[512,128]{1,0:T(8,128)(2,1)S(1)} %get-tuple-element.22), channel_id=1, source_target_pairs={{0,16},{4,20},{8,24},{12,28},{16,0},{20,4},{24,8},{28,12},{1,17},{... | collective-permute-start | bytes 393224 | tf_op jit(solution)/shard_map/ppermute | solution.py:153
  47.9 13.5 %collective-permute-start.17 = (bf16[512,128]{1,0:T(8,128)(2,1)S(1)}, bf16[512,128]{1,0:T(8,128)(2,1)S(1)}, u32[]{:S(2)}, u32[]{:S(2)}) collective-permute-start(bf16[512,128]{1,0:T(8,128)(2,1)S(1)} %get-tuple-element.21), channel_id=1, source_target_pairs={{0,20},{4,16},{8,28},{12,24},{16,4},{20,0},{24,12},{28,8},{1,21},{... | collective-permute-start | bytes 393224 | tf_op jit(solution)/shard_map/ppermute | solution.py:153
  49.4 15.2 %collective-permute-start.18 = (bf16[512,128]{1,0:T(8,128)(2,1)S(1)}, bf16[512,128]{1,0:T(8,128)(2,1)S(1)}, u32[]{:S(2)}, u32[]{:S(2)}) collective-permute-start(bf16[512,128]{1,0:T(8,128)(2,1)S(1)} %get-tuple-element.20), channel_id=1, source_target_pairs={{0,24},{4,28},{8,16},{12,20},{16,8},{20,12},{24,0},{28,4},{1,25},{... | collective-permute-start | bytes 393224 | tf_op jit(solution)/shard_map/ppermute | solution.py:153
  52.2 12.4 %collective-permute-start.19 = (bf16[512,128]{1,0:T(8,128)(2,1)S(1)}, bf16[512,128]{1,0:T(8,128)(2,1)S(1)}, u32[]{:S(2)}, u32[]{:S(2)}) collective-permute-start(bf16[512,128]{1,0:T(8,128)(2,1)S(1)} %get-tuple-element.19), channel_id=1, source_target_pairs={{0,28},{4,24},{8,20},{12,16},{16,12},{20,8},{24,4},{28,0},{1,29},{... | collective-permute-start | bytes 393224 | tf_op jit(solution)/shard_map/ppermute | solution.py:153
  54.5 13.0 %collective-permute-start.7 = (bf16[512,128]{1,0:T(8,128)(2,1)S(1)}, bf16[512,128]{1,0:T(8,128)(2,1)S(1)}, u32[]{:S(2)}, u32[]{:S(2)}) collective-permute-start(bf16[512,128]{1,0:T(8,128)(2,1)S(1)} %get-tuple-element.28), channel_id=1, source_target_pairs={{0,1},{1,2},{2,3},{3,0},{4,5},{5,6},{6,7},{7,4},{8,9},{9,10},{10,1... | collective-permute-start | bytes 393224 | tf_op jit(solution)/shard_map/ppermute | solution.py:115
  59.9 8.0 %collective-permute-start.8 = (bf16[512,128]{1,0:T(8,128)(2,1)S(1)}, bf16[512,128]{1,0:T(8,128)(2,1)S(1)}, u32[]{:S(2)}, u32[]{:S(2)}) collective-permute-start(bf16[512,128]{1,0:T(8,128)(2,1)S(1)} %get-tuple-element.30), channel_id=1, source_target_pairs={{0,2},{1,3},{2,0},{3,1},{4,6},{5,7},{6,4},{7,5},{8,10},{9,11},{10,... | collective-permute-start | bytes 393224 | tf_op jit(solution)/shard_map/ppermute | solution.py:115
  61.5 8.0 %collective-permute-start.9 = (bf16[512,128]{1,0:T(8,128)(2,1)S(1)}, bf16[512,128]{1,0:T(8,128)(2,1)S(1)}, u32[]{:S(2)}, u32[]{:S(2)}) collective-permute-start(bf16[512,128]{1,0:T(8,128)(2,1)S(1)} %get-tuple-element.29), channel_id=1, source_target_pairs={{0,3},{1,0},{2,1},{3,2},{4,7},{5,4},{6,5},{7,6},{8,11},{9,8},{10,9... | collective-permute-start | bytes 393224 | tf_op jit(solution)/shard_map/ppermute | solution.py:115
  65.7 7.8 %collective-permute-start.21 = (bf16[512,128]{1,0:T(8,128)(2,1)S(1)}, bf16[512,128]{1,0:T(8,128)(2,1)S(1)}, u32[]{:S(2)}, u32[]{:S(2)}) collective-permute-start(bf16[512,128]{1,0:T(8,128)(2,1)S(1)} %get-tuple-element.11), channel_id=1, source_target_pairs={{0,8},{4,12},{8,0},{12,4},{16,24},{20,28},{24,16},{28,20},{1,9},{5... | collective-permute-start | bytes 393224 | tf_op jit(solution)/shard_map/ppermute | solution.py:145
  67.5 6.7 %collective-permute-start.22 = (bf16[512,128]{1,0:T(8,128)(2,1)S(1)}, bf16[512,128]{1,0:T(8,128)(2,1)S(1)}, u32[]{:S(2)}, u32[]{:S(2)}) collective-permute-start(bf16[512,128]{1,0:T(8,128)(2,1)S(1)} %get-tuple-element.11), channel_id=1, source_target_pairs={{0,12},{4,8},{8,4},{12,0},{16,28},{20,24},{24,20},{28,16},{1,13},{... | collective-permute-start | bytes 393224 | tf_op jit(solution)/shard_map/ppermute | solution.py:145
  67.8 8.5 %collective-permute-start.23 = (bf16[512,128]{1,0:T(8,128)(2,1)S(1)}, bf16[512,128]{1,0:T(8,128)(2,1)S(1)}, u32[]{:S(2)}, u32[]{:S(2)}) collective-permute-start(bf16[512,128]{1,0:T(8,128)(2,1)S(1)} %get-tuple-element.11), channel_id=1, source_target_pairs={{0,16},{4,20},{8,24},{12,28},{16,0},{20,4},{24,8},{28,12},{1,17},{... | collective-permute-start | bytes 393224 | tf_op jit(solution)/shard_map/ppermute | solution.py:145
  69.4 11.3 %collective-permute-start.24 = (bf16[512,128]{1,0:T(8,128)(2,1)S(1)}, bf16[512,128]{1,0:T(8,128)(2,1)S(1)}, u32[]{:S(2)}, u32[]{:S(2)}) collective-permute-start(bf16[512,128]{1,0:T(8,128)(2,1)S(1)} %get-tuple-element.11), channel_id=1, source_target_pairs={{0,20},{4,16},{8,28},{12,24},{16,4},{20,0},{24,12},{28,8},{1,21},{... | collective-permute-start | bytes 393224 | tf_op jit(solution)/shard_map/ppermute | solution.py:145
  71.3 13.8 %collective-permute-start.25 = (bf16[512,128]{1,0:T(8,128)(2,1)S(1)}, bf16[512,128]{1,0:T(8,128)(2,1)S(1)}, u32[]{:S(2)}, u32[]{:S(2)}) collective-permute-start(bf16[512,128]{1,0:T(8,128)(2,1)S(1)} %get-tuple-element.11), channel_id=1, source_target_pairs={{0,24},{4,28},{8,16},{12,20},{16,8},{20,12},{24,0},{28,4},{1,25},{... | collective-permute-start | bytes 393224 | tf_op jit(solution)/shard_map/ppermute | solution.py:145
  73.5 11.6 %collective-permute-start.26 = (bf16[512,128]{1,0:T(8,128)(2,1)S(1)}, bf16[512,128]{1,0:T(8,128)(2,1)S(1)}, u32[]{:S(2)}, u32[]{:S(2)}) collective-permute-start(bf16[512,128]{1,0:T(8,128)(2,1)S(1)} %get-tuple-element.11), channel_id=1, source_target_pairs={{0,28},{4,24},{8,20},{12,16},{16,12},{20,8},{24,4},{28,0},{1,29},{... | collective-permute-start | bytes 393224 | tf_op jit(solution)/shard_map/ppermute | solution.py:145
  74.3 10.9 %collective-permute-start.10 = (bf16[512,128]{1,0:T(8,128)(2,1)S(1)}, bf16[512,128]{1,0:T(8,128)(2,1)S(1)}, u32[]{:S(2)}, u32[]{:S(2)}) collective-permute-start(bf16[512,128]{1,0:T(8,128)(2,1)S(1)} %fusion.6), channel_id=1, source_target_pairs={{0,1},{1,2},{2,3},{3,0},{4,5},{5,6},{6,7},{7,4},{8,9},{9,10},{10,1... | collective-permute-start | bytes 393224 | tf_op jit(solution)/shard_map/ppermute | solution.py:107
  76.4 11.2 %collective-permute-start.11 = (bf16[512,128]{1,0:T(8,128)(2,1)S(1)}, bf16[512,128]{1,0:T(8,128)(2,1)S(1)}, u32[]{:S(2)}, u32[]{:S(2)}) collective-permute-start(bf16[512,128]{1,0:T(8,128)(2,1)S(1)} %fusion.6), channel_id=1, source_target_pairs={{0,2},{1,3},{2,0},{3,1},{4,6},{5,7},{6,4},{7,5},{8,10},{9,11},{10,... | collective-permute-start | bytes 393224 | tf_op jit(solution)/shard_map/ppermute | solution.py:107
  80.7 8.9 %collective-permute-start.12 = (bf16[512,128]{1,0:T(8,128)(2,1)S(1)}, bf16[512,128]{1,0:T(8,128)(2,1)S(1)}, u32[]{:S(2)}, u32[]{:S(2)}) collective-permute-start(bf16[512,128]{1,0:T(8,128)(2,1)S(1)} %fusion.6), channel_id=1, source_target_pairs={{0,3},{1,0},{2,1},{3,2},{4,7},{5,4},{6,5},{7,6},{8,11},{9,8},{10,9... | collective-permute-start | bytes 393224 | tf_op jit(solution)/shard_map/ppermute | solution.py:107
  98.5 18.0 %collective-permute-start.30 = (bf16[1024,128]{1,0:T(8,128)(2,1)S(1)}, bf16[1024,128]{1,0:T(8,128)(2,1)S(1)}, u32[]{:S(2)}, u32[]{:S(2)}) collective-permute-start(bf16[1024,128]{1,0:T(8,128)(2,1)S(1)} %get-tuple-element.15), channel_id=1, source_target_pairs={{0,8},{4,12},{8,0},{12,4},{16,24},{20,28},{24,16},{28,20},{1,9},{5... | collective-permute-start | bytes 786440 | tf_op jit(solution)/shard_map/ppermute | solution.py:136
  109.3 10.0 %collective-permute-start.31 = (bf16[1024,128]{1,0:T(8,128)(2,1)S(1)}, bf16[1024,128]{1,0:T(8,128)(2,1)S(1)}, u32[]{:S(2)}, u32[]{:S(2)}) collective-permute-start(bf16[1024,128]{1,0:T(8,128)(2,1)S(1)} %get-tuple-element.17), channel_id=1, source_target_pairs={{0,16},{4,20},{8,24},{12,28},{16,0},{20,4},{24,8},{28,12},{1,17},{... | collective-permute-start | bytes 786440 | tf_op jit(solution)/shard_map/ppermute | solution.py:136
  109.4 10.0 %collective-permute-start.32 = (bf16[1024,128]{1,0:T(8,128)(2,1)S(1)}, bf16[1024,128]{1,0:T(8,128)(2,1)S(1)}, u32[]{:S(2)}, u32[]{:S(2)}) collective-permute-start(bf16[1024,128]{1,0:T(8,128)(2,1)S(1)} %get-tuple-element.16), channel_id=1, source_target_pairs={{0,24},{4,28},{8,16},{12,20},{16,8},{20,12},{24,0},{28,4},{1,25},{... | collective-permute-start | bytes 786440 | tf_op jit(solution)/shard_map/ppermute | solution.py:136
  112.0 8.6 %collective-permute-start.27 = (bf16[512,128]{1,0:T(8,128)(2,1)S(1)}, bf16[512,128]{1,0:T(8,128)(2,1)S(1)}, u32[]{:S(2)}, u32[]{:S(2)}) collective-permute-start(bf16[512,128]{1,0:T(8,128)(2,1)S(1)} %get-tuple-element.25), channel_id=1, source_target_pairs={{0,1},{1,2},{2,3},{3,0},{4,5},{5,6},{6,7},{7,4},{8,9},{9,10},{10,1... | collective-permute-start | bytes 393224 | tf_op jit(solution)/shard_map/ppermute | solution.py:115
  115.6 8.8 %collective-permute-start.28 = (bf16[512,128]{1,0:T(8,128)(2,1)S(1)}, bf16[512,128]{1,0:T(8,128)(2,1)S(1)}, u32[]{:S(2)}, u32[]{:S(2)}) collective-permute-start(bf16[512,128]{1,0:T(8,128)(2,1)S(1)} %get-tuple-element.27), channel_id=1, source_target_pairs={{0,2},{1,3},{2,0},{3,1},{4,6},{5,7},{6,4},{7,5},{8,10},{9,11},{10,... | collective-permute-start | bytes 393224 | tf_op jit(solution)/shard_map/ppermute | solution.py:115
  116.5 8.0 %collective-permute-start.29 = (bf16[512,128]{1,0:T(8,128)(2,1)S(1)}, bf16[512,128]{1,0:T(8,128)(2,1)S(1)}, u32[]{:S(2)}, u32[]{:S(2)}) collective-permute-start(bf16[512,128]{1,0:T(8,128)(2,1)S(1)} %get-tuple-element.26), channel_id=1, source_target_pairs={{0,3},{1,0},{2,1},{3,2},{4,7},{5,4},{6,5},{7,6},{8,11},{9,8},{10,9... | collective-permute-start | bytes 393224 | tf_op jit(solution)/shard_map/ppermute | solution.py:115
  120.5 5.8 %collective-permute-start.33 = (f32[512,128]{1,0:T(8,128)S(1)}, f32[512,128]{1,0:T(8,128)S(1)}, u32[]{:S(2)}, u32[]{:S(2)}) collective-permute-start(f32[512,128]{1,0:T(8,128)S(1)} %slice.97), channel_id=1, source_target_pairs={{0,4},{4,0},{8,12},{12,8},{16,20},{20,16},{24,28},{28,24},{1,5},{5... | collective-permute-start | bytes 786440 | tf_op jit(solution)/shard_map/ppermute | solution.py:138
  (6 other events, 92.1 us)

commit v8 on v7

--- a/solution.py
+++ b/solution.py
@@ -10,16 +10,28 @@
 ITERS = 2
 
 
-def sweep_kernel(tile, group, rows_ref, cols_ref, count_ref, emb_ref, ctx_ref, pos_ref, neg_ref,
-                 gemb_ref, gctx_ref, acc_e, acc_ct, emb_t):
+def sweep_kernel(tile, group, n_emb, n_ctx, rows_ref, cols_ref, count_ref, *refs):
+    emb_pieces = refs[:n_emb]
+    ctx_pieces = refs[n_emb : n_emb + n_ctx]
+    pos_ref, neg_ref, gemb_ref, gctx_ref, acc_e, acc_ct, emb_t, emb_ref, ctx_ref = refs[n_emb + n_ctx :]
     k = pl.program_id(0)
     n = count_ref[0]
 
     @pl.when(k == 0)
     def _():
+        at = 0
+        for piece in emb_pieces:
+            rows = piece.shape[0]
+            emb_ref[at : at + rows, :] = piece[...]
+            emb_t[:, at : at + rows] = piece[...].astype(jnp.float32).T.astype(emb_t.dtype)
+            at += rows
+        at = 0
+        for piece in ctx_pieces:
+            rows = piece.shape[0]
+            ctx_ref[at : at + rows, :] = piece[...]
+            at += rows
         acc_e[...] = jnp.zeros_like(acc_e)
         acc_ct[...] = jnp.zeros_like(acc_ct)
-        emb_t[...] = emb_ref[...].astype(jnp.float32).T.astype(emb_t.dtype)
 
     def visit(j):
         slot = k * group + j
@@ -55,10 +67,11 @@
         gctx_ref[...] = acc_ct[...].T.astype(gctx_ref.dtype)
 
 
-def tile_sweep(pos, neg, rows, cols, count, emb_low, ctx_low):
+def tile_sweep(pos, neg, rows, cols, count, emb_pieces, ctx_pieces):
     cap, tile, _ = pos.shape
-    ne, dim = emb_low.shape
-    nc = ctx_low.shape[0]
+    dim = emb_pieces[0].shape[1]
+    ne = sum(p.shape[0] for p in emb_pieces)
+    nc = sum(p.shape[0] for p in ctx_pieces)
     group = next(g for g in (8, 4, 2, 1) if cap % g == 0)
 
     def slot(k, rows_ref, cols_ref, count_ref):
@@ -68,9 +81,8 @@
     grid_spec = pltpu.PrefetchScalarGridSpec(
         num_scalar_prefetch=3,
         grid=(cap // group,),
-        in_specs=[
-            pl.BlockSpec((ne, dim), lambda k, *_: (0, 0)),
-            pl.BlockSpec((nc, dim), lambda k, *_: (0, 0)),
+        in_specs=[pl.BlockSpec(p.shape, lambda k, *_: (0, 0)) for p in emb_pieces + ctx_pieces]
+        + [
             pl.BlockSpec((group, tile, tile), slot),
             pl.BlockSpec((group, tile, tile), slot),
         ],
@@ -82,11 +94,13 @@
             pltpu.VMEM((ne, dim), jnp.float32),
             pltpu.VMEM((dim, nc), jnp.float32),
             pltpu.VMEM((dim, ne), jnp.bfloat16),
+            pltpu.VMEM((ne, dim), jnp.bfloat16),
+            pltpu.VMEM((nc, dim), jnp.bfloat16),
         ],
     )
     flops = cap * 3 * 2 * tile * tile * dim
     return pl.pallas_call(
-        functools.partial(sweep_kernel, tile, group),
+        functools.partial(sweep_kernel, tile, group, len(emb_pieces), len(ctx_pieces)),
         grid_spec=grid_spec,
         out_shape=(
             jax.ShapeDtypeStruct((ne, dim), jnp.bfloat16),
@@ -98,14 +112,14 @@
             transcendentals=cap * tile * tile,
             bytes_accessed=2 * cap * tile * tile * 2 + 3 * (ne + nc) * dim * 2,
         ),
-    )(rows, cols, count.reshape(1), emb_low, ctx_low, pos, neg)
+    )(rows, cols, count.reshape(1), *emb_pieces, *ctx_pieces, pos, neg)
 
 
 def gather_rotated(x, axis, n):
     pieces = [x]
     for s in range(1, n):
         pieces.append(lax.ppermute(x, axis, [(i, (i + s) % n) for i in range(n)]))
-    return jnp.concatenate(pieces, axis=0)
+    return pieces
 
 
 def scatter_rotated(g, axis, n):
@@ -126,7 +140,7 @@
     blocks = [pair]
     for b in range(1, n // 2):
         blocks.append(lax.ppermute(pair, axis, [(i, i ^ (2 * b)) for i in range(n)]))
-    return jnp.concatenate(blocks, axis=0)
+    return blocks
 
 
 def scatter_paired(g, axis, n):
@@ -143,7 +157,7 @@
     pieces = [x]
     for p in range(1, n):
         pieces.append(lax.ppermute(x, axis, [(i, i ^ p) for i in range(n)]))
-    return jnp.concatenate(pieces, axis=0)
+    return pieces
 
 
 def scatter_xor(g, axis, n):

time: 127 us -> 121 us (0.953)
  starting transfers between devices: 65.5 us -> 51.4 us
  Pallas kernels: 14.1 us -> 22.4 us
  other arithmetic: 10.6 us -> 8.97 us
    pallas_call x2, Pallas kernels: 14.1 us -> 22.4 us  [tile_sweep(): pl.pallas_call(functools.partial(sweep_kernel, tile, group, len(emb_piece...]
    ppermute x3, waiting for transfers between devices: 10.4 us -> 2.33 us  [gather_paired(): blocks.append(lax.ppermute(pair, axis, [(i, i ^ 2 * b) for i in range(n)]))]
    ppermute x6, starting transfers between devices: 15.4 us -> 9.29 us  [gather_rotated(): pieces.append(lax.ppermute(x, axis, [(i, (i + s) % n) for i in range(n)]))]
    ppermute x3, starting transfers between devices: 12.4 us -> 7.42 us  [scatter_paired(): lax.ppermute(g[2 * b * width:(2 * b + 2) * width], axis, [(i, i ^ 2 * b)...]
    ppermute x7, starting transfers between devices: 14.6 us -> 9.62 us  [scatter_xor(): lax.ppermute(g[p * width:(p + 1) * width], axis, [(i, i ^ p) for i in ran...]
    ppermute x6, waiting for transfers between devices: 5.14 us -> 10 us  [gather_rotated(): pieces.append(lax.ppermute(x, axis, [(i, (i + s) % n) for i in range(n)]))]
    ppermute x7, waiting for transfers between devices: 5.25 us -> 1.49 us  [scatter_xor(): lax.ppermute(g[p * width:(p + 1) * width], axis, [(i, i ^ p) for i in ran...]
    ppermute x7, waiting for transfers between devices: 2.43 us -> 5.91 us  [gather_xor(): pieces.append(lax.ppermute(x, axis, [(i, i ^ p) for i in range(n)]))]
where the time goes in v8:
time: 121 us; the launch traced here: 120 us
  starting transfers between devices  51.4 us (42%)
  waiting for transfers between devices  30 us (25%)
  Pallas kernels  22.4 us (19%)
  other arithmetic  8.97 us (7%)
  local copies, waits for them, and re-layouts  5.92 us (5%)
  between operations  1.58 us (1%)
    pallas_call x2, Pallas kernels, tile_sweep(): pl.pallas_call(functools.partial(sweep_kernel, tile, group, len(emb_piece...  22.4 us
    ppermute x6, starting transfers between devices, scatter_rotated(): lax.ppermute(chunks[(n - s) % n], axis, [(i, (i + s) % n) for i in range(...  14.9 us
    ppermute x6, waiting for transfers between devices, gather_rotated(): pieces.append(lax.ppermute(x, axis, [(i, (i + s) % n) for i in range(n)]))  10 us
    ppermute x7, starting transfers between devices, scatter_xor(): lax.ppermute(g[p * width:(p + 1) * width], axis, [(i, i ^ p) for i in ran...  9.62 us
    ppermute x6, starting transfers between devices, gather_rotated(): pieces.append(lax.ppermute(x, axis, [(i, (i + s) % n) for i in range(n)]))  9.29 us
    ppermute x3, starting transfers between devices, scatter_paired(): lax.ppermute(g[2 * b * width:(2 * b + 2) * width], axis, [(i, i ^ 2 * b)...  7.42 us
    ppermute x6, waiting for transfers between devices, scatter_rotated(): lax.ppermute(chunks[(n - s) % n], axis, [(i, (i + s) % n) for i in range(...  6.45 us
    ppermute x7, starting transfers between devices, gather_xor(): pieces.append(lax.ppermute(x, axis, [(i, i ^ p) for i in range(n)]))  5.98 us
  transfers between devices with their start and end apart: 34, of which 13 were waited for; matrix products, arithmetic and copies ran while one was open for 8% of the time, Pallas kernels for 0%

profile of v8, /device:TPU:0, one launch (start us, length us, event | category | flops | bytes accessed | tf_op | source)
XLA Modules:
  0.0 120.2 jit_solution(13800764046911377963)
XLA Ops:
  3.1 4.7 %collective-permute-start.2 = (bf16[512,128]{1,0:T(8,128)(2,1)S(1)}, bf16[512,128]{1,0:T(8,128)(2,1)S(1)}, u32[]{:S(2)}, u32[]{:S(2)}) collective-permute-start(bf16[512,128]{1,0:T(8,128)(2,1)S(1)} %convert_element_type.72.refs_0_), channel_id=1, source_target_pairs={{0,3},{1,0},{2,1},{3,2},{4,7},{5,4},{6,5},{7,6},{8,11},{9,8},{10,9... | collective-permute-start | bytes 393224 | tf_op jit(solution)/shard_map/ppermute | solution.py:121
  7.8 2.5 %collective-permute-start.6 = (bf16[1024,128]{1,0:T(8,128)(2,1)S(1)}, bf16[1024,128]{1,0:T(8,128)(2,1)S(1)}, u32[]{:S(2)}, u32[]{:S(2)}) collective-permute-start(bf16[1024,128]{1,0:T(8,128)(2,1)S(1)} %pad_maximum_fusion.refs_4_), channel_id=1, source_target_pairs={{0,24},{4,28},{8,16},{12,20},{16,8},{20,12},{24,0},{28,4},{1,25},{... | collective-permute-start | bytes 786440 | tf_op jit(solution)/shard_map/ppermute | solution.py:142
  13.1 1.3 %fusion.2 = (s32[64]{0:T(128)}, s32[64]{0:T(128)}) fusion(s32[1,1,64]{2,1,0:T(1,128)} %param.11, s32[]{:T(128)S(6)} %axis_index.22, s32[1,1,64]{2,1,0:T(1,128)} %param.12, s32[]{:T(128)S(6)} %axis_index.25), kind=kLoop, calls=%fused_computation.21 | loop fusion | flops 3520 | bytes 1032 | tf_op jit(solution)/shard_map/add | solution.py:178
  14.4 6.2 %collective-permute-done.1.refs_2_ = bf16[512,128]{1,0:T(8,128)(2,1)S(1)} collective-permute-done((bf16[512,128]{1,0:T(8,128)(2,1)S(1)}, bf16[512,128]{1,0:T(8,128)(2,1)S(1)}, u32[]{:S(2)}, u32[]{:S(2)}) %collective-permute-start.1) | collective-permute-done | bytes 131104 | tf_op jit(solution)/shard_map/ppermute | solution.py:121
  20.6 2.2 %collective-permute-done.5.refs_6_ = bf16[1024,128]{1,0:T(8,128)(2,1)S(1)} collective-permute-done((bf16[1024,128]{1,0:T(8,128)(2,1)S(1)}, bf16[1024,128]{1,0:T(8,128)(2,1)S(1)}, u32[]{:S(2)}, u32[]{:S(2)}) %collective-permute-start.5) | collective-permute-done | bytes 262176 | tf_op jit(solution)/shard_map/ppermute | solution.py:142
  23.6 11.2 %shard_map.86 = (bf16[2048,128]{1,0:T(8,128)(2,1)}, bf16[4096,128]{1,0:T(8,128)(2,1)}) custom-call(s32[64]{0:T(128)} %get-tuple-element.28.rows_ref, s32[64]{0:T(128)} %get-tuple-element.29.cols_ref, s32[1]{0:T(128)} %bitcast.29.count_ref, bf16[512,128]{1,0:T(8,128)(2,1)} %copy-done.4, bf16[512,128]{1,0:T(8,128)(2,1)} %copy-done.21, ...), custom_call_target="tpu_custom_call" | custom-call | flops 3221225472 | bytes 21495808 | tf_op jit(solution)/shard_map/pallas_call | solution.py:102
  36.0 3.8 %collective-permute-start.9 = (bf16[512,128]{1,0:T(8,128)(2,1)S(1)}, bf16[512,128]{1,0:T(8,128)(2,1)S(1)}, u32[]{:S(2)}, u32[]{:S(2)}) collective-permute-start(bf16[512,128]{1,0:T(8,128)(2,1)S(1)} %get-tuple-element.26), channel_id=1, source_target_pairs={{0,3},{1,0},{2,1},{3,2},{4,7},{5,4},{6,5},{7,6},{8,11},{9,8},{10,9... | collective-permute-start | bytes 393224 | tf_op jit(solution)/shard_map/ppermute | solution.py:129
  39.8 3.8 %collective-permute-start.8 = (bf16[512,128]{1,0:T(8,128)(2,1)S(1)}, bf16[512,128]{1,0:T(8,128)(2,1)S(1)}, u32[]{:S(2)}, u32[]{:S(2)}) collective-permute-start(bf16[512,128]{1,0:T(8,128)(2,1)S(1)} %get-tuple-element.27), channel_id=1, source_target_pairs={{0,2},{1,3},{2,0},{3,1},{4,6},{5,7},{6,4},{7,5},{8,10},{9,11},{10,... | collective-permute-start | bytes 393224 | tf_op jit(solution)/shard_map/ppermute | solution.py:129
  43.6 1.3 %fusion.9 = (bf16[512,128]{1,0:T(8,128)(2,1)S(1)}, bf16[512,128]{1,0:T(8,128)(2,1)S(1)}, bf16[512,128]{1,0:T(8,128)(2,1)S(1)}, bf16[512,128]{1,0:T(8,128)(2,1)S(...) fusion(bf16[4096,128]{1,0:T(8,128)(2,1)} %get-tuple-element.7), kind=kLoop, calls=%fused_computation.30 | loop fusion | bytes 1835008 | tf_op jit(solution)/shard_map/slice | solution.py:167
  45.0 1.8 %collective-permute-start.19 = (bf16[512,128]{1,0:T(8,128)(2,1)S(1)}, bf16[512,128]{1,0:T(8,128)(2,1)S(1)}, u32[]{:S(2)}, u32[]{:S(2)}) collective-permute-start(bf16[512,128]{1,0:T(8,128)(2,1)S(1)} %get-tuple-element.16), channel_id=1, source_target_pairs={{0,28},{4,24},{8,20},{12,16},{16,12},{20,8},{24,4},{28,0},{1,29},{... | collective-permute-start | bytes 393224 | tf_op jit(solution)/shard_map/ppermute | solution.py:167
  46.8 2.0 %collective-permute-start.18 = (bf16[512,128]{1,0:T(8,128)(2,1)S(1)}, bf16[512,128]{1,0:T(8,128)(2,1)S(1)}, u32[]{:S(2)}, u32[]{:S(2)}) collective-permute-start(bf16[512,128]{1,0:T(8,128)(2,1)S(1)} %get-tuple-element.17), channel_id=1, source_target_pairs={{0,24},{4,28},{8,16},{12,20},{16,8},{20,12},{24,0},{28,4},{1,25},{... | collective-permute-start | bytes 393224 | tf_op jit(solution)/shard_map/ppermute | solution.py:167
  48.8 1.5 %collective-permute-start.17 = (bf16[512,128]{1,0:T(8,128)(2,1)S(1)}, bf16[512,128]{1,0:T(8,128)(2,1)S(1)}, u32[]{:S(2)}, u32[]{:S(2)}) collective-permute-start(bf16[512,128]{1,0:T(8,128)(2,1)S(1)} %get-tuple-element.18), channel_id=1, source_target_pairs={{0,20},{4,16},{8,28},{12,24},{16,4},{20,0},{24,12},{28,8},{1,21},{... | collective-permute-start | bytes 393224 | tf_op jit(solution)/shard_map/ppermute | solution.py:167
  50.3 2.2 %collective-permute-done.8 = bf16[512,128]{1,0:T(8,128)(2,1)S(1)} collective-permute-done((bf16[512,128]{1,0:T(8,128)(2,1)S(1)}, bf16[512,128]{1,0:T(8,128)(2,1)S(1)}, u32[]{:S(2)}, u32[]{:S(2)}) %collective-permute-start.8) | collective-permute-done | bytes 131104 | tf_op jit(solution)/shard_map/ppermute | solution.py:129
  53.5 2.5 %collective-permute-start.15 = (bf16[512,128]{1,0:T(8,128)(2,1)S(1)}, bf16[512,128]{1,0:T(8,128)(2,1)S(1)}, u32[]{:S(2)}, u32[]{:S(2)}) collective-permute-start(bf16[512,128]{1,0:T(8,128)(2,1)S(1)} %get-tuple-element.20), channel_id=1, source_target_pairs={{0,12},{4,8},{8,4},{12,0},{16,28},{20,24},{24,20},{28,16},{1,13},{... | collective-permute-start | bytes 393224 | tf_op jit(solution)/shard_map/ppermute | solution.py:167
  57.8 2.2 %collective-permute-start.12 = (bf16[512,128]{1,0:T(8,128)(2,1)S(1)}, bf16[512,128]{1,0:T(8,128)(2,1)S(1)}, u32[]{:S(2)}, u32[]{:S(2)}) collective-permute-start(bf16[512,128]{1,0:T(8,128)(2,1)S(1)} %fusion.6.refs_0_), channel_id=1, source_target_pairs={{0,3},{1,0},{2,1},{3,2},{4,7},{5,4},{6,5},{7,6},{8,11},{9,8},{10,9... | collective-permute-start | bytes 393224 | tf_op jit(solution)/shard_map/ppermute | solution.py:121
  59.9 1.4 %collective-permute-start.11 = (bf16[512,128]{1,0:T(8,128)(2,1)S(1)}, bf16[512,128]{1,0:T(8,128)(2,1)S(1)}, u32[]{:S(2)}, u32[]{:S(2)}) collective-permute-start(bf16[512,128]{1,0:T(8,128)(2,1)S(1)} %fusion.6.refs_0_), channel_id=1, source_target_pairs={{0,2},{1,3},{2,0},{3,1},{4,6},{5,7},{6,4},{7,5},{8,10},{9,11},{10,... | collective-permute-start | bytes 393224 | tf_op jit(solution)/shard_map/ppermute | solution.py:121
  61.3 1.5 %collective-permute-done.14 = bf16[512,128]{1,0:T(8,128)(2,1)S(1)} collective-permute-done((bf16[512,128]{1,0:T(8,128)(2,1)S(1)}, bf16[512,128]{1,0:T(8,128)(2,1)S(1)}, u32[]{:S(2)}, u32[]{:S(2)}) %collective-permute-start.14) | collective-permute-done | bytes 131104 | tf_op jit(solution)/shard_map/ppermute | solution.py:167
  63.9 1.5 %collective-permute-start.26 = (bf16[512,128]{1,0:T(8,128)(2,1)S(1)}, bf16[512,128]{1,0:T(8,128)(2,1)S(1)}, u32[]{:S(2)}, u32[]{:S(2)}) collective-permute-start(bf16[512,128]{1,0:T(8,128)(2,1)S(1)} %get-tuple-element.10.refs_4_), channel_id=1, source_target_pairs={{0,28},{4,24},{8,20},{12,16},{16,12},{20,8},{24,4},{28,0},{1,29},{... | collective-permute-start | bytes 393224 | tf_op jit(solution)/shard_map/ppermute | solution.py:159
  67.4 3.9 %collective-permute-done.11.refs_2_ = bf16[512,128]{1,0:T(8,128)(2,1)S(1)} collective-permute-done((bf16[512,128]{1,0:T(8,128)(2,1)S(1)}, bf16[512,128]{1,0:T(8,128)(2,1)S(1)}, u32[]{:S(2)}, u32[]{:S(2)}) %collective-permute-start.11) | collective-permute-done | bytes 131104 | tf_op jit(solution)/shard_map/ppermute | solution.py:121
  74.2 2.1 %collective-permute-done.24.refs_9_ = bf16[512,128]{1,0:T(8,128)(2,1)S(1)} collective-permute-done((bf16[512,128]{1,0:T(8,128)(2,1)S(1)}, bf16[512,128]{1,0:T(8,128)(2,1)S(1)}, u32[]{:S(2)}, u32[]{:S(2)}) %collective-permute-start.24) | collective-permute-done | bytes 131104 | tf_op jit(solution)/shard_map/ppermute | solution.py:159
  76.2 2.8 %collective-permute-done.23.refs_8_ = bf16[512,128]{1,0:T(8,128)(2,1)S(1)} collective-permute-done((bf16[512,128]{1,0:T(8,128)(2,1)S(1)}, bf16[512,128]{1,0:T(8,128)(2,1)S(1)}, u32[]{:S(2)}, u32[]{:S(2)}) %collective-permute-start.23) | collective-permute-done | bytes 131104 | tf_op jit(solution)/shard_map/ppermute | solution.py:159
  80.4 11.1 %shard_map.87 = (bf16[2048,128]{1,0:T(8,128)(2,1)}, bf16[4096,128]{1,0:T(8,128)(2,1)}) custom-call(s32[64]{0:T(128)} %get-tuple-element.28.rows_ref, s32[64]{0:T(128)} %get-tuple-element.29.cols_ref, s32[1]{0:T(128)} %bitcast.30.count_ref, bf16[512,128]{1,0:T(8,128)(2,1)} %copy-done.3, bf16[512,128]{1,0:T(8,128)(2,1)} %copy-done.11, ...), custom_call_target="tpu_custom_call" | custom-call | flops 3221225472 | bytes 21495808 | tf_op jit(solution)/shard_map/pallas_call | solution.py:102
  91.5 1.2 fusion.8
  92.7 5.9 %collective-permute-start.30 = (bf16[1024,128]{1,0:T(8,128)(2,1)S(1)}, bf16[1024,128]{1,0:T(8,128)(2,1)S(1)}, u32[]{:S(2)}, u32[]{:S(2)}) collective-permute-start(bf16[1024,128]{1,0:T(8,128)(2,1)S(1)} %get-tuple-element.12), channel_id=1, source_target_pairs={{0,8},{4,12},{8,0},{12,4},{16,24},{20,28},{24,16},{28,20},{1,9},{5... | collective-permute-start | bytes 786440 | tf_op jit(solution)/shard_map/ppermute | solution.py:150
  98.6 1.5 %collective-permute-start.31 = (bf16[1024,128]{1,0:T(8,128)(2,1)S(1)}, bf16[1024,128]{1,0:T(8,128)(2,1)S(1)}, u32[]{:S(2)}, u32[]{:S(2)}) collective-permute-start(bf16[1024,128]{1,0:T(8,128)(2,1)S(1)} %get-tuple-element.14), channel_id=1, source_target_pairs={{0,16},{4,20},{8,24},{12,28},{16,0},{20,4},{24,8},{28,12},{1,17},{... | collective-permute-start | bytes 786440 | tf_op jit(solution)/shard_map/ppermute | solution.py:150
  101.2 4.9 %collective-permute-start.29 = (bf16[512,128]{1,0:T(8,128)(2,1)S(1)}, bf16[512,128]{1,0:T(8,128)(2,1)S(1)}, u32[]{:S(2)}, u32[]{:S(2)}) collective-permute-start(bf16[512,128]{1,0:T(8,128)(2,1)S(1)} %get-tuple-element.23), channel_id=1, source_target_pairs={{0,3},{1,0},{2,1},{3,2},{4,7},{5,4},{6,5},{7,6},{8,11},{9,8},{10,9... | collective-permute-start | bytes 393224 | tf_op jit(solution)/shard_map/ppermute | solution.py:129
  106.2 2.2 %collective-permute-start.28 = (bf16[512,128]{1,0:T(8,128)(2,1)S(1)}, bf16[512,128]{1,0:T(8,128)(2,1)S(1)}, u32[]{:S(2)}, u32[]{:S(2)}) collective-permute-start(bf16[512,128]{1,0:T(8,128)(2,1)S(1)} %get-tuple-element.24), channel_id=1, source_target_pairs={{0,2},{1,3},{2,0},{3,1},{4,6},{5,7},{6,4},{7,5},{8,10},{9,11},{10,... | collective-permute-start | bytes 393224 | tf_op jit(solution)/shard_map/ppermute | solution.py:129
  108.4 2.2 %collective-permute-done.32 = bf16[1024,128]{1,0:T(8,128)(2,1)S(1)} collective-permute-done((bf16[1024,128]{1,0:T(8,128)(2,1)S(1)}, bf16[1024,128]{1,0:T(8,128)(2,1)S(1)}, u32[]{:S(2)}, u32[]{:S(2)}) %collective-permute-start.32) | collective-permute-done | bytes 262176 | tf_op jit(solution)/shard_map/ppermute | solution.py:150
  110.6 1.6 %collective-permute-done.31 = bf16[1024,128]{1,0:T(8,128)(2,1)S(1)} collective-permute-done((bf16[1024,128]{1,0:T(8,128)(2,1)S(1)}, bf16[1024,128]{1,0:T(8,128)(2,1)S(1)}, u32[]{:S(2)}, u32[]{:S(2)}) %collective-permute-start.31) | collective-permute-done | bytes 262176 | tf_op jit(solution)/shard_map/ppermute | solution.py:150
  112.1 1.1 convert_add_fusion
  113.3 4.3 %collective-permute-done.28 = bf16[512,128]{1,0:T(8,128)(2,1)S(1)} collective-permute-done((bf16[512,128]{1,0:T(8,128)(2,1)S(1)}, bf16[512,128]{1,0:T(8,128)(2,1)S(1)}, u32[]{:S(2)}, u32[]{:S(2)}) %collective-permute-start.28) | collective-permute-done | bytes 131104 | tf_op jit(solution)/shard_map/ppermute | solution.py:129
  117.6 1.8 %multiply_add_fusion = f32[512,128]{1,0:T(8,128)} fusion(bf16[512,128]{1,0:T(8,128)(2,1)S(1)} %collective-permute-done.29, bf16[512,128]{1,0:T(8,128)(2,1)S(1)} %collective-permute-done.28, bf16[512,128]{1,0:T(8,128)(2,1)S(1)} %collective-permute-done.27, bf16[2048,128]{1,0:T(8,128)(2,1)} %get-tuple-element.8, f32[512,128]{1,0:T(8,128)S(1)} %copy-done, ...), kind=kLoop, calls=%fused_computation.5 | loop fusion | flops 1179648 | bytes 1572864 | tf_op jit(solution)/shard_map/add | solution.py:207
  (96 shorter events, 18.4 us)
Async XLA Ops:
  3.1 8.9 %collective-permute-start.2 = (bf16[512,128]{1,0:T(8,128)(2,1)S(1)}, bf16[512,128]{1,0:T(8,128)(2,1)S(1)}, u32[]{:S(2)}, u32[]{:S(2)}) collective-permute-start(bf16[512,128]{1,0:T(8,128)(2,1)S(1)} %convert_element_type.72.refs_0_), channel_id=1, source_target_pairs={{0,3},{1,0},{2,1},{3,2},{4,7},{5,4},{6,5},{7,6},{8,11},{9,8},{10,9... | collective-permute-start | bytes 393224 | tf_op jit(solution)/shard_map/ppermute | solution.py:121
  7.8 12.8 %collective-permute-start.6 = (bf16[1024,128]{1,0:T(8,128)(2,1)S(1)}, bf16[1024,128]{1,0:T(8,128)(2,1)S(1)}, u32[]{:S(2)}, u32[]{:S(2)}) collective-permute-start(bf16[1024,128]{1,0:T(8,128)(2,1)S(1)} %pad_maximum_fusion.refs_4_), channel_id=1, source_target_pairs={{0,24},{4,28},{8,16},{12,20},{16,8},{20,12},{24,0},{28,4},{1,25},{... | collective-permute-start | bytes 786440 | tf_op jit(solution)/shard_map/ppermute | solution.py:142
  10.3 12.5 %collective-permute-start.5 = (bf16[1024,128]{1,0:T(8,128)(2,1)S(1)}, bf16[1024,128]{1,0:T(8,128)(2,1)S(1)}, u32[]{:S(2)}, u32[]{:S(2)}) collective-permute-start(bf16[1024,128]{1,0:T(8,128)(2,1)S(1)} %pad_maximum_fusion.refs_4_), channel_id=1, source_target_pairs={{0,16},{4,20},{8,24},{12,28},{16,0},{20,4},{24,8},{28,12},{1,17},{... | collective-permute-start | bytes 786440 | tf_op jit(solution)/shard_map/ppermute | solution.py:142
  10.8 12.1 %collective-permute-start.4 = (bf16[1024,128]{1,0:T(8,128)(2,1)S(1)}, bf16[1024,128]{1,0:T(8,128)(2,1)S(1)}, u32[]{:S(2)}, u32[]{:S(2)}) collective-permute-start(bf16[1024,128]{1,0:T(8,128)(2,1)S(1)} %pad_maximum_fusion.refs_4_), channel_id=1, source_target_pairs={{0,8},{4,12},{8,0},{12,4},{16,24},{20,28},{24,16},{28,20},{1,9},{5... | collective-permute-start | bytes 786440 | tf_op jit(solution)/shard_map/ppermute | solution.py:142
  11.4 9.2 %collective-permute-start.1 = (bf16[512,128]{1,0:T(8,128)(2,1)S(1)}, bf16[512,128]{1,0:T(8,128)(2,1)S(1)}, u32[]{:S(2)}, u32[]{:S(2)}) collective-permute-start(bf16[512,128]{1,0:T(8,128)(2,1)S(1)} %convert_element_type.72.refs_0_), channel_id=1, source_target_pairs={{0,2},{1,3},{2,0},{3,1},{4,6},{5,7},{6,4},{7,5},{8,10},{9,11},{10,... | collective-permute-start | bytes 393224 | tf_op jit(solution)/shard_map/ppermute | solution.py:121
  12.0 8.5 %collective-permute-start = (bf16[512,128]{1,0:T(8,128)(2,1)S(1)}, bf16[512,128]{1,0:T(8,128)(2,1)S(1)}, u32[]{:S(2)}, u32[]{:S(2)}) collective-permute-start(bf16[512,128]{1,0:T(8,128)(2,1)S(1)} %convert_element_type.72.refs_0_), channel_id=1, source_target_pairs={{0,1},{1,2},{2,3},{3,0},{4,5},{5,6},{6,7},{7,4},{8,9},{9,10},{10,1... | collective-permute-start | bytes 393224 | tf_op jit(solution)/shard_map/ppermute | solution.py:121
  35.9 10.9 %collective-permute-start.7 = (bf16[512,128]{1,0:T(8,128)(2,1)S(1)}, bf16[512,128]{1,0:T(8,128)(2,1)S(1)}, u32[]{:S(2)}, u32[]{:S(2)}) collective-permute-start(bf16[512,128]{1,0:T(8,128)(2,1)S(1)} %get-tuple-element.25), channel_id=1, source_target_pairs={{0,1},{1,2},{2,3},{3,0},{4,5},{5,6},{6,7},{7,4},{8,9},{9,10},{10,1... | collective-permute-start | bytes 393224 | tf_op jit(solution)/shard_map/ppermute | solution.py:129
  36.0 12.9 %collective-permute-start.9 = (bf16[512,128]{1,0:T(8,128)(2,1)S(1)}, bf16[512,128]{1,0:T(8,128)(2,1)S(1)}, u32[]{:S(2)}, u32[]{:S(2)}) collective-permute-start(bf16[512,128]{1,0:T(8,128)(2,1)S(1)} %get-tuple-element.26), channel_id=1, source_target_pairs={{0,3},{1,0},{2,1},{3,2},{4,7},{5,4},{6,5},{7,6},{8,11},{9,8},{10,9... | collective-permute-start | bytes 393224 | tf_op jit(solution)/shard_map/ppermute | solution.py:129
  39.8 12.8 %collective-permute-start.8 = (bf16[512,128]{1,0:T(8,128)(2,1)S(1)}, bf16[512,128]{1,0:T(8,128)(2,1)S(1)}, u32[]{:S(2)}, u32[]{:S(2)}) collective-permute-start(bf16[512,128]{1,0:T(8,128)(2,1)S(1)} %get-tuple-element.27), channel_id=1, source_target_pairs={{0,2},{1,3},{2,0},{3,1},{4,6},{5,7},{6,4},{7,5},{8,10},{9,11},{10,... | collective-permute-start | bytes 393224 | tf_op jit(solution)/shard_map/ppermute | solution.py:129
  44.9 8.6 %collective-permute-start.13 = (bf16[512,128]{1,0:T(8,128)(2,1)S(1)}, bf16[512,128]{1,0:T(8,128)(2,1)S(1)}, u32[]{:S(2)}, u32[]{:S(2)}) collective-permute-start(bf16[512,128]{1,0:T(8,128)(2,1)S(1)} %get-tuple-element.15), channel_id=1, source_target_pairs={{0,4},{4,0},{8,12},{12,8},{16,20},{20,16},{24,28},{28,24},{1,5},{5... | collective-permute-start | bytes 393224 | tf_op jit(solution)/shard_map/ppermute | solution.py:167
  45.0 11.0 %collective-permute-start.19 = (bf16[512,128]{1,0:T(8,128)(2,1)S(1)}, bf16[512,128]{1,0:T(8,128)(2,1)S(1)}, u32[]{:S(2)}, u32[]{:S(2)}) collective-permute-start(bf16[512,128]{1,0:T(8,128)(2,1)S(1)} %get-tuple-element.16), channel_id=1, source_target_pairs={{0,28},{4,24},{8,20},{12,16},{16,12},{20,8},{24,4},{28,0},{1,29},{... | collective-permute-start | bytes 393224 | tf_op jit(solution)/shard_map/ppermute | solution.py:167
  46.8 11.0 %collective-permute-start.18 = (bf16[512,128]{1,0:T(8,128)(2,1)S(1)}, bf16[512,128]{1,0:T(8,128)(2,1)S(1)}, u32[]{:S(2)}, u32[]{:S(2)}) collective-permute-start(bf16[512,128]{1,0:T(8,128)(2,1)S(1)} %get-tuple-element.17), channel_id=1, source_target_pairs={{0,24},{4,28},{8,16},{12,20},{16,8},{20,12},{24,0},{28,4},{1,25},{... | collective-permute-start | bytes 393224 | tf_op jit(solution)/shard_map/ppermute | solution.py:167
  48.8 11.1 %collective-permute-start.17 = (bf16[512,128]{1,0:T(8,128)(2,1)S(1)}, bf16[512,128]{1,0:T(8,128)(2,1)S(1)}, u32[]{:S(2)}, u32[]{:S(2)}) collective-permute-start(bf16[512,128]{1,0:T(8,128)(2,1)S(1)} %get-tuple-element.18), channel_id=1, source_target_pairs={{0,20},{4,16},{8,28},{12,24},{16,4},{20,0},{24,12},{28,8},{1,21},{... | collective-permute-start | bytes 393224 | tf_op jit(solution)/shard_map/ppermute | solution.py:167
  52.5 8.8 %collective-permute-start.16 = (bf16[512,128]{1,0:T(8,128)(2,1)S(1)}, bf16[512,128]{1,0:T(8,128)(2,1)S(1)}, u32[]{:S(2)}, u32[]{:S(2)}) collective-permute-start(bf16[512,128]{1,0:T(8,128)(2,1)S(1)} %get-tuple-element.19), channel_id=1, source_target_pairs={{0,16},{4,20},{8,24},{12,28},{16,0},{20,4},{24,8},{28,12},{1,17},{... | collective-permute-start | bytes 393224 | tf_op jit(solution)/shard_map/ppermute | solution.py:167
  53.5 7.8 %collective-permute-start.15 = (bf16[512,128]{1,0:T(8,128)(2,1)S(1)}, bf16[512,128]{1,0:T(8,128)(2,1)S(1)}, u32[]{:S(2)}, u32[]{:S(2)}) collective-permute-start(bf16[512,128]{1,0:T(8,128)(2,1)S(1)} %get-tuple-element.20), channel_id=1, source_target_pairs={{0,12},{4,8},{8,4},{12,0},{16,28},{20,24},{24,20},{28,16},{1,13},{... | collective-permute-start | bytes 393224 | tf_op jit(solution)/shard_map/ppermute | solution.py:167
  56.0 6.9 %collective-permute-start.14 = (bf16[512,128]{1,0:T(8,128)(2,1)S(1)}, bf16[512,128]{1,0:T(8,128)(2,1)S(1)}, u32[]{:S(2)}, u32[]{:S(2)}) collective-permute-start(bf16[512,128]{1,0:T(8,128)(2,1)S(1)} %get-tuple-element.21), channel_id=1, source_target_pairs={{0,8},{4,12},{8,0},{12,4},{16,24},{20,28},{24,16},{28,20},{1,9},{5... | collective-permute-start | bytes 393224 | tf_op jit(solution)/shard_map/ppermute | solution.py:167
  57.8 8.7 %collective-permute-start.12 = (bf16[512,128]{1,0:T(8,128)(2,1)S(1)}, bf16[512,128]{1,0:T(8,128)(2,1)S(1)}, u32[]{:S(2)}, u32[]{:S(2)}) collective-permute-start(bf16[512,128]{1,0:T(8,128)(2,1)S(1)} %fusion.6.refs_0_), channel_id=1, source_target_pairs={{0,3},{1,0},{2,1},{3,2},{4,7},{5,4},{6,5},{7,6},{8,11},{9,8},{10,9... | collective-permute-start | bytes 393224 | tf_op jit(solution)/shard_map/ppermute | solution.py:121
  59.9 11.3 %collective-permute-start.11 = (bf16[512,128]{1,0:T(8,128)(2,1)S(1)}, bf16[512,128]{1,0:T(8,128)(2,1)S(1)}, u32[]{:S(2)}, u32[]{:S(2)}) collective-permute-start(bf16[512,128]{1,0:T(8,128)(2,1)S(1)} %fusion.6.refs_0_), channel_id=1, source_target_pairs={{0,2},{1,3},{2,0},{3,1},{4,6},{5,7},{6,4},{7,5},{8,10},{9,11},{10,... | collective-permute-start | bytes 393224 | tf_op jit(solution)/shard_map/ppermute | solution.py:121
  61.3 10.9 %collective-permute-start.10 = (bf16[512,128]{1,0:T(8,128)(2,1)S(1)}, bf16[512,128]{1,0:T(8,128)(2,1)S(1)}, u32[]{:S(2)}, u32[]{:S(2)}) collective-permute-start(bf16[512,128]{1,0:T(8,128)(2,1)S(1)} %fusion.6.refs_0_), channel_id=1, source_target_pairs={{0,1},{1,2},{2,3},{3,0},{4,5},{5,6},{6,7},{7,4},{8,9},{9,10},{10,1... | collective-permute-start | bytes 393224 | tf_op jit(solution)/shard_map/ppermute | solution.py:121
  63.9 8.7 %collective-permute-start.26 = (bf16[512,128]{1,0:T(8,128)(2,1)S(1)}, bf16[512,128]{1,0:T(8,128)(2,1)S(1)}, u32[]{:S(2)}, u32[]{:S(2)}) collective-permute-start(bf16[512,128]{1,0:T(8,128)(2,1)S(1)} %get-tuple-element.10.refs_4_), channel_id=1, source_target_pairs={{0,28},{4,24},{8,20},{12,16},{16,12},{20,8},{24,4},{28,0},{1,29},{... | collective-permute-start | bytes 393224 | tf_op jit(solution)/shard_map/ppermute | solution.py:159
  65.4 8.1 %collective-permute-start.25 = (bf16[512,128]{1,0:T(8,128)(2,1)S(1)}, bf16[512,128]{1,0:T(8,128)(2,1)S(1)}, u32[]{:S(2)}, u32[]{:S(2)}) collective-permute-start(bf16[512,128]{1,0:T(8,128)(2,1)S(1)} %get-tuple-element.10.refs_4_), channel_id=1, source_target_pairs={{0,24},{4,28},{8,16},{12,20},{16,8},{20,12},{24,0},{28,4},{1,25},{... | collective-permute-start | bytes 393224 | tf_op jit(solution)/shard_map/ppermute | solution.py:159
  66.5 9.8 %collective-permute-start.24 = (bf16[512,128]{1,0:T(8,128)(2,1)S(1)}, bf16[512,128]{1,0:T(8,128)(2,1)S(1)}, u32[]{:S(2)}, u32[]{:S(2)}) collective-permute-start(bf16[512,128]{1,0:T(8,128)(2,1)S(1)} %get-tuple-element.10.refs_4_), channel_id=1, source_target_pairs={{0,20},{4,16},{8,28},{12,24},{16,4},{20,0},{24,12},{28,8},{1,21},{... | collective-permute-start | bytes 393224 | tf_op jit(solution)/shard_map/ppermute | solution.py:159
  71.3 7.8 %collective-permute-start.23 = (bf16[512,128]{1,0:T(8,128)(2,1)S(1)}, bf16[512,128]{1,0:T(8,128)(2,1)S(1)}, u32[]{:S(2)}, u32[]{:S(2)}) collective-permute-start(bf16[512,128]{1,0:T(8,128)(2,1)S(1)} %get-tuple-element.10.refs_4_), channel_id=1, source_target_pairs={{0,16},{4,20},{8,24},{12,28},{16,0},{20,4},{24,8},{28,12},{1,17},{... | collective-permute-start | bytes 393224 | tf_op jit(solution)/shard_map/ppermute | solution.py:159
  72.3 6.8 %collective-permute-start.22 = (bf16[512,128]{1,0:T(8,128)(2,1)S(1)}, bf16[512,128]{1,0:T(8,128)(2,1)S(1)}, u32[]{:S(2)}, u32[]{:S(2)}) collective-permute-start(bf16[512,128]{1,0:T(8,128)(2,1)S(1)} %get-tuple-element.10.refs_4_), channel_id=1, source_target_pairs={{0,12},{4,8},{8,4},{12,0},{16,28},{20,24},{24,20},{28,16},{1,13},{... | collective-permute-start | bytes 393224 | tf_op jit(solution)/shard_map/ppermute | solution.py:159
  72.6 7.1 %collective-permute-start.21 = (bf16[512,128]{1,0:T(8,128)(2,1)S(1)}, bf16[512,128]{1,0:T(8,128)(2,1)S(1)}, u32[]{:S(2)}, u32[]{:S(2)}) collective-permute-start(bf16[512,128]{1,0:T(8,128)(2,1)S(1)} %get-tuple-element.10.refs_4_), channel_id=1, source_target_pairs={{0,8},{4,12},{8,0},{12,4},{16,24},{20,28},{24,16},{28,20},{1,9},{5... | collective-permute-start | bytes 393224 | tf_op jit(solution)/shard_map/ppermute | solution.py:159
  92.7 13.5 %collective-permute-start.30 = (bf16[1024,128]{1,0:T(8,128)(2,1)S(1)}, bf16[1024,128]{1,0:T(8,128)(2,1)S(1)}, u32[]{:S(2)}, u32[]{:S(2)}) collective-permute-start(bf16[1024,128]{1,0:T(8,128)(2,1)S(1)} %get-tuple-element.12), channel_id=1, source_target_pairs={{0,8},{4,12},{8,0},{12,4},{16,24},{20,28},{24,16},{28,20},{1,9},{5... | collective-permute-start | bytes 786440 | tf_op jit(solution)/shard_map/ppermute | solution.py:150
  98.6 12.0 %collective-permute-start.32 = (bf16[1024,128]{1,0:T(8,128)(2,1)S(1)}, bf16[1024,128]{1,0:T(8,128)(2,1)S(1)}, u32[]{:S(2)}, u32[]{:S(2)}) collective-permute-start(bf16[1024,128]{1,0:T(8,128)(2,1)S(1)} %get-tuple-element.13), channel_id=1, source_target_pairs={{0,24},{4,28},{8,16},{12,20},{16,8},{20,12},{24,0},{28,4},{1,25},{... | collective-permute-start | bytes 786440 | tf_op jit(solution)/shard_map/ppermute | solution.py:150
  98.6 13.6 %collective-permute-start.31 = (bf16[1024,128]{1,0:T(8,128)(2,1)S(1)}, bf16[1024,128]{1,0:T(8,128)(2,1)S(1)}, u32[]{:S(2)}, u32[]{:S(2)}) collective-permute-start(bf16[1024,128]{1,0:T(8,128)(2,1)S(1)} %get-tuple-element.14), channel_id=1, source_target_pairs={{0,16},{4,20},{8,24},{12,28},{16,0},{20,4},{24,8},{28,12},{1,17},{... | collective-permute-start | bytes 786440 | tf_op jit(solution)/shard_map/ppermute | solution.py:150
  101.2 12.2 %collective-permute-start.27 = (bf16[512,128]{1,0:T(8,128)(2,1)S(1)}, bf16[512,128]{1,0:T(8,128)(2,1)S(1)}, u32[]{:S(2)}, u32[]{:S(2)}) collective-permute-start(bf16[512,128]{1,0:T(8,128)(2,1)S(1)} %get-tuple-element.22), channel_id=1, source_target_pairs={{0,1},{1,2},{2,3},{3,0},{4,5},{5,6},{6,7},{7,4},{8,9},{9,10},{10,1... | collective-permute-start | bytes 393224 | tf_op jit(solution)/shard_map/ppermute | solution.py:129
  101.2 12.1 %collective-permute-start.29 = (bf16[512,128]{1,0:T(8,128)(2,1)S(1)}, bf16[512,128]{1,0:T(8,128)(2,1)S(1)}, u32[]{:S(2)}, u32[]{:S(2)}) collective-permute-start(bf16[512,128]{1,0:T(8,128)(2,1)S(1)} %get-tuple-element.23), channel_id=1, source_target_pairs={{0,3},{1,0},{2,1},{3,2},{4,7},{5,4},{6,5},{7,6},{8,11},{9,8},{10,9... | collective-permute-start | bytes 393224 | tf_op jit(solution)/shard_map/ppermute | solution.py:129
  106.2 11.4 %collective-permute-start.28 = (bf16[512,128]{1,0:T(8,128)(2,1)S(1)}, bf16[512,128]{1,0:T(8,128)(2,1)S(1)}, u32[]{:S(2)}, u32[]{:S(2)}) collective-permute-start(bf16[512,128]{1,0:T(8,128)(2,1)S(1)} %get-tuple-element.24), channel_id=1, source_target_pairs={{0,2},{1,3},{2,0},{3,1},{4,6},{5,7},{6,4},{7,5},{8,10},{9,11},{10,... | collective-permute-start | bytes 393224 | tf_op jit(solution)/shard_map/ppermute | solution.py:129
  113.2 6.2 %collective-permute-start.33 = (f32[512,128]{1,0:T(8,128)S(1)}, f32[512,128]{1,0:T(8,128)S(1)}, u32[]{:S(2)}, u32[]{:S(2)}) collective-permute-start(f32[512,128]{1,0:T(8,128)S(1)} %slice.97), channel_id=1, source_target_pairs={{0,4},{4,0},{8,12},{12,8},{16,20},{20,16},{24,28},{28,24},{1,5},{5... | collective-permute-start | bytes 786440 | tf_op jit(solution)/shard_map/ppermute | solution.py:152
  (24 other events, 225.4 us)

commit v9 on v8

--- a/solution.py
+++ b/solution.py
@@ -10,10 +10,13 @@
 ITERS = 2
 
 
-def sweep_kernel(tile, group, n_emb, n_ctx, rows_ref, cols_ref, count_ref, *refs):
+def sweep_kernel(tile, group, n_emb, n_ctx, n_gemb, n_gctx, rows_ref, cols_ref, count_ref, *refs):
     emb_pieces = refs[:n_emb]
     ctx_pieces = refs[n_emb : n_emb + n_ctx]
-    pos_ref, neg_ref, gemb_ref, gctx_ref, acc_e, acc_ct, emb_t, emb_ref, ctx_ref = refs[n_emb + n_ctx :]
+    pos_ref, neg_ref = refs[n_emb + n_ctx : n_emb + n_ctx + 2]
+    outs = refs[n_emb + n_ctx + 2 : n_emb + n_ctx + 2 + n_gemb + n_gctx]
+    gemb_refs, gctx_refs = outs[:n_gemb], outs[n_gemb:]
+    acc_e, acc_ct, emb_t, emb_ref, ctx_ref = refs[n_emb + n_ctx + 2 + n_gemb + n_gctx :]
     k = pl.program_id(0)
     n = count_ref[0]
 
@@ -63,11 +66,15 @@
 
     @pl.when(k == pl.num_programs(0) - 1)
     def _():
-        gemb_ref[...] = acc_e[...].astype(gemb_ref.dtype)
-        gctx_ref[...] = acc_ct[...].T.astype(gctx_ref.dtype)
-
-
-def tile_sweep(pos, neg, rows, cols, count, emb_pieces, ctx_pieces):
+        for p, out in enumerate(gemb_refs):
+            rows = out.shape[0]
+            out[...] = acc_e[p * rows : (p + 1) * rows, :].astype(out.dtype)
+        for p, out in enumerate(gctx_refs):
+            rows = out.shape[0]
+            out[...] = acc_ct[:, p * rows : (p + 1) * rows].T.astype(out.dtype)
+
+
+def tile_sweep(pos, neg, rows, cols, count, emb_pieces, ctx_pieces, n_gemb, n_gctx):
     cap, tile, _ = pos.shape
     dim = emb_pieces[0].shape[1]
     ne = sum(p.shape[0] for p in emb_pieces)
@@ -86,10 +93,8 @@
             pl.BlockSpec((group, tile, tile), slot),
             pl.BlockSpec((group, tile, tile), slot),
         ],
-        out_specs=[
-            pl.BlockSpec((ne, dim), lambda k, *_: (0, 0)),
-            pl.BlockSpec((nc, dim), lambda k, *_: (0, 0)),
-        ],
+        out_specs=[pl.BlockSpec((ne // n_gemb, dim), lambda k, *_: (0, 0))] * n_gemb
+        + [pl.BlockSpec((nc // n_gctx, dim), lambda k, *_: (0, 0))] * n_gctx,
         scratch_shapes=[
             pltpu.VMEM((ne, dim), jnp.float32),
             pltpu.VMEM((dim, nc), jnp.float32),
@@ -99,13 +104,11 @@
         ],
     )
     flops = cap * 3 * 2 * tile * tile * dim
-    return pl.pallas_call(
-        functools.partial(sweep_kernel, tile, group, len(emb_pieces), len(ctx_pieces)),
+    outs = pl.pallas_call(
+        functools.partial(sweep_kernel, tile, group, len(emb_pieces), len(ctx_pieces), n_gemb, n_gctx),
         grid_spec=grid_spec,
-        out_shape=(
-            jax.ShapeDtypeStruct((ne, dim), jnp.bfloat16),
-            jax.ShapeDtypeStruct((nc, dim), jnp.bfloat16),
-        ),
+        out_shape=[jax.ShapeDtypeStruct((ne // n_gemb, dim), jnp.bfloat16)] * n_gemb
+        + [jax.ShapeDtypeStruct((nc // n_gctx, dim), jnp.bfloat16)] * n_gctx,
         compiler_params=pltpu.CompilerParams(dimension_semantics=("arbitrary",)),
         cost_estimate=pl.CostEstimate(
             flops=flops,
@@ -113,6 +116,7 @@
             bytes_accessed=2 * cap * tile * tile * 2 + 3 * (ne + nc) * dim * 2,
         ),
     )(rows, cols, count.reshape(1), *emb_pieces, *ctx_pieces, pos, neg)
+    return outs[:n_gemb], outs[n_gemb:]
 
 
 def gather_rotated(x, axis, n):
@@ -122,8 +126,7 @@
     return pieces
 
 
-def scatter_rotated(g, axis, n):
-    chunks = g.reshape(n, -1, g.shape[-1])
+def scatter_rotated(chunks, axis, n):
     total = chunks[0].astype(jnp.float32)
     for s in range(1, n):
         got = lax.ppermute(chunks[(n - s) % n], axis, [(i, (i + s) % n) for i in range(n)])
@@ -143,12 +146,12 @@
     return blocks
 
 
-def scatter_paired(g, axis, n):
-    width = g.shape[0] // n
-    total = g[: 2 * width].astype(jnp.float32)
+def scatter_paired(blocks, axis, n):
+    total = blocks[0].astype(jnp.float32)
     for b in range(1, n // 2):
-        got = lax.ppermute(g[2 * b * width : (2 * b + 2) * width], axis, [(i, i ^ (2 * b)) for i in range(n)])
+        got = lax.ppermute(blocks[b], axis, [(i, i ^ (2 * b)) for i in range(n)])
         total = total + got.astype(jnp.float32)
+    width = total.shape[0] // 2
     got = lax.ppermute(total[width:], axis, [(i, i ^ 1) for i in range(n)])
     return total[:width] + got
 
@@ -160,11 +163,10 @@
     return pieces
 
 
-def scatter_xor(g, axis, n):
-    width = g.shape[0] // n
-    total = g[:width].astype(jnp.float32)
+def scatter_xor(chunks, axis, n):
+    total = chunks[0].astype(jnp.float32)
     for p in range(1, n):
-        got = lax.ppermute(g[p * width : (p + 1) * width], axis, [(i, i ^ p) for i in range(n)])
+        got = lax.ppermute(chunks[p], axis, [(i, i ^ p) for i in range(n)])
         total = total + got.astype(jnp.float32)
     return total
 
@@ -192,10 +194,12 @@
         cols = pair_index(tile_col[0, 0], me_row, per_run)
         gathers = (gather_paired, gather_xor)
         scatters = (scatter_xor, scatter_paired)
+        splits = (n_row, n_row // 2)
     else:
         cols = rotate_index(tile_col[0, 0], me_row, n_row, per_run)
         gathers = (gather_rotated, gather_rotated)
         scatters = (scatter_rotated, scatter_rotated)
+        splits = (n_row, n_row)
     count = tile_count[0, 0]
     emb = emb_in
     ctx = ctx_in
@@ -203,7 +207,9 @@
         emb_low = gather_rotated(emb.astype(jnp.bfloat16), "col", n_col)
         first, last = iteration == 0, iteration == ITERS - 1
         ctx_low = gathers[0 if first else 1](ctx.astype(jnp.bfloat16), "row", n_row)
-        grad_emb, grad_ctx = tile_sweep(pos, neg, rows, cols, count, emb_low, ctx_low)
+        grad_emb, grad_ctx = tile_sweep(
+            pos, neg, rows, cols, count, emb_low, ctx_low, n_col, splits[1 if last else 0]
+        )
         emb = emb + 0.05 * scatter_rotated(grad_emb, "col", n_col)
         ctx = ctx + 0.05 * scatters[1 if last else 0](grad_ctx, "row", n_row)
     return (emb, ctx)

time: 121 us -> 119 us (0.983)
  starting transfers between devices: 51.4 us -> 57.8 us
  local copies, waits for them, and re-layouts: 5.92 us -> 1.43 us
  waiting for transfers between devices: 30 us -> 27.6 us
  Pallas kernels: 22.4 us -> 20.2 us
    ppermute x10, starting transfers between devices: 17 us -> 23.7 us  [the longest x3 11.9 us: scatter_paired(): got = lax.ppermute(blocks[b], axis, [(i, i ^ 2 * b) for i in range(n)])]
    ppermute x6, waiting for transfers between devices: 6.45 us -> 1.46 us  [scatter_rotated(): lax.ppermute(chunks[(n - s) % n], axis, [(i, (i + s) % n) for i in range(...]
    ppermute x10, waiting for transfers between devices: 5.23 us -> 9.82 us  [the longest x7 5.8 us: scatter_xor(): got = lax.ppermute(chunks[p], axis, [(i, i ^ p) for i in range(n)])]
    slice x4 -> x0, local copies, waits for them, and re-layouts: 4.57 us -> none  [the longest x2 2.11 us: scatter_rotated(): chunks[(n - s) % n]]
    pallas_call x2, Pallas kernels: 22.4 us -> 20.2 us  [tile_sweep(): pl.pallas_call(functools.partial(sweep_kernel, tile, group, len(emb_piece...]
    ppermute x6, waiting for transfers between devices: 10 us -> 8.04 us  [gather_rotated(): pieces.append(lax.ppermute(x, axis, [(i, (i + s) % n) for i in range(n)]))]
    ppermute x6, starting transfers between devices: 14.9 us -> 13.1 us  [scatter_rotated(): lax.ppermute(chunks[(n - s) % n], axis, [(i, (i + s) % n) for i in range(...]
    ppermute x7, starting transfers between devices: 5.98 us -> 7.41 us  [gather_xor(): pieces.append(lax.ppermute(x, axis, [(i, i ^ p) for i in range(n)]))]
  transfers between devices with their start and end apart: 34 -> 34, of which waited for: 13 -> 11; matrix products, arithmetic and copies ran while one was open for 8% -> 6% of each run, Pallas kernels for 0% -> 0%
where the time goes in v9:
time: 119 us; the launch traced here: 117 us
  starting transfers between devices  57.8 us (49%)
  waiting for transfers between devices  27.6 us (23%)
  Pallas kernels  20.2 us (17%)
  other arithmetic  8.83 us (7%)
  between operations  1.58 us (1%)
  local copies, waits for them, and re-layouts  1.43 us (1%)
    pallas_call x2, Pallas kernels, tile_sweep(): pl.pallas_call(functools.partial(sweep_kernel, tile, group, len(emb_piece...  20.2 us
    ppermute x6, starting transfers between devices, scatter_rotated(): lax.ppermute(chunks[(n - s) % n], axis, [(i, (i + s) % n) for i in range(...  13.1 us
    ppermute x3, starting transfers between devices, scatter_paired(): got = lax.ppermute(blocks[b], axis, [(i, i ^ 2 * b) for i in range(n)])  11.9 us
    ppermute x7, starting transfers between devices, scatter_xor(): got = lax.ppermute(chunks[p], axis, [(i, i ^ p) for i in range(n)])  11.7 us
    ppermute x6, starting transfers between devices, gather_rotated(): pieces.append(lax.ppermute(x, axis, [(i, (i + s) % n) for i in range(n)]))  9.51 us
    ppermute x6, waiting for transfers between devices, gather_rotated(): pieces.append(lax.ppermute(x, axis, [(i, (i + s) % n) for i in range(n)]))  8.04 us
    ppermute x7, starting transfers between devices, gather_xor(): pieces.append(lax.ppermute(x, axis, [(i, i ^ p) for i in range(n)]))  7.41 us
    ppermute x7, waiting for transfers between devices, gather_xor(): pieces.append(lax.ppermute(x, axis, [(i, i ^ p) for i in range(n)]))  5.96 us
  transfers between devices with their start and end apart: 34, of which 11 were waited for; matrix products, arithmetic and copies ran while one was open for 6% of the time, Pallas kernels for 0%

profile of v9, /device:TPU:0, one launch (start us, length us, event | category | flops | bytes accessed | tf_op | source)
XLA Modules:
  0.0 117.5 jit_solution(17145787062960839595)
XLA Ops:
  3.1 4.7 %collective-permute-start.2 = (bf16[512,128]{1,0:T(8,128)(2,1)S(1)}, bf16[512,128]{1,0:T(8,128)(2,1)S(1)}, u32[]{:S(2)}, u32[]{:S(2)}) collective-permute-start(bf16[512,128]{1,0:T(8,128)(2,1)S(1)} %convert_element_type.72.refs_0_), channel_id=1, source_target_pairs={{0,3},{1,0},{2,1},{3,2},{4,7},{5,4},{6,5},{7,6},{8,11},{9,8},{10,9... | collective-permute-start | bytes 393224 | tf_op jit(solution)/shard_map/ppermute | solution.py:125
  7.8 2.5 %collective-permute-start.6 = (bf16[1024,128]{1,0:T(8,128)(2,1)S(1)}, bf16[1024,128]{1,0:T(8,128)(2,1)S(1)}, u32[]{:S(2)}, u32[]{:S(2)}) collective-permute-start(bf16[1024,128]{1,0:T(8,128)(2,1)S(1)} %pad_maximum_fusion.refs_4_), channel_id=1, source_target_pairs={{0,24},{4,28},{8,16},{12,20},{16,8},{20,12},{24,0},{28,4},{1,25},{... | collective-permute-start | bytes 786440 | tf_op jit(solution)/shard_map/ppermute | solution.py:145
  12.0 1.1 collective-permute-start
  13.1 1.2 %fusion.2 = (s32[64]{0:T(128)}, s32[64]{0:T(128)}) fusion(s32[1,1,64]{2,1,0:T(1,128)} %param.11, s32[]{:T(128)S(6)} %axis_index.22, s32[1,1,64]{2,1,0:T(1,128)} %param.12, s32[]{:T(128)S(6)} %axis_index.25), kind=kLoop, calls=%fused_computation.21 | loop fusion | flops 3520 | bytes 1032 | tf_op jit(solution)/shard_map/add | solution.py:180
  14.3 6.3 %collective-permute-done.1.refs_2_ = bf16[512,128]{1,0:T(8,128)(2,1)S(1)} collective-permute-done((bf16[512,128]{1,0:T(8,128)(2,1)S(1)}, bf16[512,128]{1,0:T(8,128)(2,1)S(1)}, u32[]{:S(2)}, u32[]{:S(2)}) %collective-permute-start.1) | collective-permute-done | bytes 131104 | tf_op jit(solution)/shard_map/ppermute | solution.py:125
  20.6 2.2 %collective-permute-done.5.refs_6_ = bf16[1024,128]{1,0:T(8,128)(2,1)S(1)} collective-permute-done((bf16[1024,128]{1,0:T(8,128)(2,1)S(1)}, bf16[1024,128]{1,0:T(8,128)(2,1)S(1)}, u32[]{:S(2)}, u32[]{:S(2)}) %collective-permute-start.5) | collective-permute-done | bytes 262176 | tf_op jit(solution)/shard_map/ppermute | solution.py:145
  23.6 10.1 %shard_map.86 = (bf16[512,128]{1,0:T(8,128)(2,1)}, bf16[512,128]{1,0:T(8,128)(2,1)}, bf16[512,128]{1,0:T(8,128)(2,1)}, bf16[512,128]{1,0:T(8,128)(2,1)}, bf16[51...) custom-call(s32[64]{0:T(128)} %get-tuple-element.44.rows_ref, ...), custom_call_target="tpu_custom_call" | custom-call | flops 3221225472 | bytes 21495808 | tf_op jit(solution)/shard_map/pallas_call | solution.py:107
  33.7 1.5 %collective-permute-start.7 = (bf16[512,128]{1,0:T(8,128)(2,1)}, bf16[512,128]{1,0:T(8,128)(2,1)S(1)}, u32[]{:S(2)}, u32[]{:S(2)}) collective-permute-start(bf16[512,128]{1,0:T(8,128)(2,1)} %get-tuple-element.23), channel_id=1, source_target_pairs={{0,1},{1,2},{2,3},{3,0},{4,5},{5,6},{6,7},{7,4},{8,9},{9,10},{10,1... | collective-permute-start | bytes 393224 | tf_op jit(solution)/shard_map/ppermute | solution.py:132
  35.2 4.9 %collective-permute-start.8 = (bf16[512,128]{1,0:T(8,128)(2,1)}, bf16[512,128]{1,0:T(8,128)(2,1)S(1)}, u32[]{:S(2)}, u32[]{:S(2)}) collective-permute-start(bf16[512,128]{1,0:T(8,128)(2,1)} %get-tuple-element.24), channel_id=1, source_target_pairs={{0,2},{1,3},{2,0},{3,1},{4,6},{5,7},{6,4},{7,5},{8,10},{9,11},{10,... | collective-permute-start | bytes 393224 | tf_op jit(solution)/shard_map/ppermute | solution.py:132
  40.1 2.8 %collective-permute-start.9 = (bf16[512,128]{1,0:T(8,128)(2,1)}, bf16[512,128]{1,0:T(8,128)(2,1)S(1)}, u32[]{:S(2)}, u32[]{:S(2)}) collective-permute-start(bf16[512,128]{1,0:T(8,128)(2,1)} %get-tuple-element.25), channel_id=1, source_target_pairs={{0,3},{1,0},{2,1},{3,2},{4,7},{5,4},{6,5},{7,6},{8,11},{9,8},{10,9... | collective-permute-start | bytes 393224 | tf_op jit(solution)/shard_map/ppermute | solution.py:132
  43.0 5.0 %collective-permute-start.14 = (bf16[512,128]{1,0:T(8,128)(2,1)}, bf16[512,128]{1,0:T(8,128)(2,1)S(1)}, u32[]{:S(2)}, u32[]{:S(2)}) collective-permute-start(bf16[512,128]{1,0:T(8,128)(2,1)} %get-tuple-element.28), channel_id=1, source_target_pairs={{0,8},{4,12},{8,0},{12,4},{16,24},{20,28},{24,16},{28,20},{1,9},{5... | collective-permute-start | bytes 393224 | tf_op jit(solution)/shard_map/ppermute | solution.py:169
  48.1 4.2 %collective-permute-start.16 = (bf16[512,128]{1,0:T(8,128)(2,1)}, bf16[512,128]{1,0:T(8,128)(2,1)S(1)}, u32[]{:S(2)}, u32[]{:S(2)}) collective-permute-start(bf16[512,128]{1,0:T(8,128)(2,1)} %get-tuple-element.30), channel_id=1, source_target_pairs={{0,16},{4,20},{8,24},{12,28},{16,0},{20,4},{24,8},{28,12},{1,17},{... | collective-permute-start | bytes 393224 | tf_op jit(solution)/shard_map/ppermute | solution.py:169
  52.7 1.9 %collective-permute-start.18 = (bf16[512,128]{1,0:T(8,128)(2,1)}, bf16[512,128]{1,0:T(8,128)(2,1)S(1)}, u32[]{:S(2)}, u32[]{:S(2)}) collective-permute-start(bf16[512,128]{1,0:T(8,128)(2,1)} %get-tuple-element.32), channel_id=1, source_target_pairs={{0,24},{4,28},{8,16},{12,20},{16,8},{20,12},{24,0},{28,4},{1,25},{... | collective-permute-start | bytes 393224 | tf_op jit(solution)/shard_map/ppermute | solution.py:169
  55.7 3.2 %collective-permute-start.12 = (bf16[512,128]{1,0:T(8,128)(2,1)S(1)}, bf16[512,128]{1,0:T(8,128)(2,1)S(1)}, u32[]{:S(2)}, u32[]{:S(2)}) collective-permute-start(bf16[512,128]{1,0:T(8,128)(2,1)S(1)} %fusion.6.refs_0_), channel_id=1, source_target_pairs={{0,3},{1,0},{2,1},{3,2},{4,7},{5,4},{6,5},{7,6},{8,11},{9,8},{10,9... | collective-permute-start | bytes 393224 | tf_op jit(solution)/shard_map/ppermute | solution.py:125
  58.9 3.4 %collective-permute-done.16 = bf16[512,128]{1,0:T(8,128)(2,1)S(1)} collective-permute-done((bf16[512,128]{1,0:T(8,128)(2,1)}, bf16[512,128]{1,0:T(8,128)(2,1)S(1)}, u32[]{:S(2)}, u32[]{:S(2)}) %collective-permute-start.16) | collective-permute-done | bytes 131104 | tf_op jit(solution)/shard_map/ppermute | solution.py:169
  62.9 2.4 %collective-permute-done.17 = bf16[512,128]{1,0:T(8,128)(2,1)S(1)} collective-permute-done((bf16[512,128]{1,0:T(8,128)(2,1)}, bf16[512,128]{1,0:T(8,128)(2,1)S(1)}, u32[]{:S(2)}, u32[]{:S(2)}) %collective-permute-start.17) | collective-permute-done | bytes 131104 | tf_op jit(solution)/shard_map/ppermute | solution.py:169
  65.3 1.1 fusion.7
  67.3 1.7 %collective-permute-start.25 = (bf16[512,128]{1,0:T(8,128)(2,1)S(1)}, bf16[512,128]{1,0:T(8,128)(2,1)S(1)}, u32[]{:S(2)}, u32[]{:S(2)}) collective-permute-start(bf16[512,128]{1,0:T(8,128)(2,1)S(1)} %get-tuple-element.42.refs_4_), channel_id=1, source_target_pairs={{0,24},{4,28},{8,16},{12,20},{16,8},{20,12},{24,0},{28,4},{1,25},{... | collective-permute-start | bytes 393224 | tf_op jit(solution)/shard_map/ppermute | solution.py:162
  69.0 2.2 %collective-permute-start.24 = (bf16[512,128]{1,0:T(8,128)(2,1)S(1)}, bf16[512,128]{1,0:T(8,128)(2,1)S(1)}, u32[]{:S(2)}, u32[]{:S(2)}) collective-permute-start(bf16[512,128]{1,0:T(8,128)(2,1)S(1)} %get-tuple-element.42.refs_4_), channel_id=1, source_target_pairs={{0,20},{4,16},{8,28},{12,24},{16,4},{20,0},{24,12},{28,8},{1,21},{... | collective-permute-start | bytes 393224 | tf_op jit(solution)/shard_map/ppermute | solution.py:162
  71.2 1.8 %collective-permute-done.11.refs_2_ = bf16[512,128]{1,0:T(8,128)(2,1)S(1)} collective-permute-done((bf16[512,128]{1,0:T(8,128)(2,1)S(1)}, bf16[512,128]{1,0:T(8,128)(2,1)S(1)}, u32[]{:S(2)}, u32[]{:S(2)}) %collective-permute-start.11) | collective-permute-done | bytes 131104 | tf_op jit(solution)/shard_map/ppermute | solution.py:125
  73.0 1.3 %collective-permute-start.23 = (bf16[512,128]{1,0:T(8,128)(2,1)S(1)}, bf16[512,128]{1,0:T(8,128)(2,1)S(1)}, u32[]{:S(2)}, u32[]{:S(2)}) collective-permute-start(bf16[512,128]{1,0:T(8,128)(2,1)S(1)} %get-tuple-element.42.refs_4_), channel_id=1, source_target_pairs={{0,16},{4,20},{8,24},{12,28},{16,0},{20,4},{24,8},{28,12},{1,17},{... | collective-permute-start | bytes 393224 | tf_op jit(solution)/shard_map/ppermute | solution.py:162
  74.3 1.3 %collective-permute-start.21 = (bf16[512,128]{1,0:T(8,128)(2,1)S(1)}, bf16[512,128]{1,0:T(8,128)(2,1)S(1)}, u32[]{:S(2)}, u32[]{:S(2)}) collective-permute-start(bf16[512,128]{1,0:T(8,128)(2,1)S(1)} %get-tuple-element.42.refs_4_), channel_id=1, source_target_pairs={{0,8},{4,12},{8,0},{12,4},{16,24},{20,28},{24,16},{28,20},{1,9},{5... | collective-permute-start | bytes 393224 | tf_op jit(solution)/shard_map/ppermute | solution.py:162
  76.1 2.6 %collective-permute-done.24.refs_9_ = bf16[512,128]{1,0:T(8,128)(2,1)S(1)} collective-permute-done((bf16[512,128]{1,0:T(8,128)(2,1)S(1)}, bf16[512,128]{1,0:T(8,128)(2,1)S(1)}, u32[]{:S(2)}, u32[]{:S(2)}) %collective-permute-start.24) | collective-permute-done | bytes 131104 | tf_op jit(solution)/shard_map/ppermute | solution.py:162
  78.8 2.8 %collective-permute-done.23.refs_8_ = bf16[512,128]{1,0:T(8,128)(2,1)S(1)} collective-permute-done((bf16[512,128]{1,0:T(8,128)(2,1)S(1)}, bf16[512,128]{1,0:T(8,128)(2,1)S(1)}, u32[]{:S(2)}, u32[]{:S(2)}) %collective-permute-start.23) | collective-permute-done | bytes 131104 | tf_op jit(solution)/shard_map/ppermute | solution.py:162
  82.4 10.1 %shard_map.87 = (bf16[512,128]{1,0:T(8,128)(2,1)}, bf16[512,128]{1,0:T(8,128)(2,1)}, bf16[512,128]{1,0:T(8,128)(2,1)}, bf16[512,128]{1,0:T(8,128)(2,1)}, bf16[10...) custom-call(s32[64]{0:T(128)} %get-tuple-element.44.rows_ref, ...), custom_call_target="tpu_custom_call" | custom-call | flops 3221225472 | bytes 21495808 | tf_op jit(solution)/shard_map/pallas_call | solution.py:107
  92.5 10.4 %collective-permute-start.30 = (bf16[1024,128]{1,0:T(8,128)(2,1)}, bf16[1024,128]{1,0:T(8,128)(2,1)S(1)}, u32[]{:S(2)}, u32[]{:S(2)}) collective-permute-start(bf16[1024,128]{1,0:T(8,128)(2,1)} %get-tuple-element.39), channel_id=1, source_target_pairs={{0,8},{4,12},{8,0},{12,4},{16,24},{20,28},{24,16},{28,20},{1,9},{5... | collective-permute-start | bytes 786440 | tf_op jit(solution)/shard_map/ppermute | solution.py:152
  102.9 1.5 %collective-permute-start.32 = (bf16[1024,128]{1,0:T(8,128)(2,1)}, bf16[1024,128]{1,0:T(8,128)(2,1)S(1)}, u32[]{:S(2)}, u32[]{:S(2)}) collective-permute-start(bf16[1024,128]{1,0:T(8,128)(2,1)} %get-tuple-element.41), channel_id=1, source_target_pairs={{0,24},{4,28},{8,16},{12,20},{16,8},{20,12},{24,0},{28,4},{1,25},{... | collective-permute-start | bytes 786440 | tf_op jit(solution)/shard_map/ppermute | solution.py:152
  104.4 3.1 %collective-permute-start.28 = (bf16[512,128]{1,0:T(8,128)(2,1)}, bf16[512,128]{1,0:T(8,128)(2,1)S(1)}, u32[]{:S(2)}, u32[]{:S(2)}) collective-permute-start(bf16[512,128]{1,0:T(8,128)(2,1)} %get-tuple-element.36), channel_id=1, source_target_pairs={{0,2},{1,3},{2,0},{3,1},{4,6},{5,7},{6,4},{7,5},{8,10},{9,11},{10,... | collective-permute-start | bytes 393224 | tf_op jit(solution)/shard_map/ppermute | solution.py:132
  108.2 4.0 %collective-permute-done.31 = bf16[1024,128]{1,0:T(8,128)(2,1)S(1)} collective-permute-done((bf16[1024,128]{1,0:T(8,128)(2,1)}, bf16[1024,128]{1,0:T(8,128)(2,1)S(1)}, u32[]{:S(2)}, u32[]{:S(2)}) %collective-permute-start.31) | collective-permute-done | bytes 262176 | tf_op jit(solution)/shard_map/ppermute | solution.py:152
  112.3 1.1 convert_add_fusion
  113.5 1.5 %collective-permute-done.28 = bf16[512,128]{1,0:T(8,128)(2,1)S(1)} collective-permute-done((bf16[512,128]{1,0:T(8,128)(2,1)}, bf16[512,128]{1,0:T(8,128)(2,1)S(1)}, u32[]{:S(2)}, u32[]{:S(2)}) %collective-permute-start.28) | collective-permute-done | bytes 131104 | tf_op jit(solution)/shard_map/ppermute | solution.py:132
  114.9 1.8 %multiply_add_fusion = f32[512,128]{1,0:T(8,128)} fusion(bf16[512,128]{1,0:T(8,128)(2,1)S(1)} %collective-permute-done.29, bf16[512,128]{1,0:T(8,128)(2,1)S(1)} %collective-permute-done.28, bf16[512,128]{1,0:T(8,128)(2,1)S(1)} %collective-permute-done.27, bf16[512,128]{1,0:T(8,128)(2,1)} %get-tuple-element.34, f32[512,128]{1,0:T(8,128)S(1)} %copy-done, ...), kind=kLoop, calls=%fused_computation.5 | loop fusion | flops 1179648 | bytes 1572864 | tf_op jit(solution)/shard_map/add | solution.py:213
  (94 shorter events, 10.4 us)
Async XLA Ops:
  1.6 6.2 %collective-permute-start.3 = (bf16[512,128]{1,0:T(8,128)(2,1)S(1)}, bf16[512,128]{1,0:T(8,128)(2,1)S(1)}, u32[]{:S(2)}, u32[]{:S(2)}) collective-permute-start(bf16[512,128]{1,0:T(8,128)(2,1)S(1)} %convert_element_type.73), channel_id=1, source_target_pairs={{0,4},{4,0},{8,12},{12,8},{16,20},{20,16},{24,28},{28,24},{1,5},{5... | collective-permute-start | bytes 393224 | tf_op jit(solution)/shard_map/ppermute | solution.py:142
  3.1 8.9 %collective-permute-start.2 = (bf16[512,128]{1,0:T(8,128)(2,1)S(1)}, bf16[512,128]{1,0:T(8,128)(2,1)S(1)}, u32[]{:S(2)}, u32[]{:S(2)}) collective-permute-start(bf16[512,128]{1,0:T(8,128)(2,1)S(1)} %convert_element_type.72.refs_0_), channel_id=1, source_target_pairs={{0,3},{1,0},{2,1},{3,2},{4,7},{5,4},{6,5},{7,6},{8,11},{9,8},{10,9... | collective-permute-start | bytes 393224 | tf_op jit(solution)/shard_map/ppermute | solution.py:125
  7.8 12.8 %collective-permute-start.6 = (bf16[1024,128]{1,0:T(8,128)(2,1)S(1)}, bf16[1024,128]{1,0:T(8,128)(2,1)S(1)}, u32[]{:S(2)}, u32[]{:S(2)}) collective-permute-start(bf16[1024,128]{1,0:T(8,128)(2,1)S(1)} %pad_maximum_fusion.refs_4_), channel_id=1, source_target_pairs={{0,24},{4,28},{8,16},{12,20},{16,8},{20,12},{24,0},{28,4},{1,25},{... | collective-permute-start | bytes 786440 | tf_op jit(solution)/shard_map/ppermute | solution.py:145
  10.3 12.5 %collective-permute-start.5 = (bf16[1024,128]{1,0:T(8,128)(2,1)S(1)}, bf16[1024,128]{1,0:T(8,128)(2,1)S(1)}, u32[]{:S(2)}, u32[]{:S(2)}) collective-permute-start(bf16[1024,128]{1,0:T(8,128)(2,1)S(1)} %pad_maximum_fusion.refs_4_), channel_id=1, source_target_pairs={{0,16},{4,20},{8,24},{12,28},{16,0},{20,4},{24,8},{28,12},{1,17},{... | collective-permute-start | bytes 786440 | tf_op jit(solution)/shard_map/ppermute | solution.py:145
  10.8 12.1 %collective-permute-start.4 = (bf16[1024,128]{1,0:T(8,128)(2,1)S(1)}, bf16[1024,128]{1,0:T(8,128)(2,1)S(1)}, u32[]{:S(2)}, u32[]{:S(2)}) collective-permute-start(bf16[1024,128]{1,0:T(8,128)(2,1)S(1)} %pad_maximum_fusion.refs_4_), channel_id=1, source_target_pairs={{0,8},{4,12},{8,0},{12,4},{16,24},{20,28},{24,16},{28,20},{1,9},{5... | collective-permute-start | bytes 786440 | tf_op jit(solution)/shard_map/ppermute | solution.py:145
  11.4 9.2 %collective-permute-start.1 = (bf16[512,128]{1,0:T(8,128)(2,1)S(1)}, bf16[512,128]{1,0:T(8,128)(2,1)S(1)}, u32[]{:S(2)}, u32[]{:S(2)}) collective-permute-start(bf16[512,128]{1,0:T(8,128)(2,1)S(1)} %convert_element_type.72.refs_0_), channel_id=1, source_target_pairs={{0,2},{1,3},{2,0},{3,1},{4,6},{5,7},{6,4},{7,5},{8,10},{9,11},{10,... | collective-permute-start | bytes 393224 | tf_op jit(solution)/shard_map/ppermute | solution.py:125
  12.0 8.5 %collective-permute-start = (bf16[512,128]{1,0:T(8,128)(2,1)S(1)}, bf16[512,128]{1,0:T(8,128)(2,1)S(1)}, u32[]{:S(2)}, u32[]{:S(2)}) collective-permute-start(bf16[512,128]{1,0:T(8,128)(2,1)S(1)} %convert_element_type.72.refs_0_), channel_id=1, source_target_pairs={{0,1},{1,2},{2,3},{3,0},{4,5},{5,6},{6,7},{7,4},{8,9},{9,10},{10,1... | collective-permute-start | bytes 393224 | tf_op jit(solution)/shard_map/ppermute | solution.py:125
  33.7 14.2 %collective-permute-start.7 = (bf16[512,128]{1,0:T(8,128)(2,1)}, bf16[512,128]{1,0:T(8,128)(2,1)S(1)}, u32[]{:S(2)}, u32[]{:S(2)}) collective-permute-start(bf16[512,128]{1,0:T(8,128)(2,1)} %get-tuple-element.23), channel_id=1, source_target_pairs={{0,1},{1,2},{2,3},{3,0},{4,5},{5,6},{6,7},{7,4},{8,9},{9,10},{10,1... | collective-permute-start | bytes 393224 | tf_op jit(solution)/shard_map/ppermute | solution.py:132
  35.2 12.9 %collective-permute-start.8 = (bf16[512,128]{1,0:T(8,128)(2,1)}, bf16[512,128]{1,0:T(8,128)(2,1)S(1)}, u32[]{:S(2)}, u32[]{:S(2)}) collective-permute-start(bf16[512,128]{1,0:T(8,128)(2,1)} %get-tuple-element.24), channel_id=1, source_target_pairs={{0,2},{1,3},{2,0},{3,1},{4,6},{5,7},{6,4},{7,5},{8,10},{9,11},{10,... | collective-permute-start | bytes 393224 | tf_op jit(solution)/shard_map/ppermute | solution.py:132
  40.1 12.2 %collective-permute-start.9 = (bf16[512,128]{1,0:T(8,128)(2,1)}, bf16[512,128]{1,0:T(8,128)(2,1)S(1)}, u32[]{:S(2)}, u32[]{:S(2)}) collective-permute-start(bf16[512,128]{1,0:T(8,128)(2,1)} %get-tuple-element.25), channel_id=1, source_target_pairs={{0,3},{1,0},{2,1},{3,2},{4,7},{5,4},{6,5},{7,6},{8,11},{9,8},{10,9... | collective-permute-start | bytes 393224 | tf_op jit(solution)/shard_map/ppermute | solution.py:132
  42.9 9.8 %collective-permute-start.13 = (bf16[512,128]{1,0:T(8,128)(2,1)}, bf16[512,128]{1,0:T(8,128)(2,1)S(1)}, u32[]{:S(2)}, u32[]{:S(2)}) collective-permute-start(bf16[512,128]{1,0:T(8,128)(2,1)} %get-tuple-element.27), channel_id=1, source_target_pairs={{0,4},{4,0},{8,12},{12,8},{16,20},{20,16},{24,28},{28,24},{1,5},{5... | collective-permute-start | bytes 393224 | tf_op jit(solution)/shard_map/ppermute | solution.py:169
  43.0 11.6 %collective-permute-start.14 = (bf16[512,128]{1,0:T(8,128)(2,1)}, bf16[512,128]{1,0:T(8,128)(2,1)S(1)}, u32[]{:S(2)}, u32[]{:S(2)}) collective-permute-start(bf16[512,128]{1,0:T(8,128)(2,1)} %get-tuple-element.28), channel_id=1, source_target_pairs={{0,8},{4,12},{8,0},{12,4},{16,24},{20,28},{24,16},{28,20},{1,9},{5... | collective-permute-start | bytes 393224 | tf_op jit(solution)/shard_map/ppermute | solution.py:169
  47.9 7.8 %collective-permute-start.15 = (bf16[512,128]{1,0:T(8,128)(2,1)}, bf16[512,128]{1,0:T(8,128)(2,1)S(1)}, u32[]{:S(2)}, u32[]{:S(2)}) collective-permute-start(bf16[512,128]{1,0:T(8,128)(2,1)} %get-tuple-element.29), channel_id=1, source_target_pairs={{0,12},{4,8},{8,4},{12,0},{16,28},{20,24},{24,20},{28,16},{1,13},{... | collective-permute-start | bytes 393224 | tf_op jit(solution)/shard_map/ppermute | solution.py:169
  48.1 14.3 %collective-permute-start.16 = (bf16[512,128]{1,0:T(8,128)(2,1)}, bf16[512,128]{1,0:T(8,128)(2,1)S(1)}, u32[]{:S(2)}, u32[]{:S(2)}) collective-permute-start(bf16[512,128]{1,0:T(8,128)(2,1)} %get-tuple-element.30), channel_id=1, source_target_pairs={{0,16},{4,20},{8,24},{12,28},{16,0},{20,4},{24,8},{28,12},{1,17},{... | collective-permute-start | bytes 393224 | tf_op jit(solution)/shard_map/ppermute | solution.py:169
  52.3 13.0 %collective-permute-start.17 = (bf16[512,128]{1,0:T(8,128)(2,1)}, bf16[512,128]{1,0:T(8,128)(2,1)S(1)}, u32[]{:S(2)}, u32[]{:S(2)}) collective-permute-start(bf16[512,128]{1,0:T(8,128)(2,1)} %get-tuple-element.31), channel_id=1, source_target_pairs={{0,20},{4,16},{8,28},{12,24},{16,4},{20,0},{24,12},{28,8},{1,21},{... | collective-permute-start | bytes 393224 | tf_op jit(solution)/shard_map/ppermute | solution.py:169
  52.7 12.6 %collective-permute-start.18 = (bf16[512,128]{1,0:T(8,128)(2,1)}, bf16[512,128]{1,0:T(8,128)(2,1)S(1)}, u32[]{:S(2)}, u32[]{:S(2)}) collective-permute-start(bf16[512,128]{1,0:T(8,128)(2,1)} %get-tuple-element.32), channel_id=1, source_target_pairs={{0,24},{4,28},{8,16},{12,20},{16,8},{20,12},{24,0},{28,4},{1,25},{... | collective-permute-start | bytes 393224 | tf_op jit(solution)/shard_map/ppermute | solution.py:169
  54.6 10.7 %collective-permute-start.19 = (bf16[512,128]{1,0:T(8,128)(2,1)}, bf16[512,128]{1,0:T(8,128)(2,1)S(1)}, u32[]{:S(2)}, u32[]{:S(2)}) collective-permute-start(bf16[512,128]{1,0:T(8,128)(2,1)} %get-tuple-element.33), channel_id=1, source_target_pairs={{0,28},{4,24},{8,20},{12,16},{16,12},{20,8},{24,4},{28,0},{1,29},{... | collective-permute-start | bytes 393224 | tf_op jit(solution)/shard_map/ppermute | solution.py:169
  55.7 13.2 %collective-permute-start.12 = (bf16[512,128]{1,0:T(8,128)(2,1)S(1)}, bf16[512,128]{1,0:T(8,128)(2,1)S(1)}, u32[]{:S(2)}, u32[]{:S(2)}) collective-permute-start(bf16[512,128]{1,0:T(8,128)(2,1)S(1)} %fusion.6.refs_0_), channel_id=1, source_target_pairs={{0,3},{1,0},{2,1},{3,2},{4,7},{5,4},{6,5},{7,6},{8,11},{9,8},{10,9... | collective-permute-start | bytes 393224 | tf_op jit(solution)/shard_map/ppermute | solution.py:125
  62.3 10.6 %collective-permute-start.11 = (bf16[512,128]{1,0:T(8,128)(2,1)S(1)}, bf16[512,128]{1,0:T(8,128)(2,1)S(1)}, u32[]{:S(2)}, u32[]{:S(2)}) collective-permute-start(bf16[512,128]{1,0:T(8,128)(2,1)S(1)} %fusion.6.refs_0_), channel_id=1, source_target_pairs={{0,2},{1,3},{2,0},{3,1},{4,6},{5,7},{6,4},{7,5},{8,10},{9,11},{10,... | collective-permute-start | bytes 393224 | tf_op jit(solution)/shard_map/ppermute | solution.py:125
  65.3 9.0 %collective-permute-start.10 = (bf16[512,128]{1,0:T(8,128)(2,1)S(1)}, bf16[512,128]{1,0:T(8,128)(2,1)S(1)}, u32[]{:S(2)}, u32[]{:S(2)}) collective-permute-start(bf16[512,128]{1,0:T(8,128)(2,1)S(1)} %fusion.6.refs_0_), channel_id=1, source_target_pairs={{0,1},{1,2},{2,3},{3,0},{4,5},{5,6},{6,7},{7,4},{8,9},{9,10},{10,1... | collective-permute-start | bytes 393224 | tf_op jit(solution)/shard_map/ppermute | solution.py:125
  66.4 7.9 %collective-permute-start.26 = (bf16[512,128]{1,0:T(8,128)(2,1)S(1)}, bf16[512,128]{1,0:T(8,128)(2,1)S(1)}, u32[]{:S(2)}, u32[]{:S(2)}) collective-permute-start(bf16[512,128]{1,0:T(8,128)(2,1)S(1)} %get-tuple-element.42.refs_4_), channel_id=1, source_target_pairs={{0,28},{4,24},{8,20},{12,16},{16,12},{20,8},{24,4},{28,0},{1,29},{... | collective-permute-start | bytes 393224 | tf_op jit(solution)/shard_map/ppermute | solution.py:162
  67.3 8.8 %collective-permute-start.25 = (bf16[512,128]{1,0:T(8,128)(2,1)S(1)}, bf16[512,128]{1,0:T(8,128)(2,1)S(1)}, u32[]{:S(2)}, u32[]{:S(2)}) collective-permute-start(bf16[512,128]{1,0:T(8,128)(2,1)S(1)} %get-tuple-element.42.refs_4_), channel_id=1, source_target_pairs={{0,24},{4,28},{8,16},{12,20},{16,8},{20,12},{24,0},{28,4},{1,25},{... | collective-permute-start | bytes 393224 | tf_op jit(solution)/shard_map/ppermute | solution.py:162
  69.0 9.8 %collective-permute-start.24 = (bf16[512,128]{1,0:T(8,128)(2,1)S(1)}, bf16[512,128]{1,0:T(8,128)(2,1)S(1)}, u32[]{:S(2)}, u32[]{:S(2)}) collective-permute-start(bf16[512,128]{1,0:T(8,128)(2,1)S(1)} %get-tuple-element.42.refs_4_), channel_id=1, source_target_pairs={{0,20},{4,16},{8,28},{12,24},{16,4},{20,0},{24,12},{28,8},{1,21},{... | collective-permute-start | bytes 393224 | tf_op jit(solution)/shard_map/ppermute | solution.py:162
  73.0 8.6 %collective-permute-start.23 = (bf16[512,128]{1,0:T(8,128)(2,1)S(1)}, bf16[512,128]{1,0:T(8,128)(2,1)S(1)}, u32[]{:S(2)}, u32[]{:S(2)}) collective-permute-start(bf16[512,128]{1,0:T(8,128)(2,1)S(1)} %get-tuple-element.42.refs_4_), channel_id=1, source_target_pairs={{0,16},{4,20},{8,24},{12,28},{16,0},{20,4},{24,8},{28,12},{1,17},{... | collective-permute-start | bytes 393224 | tf_op jit(solution)/shard_map/ppermute | solution.py:162
  74.3 7.3 %collective-permute-start.22 = (bf16[512,128]{1,0:T(8,128)(2,1)S(1)}, bf16[512,128]{1,0:T(8,128)(2,1)S(1)}, u32[]{:S(2)}, u32[]{:S(2)}) collective-permute-start(bf16[512,128]{1,0:T(8,128)(2,1)S(1)} %get-tuple-element.42.refs_4_), channel_id=1, source_target_pairs={{0,12},{4,8},{8,4},{12,0},{16,28},{20,24},{24,20},{28,16},{1,13},{... | collective-permute-start | bytes 393224 | tf_op jit(solution)/shard_map/ppermute | solution.py:162
  74.3 7.3 %collective-permute-start.21 = (bf16[512,128]{1,0:T(8,128)(2,1)S(1)}, bf16[512,128]{1,0:T(8,128)(2,1)S(1)}, u32[]{:S(2)}, u32[]{:S(2)}) collective-permute-start(bf16[512,128]{1,0:T(8,128)(2,1)S(1)} %get-tuple-element.42.refs_4_), channel_id=1, source_target_pairs={{0,8},{4,12},{8,0},{12,4},{16,24},{20,28},{24,16},{28,20},{1,9},{5... | collective-permute-start | bytes 393224 | tf_op jit(solution)/shard_map/ppermute | solution.py:162
  92.5 15.0 %collective-permute-start.30 = (bf16[1024,128]{1,0:T(8,128)(2,1)}, bf16[1024,128]{1,0:T(8,128)(2,1)S(1)}, u32[]{:S(2)}, u32[]{:S(2)}) collective-permute-start(bf16[1024,128]{1,0:T(8,128)(2,1)} %get-tuple-element.39), channel_id=1, source_target_pairs={{0,8},{4,12},{8,0},{12,4},{16,24},{20,28},{24,16},{28,20},{1,9},{5... | collective-permute-start | bytes 786440 | tf_op jit(solution)/shard_map/ppermute | solution.py:152
  102.9 9.4 %collective-permute-start.31 = (bf16[1024,128]{1,0:T(8,128)(2,1)}, bf16[1024,128]{1,0:T(8,128)(2,1)S(1)}, u32[]{:S(2)}, u32[]{:S(2)}) collective-permute-start(bf16[1024,128]{1,0:T(8,128)(2,1)} %get-tuple-element.40), channel_id=1, source_target_pairs={{0,16},{4,20},{8,24},{12,28},{16,0},{20,4},{24,8},{28,12},{1,17},{... | collective-permute-start | bytes 786440 | tf_op jit(solution)/shard_map/ppermute | solution.py:152
  102.9 9.4 %collective-permute-start.32 = (bf16[1024,128]{1,0:T(8,128)(2,1)}, bf16[1024,128]{1,0:T(8,128)(2,1)S(1)}, u32[]{:S(2)}, u32[]{:S(2)}) collective-permute-start(bf16[1024,128]{1,0:T(8,128)(2,1)} %get-tuple-element.41), channel_id=1, source_target_pairs={{0,24},{4,28},{8,16},{12,20},{16,8},{20,12},{24,0},{28,4},{1,25},{... | collective-permute-start | bytes 786440 | tf_op jit(solution)/shard_map/ppermute | solution.py:152
  104.4 9.1 %collective-permute-start.27 = (bf16[512,128]{1,0:T(8,128)(2,1)}, bf16[512,128]{1,0:T(8,128)(2,1)S(1)}, u32[]{:S(2)}, u32[]{:S(2)}) collective-permute-start(bf16[512,128]{1,0:T(8,128)(2,1)} %get-tuple-element.35), channel_id=1, source_target_pairs={{0,1},{1,2},{2,3},{3,0},{4,5},{5,6},{6,7},{7,4},{8,9},{9,10},{10,1... | collective-permute-start | bytes 393224 | tf_op jit(solution)/shard_map/ppermute | solution.py:132
  104.4 10.5 %collective-permute-start.28 = (bf16[512,128]{1,0:T(8,128)(2,1)}, bf16[512,128]{1,0:T(8,128)(2,1)S(1)}, u32[]{:S(2)}, u32[]{:S(2)}) collective-permute-start(bf16[512,128]{1,0:T(8,128)(2,1)} %get-tuple-element.36), channel_id=1, source_target_pairs={{0,2},{1,3},{2,0},{3,1},{4,6},{5,7},{6,4},{7,5},{8,10},{9,11},{10,... | collective-permute-start | bytes 393224 | tf_op jit(solution)/shard_map/ppermute | solution.py:132
  107.5 7.4 %collective-permute-start.29 = (bf16[512,128]{1,0:T(8,128)(2,1)}, bf16[512,128]{1,0:T(8,128)(2,1)S(1)}, u32[]{:S(2)}, u32[]{:S(2)}) collective-permute-start(bf16[512,128]{1,0:T(8,128)(2,1)} %get-tuple-element.37), channel_id=1, source_target_pairs={{0,3},{1,0},{2,1},{3,2},{4,7},{5,4},{6,5},{7,6},{8,11},{9,8},{10,9... | collective-permute-start | bytes 393224 | tf_op jit(solution)/shard_map/ppermute | solution.py:132
  (25 other events, 257.3 us)

commit v10 on v9

--- a/solution.py
+++ b/solution.py
@@ -180,6 +180,20 @@
     return ((me - run) % n) * per_run + index % per_run
 
 
+def plan(index, me, n, per_run):
+    if paired(n):
+        return pair_index(index, me, per_run), (
+            (gather_paired, gather_xor),
+            (scatter_xor, scatter_paired),
+            (n, n // 2),
+        )
+    return rotate_index(index, me, n, per_run), (
+        (gather_rotated, gather_rotated),
+        (scatter_rotated, scatter_rotated),
+        (n, n),
+    )
+
+
 def body(emb_in, ctx_in, pos_weight, neg_weight, tile_row, tile_col, tile_count):
     n_row = lax.axis_size("row")
     n_col = lax.axis_size("col")
@@ -189,29 +203,21 @@
     neg = neg_weight[0, 0]
     tile = pos.shape[-1]
     per_run = emb_in.shape[0] // tile
-    rows = rotate_index(tile_row[0, 0], me_col, n_col, per_run)
-    if paired(n_row):
-        cols = pair_index(tile_col[0, 0], me_row, per_run)
-        gathers = (gather_paired, gather_xor)
-        scatters = (scatter_xor, scatter_paired)
-        splits = (n_row, n_row // 2)
-    else:
-        cols = rotate_index(tile_col[0, 0], me_row, n_row, per_run)
-        gathers = (gather_rotated, gather_rotated)
-        scatters = (scatter_rotated, scatter_rotated)
-        splits = (n_row, n_row)
+    rows, emb_plan = plan(tile_row[0, 0], me_col, n_col, per_run)
+    cols, ctx_plan = plan(tile_col[0, 0], me_row, n_row, per_run)
     count = tile_count[0, 0]
     emb = emb_in
     ctx = ctx_in
     for iteration in range(ITERS):
-        emb_low = gather_rotated(emb.astype(jnp.bfloat16), "col", n_col)
         first, last = iteration == 0, iteration == ITERS - 1
-        ctx_low = gathers[0 if first else 1](ctx.astype(jnp.bfloat16), "row", n_row)
+        emb_low = emb_plan[0][0 if first else 1](emb.astype(jnp.bfloat16), "col", n_col)
+        ctx_low = ctx_plan[0][0 if first else 1](ctx.astype(jnp.bfloat16), "row", n_row)
         grad_emb, grad_ctx = tile_sweep(
-            pos, neg, rows, cols, count, emb_low, ctx_low, n_col, splits[1 if last else 0]
+            pos, neg, rows, cols, count, emb_low, ctx_low,
+            emb_plan[2][1 if last else 0], ctx_plan[2][1 if last else 0],
         )
-        emb = emb + 0.05 * scatter_rotated(grad_emb, "col", n_col)
-        ctx = ctx + 0.05 * scatters[1 if last else 0](grad_ctx, "row", n_row)
+        emb = emb + 0.05 * emb_plan[1][1 if last else 0](grad_emb, "col", n_col)
+        ctx = ctx + 0.05 * ctx_plan[1][1 if last else 0](grad_ctx, "row", n_row)
     return (emb, ctx)
 
 

time: 119 us -> 124 us (1.042); the launches traced: 117 us -> 125 us
  waiting for transfers between devices: 27.6 us -> 39.9 us
  starting transfers between devices: 57.8 us -> 47.1 us
  Pallas kernels: 20.2 us -> 26.6 us
    ppermute x12 -> x0, starting transfers between devices: 22.6 us -> none  [the longest x6 13.1 us: scatter_rotated(): lax.ppermute(chunks[(n - s) % n], axis, [(i, (i + s) % n) for i in range(...]
    ppermute x12 -> x0, waiting for transfers between devices: 9.51 us -> none  [the longest x6 8.04 us: gather_rotated(): pieces.append(lax.ppermute(x, axis, [(i, (i + s) % n) for i in range(n)]))]
    ppermute x3 -> x4, waiting for transfers between devices: 2.33 us -> 9.95 us  [gather_paired(): blocks.append(lax.ppermute(pair, axis, [(i, i ^ 2 * b) for i in range(n)]))]
    pallas_call x2, Pallas kernels: 20.2 us -> 26.6 us  [tile_sweep(): pl.pallas_call(functools.partial(sweep_kernel, tile, group, len(emb_piece...]
    ppermute x3 -> x4, waiting for transfers between devices: 4.02 us -> 10 us  [scatter_paired(): got = lax.ppermute(blocks[b], axis, [(i, i ^ 2 * b) for i in range(n)])]
    ppermute x7 -> x10, starting transfers between devices: 7.41 us -> 13.3 us  [gather_xor(): pieces.append(lax.ppermute(x, axis, [(i, i ^ p) for i in range(n)]))]
    ppermute x7 -> x10, waiting for transfers between devices: 5.8 us -> 11.1 us  [scatter_xor(): got = lax.ppermute(chunks[p], axis, [(i, i ^ p) for i in range(n)])]
    ppermute x3 -> x4, starting transfers between devices: 3.55 us -> 6.37 us  [gather_paired(): blocks.append(lax.ppermute(pair, axis, [(i, i ^ 2 * b) for i in range(n)]))]
  transfers between devices with their start and end apart: 34 -> 32, of which waited for: 11 -> 16; matrix products, arithmetic and copies ran while one was open for 6% -> 6% of each run, Pallas kernels for 0% -> 0%
where the time goes in v10:
time: 124 us; the launch traced here: 125 us
  starting transfers between devices  47.1 us (38%)
  waiting for transfers between devices  39.9 us (32%)
  Pallas kernels  26.6 us (21%)
  other arithmetic  8.99 us (7%)
  between operations  1.53 us (1%)
  local copies, waits for them, and re-layouts  1.39 us (1%)
    pallas_call x2, Pallas kernels, tile_sweep(): pl.pallas_call(functools.partial(sweep_kernel, tile, group, len(emb_piece...  26.6 us
    ppermute x10, starting transfers between devices, gather_xor(): pieces.append(lax.ppermute(x, axis, [(i, i ^ p) for i in range(n)]))  13.3 us
    ppermute x10, starting transfers between devices, scatter_xor(): got = lax.ppermute(chunks[p], axis, [(i, i ^ p) for i in range(n)])  13.1 us
    ppermute x4, starting transfers between devices, scatter_paired(): got = lax.ppermute(blocks[b], axis, [(i, i ^ 2 * b) for i in range(n)])  11.1 us
    ppermute x10, waiting for transfers between devices, scatter_xor(): got = lax.ppermute(chunks[p], axis, [(i, i ^ p) for i in range(n)])  11.1 us
    ppermute x4, waiting for transfers between devices, scatter_paired(): got = lax.ppermute(blocks[b], axis, [(i, i ^ 2 * b) for i in range(n)])  10 us
    ppermute x4, waiting for transfers between devices, gather_paired(): blocks.append(lax.ppermute(pair, axis, [(i, i ^ 2 * b) for i in range(n)]))  9.95 us
    ppermute x4, starting transfers between devices, gather_paired(): blocks.append(lax.ppermute(pair, axis, [(i, i ^ 2 * b) for i in range(n)]))  6.37 us
  transfers between devices with their start and end apart: 32, of which 16 were waited for; matrix products, arithmetic and copies ran while one was open for 6% of the time, Pallas kernels for 0%

profile of v10, /device:TPU:0, one launch (start us, length us, event | category | flops | bytes accessed | tf_op | source)
XLA Modules:
  0.0 125.5 jit_solution(7566002154910909764)
XLA Ops:
  3.1 2.7 %collective-permute-start = (bf16[512,128]{1,0:T(8,128)(2,1)S(1)}, bf16[512,128]{1,0:T(8,128)(2,1)S(1)}, u32[]{:S(2)}, u32[]{:S(2)}) collective-permute-start(bf16[512,128]{1,0:T(8,128)(2,1)S(1)} %convert_element_type.66), channel_id=1, source_target_pairs={{0,1},{1,0},{2,3},{3,2},{4,5},{5,4},{6,7},{7,6},{8,9},{9,8},{10,11... | collective-permute-start | bytes 393224 | tf_op jit(solution)/shard_map/ppermute | solution.py:142
  5.8 2.5 %collective-permute-start.5 = (bf16[1024,128]{1,0:T(8,128)(2,1)S(1)}, bf16[1024,128]{1,0:T(8,128)(2,1)S(1)}, u32[]{:S(2)}, u32[]{:S(2)}) collective-permute-start(bf16[1024,128]{1,0:T(8,128)(2,1)S(1)} %pad_maximum_fusion.1.refs_2_), channel_id=1, source_target_pairs={{0,24},{4,28},{8,16},{12,20},{16,8},{20,12},{24,0},{28,4},{1,25},{... | collective-permute-start | bytes 786440 | tf_op jit(solution)/shard_map/ppermute | solution.py:145
  9.9 2.8 %collective-permute-start.1 = (bf16[1024,128]{1,0:T(8,128)(2,1)S(1)}, bf16[1024,128]{1,0:T(8,128)(2,1)S(1)}, u32[]{:S(2)}, u32[]{:S(2)}) collective-permute-start(bf16[1024,128]{1,0:T(8,128)(2,1)S(1)} %pad_maximum_fusion.refs_0_), channel_id=1, source_target_pairs={{0,2},{1,3},{2,0},{3,1},{4,6},{5,7},{6,4},{7,5},{8,10},{9,11},{10,... | collective-permute-start | bytes 786440 | tf_op jit(solution)/shard_map/ppermute | solution.py:145
  13.4 1.3 %fusion.4 = (s32[64]{0:T(128)}, s32[64]{0:T(128)}) fusion(s32[1,1,64]{2,1,0:T(1,128)} %param.11, s32[]{:T(128)S(6)} %axis_index.22, s32[1,1,64]{2,1,0:T(1,128)} %param.12, s32[]{:T(128)S(6)} %axis_index.25), kind=kLoop, calls=%fused_computation.22 | loop fusion | flops 2816 | bytes 1032 | tf_op jit(solution)/shard_map/add | solution.py:175
  14.7 1.2 collective-permute-done.5.refs_5_
  15.9 4.9 %collective-permute-done.4.refs_4_ = bf16[1024,128]{1,0:T(8,128)(2,1)S(1)} collective-permute-done((bf16[1024,128]{1,0:T(8,128)(2,1)S(1)}, bf16[1024,128]{1,0:T(8,128)(2,1)S(1)}, u32[]{:S(2)}, u32[]{:S(2)}) %collective-permute-start.4) | collective-permute-done | bytes 262176 | tf_op jit(solution)/shard_map/ppermute | solution.py:145
  20.9 3.8 %collective-permute-done.1.refs_1_ = bf16[1024,128]{1,0:T(8,128)(2,1)S(1)} collective-permute-done((bf16[1024,128]{1,0:T(8,128)(2,1)S(1)}, bf16[1024,128]{1,0:T(8,128)(2,1)S(1)}, u32[]{:S(2)}, u32[]{:S(2)}) %collective-permute-start.1) | collective-permute-done | bytes 262176 | tf_op jit(solution)/shard_map/ppermute | solution.py:145
  25.3 13.3 %shard_map.86 = (bf16[512,128]{1,0:T(8,128)(2,1)}, bf16[512,128]{1,0:T(8,128)(2,1)}, bf16[512,128]{1,0:T(8,128)(2,1)}, bf16[512,128]{1,0:T(8,128)(2,1)}, bf16[51...) custom-call(s32[64]{0:T(128)} %get-tuple-element.40.rows_ref, ...), custom_call_target="tpu_custom_call" | custom-call | flops 3221225472 | bytes 21495808 | tf_op jit(solution)/shard_map/pallas_call | solution.py:107
  38.7 6.2 %collective-permute-start.6 = (bf16[512,128]{1,0:T(8,128)(2,1)}, bf16[512,128]{1,0:T(8,128)(2,1)S(1)}, u32[]{:S(2)}, u32[]{:S(2)}) collective-permute-start(bf16[512,128]{1,0:T(8,128)(2,1)} %get-tuple-element.21), channel_id=1, source_target_pairs={{0,1},{1,0},{2,3},{3,2},{4,5},{5,4},{6,7},{7,6},{8,9},{9,8},{10,11... | collective-permute-start | bytes 393224 | tf_op jit(solution)/shard_map/ppermute | solution.py:169
  44.9 1.7 %collective-permute-start.7 = (bf16[512,128]{1,0:T(8,128)(2,1)}, bf16[512,128]{1,0:T(8,128)(2,1)S(1)}, u32[]{:S(2)}, u32[]{:S(2)}) collective-permute-start(bf16[512,128]{1,0:T(8,128)(2,1)} %get-tuple-element.22), channel_id=1, source_target_pairs={{0,2},{1,3},{2,0},{3,1},{4,6},{5,7},{6,4},{7,5},{8,10},{9,11},{10,... | collective-permute-start | bytes 393224 | tf_op jit(solution)/shard_map/ppermute | solution.py:169
  47.4 2.4 %collective-permute-done.6 = bf16[512,128]{1,0:T(8,128)(2,1)S(1)} collective-permute-done((bf16[512,128]{1,0:T(8,128)(2,1)}, bf16[512,128]{1,0:T(8,128)(2,1)S(1)}, u32[]{:S(2)}, u32[]{:S(2)}) %collective-permute-start.6) | collective-permute-done | bytes 131104 | tf_op jit(solution)/shard_map/ppermute | solution.py:169
  49.8 4.4 %collective-permute-done.7 = bf16[512,128]{1,0:T(8,128)(2,1)S(1)} collective-permute-done((bf16[512,128]{1,0:T(8,128)(2,1)}, bf16[512,128]{1,0:T(8,128)(2,1)S(1)}, u32[]{:S(2)}, u32[]{:S(2)}) %collective-permute-start.7) | collective-permute-done | bytes 131104 | tf_op jit(solution)/shard_map/ppermute | solution.py:169
  54.5 2.8 %collective-permute-start.17 = (bf16[512,128]{1,0:T(8,128)(2,1)}, bf16[512,128]{1,0:T(8,128)(2,1)S(1)}, u32[]{:S(2)}, u32[]{:S(2)}) collective-permute-start(bf16[512,128]{1,0:T(8,128)(2,1)} %get-tuple-element.30), channel_id=1, source_target_pairs={{0,24},{4,28},{8,16},{12,20},{16,8},{20,12},{24,0},{28,4},{1,25},{... | collective-permute-start | bytes 393224 | tf_op jit(solution)/shard_map/ppermute | solution.py:169
  57.3 1.3 %collective-permute-start.18 = (bf16[512,128]{1,0:T(8,128)(2,1)}, bf16[512,128]{1,0:T(8,128)(2,1)S(1)}, u32[]{:S(2)}, u32[]{:S(2)}) collective-permute-start(bf16[512,128]{1,0:T(8,128)(2,1)} %get-tuple-element.31), channel_id=1, source_target_pairs={{0,28},{4,24},{8,20},{12,16},{16,12},{20,8},{24,4},{28,0},{1,29},{... | collective-permute-start | bytes 393224 | tf_op jit(solution)/shard_map/ppermute | solution.py:169
  59.6 2.3 %collective-permute-start.11 = (bf16[512,128]{1,0:T(8,128)(2,1)S(1)}, bf16[512,128]{1,0:T(8,128)(2,1)S(1)}, u32[]{:S(2)}, u32[]{:S(2)}) collective-permute-start(bf16[512,128]{1,0:T(8,128)(2,1)S(1)} %fusion.6.refs_0_), channel_id=1, source_target_pairs={{0,3},{1,2},{2,1},{3,0},{4,7},{5,6},{6,5},{7,4},{8,11},{9,10},{10,... | collective-permute-start | bytes 393224 | tf_op jit(solution)/shard_map/ppermute | solution.py:162
  61.9 4.3 %collective-permute-done.15 = bf16[512,128]{1,0:T(8,128)(2,1)S(1)} collective-permute-done((bf16[512,128]{1,0:T(8,128)(2,1)}, bf16[512,128]{1,0:T(8,128)(2,1)S(1)}, u32[]{:S(2)}, u32[]{:S(2)}) %collective-permute-start.15) | collective-permute-done | bytes 131104 | tf_op jit(solution)/shard_map/ppermute | solution.py:169
  66.6 1.1 fusion.7
  67.7 2.6 %collective-permute-start.25 = (bf16[512,128]{1,0:T(8,128)(2,1)S(1)}, bf16[512,128]{1,0:T(8,128)(2,1)S(1)}, u32[]{:S(2)}, u32[]{:S(2)}) collective-permute-start(bf16[512,128]{1,0:T(8,128)(2,1)S(1)} %get-tuple-element.38.refs_4_), channel_id=1, source_target_pairs={{0,28},{4,24},{8,20},{12,16},{16,12},{20,8},{24,4},{28,0},{1,29},{... | collective-permute-start | bytes 393224 | tf_op jit(solution)/shard_map/ppermute | solution.py:162
  70.3 1.5 %collective-permute-start.24 = (bf16[512,128]{1,0:T(8,128)(2,1)S(1)}, bf16[512,128]{1,0:T(8,128)(2,1)S(1)}, u32[]{:S(2)}, u32[]{:S(2)}) collective-permute-start(bf16[512,128]{1,0:T(8,128)(2,1)S(1)} %get-tuple-element.38.refs_4_), channel_id=1, source_target_pairs={{0,24},{4,28},{8,16},{12,20},{16,8},{20,12},{24,0},{28,4},{1,25},{... | collective-permute-start | bytes 393224 | tf_op jit(solution)/shard_map/ppermute | solution.py:162
  71.8 2.1 %collective-permute-start.23 = (bf16[512,128]{1,0:T(8,128)(2,1)S(1)}, bf16[512,128]{1,0:T(8,128)(2,1)S(1)}, u32[]{:S(2)}, u32[]{:S(2)}) collective-permute-start(bf16[512,128]{1,0:T(8,128)(2,1)S(1)} %get-tuple-element.38.refs_4_), channel_id=1, source_target_pairs={{0,20},{4,16},{8,28},{12,24},{16,4},{20,0},{24,12},{28,8},{1,21},{... | collective-permute-start | bytes 393224 | tf_op jit(solution)/shard_map/ppermute | solution.py:162
  74.8 2.2 %collective-permute-start.21 = (bf16[512,128]{1,0:T(8,128)(2,1)S(1)}, bf16[512,128]{1,0:T(8,128)(2,1)S(1)}, u32[]{:S(2)}, u32[]{:S(2)}) collective-permute-start(bf16[512,128]{1,0:T(8,128)(2,1)S(1)} %get-tuple-element.38.refs_4_), channel_id=1, source_target_pairs={{0,12},{4,8},{8,4},{12,0},{16,28},{20,24},{24,20},{28,16},{1,13},{... | collective-permute-start | bytes 393224 | tf_op jit(solution)/shard_map/ppermute | solution.py:162
  77.0 2.0 %collective-permute-start.20 = (bf16[512,128]{1,0:T(8,128)(2,1)S(1)}, bf16[512,128]{1,0:T(8,128)(2,1)S(1)}, u32[]{:S(2)}, u32[]{:S(2)}) collective-permute-start(bf16[512,128]{1,0:T(8,128)(2,1)S(1)} %get-tuple-element.38.refs_4_), channel_id=1, source_target_pairs={{0,8},{4,12},{8,0},{12,4},{16,24},{20,28},{24,16},{28,20},{1,9},{5... | collective-permute-start | bytes 393224 | tf_op jit(solution)/shard_map/ppermute | solution.py:162
  79.0 1.3 %collective-permute-done.23.refs_9_ = bf16[512,128]{1,0:T(8,128)(2,1)S(1)} collective-permute-done((bf16[512,128]{1,0:T(8,128)(2,1)S(1)}, bf16[512,128]{1,0:T(8,128)(2,1)S(1)}, u32[]{:S(2)}, u32[]{:S(2)}) %collective-permute-start.23) | collective-permute-done | bytes 131104 | tf_op jit(solution)/shard_map/ppermute | solution.py:162
  80.3 2.9 %collective-permute-done.22.refs_8_ = bf16[512,128]{1,0:T(8,128)(2,1)S(1)} collective-permute-done((bf16[512,128]{1,0:T(8,128)(2,1)S(1)}, bf16[512,128]{1,0:T(8,128)(2,1)S(1)}, u32[]{:S(2)}, u32[]{:S(2)}) %collective-permute-start.22) | collective-permute-done | bytes 131104 | tf_op jit(solution)/shard_map/ppermute | solution.py:162
  84.7 13.3 %shard_map.87 = (bf16[1024,128]{1,0:T(8,128)(2,1)}, bf16[1024,128]{1,0:T(8,128)(2,1)}, bf16[1024,128]{1,0:T(8,128)(2,1)}, bf16[1024,128]{1,0:T(8,128)(2,1)}, bf1...) custom-call(s32[64]{0:T(128)} %get-tuple-element.40.rows_ref, s32[64]{0:T(128)} %get-tuple-element.41.cols_ref, ...), custom_call_target="tpu_custom_call" | custom-call | flops 3221225472 | bytes 21495808 | tf_op jit(solution)/shard_map/pallas_call | solution.py:107
  98.0 6.6 %collective-permute-start.26 = (bf16[1024,128]{1,0:T(8,128)(2,1)}, bf16[1024,128]{1,0:T(8,128)(2,1)S(1)}, u32[]{:S(2)}, u32[]{:S(2)}) collective-permute-start(bf16[1024,128]{1,0:T(8,128)(2,1)} %get-tuple-element.33), channel_id=1, source_target_pairs={{0,2},{1,3},{2,0},{3,1},{4,6},{5,7},{6,4},{7,5},{8,10},{9,11},{10,... | collective-permute-start | bytes 786440 | tf_op jit(solution)/shard_map/ppermute | solution.py:152
  104.6 3.0 %collective-permute-start.28 = (bf16[1024,128]{1,0:T(8,128)(2,1)}, bf16[1024,128]{1,0:T(8,128)(2,1)S(1)}, u32[]{:S(2)}, u32[]{:S(2)}) collective-permute-start(bf16[1024,128]{1,0:T(8,128)(2,1)} %get-tuple-element.35), channel_id=1, source_target_pairs={{0,8},{4,12},{8,0},{12,4},{16,24},{20,28},{24,16},{28,20},{1,9},{5... | collective-permute-start | bytes 786440 | tf_op jit(solution)/shard_map/ppermute | solution.py:152
  107.6 1.5 %collective-permute-start.30 = (bf16[1024,128]{1,0:T(8,128)(2,1)}, bf16[1024,128]{1,0:T(8,128)(2,1)S(1)}, u32[]{:S(2)}, u32[]{:S(2)}) collective-permute-start(bf16[1024,128]{1,0:T(8,128)(2,1)} %get-tuple-element.37), channel_id=1, source_target_pairs={{0,24},{4,28},{8,16},{12,20},{16,8},{20,12},{24,0},{28,4},{1,25},{... | collective-permute-start | bytes 786440 | tf_op jit(solution)/shard_map/ppermute | solution.py:152
  109.1 5.5 %collective-permute-done.26 = bf16[1024,128]{1,0:T(8,128)(2,1)S(1)} collective-permute-done((bf16[1024,128]{1,0:T(8,128)(2,1)}, bf16[1024,128]{1,0:T(8,128)(2,1)S(1)}, u32[]{:S(2)}, u32[]{:S(2)}) %collective-permute-start.26) | collective-permute-done | bytes 262176 | tf_op jit(solution)/shard_map/ppermute | solution.py:152
  115.8 4.5 %collective-permute-done.29 = bf16[1024,128]{1,0:T(8,128)(2,1)S(1)} collective-permute-done((bf16[1024,128]{1,0:T(8,128)(2,1)}, bf16[1024,128]{1,0:T(8,128)(2,1)S(1)}, u32[]{:S(2)}, u32[]{:S(2)}) %collective-permute-start.29) | collective-permute-done | bytes 262176 | tf_op jit(solution)/shard_map/ppermute | solution.py:152
  120.2 1.1 convert_add_fusion
  121.4 2.5 %collective-permute-done.27 = f32[512,128]{1,0:T(8,128)S(1)} collective-permute-done((f32[512,128]{1,0:T(8,128)S(1)}, f32[512,128]{1,0:T(8,128)S(1)}, u32[]{:S(2)}, u32[]{:S(2)}) %collective-permute-start.27) | collective-permute-done | bytes 262176 | tf_op jit(solution)/shard_map/ppermute | solution.py:155
  (89 shorter events, 12.7 us)
Async XLA Ops:
  1.6 4.1 %collective-permute-start.2 = (bf16[512,128]{1,0:T(8,128)(2,1)S(1)}, bf16[512,128]{1,0:T(8,128)(2,1)S(1)}, u32[]{:S(2)}, u32[]{:S(2)}) collective-permute-start(bf16[512,128]{1,0:T(8,128)(2,1)S(1)} %convert_element_type.67), channel_id=1, source_target_pairs={{0,4},{4,0},{8,12},{12,8},{16,20},{20,16},{24,28},{28,24},{1,5},{5... | collective-permute-start | bytes 393224 | tf_op jit(solution)/shard_map/ppermute | solution.py:142
  3.1 6.8 %collective-permute-start = (bf16[512,128]{1,0:T(8,128)(2,1)S(1)}, bf16[512,128]{1,0:T(8,128)(2,1)S(1)}, u32[]{:S(2)}, u32[]{:S(2)}) collective-permute-start(bf16[512,128]{1,0:T(8,128)(2,1)S(1)} %convert_element_type.66), channel_id=1, source_target_pairs={{0,1},{1,0},{2,3},{3,2},{4,5},{5,4},{6,7},{7,6},{8,9},{9,8},{10,11... | collective-permute-start | bytes 393224 | tf_op jit(solution)/shard_map/ppermute | solution.py:142
  5.8 10.1 %collective-permute-start.5 = (bf16[1024,128]{1,0:T(8,128)(2,1)S(1)}, bf16[1024,128]{1,0:T(8,128)(2,1)S(1)}, u32[]{:S(2)}, u32[]{:S(2)}) collective-permute-start(bf16[1024,128]{1,0:T(8,128)(2,1)S(1)} %pad_maximum_fusion.1.refs_2_), channel_id=1, source_target_pairs={{0,24},{4,28},{8,16},{12,20},{16,8},{20,12},{24,0},{28,4},{1,25},{... | collective-permute-start | bytes 786440 | tf_op jit(solution)/shard_map/ppermute | solution.py:145
  8.3 12.5 %collective-permute-start.4 = (bf16[1024,128]{1,0:T(8,128)(2,1)S(1)}, bf16[1024,128]{1,0:T(8,128)(2,1)S(1)}, u32[]{:S(2)}, u32[]{:S(2)}) collective-permute-start(bf16[1024,128]{1,0:T(8,128)(2,1)S(1)} %pad_maximum_fusion.1.refs_2_), channel_id=1, source_target_pairs={{0,16},{4,20},{8,24},{12,28},{16,0},{20,4},{24,8},{28,12},{1,17},{... | collective-permute-start | bytes 786440 | tf_op jit(solution)/shard_map/ppermute | solution.py:145
  8.8 12.1 %collective-permute-start.3 = (bf16[1024,128]{1,0:T(8,128)(2,1)S(1)}, bf16[1024,128]{1,0:T(8,128)(2,1)S(1)}, u32[]{:S(2)}, u32[]{:S(2)}) collective-permute-start(bf16[1024,128]{1,0:T(8,128)(2,1)S(1)} %pad_maximum_fusion.1.refs_2_), channel_id=1, source_target_pairs={{0,8},{4,12},{8,0},{12,4},{16,24},{20,28},{24,16},{28,20},{1,9},{5... | collective-permute-start | bytes 786440 | tf_op jit(solution)/shard_map/ppermute | solution.py:145
  9.9 14.7 %collective-permute-start.1 = (bf16[1024,128]{1,0:T(8,128)(2,1)S(1)}, bf16[1024,128]{1,0:T(8,128)(2,1)S(1)}, u32[]{:S(2)}, u32[]{:S(2)}) collective-permute-start(bf16[1024,128]{1,0:T(8,128)(2,1)S(1)} %pad_maximum_fusion.refs_0_), channel_id=1, source_target_pairs={{0,2},{1,3},{2,0},{3,1},{4,6},{5,7},{6,4},{7,5},{8,10},{9,11},{10,... | collective-permute-start | bytes 786440 | tf_op jit(solution)/shard_map/ppermute | solution.py:145
  38.7 11.1 %collective-permute-start.6 = (bf16[512,128]{1,0:T(8,128)(2,1)}, bf16[512,128]{1,0:T(8,128)(2,1)S(1)}, u32[]{:S(2)}, u32[]{:S(2)}) collective-permute-start(bf16[512,128]{1,0:T(8,128)(2,1)} %get-tuple-element.21), channel_id=1, source_target_pairs={{0,1},{1,0},{2,3},{3,2},{4,5},{5,4},{6,7},{7,6},{8,9},{9,8},{10,11... | collective-permute-start | bytes 393224 | tf_op jit(solution)/shard_map/ppermute | solution.py:169
  44.9 9.2 %collective-permute-start.7 = (bf16[512,128]{1,0:T(8,128)(2,1)}, bf16[512,128]{1,0:T(8,128)(2,1)S(1)}, u32[]{:S(2)}, u32[]{:S(2)}) collective-permute-start(bf16[512,128]{1,0:T(8,128)(2,1)} %get-tuple-element.22), channel_id=1, source_target_pairs={{0,2},{1,3},{2,0},{3,1},{4,6},{5,7},{6,4},{7,5},{8,10},{9,11},{10,... | collective-permute-start | bytes 393224 | tf_op jit(solution)/shard_map/ppermute | solution.py:169
  46.7 7.8 %collective-permute-start.8 = (bf16[512,128]{1,0:T(8,128)(2,1)}, bf16[512,128]{1,0:T(8,128)(2,1)S(1)}, u32[]{:S(2)}, u32[]{:S(2)}) collective-permute-start(bf16[512,128]{1,0:T(8,128)(2,1)} %get-tuple-element.23), channel_id=1, source_target_pairs={{0,3},{1,2},{2,1},{3,0},{4,7},{5,6},{6,5},{7,4},{8,11},{9,10},{10,... | collective-permute-start | bytes 393224 | tf_op jit(solution)/shard_map/ppermute | solution.py:169
  47.4 7.1 %collective-permute-start.12 = (bf16[512,128]{1,0:T(8,128)(2,1)}, bf16[512,128]{1,0:T(8,128)(2,1)S(1)}, u32[]{:S(2)}, u32[]{:S(2)}) collective-permute-start(bf16[512,128]{1,0:T(8,128)(2,1)} %get-tuple-element.25), channel_id=1, source_target_pairs={{0,4},{4,0},{8,12},{12,8},{16,20},{20,16},{24,28},{28,24},{1,5},{5... | collective-permute-start | bytes 393224 | tf_op jit(solution)/shard_map/ppermute | solution.py:169
  47.4 9.9 %collective-permute-start.13 = (bf16[512,128]{1,0:T(8,128)(2,1)}, bf16[512,128]{1,0:T(8,128)(2,1)S(1)}, u32[]{:S(2)}, u32[]{:S(2)}) collective-permute-start(bf16[512,128]{1,0:T(8,128)(2,1)} %get-tuple-element.26), channel_id=1, source_target_pairs={{0,8},{4,12},{8,0},{12,4},{16,24},{20,28},{24,16},{28,20},{1,9},{5... | collective-permute-start | bytes 393224 | tf_op jit(solution)/shard_map/ppermute | solution.py:169
  49.7 9.8 %collective-permute-start.14 = (bf16[512,128]{1,0:T(8,128)(2,1)}, bf16[512,128]{1,0:T(8,128)(2,1)S(1)}, u32[]{:S(2)}, u32[]{:S(2)}) collective-permute-start(bf16[512,128]{1,0:T(8,128)(2,1)} %get-tuple-element.27), channel_id=1, source_target_pairs={{0,12},{4,8},{8,4},{12,0},{16,28},{20,24},{24,20},{28,16},{1,13},{... | collective-permute-start | bytes 393224 | tf_op jit(solution)/shard_map/ppermute | solution.py:169
  54.2 11.9 %collective-permute-start.15 = (bf16[512,128]{1,0:T(8,128)(2,1)}, bf16[512,128]{1,0:T(8,128)(2,1)S(1)}, u32[]{:S(2)}, u32[]{:S(2)}) collective-permute-start(bf16[512,128]{1,0:T(8,128)(2,1)} %get-tuple-element.28), channel_id=1, source_target_pairs={{0,16},{4,20},{8,24},{12,28},{16,0},{20,4},{24,8},{28,12},{1,17},{... | collective-permute-start | bytes 393224 | tf_op jit(solution)/shard_map/ppermute | solution.py:169
  54.5 11.6 %collective-permute-start.16 = (bf16[512,128]{1,0:T(8,128)(2,1)}, bf16[512,128]{1,0:T(8,128)(2,1)S(1)}, u32[]{:S(2)}, u32[]{:S(2)}) collective-permute-start(bf16[512,128]{1,0:T(8,128)(2,1)} %get-tuple-element.29), channel_id=1, source_target_pairs={{0,20},{4,16},{8,28},{12,24},{16,4},{20,0},{24,12},{28,8},{1,21},{... | collective-permute-start | bytes 393224 | tf_op jit(solution)/shard_map/ppermute | solution.py:169
  54.5 12.1 %collective-permute-start.17 = (bf16[512,128]{1,0:T(8,128)(2,1)}, bf16[512,128]{1,0:T(8,128)(2,1)S(1)}, u32[]{:S(2)}, u32[]{:S(2)}) collective-permute-start(bf16[512,128]{1,0:T(8,128)(2,1)} %get-tuple-element.30), channel_id=1, source_target_pairs={{0,24},{4,28},{8,16},{12,20},{16,8},{20,12},{24,0},{28,4},{1,25},{... | collective-permute-start | bytes 393224 | tf_op jit(solution)/shard_map/ppermute | solution.py:169
  57.3 9.4 %collective-permute-start.18 = (bf16[512,128]{1,0:T(8,128)(2,1)}, bf16[512,128]{1,0:T(8,128)(2,1)S(1)}, u32[]{:S(2)}, u32[]{:S(2)}) collective-permute-start(bf16[512,128]{1,0:T(8,128)(2,1)} %get-tuple-element.31), channel_id=1, source_target_pairs={{0,28},{4,24},{8,20},{12,16},{16,12},{20,8},{24,4},{28,0},{1,29},{... | collective-permute-start | bytes 393224 | tf_op jit(solution)/shard_map/ppermute | solution.py:169
  59.6 12.2 %collective-permute-start.11 = (bf16[512,128]{1,0:T(8,128)(2,1)S(1)}, bf16[512,128]{1,0:T(8,128)(2,1)S(1)}, u32[]{:S(2)}, u32[]{:S(2)}) collective-permute-start(bf16[512,128]{1,0:T(8,128)(2,1)S(1)} %fusion.6.refs_0_), channel_id=1, source_target_pairs={{0,3},{1,2},{2,1},{3,0},{4,7},{5,6},{6,5},{7,4},{8,11},{9,10},{10,... | collective-permute-start | bytes 393224 | tf_op jit(solution)/shard_map/ppermute | solution.py:162
  66.1 8.3 %collective-permute-start.10 = (bf16[512,128]{1,0:T(8,128)(2,1)S(1)}, bf16[512,128]{1,0:T(8,128)(2,1)S(1)}, u32[]{:S(2)}, u32[]{:S(2)}) collective-permute-start(bf16[512,128]{1,0:T(8,128)(2,1)S(1)} %fusion.6.refs_0_), channel_id=1, source_target_pairs={{0,2},{1,3},{2,0},{3,1},{4,6},{5,7},{6,4},{7,5},{8,10},{9,11},{10,... | collective-permute-start | bytes 393224 | tf_op jit(solution)/shard_map/ppermute | solution.py:162
  66.1 8.7 %collective-permute-start.9 = (bf16[512,128]{1,0:T(8,128)(2,1)S(1)}, bf16[512,128]{1,0:T(8,128)(2,1)S(1)}, u32[]{:S(2)}, u32[]{:S(2)}) collective-permute-start(bf16[512,128]{1,0:T(8,128)(2,1)S(1)} %fusion.6.refs_0_), channel_id=1, source_target_pairs={{0,1},{1,0},{2,3},{3,2},{4,5},{5,4},{6,7},{7,6},{8,9},{9,8},{10,11... | collective-permute-start | bytes 393224 | tf_op jit(solution)/shard_map/ppermute | solution.py:162
  67.7 9.3 %collective-permute-start.25 = (bf16[512,128]{1,0:T(8,128)(2,1)S(1)}, bf16[512,128]{1,0:T(8,128)(2,1)S(1)}, u32[]{:S(2)}, u32[]{:S(2)}) collective-permute-start(bf16[512,128]{1,0:T(8,128)(2,1)S(1)} %get-tuple-element.38.refs_4_), channel_id=1, source_target_pairs={{0,28},{4,24},{8,20},{12,16},{16,12},{20,8},{24,4},{28,0},{1,29},{... | collective-permute-start | bytes 393224 | tf_op jit(solution)/shard_map/ppermute | solution.py:162
  70.3 8.7 %collective-permute-start.24 = (bf16[512,128]{1,0:T(8,128)(2,1)S(1)}, bf16[512,128]{1,0:T(8,128)(2,1)S(1)}, u32[]{:S(2)}, u32[]{:S(2)}) collective-permute-start(bf16[512,128]{1,0:T(8,128)(2,1)S(1)} %get-tuple-element.38.refs_4_), channel_id=1, source_target_pairs={{0,24},{4,28},{8,16},{12,20},{16,8},{20,12},{24,0},{28,4},{1,25},{... | collective-permute-start | bytes 393224 | tf_op jit(solution)/shard_map/ppermute | solution.py:162
  71.8 8.5 %collective-permute-start.23 = (bf16[512,128]{1,0:T(8,128)(2,1)S(1)}, bf16[512,128]{1,0:T(8,128)(2,1)S(1)}, u32[]{:S(2)}, u32[]{:S(2)}) collective-permute-start(bf16[512,128]{1,0:T(8,128)(2,1)S(1)} %get-tuple-element.38.refs_4_), channel_id=1, source_target_pairs={{0,20},{4,16},{8,28},{12,24},{16,4},{20,0},{24,12},{28,8},{1,21},{... | collective-permute-start | bytes 393224 | tf_op jit(solution)/shard_map/ppermute | solution.py:162
  74.4 8.7 %collective-permute-start.22 = (bf16[512,128]{1,0:T(8,128)(2,1)S(1)}, bf16[512,128]{1,0:T(8,128)(2,1)S(1)}, u32[]{:S(2)}, u32[]{:S(2)}) collective-permute-start(bf16[512,128]{1,0:T(8,128)(2,1)S(1)} %get-tuple-element.38.refs_4_), channel_id=1, source_target_pairs={{0,16},{4,20},{8,24},{12,28},{16,0},{20,4},{24,8},{28,12},{1,17},{... | collective-permute-start | bytes 393224 | tf_op jit(solution)/shard_map/ppermute | solution.py:162
  74.8 8.3 %collective-permute-start.21 = (bf16[512,128]{1,0:T(8,128)(2,1)S(1)}, bf16[512,128]{1,0:T(8,128)(2,1)S(1)}, u32[]{:S(2)}, u32[]{:S(2)}) collective-permute-start(bf16[512,128]{1,0:T(8,128)(2,1)S(1)} %get-tuple-element.38.refs_4_), channel_id=1, source_target_pairs={{0,12},{4,8},{8,4},{12,0},{16,28},{20,24},{24,20},{28,16},{1,13},{... | collective-permute-start | bytes 393224 | tf_op jit(solution)/shard_map/ppermute | solution.py:162
  77.0 7.0 %collective-permute-start.20 = (bf16[512,128]{1,0:T(8,128)(2,1)S(1)}, bf16[512,128]{1,0:T(8,128)(2,1)S(1)}, u32[]{:S(2)}, u32[]{:S(2)}) collective-permute-start(bf16[512,128]{1,0:T(8,128)(2,1)S(1)} %get-tuple-element.38.refs_4_), channel_id=1, source_target_pairs={{0,8},{4,12},{8,0},{12,4},{16,24},{20,28},{24,16},{28,20},{1,9},{5... | collective-permute-start | bytes 393224 | tf_op jit(solution)/shard_map/ppermute | solution.py:162
  79.0 5.1 %collective-permute-start.19 = (bf16[512,128]{1,0:T(8,128)(2,1)S(1)}, bf16[512,128]{1,0:T(8,128)(2,1)S(1)}, u32[]{:S(2)}, u32[]{:S(2)}) collective-permute-start(bf16[512,128]{1,0:T(8,128)(2,1)S(1)} %get-tuple-element.38.refs_4_), channel_id=1, source_target_pairs={{0,4},{4,0},{8,12},{12,8},{16,20},{20,16},{24,28},{28,24},{1,5},{5... | collective-permute-start | bytes 393224 | tf_op jit(solution)/shard_map/ppermute | solution.py:162
  98.0 16.6 %collective-permute-start.26 = (bf16[1024,128]{1,0:T(8,128)(2,1)}, bf16[1024,128]{1,0:T(8,128)(2,1)S(1)}, u32[]{:S(2)}, u32[]{:S(2)}) collective-permute-start(bf16[1024,128]{1,0:T(8,128)(2,1)} %get-tuple-element.33), channel_id=1, source_target_pairs={{0,2},{1,3},{2,0},{3,1},{4,6},{5,7},{6,4},{7,5},{8,10},{9,11},{10,... | collective-permute-start | bytes 786440 | tf_op jit(solution)/shard_map/ppermute | solution.py:152
  104.6 11.2 %collective-permute-start.28 = (bf16[1024,128]{1,0:T(8,128)(2,1)}, bf16[1024,128]{1,0:T(8,128)(2,1)S(1)}, u32[]{:S(2)}, u32[]{:S(2)}) collective-permute-start(bf16[1024,128]{1,0:T(8,128)(2,1)} %get-tuple-element.35), channel_id=1, source_target_pairs={{0,8},{4,12},{8,0},{12,4},{16,24},{20,28},{24,16},{28,20},{1,9},{5... | collective-permute-start | bytes 786440 | tf_op jit(solution)/shard_map/ppermute | solution.py:152
  107.6 12.6 %collective-permute-start.29 = (bf16[1024,128]{1,0:T(8,128)(2,1)}, bf16[1024,128]{1,0:T(8,128)(2,1)S(1)}, u32[]{:S(2)}, u32[]{:S(2)}) collective-permute-start(bf16[1024,128]{1,0:T(8,128)(2,1)} %get-tuple-element.36), channel_id=1, source_target_pairs={{0,16},{4,20},{8,24},{12,28},{16,0},{20,4},{24,8},{28,12},{1,17},{... | collective-permute-start | bytes 786440 | tf_op jit(solution)/shard_map/ppermute | solution.py:152
  107.6 12.6 %collective-permute-start.30 = (bf16[1024,128]{1,0:T(8,128)(2,1)}, bf16[1024,128]{1,0:T(8,128)(2,1)S(1)}, u32[]{:S(2)}, u32[]{:S(2)}) collective-permute-start(bf16[1024,128]{1,0:T(8,128)(2,1)} %get-tuple-element.37), channel_id=1, source_target_pairs={{0,24},{4,28},{8,16},{12,20},{16,8},{20,12},{24,0},{28,4},{1,25},{... | collective-permute-start | bytes 786440 | tf_op jit(solution)/shard_map/ppermute | solution.py:152
  115.7 8.2 %collective-permute-start.27 = (f32[512,128]{1,0:T(8,128)S(1)}, f32[512,128]{1,0:T(8,128)S(1)}, u32[]{:S(2)}, u32[]{:S(2)}) collective-permute-start(f32[512,128]{1,0:T(8,128)S(1)} %slice.17), channel_id=1, source_target_pairs={{0,1},{1,0},{2,3},{3,2},{4,5},{5,4},{6,7},{7,6},{8,9},{9,8},{10,11... | collective-permute-start | bytes 786440 | tf_op jit(solution)/shard_map/ppermute | solution.py:155
  121.4 3.4 %collective-permute-start.31 = (f32[512,128]{1,0:T(8,128)S(1)}, f32[512,128]{1,0:T(8,128)S(1)}, u32[]{:S(2)}, u32[]{:S(2)}) collective-permute-start(f32[512,128]{1,0:T(8,128)S(1)} %slice.19), channel_id=1, source_target_pairs={{0,4},{4,0},{8,12},{12,8},{16,20},{20,16},{24,28},{28,24},{1,5},{5... | collective-permute-start | bytes 786440 | tf_op jit(solution)/shard_map/ppermute | solution.py:155
  (21 other events, 255.5 us)

commit v11 on v9

--- a/solution.py
+++ b/solution.py
@@ -193,8 +193,8 @@
     if paired(n_row):
         cols = pair_index(tile_col[0, 0], me_row, per_run)
         gathers = (gather_paired, gather_xor)
-        scatters = (scatter_xor, scatter_paired)
-        splits = (n_row, n_row // 2)
+        scatters = (scatter_paired, scatter_paired)
+        splits = (n_row // 2, n_row // 2)
     else:
         cols = rotate_index(tile_col[0, 0], me_row, n_row, per_run)
         gathers = (gather_rotated, gather_rotated)

time: 119 us -> 116 us (0.975)
  Pallas kernels: 20.2 us -> 14.8 us
  starting transfers between devices: 57.8 us -> 60 us
    ppermute x7 -> x0, starting transfers between devices: 11.7 us -> none  [scatter_xor(): got = lax.ppermute(chunks[p], axis, [(i, i ^ p) for i in range(n)])]
    ppermute x6, starting transfers between devices: 13.1 us -> 23 us  [scatter_rotated(): lax.ppermute(chunks[(n - s) % n], axis, [(i, (i + s) % n) for i in range(...]
    ppermute x6, waiting for transfers between devices: 8.04 us -> 14.1 us  [gather_rotated(): pieces.append(lax.ppermute(x, axis, [(i, (i + s) % n) for i in range(n)]))]
    ppermute x7 -> x0, waiting for transfers between devices: 5.8 us -> none  [scatter_xor(): got = lax.ppermute(chunks[p], axis, [(i, i ^ p) for i in range(n)])]
    pallas_call x2, Pallas kernels: 20.2 us -> 14.8 us  [tile_sweep(): pl.pallas_call(functools.partial(sweep_kernel, tile, group, len(emb_piece...]
    ppermute x6, waiting for transfers between devices: 1.46 us -> 6.02 us  [scatter_rotated(): lax.ppermute(chunks[(n - s) % n], axis, [(i, (i + s) % n) for i in range(...]
    ppermute x3 -> x6, waiting for transfers between devices: 4.02 us -> 0.02 us  [scatter_paired(): got = lax.ppermute(blocks[b], axis, [(i, i ^ 2 * b) for i in range(n)])]
    ppermute x1 -> x2, starting transfers between devices: 0.07 us -> 3.38 us  [scatter_paired(): got = lax.ppermute(total[width:], axis, [(i, i ^ 1) for i in range(n)])]
  transfers between devices with their start and end apart: 34 -> 31, of which waited for: 11 -> 12; matrix products, arithmetic and copies ran while one was open for 6% -> 6% of each run, Pallas kernels for 0% -> 0%
where the time goes in v11:
time: 116 us; the launch traced here: 114 us
  starting transfers between devices  60 us (52%)
  waiting for transfers between devices  27.4 us (24%)
  Pallas kernels  14.8 us (13%)
  other arithmetic  9.03 us (8%)
  between operations  1.54 us (1%)
  local copies, waits for them, and re-layouts  1.38 us (1%)
    ppermute x6, starting transfers between devices, scatter_rotated(): lax.ppermute(chunks[(n - s) % n], axis, [(i, (i + s) % n) for i in range(...  23 us
    pallas_call x2, Pallas kernels, tile_sweep(): pl.pallas_call(functools.partial(sweep_kernel, tile, group, len(emb_piece...  14.8 us
    ppermute x6, waiting for transfers between devices, gather_rotated(): pieces.append(lax.ppermute(x, axis, [(i, (i + s) % n) for i in range(n)]))  14.1 us
    ppermute x6, starting transfers between devices, scatter_paired(): got = lax.ppermute(blocks[b], axis, [(i, i ^ 2 * b) for i in range(n)])  11.9 us
    ppermute x6, starting transfers between devices, gather_rotated(): pieces.append(lax.ppermute(x, axis, [(i, (i + s) % n) for i in range(n)]))  11.2 us
    ppermute x7, starting transfers between devices, gather_xor(): pieces.append(lax.ppermute(x, axis, [(i, i ^ p) for i in range(n)]))  6.47 us
    ppermute x6, waiting for transfers between devices, scatter_rotated(): lax.ppermute(chunks[(n - s) % n], axis, [(i, (i + s) % n) for i in range(...  6.02 us
    ppermute x7, waiting for transfers between devices, gather_xor(): pieces.append(lax.ppermute(x, axis, [(i, i ^ p) for i in range(n)]))  4.88 us
  transfers between devices with their start and end apart: 31, of which 12 were waited for; matrix products, arithmetic and copies ran while one was open for 6% of the time, Pallas kernels for 0%

profile of v11, /device:TPU:0, one launch (start us, length us, event | category | flops | bytes accessed | tf_op | source)
XLA Modules:
  0.0 114.2 jit_solution(4417879364995357011)
XLA Ops:
  3.1 4.7 %collective-permute-start.2 = (bf16[512,128]{1,0:T(8,128)(2,1)S(1)}, bf16[512,128]{1,0:T(8,128)(2,1)S(1)}, u32[]{:S(2)}, u32[]{:S(2)}) collective-permute-start(bf16[512,128]{1,0:T(8,128)(2,1)S(1)} %convert_element_type.60.refs_0_), channel_id=1, source_target_pairs={{0,3},{1,0},{2,1},{3,2},{4,7},{5,4},{6,5},{7,6},{8,11},{9,8},{10,9... | collective-permute-start | bytes 393224 | tf_op jit(solution)/shard_map/ppermute | solution.py:125
  7.8 2.5 %collective-permute-start.6 = (bf16[1024,128]{1,0:T(8,128)(2,1)S(1)}, bf16[1024,128]{1,0:T(8,128)(2,1)S(1)}, u32[]{:S(2)}, u32[]{:S(2)}) collective-permute-start(bf16[1024,128]{1,0:T(8,128)(2,1)S(1)} %pad_maximum_fusion.refs_4_), channel_id=1, source_target_pairs={{0,24},{4,28},{8,16},{12,20},{16,8},{20,12},{24,0},{28,4},{1,25},{... | collective-permute-start | bytes 786440 | tf_op jit(solution)/shard_map/ppermute | solution.py:145
  13.1 1.3 %fusion.4 = (s32[64]{0:T(128)}, s32[64]{0:T(128)}) fusion(s32[1,1,64]{2,1,0:T(1,128)} %param.11, s32[]{:T(128)S(6)} %axis_index.22, s32[1,1,64]{2,1,0:T(1,128)} %param.12, s32[]{:T(128)S(6)} %axis_index.25), kind=kLoop, calls=%fused_computation.24 | loop fusion | flops 3520 | bytes 1032 | tf_op jit(solution)/shard_map/add | solution.py:180
  14.4 6.2 %collective-permute-done.1.refs_2_ = bf16[512,128]{1,0:T(8,128)(2,1)S(1)} collective-permute-done((bf16[512,128]{1,0:T(8,128)(2,1)S(1)}, bf16[512,128]{1,0:T(8,128)(2,1)S(1)}, u32[]{:S(2)}, u32[]{:S(2)}) %collective-permute-start.1) | collective-permute-done | bytes 131104 | tf_op jit(solution)/shard_map/ppermute | solution.py:125
  20.6 2.2 %collective-permute-done.5.refs_6_ = bf16[1024,128]{1,0:T(8,128)(2,1)S(1)} collective-permute-done((bf16[1024,128]{1,0:T(8,128)(2,1)S(1)}, bf16[1024,128]{1,0:T(8,128)(2,1)S(1)}, u32[]{:S(2)}, u32[]{:S(2)}) %collective-permute-start.5) | collective-permute-done | bytes 262176 | tf_op jit(solution)/shard_map/ppermute | solution.py:145
  23.6 7.4 %shard_map.86 = (bf16[512,128]{1,0:T(8,128)(2,1)}, bf16[512,128]{1,0:T(8,128)(2,1)}, bf16[512,128]{1,0:T(8,128)(2,1)}, bf16[512,128]{1,0:T(8,128)(2,1)}, bf16[10...) custom-call(s32[64]{0:T(128)} %get-tuple-element.34.rows_ref, ...), custom_call_target="tpu_custom_call" | custom-call | flops 3221225472 | bytes 21495808 | tf_op jit(solution)/shard_map/pallas_call | solution.py:107
  31.0 1.5 %collective-permute-start.13 = (bf16[1024,128]{1,0:T(8,128)(2,1)}, bf16[1024,128]{1,0:T(8,128)(2,1)S(1)}, u32[]{:S(2)}, u32[]{:S(2)}) collective-permute-start(bf16[1024,128]{1,0:T(8,128)(2,1)} %get-tuple-element.23), channel_id=1, source_target_pairs={{0,8},{4,12},{8,0},{12,4},{16,24},{20,28},{24,16},{28,20},{1,9},{5... | collective-permute-start | bytes 786440 | tf_op jit(solution)/shard_map/ppermute | solution.py:152
  32.5 3.9 %collective-permute-start.14 = (bf16[1024,128]{1,0:T(8,128)(2,1)}, bf16[1024,128]{1,0:T(8,128)(2,1)S(1)}, u32[]{:S(2)}, u32[]{:S(2)}) collective-permute-start(bf16[1024,128]{1,0:T(8,128)(2,1)} %get-tuple-element.24), channel_id=1, source_target_pairs={{0,16},{4,20},{8,24},{12,28},{16,0},{20,4},{24,8},{28,12},{1,17},{... | collective-permute-start | bytes 786440 | tf_op jit(solution)/shard_map/ppermute | solution.py:152
  37.1 5.0 %collective-permute-start.7 = (bf16[512,128]{1,0:T(8,128)(2,1)}, bf16[512,128]{1,0:T(8,128)(2,1)S(1)}, u32[]{:S(2)}, u32[]{:S(2)}) collective-permute-start(bf16[512,128]{1,0:T(8,128)(2,1)} %get-tuple-element.19), channel_id=1, source_target_pairs={{0,1},{1,2},{2,3},{3,0},{4,5},{5,6},{6,7},{7,4},{8,9},{9,10},{10,1... | collective-permute-start | bytes 393224 | tf_op jit(solution)/shard_map/ppermute | solution.py:132
  42.1 4.1 %collective-permute-start.8 = (bf16[512,128]{1,0:T(8,128)(2,1)}, bf16[512,128]{1,0:T(8,128)(2,1)S(1)}, u32[]{:S(2)}, u32[]{:S(2)}) collective-permute-start(bf16[512,128]{1,0:T(8,128)(2,1)} %get-tuple-element.20), channel_id=1, source_target_pairs={{0,2},{1,3},{2,0},{3,1},{4,6},{5,7},{6,4},{7,5},{8,10},{9,11},{10,... | collective-permute-start | bytes 393224 | tf_op jit(solution)/shard_map/ppermute | solution.py:132
  46.2 2.5 %collective-permute-start.9 = (bf16[512,128]{1,0:T(8,128)(2,1)}, bf16[512,128]{1,0:T(8,128)(2,1)S(1)}, u32[]{:S(2)}, u32[]{:S(2)}) collective-permute-start(bf16[512,128]{1,0:T(8,128)(2,1)} %get-tuple-element.21), channel_id=1, source_target_pairs={{0,3},{1,0},{2,1},{3,2},{4,7},{5,4},{6,5},{7,6},{8,11},{9,8},{10,9... | collective-permute-start | bytes 393224 | tf_op jit(solution)/shard_map/ppermute | solution.py:132
  48.8 1.1 convert_add_fusion.1
  49.9 1.5 %collective-permute-start.16 = (f32[512,128]{1,0:T(8,128)S(1)}, f32[512,128]{1,0:T(8,128)S(1)}, u32[]{:S(2)}, u32[]{:S(2)}) collective-permute-start(f32[512,128]{1,0:T(8,128)S(1)} %slice.17), channel_id=1, source_target_pairs={{0,4},{4,0},{8,12},{12,8},{16,20},{20,16},{24,28},{28,24},{1,5},{5... | collective-permute-start | bytes 786440 | tf_op jit(solution)/shard_map/ppermute | solution.py:155
  51.4 2.5 %collective-permute-done.8 = bf16[512,128]{1,0:T(8,128)(2,1)S(1)} collective-permute-done((bf16[512,128]{1,0:T(8,128)(2,1)}, bf16[512,128]{1,0:T(8,128)(2,1)S(1)}, u32[]{:S(2)}, u32[]{:S(2)}) %collective-permute-start.8) | collective-permute-done | bytes 131104 | tf_op jit(solution)/shard_map/ppermute | solution.py:132
  55.2 4.8 %collective-permute-start.12 = (bf16[512,128]{1,0:T(8,128)(2,1)S(1)}, bf16[512,128]{1,0:T(8,128)(2,1)S(1)}, u32[]{:S(2)}, u32[]{:S(2)}) collective-permute-start(bf16[512,128]{1,0:T(8,128)(2,1)S(1)} %fusion.9.refs_0_), channel_id=1, source_target_pairs={{0,3},{1,0},{2,1},{3,2},{4,7},{5,4},{6,5},{7,6},{8,11},{9,8},{10,9... | collective-permute-start | bytes 393224 | tf_op jit(solution)/shard_map/ppermute | solution.py:125
  60.8 1.9 %collective-permute-start.22 = (bf16[512,128]{1,0:T(8,128)(2,1)S(1)}, bf16[512,128]{1,0:T(8,128)(2,1)S(1)}, u32[]{:S(2)}, u32[]{:S(2)}) collective-permute-start(bf16[512,128]{1,0:T(8,128)(2,1)S(1)} %fusion.8.refs_4_), channel_id=1, source_target_pairs={{0,24},{4,28},{8,16},{12,20},{16,8},{20,12},{24,0},{28,4},{1,25},{... | collective-permute-start | bytes 393224 | tf_op jit(solution)/shard_map/ppermute | solution.py:162
  62.7 1.1 collective-permute-done.12.refs_3_
  64.7 6.8 %collective-permute-done.11.refs_2_ = bf16[512,128]{1,0:T(8,128)(2,1)S(1)} collective-permute-done((bf16[512,128]{1,0:T(8,128)(2,1)S(1)}, bf16[512,128]{1,0:T(8,128)(2,1)S(1)}, u32[]{:S(2)}, u32[]{:S(2)}) %collective-permute-start.11) | collective-permute-done | bytes 131104 | tf_op jit(solution)/shard_map/ppermute | solution.py:125
  71.5 1.7 %collective-permute-start.20 = (bf16[512,128]{1,0:T(8,128)(2,1)S(1)}, bf16[512,128]{1,0:T(8,128)(2,1)S(1)}, u32[]{:S(2)}, u32[]{:S(2)}) collective-permute-start(bf16[512,128]{1,0:T(8,128)(2,1)S(1)} %fusion.8.refs_4_), channel_id=1, source_target_pairs={{0,16},{4,20},{8,24},{12,28},{16,0},{20,4},{24,8},{28,12},{1,17},{... | collective-permute-start | bytes 393224 | tf_op jit(solution)/shard_map/ppermute | solution.py:162
  73.8 1.3 %collective-permute-start.17 = (bf16[512,128]{1,0:T(8,128)(2,1)S(1)}, bf16[512,128]{1,0:T(8,128)(2,1)S(1)}, u32[]{:S(2)}, u32[]{:S(2)}) collective-permute-start(bf16[512,128]{1,0:T(8,128)(2,1)S(1)} %fusion.8.refs_4_), channel_id=1, source_target_pairs={{0,4},{4,0},{8,12},{12,8},{16,20},{20,16},{24,28},{28,24},{1,5},{5... | collective-permute-start | bytes 393224 | tf_op jit(solution)/shard_map/ppermute | solution.py:162
  75.2 1.3 %collective-permute-done.20.refs_8_ = bf16[512,128]{1,0:T(8,128)(2,1)S(1)} collective-permute-done((bf16[512,128]{1,0:T(8,128)(2,1)S(1)}, bf16[512,128]{1,0:T(8,128)(2,1)S(1)}, u32[]{:S(2)}, u32[]{:S(2)}) %collective-permute-start.20) | collective-permute-done | bytes 131104 | tf_op jit(solution)/shard_map/ppermute | solution.py:162
  76.5 2.6 %collective-permute-done.19.refs_7_ = bf16[512,128]{1,0:T(8,128)(2,1)S(1)} collective-permute-done((bf16[512,128]{1,0:T(8,128)(2,1)S(1)}, bf16[512,128]{1,0:T(8,128)(2,1)S(1)}, u32[]{:S(2)}, u32[]{:S(2)}) %collective-permute-start.19) | collective-permute-done | bytes 131104 | tf_op jit(solution)/shard_map/ppermute | solution.py:162
  80.7 7.4 %shard_map.87 = (bf16[512,128]{1,0:T(8,128)(2,1)}, bf16[512,128]{1,0:T(8,128)(2,1)}, bf16[512,128]{1,0:T(8,128)(2,1)}, bf16[512,128]{1,0:T(8,128)(2,1)}, bf16[10...) custom-call(s32[64]{0:T(128)} %get-tuple-element.34.rows_ref, ...), custom_call_target="tpu_custom_call" | custom-call | flops 3221225472 | bytes 21495808 | tf_op jit(solution)/shard_map/pallas_call | solution.py:107
  88.2 2.0 %collective-permute-start.27 = (bf16[1024,128]{1,0:T(8,128)(2,1)}, bf16[1024,128]{1,0:T(8,128)(2,1)S(1)}, u32[]{:S(2)}, u32[]{:S(2)}) collective-permute-start(bf16[1024,128]{1,0:T(8,128)(2,1)} %get-tuple-element.31), channel_id=1, source_target_pairs={{0,8},{4,12},{8,0},{12,4},{16,24},{20,28},{24,16},{28,20},{1,9},{5... | collective-permute-start | bytes 786440 | tf_op jit(solution)/shard_map/ppermute | solution.py:152
  90.2 3.7 %collective-permute-start.28 = (bf16[1024,128]{1,0:T(8,128)(2,1)}, bf16[1024,128]{1,0:T(8,128)(2,1)S(1)}, u32[]{:S(2)}, u32[]{:S(2)}) collective-permute-start(bf16[1024,128]{1,0:T(8,128)(2,1)} %get-tuple-element.32), channel_id=1, source_target_pairs={{0,16},{4,20},{8,24},{12,28},{16,0},{20,4},{24,8},{28,12},{1,17},{... | collective-permute-start | bytes 786440 | tf_op jit(solution)/shard_map/ppermute | solution.py:152
  93.9 6.4 %collective-permute-start.24 = (bf16[512,128]{1,0:T(8,128)(2,1)}, bf16[512,128]{1,0:T(8,128)(2,1)S(1)}, u32[]{:S(2)}, u32[]{:S(2)}) collective-permute-start(bf16[512,128]{1,0:T(8,128)(2,1)} %get-tuple-element.27), channel_id=1, source_target_pairs={{0,1},{1,2},{2,3},{3,0},{4,5},{5,6},{6,7},{7,4},{8,9},{9,10},{10,1... | collective-permute-start | bytes 393224 | tf_op jit(solution)/shard_map/ppermute | solution.py:132
  100.3 2.1 %collective-permute-start.25 = (bf16[512,128]{1,0:T(8,128)(2,1)}, bf16[512,128]{1,0:T(8,128)(2,1)S(1)}, u32[]{:S(2)}, u32[]{:S(2)}) collective-permute-start(bf16[512,128]{1,0:T(8,128)(2,1)} %get-tuple-element.28), channel_id=1, source_target_pairs={{0,2},{1,3},{2,0},{3,1},{4,6},{5,7},{6,4},{7,5},{8,10},{9,11},{10,... | collective-permute-start | bytes 393224 | tf_op jit(solution)/shard_map/ppermute | solution.py:132
  102.4 2.9 %collective-permute-start.26 = (bf16[512,128]{1,0:T(8,128)(2,1)}, bf16[512,128]{1,0:T(8,128)(2,1)S(1)}, u32[]{:S(2)}, u32[]{:S(2)}) collective-permute-start(bf16[512,128]{1,0:T(8,128)(2,1)} %get-tuple-element.29), channel_id=1, source_target_pairs={{0,3},{1,0},{2,1},{3,2},{4,7},{5,4},{6,5},{7,6},{8,11},{9,8},{10,9... | collective-permute-start | bytes 393224 | tf_op jit(solution)/shard_map/ppermute | solution.py:132
  105.3 1.1 convert_add_fusion
  106.4 1.9 %collective-permute-start.30 = (f32[512,128]{1,0:T(8,128)S(1)}, f32[512,128]{1,0:T(8,128)S(1)}, u32[]{:S(2)}, u32[]{:S(2)}) collective-permute-start(f32[512,128]{1,0:T(8,128)S(1)} %slice.19), channel_id=1, source_target_pairs={{0,4},{4,0},{8,12},{12,8},{16,20},{20,16},{24,28},{28,24},{1,5},{5... | collective-permute-start | bytes 786440 | tf_op jit(solution)/shard_map/ppermute | solution.py:155
  108.3 2.4 %collective-permute-done.25 = bf16[512,128]{1,0:T(8,128)(2,1)S(1)} collective-permute-done((bf16[512,128]{1,0:T(8,128)(2,1)}, bf16[512,128]{1,0:T(8,128)(2,1)S(1)}, u32[]{:S(2)}, u32[]{:S(2)}) %collective-permute-start.25) | collective-permute-done | bytes 131104 | tf_op jit(solution)/shard_map/ppermute | solution.py:132
  111.6 1.8 %multiply_add_fusion = f32[512,128]{1,0:T(8,128)} fusion(bf16[512,128]{1,0:T(8,128)(2,1)S(1)} %collective-permute-done.26, bf16[512,128]{1,0:T(8,128)(2,1)S(1)} %collective-permute-done.25, bf16[512,128]{1,0:T(8,128)(2,1)S(1)} %collective-permute-done.24, bf16[512,128]{1,0:T(8,128)(2,1)} %get-tuple-element.26, f32[512,128]{1,0:T(8,128)S(1)} %copy-done, ...), kind=kLoop, calls=%fused_computation.9 | loop fusion | flops 1179648 | bytes 1572864 | tf_op jit(solution)/shard_map/add | solution.py:213
  (90 shorter events, 12.8 us)
Async XLA Ops:
  1.6 6.2 %collective-permute-start.3 = (bf16[512,128]{1,0:T(8,128)(2,1)S(1)}, bf16[512,128]{1,0:T(8,128)(2,1)S(1)}, u32[]{:S(2)}, u32[]{:S(2)}) collective-permute-start(bf16[512,128]{1,0:T(8,128)(2,1)S(1)} %convert_element_type.61), channel_id=1, source_target_pairs={{0,4},{4,0},{8,12},{12,8},{16,20},{20,16},{24,28},{28,24},{1,5},{5... | collective-permute-start | bytes 393224 | tf_op jit(solution)/shard_map/ppermute | solution.py:142
  3.1 8.9 %collective-permute-start.2 = (bf16[512,128]{1,0:T(8,128)(2,1)S(1)}, bf16[512,128]{1,0:T(8,128)(2,1)S(1)}, u32[]{:S(2)}, u32[]{:S(2)}) collective-permute-start(bf16[512,128]{1,0:T(8,128)(2,1)S(1)} %convert_element_type.60.refs_0_), channel_id=1, source_target_pairs={{0,3},{1,0},{2,1},{3,2},{4,7},{5,4},{6,5},{7,6},{8,11},{9,8},{10,9... | collective-permute-start | bytes 393224 | tf_op jit(solution)/shard_map/ppermute | solution.py:125
  7.8 12.8 %collective-permute-start.6 = (bf16[1024,128]{1,0:T(8,128)(2,1)S(1)}, bf16[1024,128]{1,0:T(8,128)(2,1)S(1)}, u32[]{:S(2)}, u32[]{:S(2)}) collective-permute-start(bf16[1024,128]{1,0:T(8,128)(2,1)S(1)} %pad_maximum_fusion.refs_4_), channel_id=1, source_target_pairs={{0,24},{4,28},{8,16},{12,20},{16,8},{20,12},{24,0},{28,4},{1,25},{... | collective-permute-start | bytes 786440 | tf_op jit(solution)/shard_map/ppermute | solution.py:145
  10.3 12.5 %collective-permute-start.5 = (bf16[1024,128]{1,0:T(8,128)(2,1)S(1)}, bf16[1024,128]{1,0:T(8,128)(2,1)S(1)}, u32[]{:S(2)}, u32[]{:S(2)}) collective-permute-start(bf16[1024,128]{1,0:T(8,128)(2,1)S(1)} %pad_maximum_fusion.refs_4_), channel_id=1, source_target_pairs={{0,16},{4,20},{8,24},{12,28},{16,0},{20,4},{24,8},{28,12},{1,17},{... | collective-permute-start | bytes 786440 | tf_op jit(solution)/shard_map/ppermute | solution.py:145
  10.8 12.1 %collective-permute-start.4 = (bf16[1024,128]{1,0:T(8,128)(2,1)S(1)}, bf16[1024,128]{1,0:T(8,128)(2,1)S(1)}, u32[]{:S(2)}, u32[]{:S(2)}) collective-permute-start(bf16[1024,128]{1,0:T(8,128)(2,1)S(1)} %pad_maximum_fusion.refs_4_), channel_id=1, source_target_pairs={{0,8},{4,12},{8,0},{12,4},{16,24},{20,28},{24,16},{28,20},{1,9},{5... | collective-permute-start | bytes 786440 | tf_op jit(solution)/shard_map/ppermute | solution.py:145
  11.4 9.2 %collective-permute-start.1 = (bf16[512,128]{1,0:T(8,128)(2,1)S(1)}, bf16[512,128]{1,0:T(8,128)(2,1)S(1)}, u32[]{:S(2)}, u32[]{:S(2)}) collective-permute-start(bf16[512,128]{1,0:T(8,128)(2,1)S(1)} %convert_element_type.60.refs_0_), channel_id=1, source_target_pairs={{0,2},{1,3},{2,0},{3,1},{4,6},{5,7},{6,4},{7,5},{8,10},{9,11},{10,... | collective-permute-start | bytes 393224 | tf_op jit(solution)/shard_map/ppermute | solution.py:125
  12.0 8.5 %collective-permute-start = (bf16[512,128]{1,0:T(8,128)(2,1)S(1)}, bf16[512,128]{1,0:T(8,128)(2,1)S(1)}, u32[]{:S(2)}, u32[]{:S(2)}) collective-permute-start(bf16[512,128]{1,0:T(8,128)(2,1)S(1)} %convert_element_type.60.refs_0_), channel_id=1, source_target_pairs={{0,1},{1,2},{2,3},{3,0},{4,5},{5,6},{6,7},{7,4},{8,9},{9,10},{10,1... | collective-permute-start | bytes 393224 | tf_op jit(solution)/shard_map/ppermute | solution.py:125
  23.6 37.0 %copy-start.1 = (f32[512,128]{1,0:T(8,128)S(1)}, f32[512,128]{1,0:T(8,128)}, u32[]{:S(2)}) copy-start(f32[512,128]{1,0:T(8,128)} %param.8) | copy-start | bytes 786436
  31.0 15.2 %collective-permute-start.13 = (bf16[1024,128]{1,0:T(8,128)(2,1)}, bf16[1024,128]{1,0:T(8,128)(2,1)S(1)}, u32[]{:S(2)}, u32[]{:S(2)}) collective-permute-start(bf16[1024,128]{1,0:T(8,128)(2,1)} %get-tuple-element.23), channel_id=1, source_target_pairs={{0,8},{4,12},{8,0},{12,4},{16,24},{20,28},{24,16},{28,20},{1,9},{5... | collective-permute-start | bytes 786440 | tf_op jit(solution)/shard_map/ppermute | solution.py:152
  32.5 16.3 %collective-permute-start.14 = (bf16[1024,128]{1,0:T(8,128)(2,1)}, bf16[1024,128]{1,0:T(8,128)(2,1)S(1)}, u32[]{:S(2)}, u32[]{:S(2)}) collective-permute-start(bf16[1024,128]{1,0:T(8,128)(2,1)} %get-tuple-element.24), channel_id=1, source_target_pairs={{0,16},{4,20},{8,24},{12,28},{16,0},{20,4},{24,8},{28,12},{1,17},{... | collective-permute-start | bytes 786440 | tf_op jit(solution)/shard_map/ppermute | solution.py:152
  36.4 12.3 %collective-permute-start.15 = (bf16[1024,128]{1,0:T(8,128)(2,1)}, bf16[1024,128]{1,0:T(8,128)(2,1)S(1)}, u32[]{:S(2)}, u32[]{:S(2)}) collective-permute-start(bf16[1024,128]{1,0:T(8,128)(2,1)} %get-tuple-element.25), channel_id=1, source_target_pairs={{0,24},{4,28},{8,16},{12,20},{16,8},{20,12},{24,0},{28,4},{1,25},{... | collective-permute-start | bytes 786440 | tf_op jit(solution)/shard_map/ppermute | solution.py:152
  37.1 14.3 %collective-permute-start.7 = (bf16[512,128]{1,0:T(8,128)(2,1)}, bf16[512,128]{1,0:T(8,128)(2,1)S(1)}, u32[]{:S(2)}, u32[]{:S(2)}) collective-permute-start(bf16[512,128]{1,0:T(8,128)(2,1)} %get-tuple-element.19), channel_id=1, source_target_pairs={{0,1},{1,2},{2,3},{3,0},{4,5},{5,6},{6,7},{7,4},{8,9},{9,10},{10,1... | collective-permute-start | bytes 393224 | tf_op jit(solution)/shard_map/ppermute | solution.py:132
  42.1 11.8 %collective-permute-start.8 = (bf16[512,128]{1,0:T(8,128)(2,1)}, bf16[512,128]{1,0:T(8,128)(2,1)S(1)}, u32[]{:S(2)}, u32[]{:S(2)}) collective-permute-start(bf16[512,128]{1,0:T(8,128)(2,1)} %get-tuple-element.20), channel_id=1, source_target_pairs={{0,2},{1,3},{2,0},{3,1},{4,6},{5,7},{6,4},{7,5},{8,10},{9,11},{10,... | collective-permute-start | bytes 393224 | tf_op jit(solution)/shard_map/ppermute | solution.py:132
  46.2 7.9 %collective-permute-start.9 = (bf16[512,128]{1,0:T(8,128)(2,1)}, bf16[512,128]{1,0:T(8,128)(2,1)S(1)}, u32[]{:S(2)}, u32[]{:S(2)}) collective-permute-start(bf16[512,128]{1,0:T(8,128)(2,1)} %get-tuple-element.21), channel_id=1, source_target_pairs={{0,3},{1,0},{2,1},{3,2},{4,7},{5,4},{6,5},{7,6},{8,11},{9,8},{10,9... | collective-permute-start | bytes 393224 | tf_op jit(solution)/shard_map/ppermute | solution.py:132
  49.9 10.7 %collective-permute-start.16 = (f32[512,128]{1,0:T(8,128)S(1)}, f32[512,128]{1,0:T(8,128)S(1)}, u32[]{:S(2)}, u32[]{:S(2)}) collective-permute-start(f32[512,128]{1,0:T(8,128)S(1)} %slice.17), channel_id=1, source_target_pairs={{0,4},{4,0},{8,12},{12,8},{16,20},{20,16},{24,28},{28,24},{1,5},{5... | collective-permute-start | bytes 786440 | tf_op jit(solution)/shard_map/ppermute | solution.py:155
  55.2 8.7 %collective-permute-start.12 = (bf16[512,128]{1,0:T(8,128)(2,1)S(1)}, bf16[512,128]{1,0:T(8,128)(2,1)S(1)}, u32[]{:S(2)}, u32[]{:S(2)}) collective-permute-start(bf16[512,128]{1,0:T(8,128)(2,1)S(1)} %fusion.9.refs_0_), channel_id=1, source_target_pairs={{0,3},{1,0},{2,1},{3,2},{4,7},{5,4},{6,5},{7,6},{8,11},{9,8},{10,9... | collective-permute-start | bytes 393224 | tf_op jit(solution)/shard_map/ppermute | solution.py:125
  60.0 11.5 %collective-permute-start.11 = (bf16[512,128]{1,0:T(8,128)(2,1)S(1)}, bf16[512,128]{1,0:T(8,128)(2,1)S(1)}, u32[]{:S(2)}, u32[]{:S(2)}) collective-permute-start(bf16[512,128]{1,0:T(8,128)(2,1)S(1)} %fusion.9.refs_0_), channel_id=1, source_target_pairs={{0,2},{1,3},{2,0},{3,1},{4,6},{5,7},{6,4},{7,5},{8,10},{9,11},{10,... | collective-permute-start | bytes 393224 | tf_op jit(solution)/shard_map/ppermute | solution.py:125
  60.0 13.3 %collective-permute-start.10 = (bf16[512,128]{1,0:T(8,128)(2,1)S(1)}, bf16[512,128]{1,0:T(8,128)(2,1)S(1)}, u32[]{:S(2)}, u32[]{:S(2)}) collective-permute-start(bf16[512,128]{1,0:T(8,128)(2,1)S(1)} %fusion.9.refs_0_), channel_id=1, source_target_pairs={{0,1},{1,2},{2,3},{3,0},{4,5},{5,6},{6,7},{7,4},{8,9},{9,10},{10,1... | collective-permute-start | bytes 393224 | tf_op jit(solution)/shard_map/ppermute | solution.py:125
  60.7 12.6 %collective-permute-start.23 = (bf16[512,128]{1,0:T(8,128)(2,1)S(1)}, bf16[512,128]{1,0:T(8,128)(2,1)S(1)}, u32[]{:S(2)}, u32[]{:S(2)}) collective-permute-start(bf16[512,128]{1,0:T(8,128)(2,1)S(1)} %fusion.8.refs_4_), channel_id=1, source_target_pairs={{0,28},{4,24},{8,20},{12,16},{16,12},{20,8},{24,4},{28,0},{1,29},{... | collective-permute-start | bytes 393224 | tf_op jit(solution)/shard_map/ppermute | solution.py:162
  60.8 13.0 %collective-permute-start.22 = (bf16[512,128]{1,0:T(8,128)(2,1)S(1)}, bf16[512,128]{1,0:T(8,128)(2,1)S(1)}, u32[]{:S(2)}, u32[]{:S(2)}) collective-permute-start(bf16[512,128]{1,0:T(8,128)(2,1)S(1)} %fusion.8.refs_4_), channel_id=1, source_target_pairs={{0,24},{4,28},{8,16},{12,20},{16,8},{20,12},{24,0},{28,4},{1,25},{... | collective-permute-start | bytes 393224 | tf_op jit(solution)/shard_map/ppermute | solution.py:162
  63.8 11.3 %collective-permute-start.21 = (bf16[512,128]{1,0:T(8,128)(2,1)S(1)}, bf16[512,128]{1,0:T(8,128)(2,1)S(1)}, u32[]{:S(2)}, u32[]{:S(2)}) collective-permute-start(bf16[512,128]{1,0:T(8,128)(2,1)S(1)} %fusion.8.refs_4_), channel_id=1, source_target_pairs={{0,20},{4,16},{8,28},{12,24},{16,4},{20,0},{24,12},{28,8},{1,21},{... | collective-permute-start | bytes 393224 | tf_op jit(solution)/shard_map/ppermute | solution.py:162
  71.5 5.0 %collective-permute-start.20 = (bf16[512,128]{1,0:T(8,128)(2,1)S(1)}, bf16[512,128]{1,0:T(8,128)(2,1)S(1)}, u32[]{:S(2)}, u32[]{:S(2)}) collective-permute-start(bf16[512,128]{1,0:T(8,128)(2,1)S(1)} %fusion.8.refs_4_), channel_id=1, source_target_pairs={{0,16},{4,20},{8,24},{12,28},{16,0},{20,4},{24,8},{28,12},{1,17},{... | collective-permute-start | bytes 393224 | tf_op jit(solution)/shard_map/ppermute | solution.py:162
  73.3 5.8 %collective-permute-start.19 = (bf16[512,128]{1,0:T(8,128)(2,1)S(1)}, bf16[512,128]{1,0:T(8,128)(2,1)S(1)}, u32[]{:S(2)}, u32[]{:S(2)}) collective-permute-start(bf16[512,128]{1,0:T(8,128)(2,1)S(1)} %fusion.8.refs_4_), channel_id=1, source_target_pairs={{0,12},{4,8},{8,4},{12,0},{16,28},{20,24},{24,20},{28,16},{1,13},{... | collective-permute-start | bytes 393224 | tf_op jit(solution)/shard_map/ppermute | solution.py:162
  73.3 6.7 %collective-permute-start.18 = (bf16[512,128]{1,0:T(8,128)(2,1)S(1)}, bf16[512,128]{1,0:T(8,128)(2,1)S(1)}, u32[]{:S(2)}, u32[]{:S(2)}) collective-permute-start(bf16[512,128]{1,0:T(8,128)(2,1)S(1)} %fusion.8.refs_4_), channel_id=1, source_target_pairs={{0,8},{4,12},{8,0},{12,4},{16,24},{20,28},{24,16},{28,20},{1,9},{5... | collective-permute-start | bytes 393224 | tf_op jit(solution)/shard_map/ppermute | solution.py:162
  73.8 6.2 %collective-permute-start.17 = (bf16[512,128]{1,0:T(8,128)(2,1)S(1)}, bf16[512,128]{1,0:T(8,128)(2,1)S(1)}, u32[]{:S(2)}, u32[]{:S(2)}) collective-permute-start(bf16[512,128]{1,0:T(8,128)(2,1)S(1)} %fusion.8.refs_4_), channel_id=1, source_target_pairs={{0,4},{4,0},{8,12},{12,8},{16,20},{20,16},{24,28},{28,24},{1,5},{5... | collective-permute-start | bytes 393224 | tf_op jit(solution)/shard_map/ppermute | solution.py:162
  88.2 14.2 %collective-permute-start.27 = (bf16[1024,128]{1,0:T(8,128)(2,1)}, bf16[1024,128]{1,0:T(8,128)(2,1)S(1)}, u32[]{:S(2)}, u32[]{:S(2)}) collective-permute-start(bf16[1024,128]{1,0:T(8,128)(2,1)} %get-tuple-element.31), channel_id=1, source_target_pairs={{0,8},{4,12},{8,0},{12,4},{16,24},{20,28},{24,16},{28,20},{1,9},{5... | collective-permute-start | bytes 786440 | tf_op jit(solution)/shard_map/ppermute | solution.py:152
  90.2 15.1 %collective-permute-start.28 = (bf16[1024,128]{1,0:T(8,128)(2,1)}, bf16[1024,128]{1,0:T(8,128)(2,1)S(1)}, u32[]{:S(2)}, u32[]{:S(2)}) collective-permute-start(bf16[1024,128]{1,0:T(8,128)(2,1)} %get-tuple-element.32), channel_id=1, source_target_pairs={{0,16},{4,20},{8,24},{12,28},{16,0},{20,4},{24,8},{28,12},{1,17},{... | collective-permute-start | bytes 786440 | tf_op jit(solution)/shard_map/ppermute | solution.py:152
  93.9 11.4 %collective-permute-start.29 = (bf16[1024,128]{1,0:T(8,128)(2,1)}, bf16[1024,128]{1,0:T(8,128)(2,1)S(1)}, u32[]{:S(2)}, u32[]{:S(2)}) collective-permute-start(bf16[1024,128]{1,0:T(8,128)(2,1)} %get-tuple-element.33), channel_id=1, source_target_pairs={{0,24},{4,28},{8,16},{12,20},{16,8},{20,12},{24,0},{28,4},{1,25},{... | collective-permute-start | bytes 786440 | tf_op jit(solution)/shard_map/ppermute | solution.py:152
  93.9 14.4 %collective-permute-start.24 = (bf16[512,128]{1,0:T(8,128)(2,1)}, bf16[512,128]{1,0:T(8,128)(2,1)S(1)}, u32[]{:S(2)}, u32[]{:S(2)}) collective-permute-start(bf16[512,128]{1,0:T(8,128)(2,1)} %get-tuple-element.27), channel_id=1, source_target_pairs={{0,1},{1,2},{2,3},{3,0},{4,5},{5,6},{6,7},{7,4},{8,9},{9,10},{10,1... | collective-permute-start | bytes 393224 | tf_op jit(solution)/shard_map/ppermute | solution.py:132
  100.3 10.4 %collective-permute-start.25 = (bf16[512,128]{1,0:T(8,128)(2,1)}, bf16[512,128]{1,0:T(8,128)(2,1)S(1)}, u32[]{:S(2)}, u32[]{:S(2)}) collective-permute-start(bf16[512,128]{1,0:T(8,128)(2,1)} %get-tuple-element.28), channel_id=1, source_target_pairs={{0,2},{1,3},{2,0},{3,1},{4,6},{5,7},{6,4},{7,5},{8,10},{9,11},{10,... | collective-permute-start | bytes 393224 | tf_op jit(solution)/shard_map/ppermute | solution.py:132
  102.4 9.2 %collective-permute-start.26 = (bf16[512,128]{1,0:T(8,128)(2,1)}, bf16[512,128]{1,0:T(8,128)(2,1)S(1)}, u32[]{:S(2)}, u32[]{:S(2)}) collective-permute-start(bf16[512,128]{1,0:T(8,128)(2,1)} %get-tuple-element.29), channel_id=1, source_target_pairs={{0,3},{1,0},{2,1},{3,2},{4,7},{5,4},{6,5},{7,6},{8,11},{9,8},{10,9... | collective-permute-start | bytes 393224 | tf_op jit(solution)/shard_map/ppermute | solution.py:132
  106.4 6.9 %collective-permute-start.30 = (f32[512,128]{1,0:T(8,128)S(1)}, f32[512,128]{1,0:T(8,128)S(1)}, u32[]{:S(2)}, u32[]{:S(2)}) collective-permute-start(f32[512,128]{1,0:T(8,128)S(1)} %slice.19), channel_id=1, source_target_pairs={{0,4},{4,0},{8,12},{12,8},{16,20},{20,16},{24,28},{28,24},{1,5},{5... | collective-permute-start | bytes 786440 | tf_op jit(solution)/shard_map/ppermute | solution.py:155
  (22 other events, 215.7 us)

commit v12 on v11

--- a/solution.py
+++ b/solution.py
@@ -192,7 +192,7 @@
     rows = rotate_index(tile_row[0, 0], me_col, n_col, per_run)
     if paired(n_row):
         cols = pair_index(tile_col[0, 0], me_row, per_run)
-        gathers = (gather_paired, gather_xor)
+        gathers = (gather_paired, gather_paired)
         scatters = (scatter_paired, scatter_paired)
         splits = (n_row // 2, n_row // 2)
     else:

time: 116 us -> 121 us (1.043); the launches traced: 114 us -> 123 us
  starting transfers between devices: 60 us -> 28.8 us
  Pallas kernels: 14.8 us -> 37.5 us
  waiting for transfers between devices: 27.4 us -> 44.6 us
    pallas_call x2, Pallas kernels: 14.8 us -> 37.5 us  [tile_sweep(): pl.pallas_call(functools.partial(sweep_kernel, tile, group, len(emb_piece...]
    ppermute x6, starting transfers between devices: 23 us -> 3.93 us  [scatter_rotated(): lax.ppermute(chunks[(n - s) % n], axis, [(i, (i + s) % n) for i in range(...]
    ppermute x6, waiting for transfers between devices: 0.02 us -> 15.4 us  [scatter_paired(): got = lax.ppermute(blocks[b], axis, [(i, i ^ 2 * b) for i in range(n)])]
    ppermute x7 -> x0, starting transfers between devices: 6.47 us -> none  [gather_xor(): pieces.append(lax.ppermute(x, axis, [(i, i ^ p) for i in range(n)]))]
    ppermute x6, waiting for transfers between devices: 6.02 us -> 11.3 us  [scatter_rotated(): lax.ppermute(chunks[(n - s) % n], axis, [(i, (i + s) % n) for i in range(...]
    ppermute x7 -> x0, waiting for transfers between devices: 4.88 us -> none  [gather_xor(): pieces.append(lax.ppermute(x, axis, [(i, i ^ p) for i in range(n)]))]
    ppermute x6, starting transfers between devices: 11.9 us -> 7 us  [scatter_paired(): got = lax.ppermute(blocks[b], axis, [(i, i ^ 2 * b) for i in range(n)])]
    ppermute x3 -> x6, starting transfers between devices: 3.55 us -> 7.11 us  [gather_paired(): blocks.append(lax.ppermute(pair, axis, [(i, i ^ 2 * b) for i in range(n)]))]
  transfers between devices with their start and end apart: 31 -> 28, of which waited for: 12 -> 14; matrix products, arithmetic and copies ran while one was open for 6% -> 5% of each run, Pallas kernels for 0% -> 0%
where the time goes in v12:
time: 121 us; the launch traced here: 123 us
  waiting for transfers between devices  44.6 us (37%)
  Pallas kernels  37.5 us (31%)
  starting transfers between devices  28.8 us (24%)
  other arithmetic  8.99 us (7%)
  between operations  1.54 us (1%)
  local copies, waits for them, and re-layouts  1.47 us (1%)
    pallas_call x2, Pallas kernels, tile_sweep(): pl.pallas_call(functools.partial(sweep_kernel, tile, group, len(emb_piece...  37.5 us
    ppermute x6, waiting for transfers between devices, scatter_paired(): got = lax.ppermute(blocks[b], axis, [(i, i ^ 2 * b) for i in range(n)])  15.4 us
    ppermute x6, waiting for transfers between devices, gather_rotated(): pieces.append(lax.ppermute(x, axis, [(i, (i + s) % n) for i in range(n)]))  14.9 us
    ppermute x6, waiting for transfers between devices, scatter_rotated(): lax.ppermute(chunks[(n - s) % n], axis, [(i, (i + s) % n) for i in range(...  11.3 us
    ppermute x6, starting transfers between devices, gather_rotated(): pieces.append(lax.ppermute(x, axis, [(i, (i + s) % n) for i in range(n)]))  10.1 us
    ppermute x6, starting transfers between devices, gather_paired(): blocks.append(lax.ppermute(pair, axis, [(i, i ^ 2 * b) for i in range(n)]))  7.11 us
    ppermute x6, starting transfers between devices, scatter_paired(): got = lax.ppermute(blocks[b], axis, [(i, i ^ 2 * b) for i in range(n)])  7 us
    ppermute x6, starting transfers between devices, scatter_rotated(): lax.ppermute(chunks[(n - s) % n], axis, [(i, (i + s) % n) for i in range(...  3.93 us
  transfers between devices with their start and end apart: 28, of which 14 were waited for; matrix products, arithmetic and copies ran while one was open for 5% of the time, Pallas kernels for 0%

profile of v12, /device:TPU:0, one launch (start us, length us, event | category | flops | bytes accessed | tf_op | source)
XLA Modules:
  0.0 122.9 jit_solution(9896127128837485119)
XLA Ops:
  0.6 1.0 convert_element_type.61
  2.1 1.0 convert_element_type.60.refs_0_
  3.1 4.7 %collective-permute-start.2 = (bf16[512,128]{1,0:T(8,128)(2,1)S(1)}, bf16[512,128]{1,0:T(8,128)(2,1)S(1)}, u32[]{:S(2)}, u32[]{:S(2)}) collective-permute-start(bf16[512,128]{1,0:T(8,128)(2,1)S(1)} %convert_element_type.60.refs_0_), channel_id=1, source_target_pairs={{0,3},{1,0},{2,1},{3,2},{4,7},{5,4},{6,5},{7,6},{8,11},{9,8},{10,9... | collective-permute-start | bytes 393224 | tf_op jit(solution)/shard_map/ppermute | solution.py:125
  7.8 2.5 %collective-permute-start.6 = (bf16[1024,128]{1,0:T(8,128)(2,1)S(1)}, bf16[1024,128]{1,0:T(8,128)(2,1)S(1)}, u32[]{:S(2)}, u32[]{:S(2)}) collective-permute-start(bf16[1024,128]{1,0:T(8,128)(2,1)S(1)} %pad_maximum_fusion.refs_4_), channel_id=1, source_target_pairs={{0,24},{4,28},{8,16},{12,20},{16,8},{20,12},{24,0},{28,4},{1,25},{... | collective-permute-start | bytes 786440 | tf_op jit(solution)/shard_map/ppermute | solution.py:145
  12.0 1.1 collective-permute-start
  13.1 1.2 fusion.4
  14.3 6.2 %collective-permute-done.1.refs_2_ = bf16[512,128]{1,0:T(8,128)(2,1)S(1)} collective-permute-done((bf16[512,128]{1,0:T(8,128)(2,1)S(1)}, bf16[512,128]{1,0:T(8,128)(2,1)S(1)}, u32[]{:S(2)}, u32[]{:S(2)}) %collective-permute-start.1) | collective-permute-done | bytes 131104 | tf_op jit(solution)/shard_map/ppermute | solution.py:125
  20.6 2.2 %collective-permute-done.5.refs_6_ = bf16[1024,128]{1,0:T(8,128)(2,1)S(1)} collective-permute-done((bf16[1024,128]{1,0:T(8,128)(2,1)S(1)}, bf16[1024,128]{1,0:T(8,128)(2,1)S(1)}, u32[]{:S(2)}, u32[]{:S(2)}) %collective-permute-start.5) | collective-permute-done | bytes 262176 | tf_op jit(solution)/shard_map/ppermute | solution.py:145
  23.6 18.7 %shard_map.86 = (bf16[512,128]{1,0:T(8,128)(2,1)}, bf16[512,128]{1,0:T(8,128)(2,1)}, bf16[512,128]{1,0:T(8,128)(2,1)}, bf16[512,128]{1,0:T(8,128)(2,1)}, bf16[10...) custom-call(s32[64]{0:T(128)} %get-tuple-element.34.rows_ref, ...), custom_call_target="tpu_custom_call" | custom-call | flops 3221225472 | bytes 21495808 | tf_op jit(solution)/shard_map/pallas_call | solution.py:107
  42.4 1.7 %collective-permute-start.14 = (bf16[1024,128]{1,0:T(8,128)(2,1)}, bf16[1024,128]{1,0:T(8,128)(2,1)S(1)}, u32[]{:S(2)}, u32[]{:S(2)}) collective-permute-start(bf16[1024,128]{1,0:T(8,128)(2,1)} %get-tuple-element.24), channel_id=1, source_target_pairs={{0,16},{4,20},{8,24},{12,28},{16,0},{20,4},{24,8},{28,12},{1,17},{... | collective-permute-start | bytes 786440 | tf_op jit(solution)/shard_map/ppermute | solution.py:152
  44.1 1.8 %collective-permute-start.15 = (bf16[1024,128]{1,0:T(8,128)(2,1)}, bf16[1024,128]{1,0:T(8,128)(2,1)S(1)}, u32[]{:S(2)}, u32[]{:S(2)}) collective-permute-start(bf16[1024,128]{1,0:T(8,128)(2,1)} %get-tuple-element.25), channel_id=1, source_target_pairs={{0,24},{4,28},{8,16},{12,20},{16,8},{20,12},{24,0},{28,4},{1,25},{... | collective-permute-start | bytes 786440 | tf_op jit(solution)/shard_map/ppermute | solution.py:152
  45.8 4.8 %collective-permute-done.13 = bf16[1024,128]{1,0:T(8,128)(2,1)S(1)} collective-permute-done((bf16[1024,128]{1,0:T(8,128)(2,1)}, bf16[1024,128]{1,0:T(8,128)(2,1)S(1)}, u32[]{:S(2)}, u32[]{:S(2)}) %collective-permute-start.13) | collective-permute-done | bytes 262176 | tf_op jit(solution)/shard_map/ppermute | solution.py:152
  50.7 2.9 %collective-permute-done.14 = bf16[1024,128]{1,0:T(8,128)(2,1)S(1)} collective-permute-done((bf16[1024,128]{1,0:T(8,128)(2,1)}, bf16[1024,128]{1,0:T(8,128)(2,1)S(1)}, u32[]{:S(2)}, u32[]{:S(2)}) %collective-permute-start.14) | collective-permute-done | bytes 262176 | tf_op jit(solution)/shard_map/ppermute | solution.py:152
  53.6 1.1 convert_add_fusion.1
  54.9 3.7 %collective-permute-start.9 = (bf16[512,128]{1,0:T(8,128)(2,1)}, bf16[512,128]{1,0:T(8,128)(2,1)S(1)}, u32[]{:S(2)}, u32[]{:S(2)}) collective-permute-start(bf16[512,128]{1,0:T(8,128)(2,1)} %get-tuple-element.21), channel_id=1, source_target_pairs={{0,3},{1,0},{2,1},{3,2},{4,7},{5,4},{6,5},{7,6},{8,11},{9,8},{10,9... | collective-permute-start | bytes 393224 | tf_op jit(solution)/shard_map/ppermute | solution.py:132
  58.8 4.5 %collective-permute-done.7 = bf16[512,128]{1,0:T(8,128)(2,1)S(1)} collective-permute-done((bf16[512,128]{1,0:T(8,128)(2,1)}, bf16[512,128]{1,0:T(8,128)(2,1)S(1)}, u32[]{:S(2)}, u32[]{:S(2)}) %collective-permute-start.7) | collective-permute-done | bytes 131104 | tf_op jit(solution)/shard_map/ppermute | solution.py:132
  63.3 4.7 %collective-permute-done.8 = bf16[512,128]{1,0:T(8,128)(2,1)S(1)} collective-permute-done((bf16[512,128]{1,0:T(8,128)(2,1)}, bf16[512,128]{1,0:T(8,128)(2,1)S(1)}, u32[]{:S(2)}, u32[]{:S(2)}) %collective-permute-start.8) | collective-permute-done | bytes 131104 | tf_op jit(solution)/shard_map/ppermute | solution.py:132
  68.0 1.0 fusion.9.refs_0_
  69.0 3.0 %collective-permute-start.12 = (bf16[512,128]{1,0:T(8,128)(2,1)S(1)}, bf16[512,128]{1,0:T(8,128)(2,1)S(1)}, u32[]{:S(2)}, u32[]{:S(2)}) collective-permute-start(bf16[512,128]{1,0:T(8,128)(2,1)S(1)} %fusion.9.refs_0_), channel_id=1, source_target_pairs={{0,3},{1,0},{2,1},{3,2},{4,7},{5,4},{6,5},{7,6},{8,11},{9,8},{10,9... | collective-permute-start | bytes 393224 | tf_op jit(solution)/shard_map/ppermute | solution.py:125
  72.0 2.2 %collective-permute-start.20 = (bf16[1024,128]{1,0:T(8,128)(2,1)S(1)}, bf16[1024,128]{1,0:T(8,128)(2,1)S(1)}, u32[]{:S(2)}, u32[]{:S(2)}) collective-permute-start(bf16[1024,128]{1,0:T(8,128)(2,1)S(1)} %pad_maximum_fusion.1.refs_4_), channel_id=1, source_target_pairs={{0,24},{4,28},{8,16},{12,20},{16,8},{20,12},{24,0},{28,4},{1,25},{... | collective-permute-start | bytes 786440 | tf_op jit(solution)/shard_map/ppermute | solution.py:145
  74.3 1.0 collective-permute-start.19
  75.6 1.3 %collective-permute-start.11 = (bf16[512,128]{1,0:T(8,128)(2,1)S(1)}, bf16[512,128]{1,0:T(8,128)(2,1)S(1)}, u32[]{:S(2)}, u32[]{:S(2)}) collective-permute-start(bf16[512,128]{1,0:T(8,128)(2,1)S(1)} %fusion.9.refs_0_), channel_id=1, source_target_pairs={{0,2},{1,3},{2,0},{3,1},{4,6},{5,7},{6,4},{7,5},{8,10},{9,11},{10,... | collective-permute-start | bytes 393224 | tf_op jit(solution)/shard_map/ppermute | solution.py:125
  76.9 8.6 %collective-permute-done.11.refs_2_ = bf16[512,128]{1,0:T(8,128)(2,1)S(1)} collective-permute-done((bf16[512,128]{1,0:T(8,128)(2,1)S(1)}, bf16[512,128]{1,0:T(8,128)(2,1)S(1)}, u32[]{:S(2)}, u32[]{:S(2)}) %collective-permute-start.11) | collective-permute-done | bytes 131104 | tf_op jit(solution)/shard_map/ppermute | solution.py:125
  86.9 18.8 %shard_map.87 = (bf16[512,128]{1,0:T(8,128)(2,1)}, bf16[512,128]{1,0:T(8,128)(2,1)}, bf16[512,128]{1,0:T(8,128)(2,1)}, bf16[512,128]{1,0:T(8,128)(2,1)}, bf16[10...) custom-call(s32[64]{0:T(128)} %get-tuple-element.34.rows_ref, ...), custom_call_target="tpu_custom_call" | custom-call | flops 3221225472 | bytes 21495808 | tf_op jit(solution)/shard_map/pallas_call | solution.py:107
  105.7 1.7 %collective-permute-start.25 = (bf16[1024,128]{1,0:T(8,128)(2,1)}, bf16[1024,128]{1,0:T(8,128)(2,1)S(1)}, u32[]{:S(2)}, u32[]{:S(2)}) collective-permute-start(bf16[1024,128]{1,0:T(8,128)(2,1)} %get-tuple-element.32), channel_id=1, source_target_pairs={{0,16},{4,20},{8,24},{12,28},{16,0},{20,4},{24,8},{28,12},{1,17},{... | collective-permute-start | bytes 786440 | tf_op jit(solution)/shard_map/ppermute | solution.py:152
  107.4 1.8 %collective-permute-start.26 = (bf16[1024,128]{1,0:T(8,128)(2,1)}, bf16[1024,128]{1,0:T(8,128)(2,1)S(1)}, u32[]{:S(2)}, u32[]{:S(2)}) collective-permute-start(bf16[1024,128]{1,0:T(8,128)(2,1)} %get-tuple-element.33), channel_id=1, source_target_pairs={{0,24},{4,28},{8,16},{12,20},{16,8},{20,12},{24,0},{28,4},{1,25},{... | collective-permute-start | bytes 786440 | tf_op jit(solution)/shard_map/ppermute | solution.py:152
  109.3 4.8 %collective-permute-done.24 = bf16[1024,128]{1,0:T(8,128)(2,1)S(1)} collective-permute-done((bf16[1024,128]{1,0:T(8,128)(2,1)}, bf16[1024,128]{1,0:T(8,128)(2,1)S(1)}, u32[]{:S(2)}, u32[]{:S(2)}) %collective-permute-start.24) | collective-permute-done | bytes 262176 | tf_op jit(solution)/shard_map/ppermute | solution.py:152
  114.1 2.9 %collective-permute-done.25 = bf16[1024,128]{1,0:T(8,128)(2,1)S(1)} collective-permute-done((bf16[1024,128]{1,0:T(8,128)(2,1)}, bf16[1024,128]{1,0:T(8,128)(2,1)S(1)}, u32[]{:S(2)}, u32[]{:S(2)}) %collective-permute-start.25) | collective-permute-done | bytes 262176 | tf_op jit(solution)/shard_map/ppermute | solution.py:152
  116.9 1.1 convert_add_fusion
  118.1 1.5 %collective-permute-done.22 = bf16[512,128]{1,0:T(8,128)(2,1)S(1)} collective-permute-done((bf16[512,128]{1,0:T(8,128)(2,1)}, bf16[512,128]{1,0:T(8,128)(2,1)S(1)}, u32[]{:S(2)}, u32[]{:S(2)}) %collective-permute-start.22) | collective-permute-done | bytes 131104 | tf_op jit(solution)/shard_map/ppermute | solution.py:132
  120.3 1.8 %multiply_add_fusion = f32[512,128]{1,0:T(8,128)} fusion(bf16[512,128]{1,0:T(8,128)(2,1)S(1)} %collective-permute-done.23, bf16[512,128]{1,0:T(8,128)(2,1)S(1)} %collective-permute-done.22, bf16[512,128]{1,0:T(8,128)(2,1)S(1)} %collective-permute-done.21, bf16[512,128]{1,0:T(8,128)(2,1)} %get-tuple-element.26, f32[512,128]{1,0:T(8,128)S(1)} %copy-done, ...), kind=kLoop, calls=%fused_computation.10 | loop fusion | flops 1179648 | bytes 1572864 | tf_op jit(solution)/shard_map/add | solution.py:213
  122.0 0.8 fusion.1
  (77 shorter events, 5.3 us)
Async XLA Ops:
  1.6 6.2 %collective-permute-start.3 = (bf16[512,128]{1,0:T(8,128)(2,1)S(1)}, bf16[512,128]{1,0:T(8,128)(2,1)S(1)}, u32[]{:S(2)}, u32[]{:S(2)}) collective-permute-start(bf16[512,128]{1,0:T(8,128)(2,1)S(1)} %convert_element_type.61), channel_id=1, source_target_pairs={{0,4},{4,0},{8,12},{12,8},{16,20},{20,16},{24,28},{28,24},{1,5},{5... | collective-permute-start | bytes 393224 | tf_op jit(solution)/shard_map/ppermute | solution.py:142
  3.1 19.8 %copy-start.4 = (bf16[512,128]{1,0:T(8,128)(2,1)}, bf16[512,128]{1,0:T(8,128)(2,1)S(1)}, u32[]{:S(2)}) copy-start(bf16[512,128]{1,0:T(8,128)(2,1)S(1)} %convert_element_type.60.refs_0_) | copy-start | bytes 393220
  3.1 8.9 %collective-permute-start.2 = (bf16[512,128]{1,0:T(8,128)(2,1)S(1)}, bf16[512,128]{1,0:T(8,128)(2,1)S(1)}, u32[]{:S(2)}, u32[]{:S(2)}) collective-permute-start(bf16[512,128]{1,0:T(8,128)(2,1)S(1)} %convert_element_type.60.refs_0_), channel_id=1, source_target_pairs={{0,3},{1,0},{2,1},{3,2},{4,7},{5,4},{6,5},{7,6},{8,11},{9,8},{10,9... | collective-permute-start | bytes 393224 | tf_op jit(solution)/shard_map/ppermute | solution.py:125
  7.8 12.8 %collective-permute-start.6 = (bf16[1024,128]{1,0:T(8,128)(2,1)S(1)}, bf16[1024,128]{1,0:T(8,128)(2,1)S(1)}, u32[]{:S(2)}, u32[]{:S(2)}) collective-permute-start(bf16[1024,128]{1,0:T(8,128)(2,1)S(1)} %pad_maximum_fusion.refs_4_), channel_id=1, source_target_pairs={{0,24},{4,28},{8,16},{12,20},{16,8},{20,12},{24,0},{28,4},{1,25},{... | collective-permute-start | bytes 786440 | tf_op jit(solution)/shard_map/ppermute | solution.py:145
  10.3 12.5 %collective-permute-start.5 = (bf16[1024,128]{1,0:T(8,128)(2,1)S(1)}, bf16[1024,128]{1,0:T(8,128)(2,1)S(1)}, u32[]{:S(2)}, u32[]{:S(2)}) collective-permute-start(bf16[1024,128]{1,0:T(8,128)(2,1)S(1)} %pad_maximum_fusion.refs_4_), channel_id=1, source_target_pairs={{0,16},{4,20},{8,24},{12,28},{16,0},{20,4},{24,8},{28,12},{1,17},{... | collective-permute-start | bytes 786440 | tf_op jit(solution)/shard_map/ppermute | solution.py:145
  10.8 12.1 %collective-permute-start.4 = (bf16[1024,128]{1,0:T(8,128)(2,1)S(1)}, bf16[1024,128]{1,0:T(8,128)(2,1)S(1)}, u32[]{:S(2)}, u32[]{:S(2)}) collective-permute-start(bf16[1024,128]{1,0:T(8,128)(2,1)S(1)} %pad_maximum_fusion.refs_4_), channel_id=1, source_target_pairs={{0,8},{4,12},{8,0},{12,4},{16,24},{20,28},{24,16},{28,20},{1,9},{5... | collective-permute-start | bytes 786440 | tf_op jit(solution)/shard_map/ppermute | solution.py:145
  11.4 9.2 %collective-permute-start.1 = (bf16[512,128]{1,0:T(8,128)(2,1)S(1)}, bf16[512,128]{1,0:T(8,128)(2,1)S(1)}, u32[]{:S(2)}, u32[]{:S(2)}) collective-permute-start(bf16[512,128]{1,0:T(8,128)(2,1)S(1)} %convert_element_type.60.refs_0_), channel_id=1, source_target_pairs={{0,2},{1,3},{2,0},{3,1},{4,6},{5,7},{6,4},{7,5},{8,10},{9,11},{10,... | collective-permute-start | bytes 393224 | tf_op jit(solution)/shard_map/ppermute | solution.py:125
  12.0 8.5 %collective-permute-start = (bf16[512,128]{1,0:T(8,128)(2,1)S(1)}, bf16[512,128]{1,0:T(8,128)(2,1)S(1)}, u32[]{:S(2)}, u32[]{:S(2)}) collective-permute-start(bf16[512,128]{1,0:T(8,128)(2,1)S(1)} %convert_element_type.60.refs_0_), channel_id=1, source_target_pairs={{0,1},{1,2},{2,3},{3,0},{4,5},{5,6},{6,7},{7,4},{8,9},{9,10},{10,1... | collective-permute-start | bytes 393224 | tf_op jit(solution)/shard_map/ppermute | solution.py:125
  23.6 35.0 %copy-start.1 = (f32[512,128]{1,0:T(8,128)S(1)}, f32[512,128]{1,0:T(8,128)}, u32[]{:S(2)}) copy-start(f32[512,128]{1,0:T(8,128)} %param.8) | copy-start | bytes 786436
  23.6 44.4 %copy-start = (f32[512,128]{1,0:T(8,128)S(1)}, f32[512,128]{1,0:T(8,128)}, u32[]{:S(2)}) copy-start(f32[512,128]{1,0:T(8,128)} %param.7) | copy-start | bytes 786436
  42.3 8.3 %collective-permute-start.13 = (bf16[1024,128]{1,0:T(8,128)(2,1)}, bf16[1024,128]{1,0:T(8,128)(2,1)S(1)}, u32[]{:S(2)}, u32[]{:S(2)}) collective-permute-start(bf16[1024,128]{1,0:T(8,128)(2,1)} %get-tuple-element.23), channel_id=1, source_target_pairs={{0,8},{4,12},{8,0},{12,4},{16,24},{20,28},{24,16},{28,20},{1,9},{5... | collective-permute-start | bytes 786440 | tf_op jit(solution)/shard_map/ppermute | solution.py:152
  42.4 11.2 %collective-permute-start.14 = (bf16[1024,128]{1,0:T(8,128)(2,1)}, bf16[1024,128]{1,0:T(8,128)(2,1)S(1)}, u32[]{:S(2)}, u32[]{:S(2)}) collective-permute-start(bf16[1024,128]{1,0:T(8,128)(2,1)} %get-tuple-element.24), channel_id=1, source_target_pairs={{0,16},{4,20},{8,24},{12,28},{16,0},{20,4},{24,8},{28,12},{1,17},{... | collective-permute-start | bytes 786440 | tf_op jit(solution)/shard_map/ppermute | solution.py:152
  44.1 9.5 %collective-permute-start.15 = (bf16[1024,128]{1,0:T(8,128)(2,1)}, bf16[1024,128]{1,0:T(8,128)(2,1)S(1)}, u32[]{:S(2)}, u32[]{:S(2)}) collective-permute-start(bf16[1024,128]{1,0:T(8,128)(2,1)} %get-tuple-element.25), channel_id=1, source_target_pairs={{0,24},{4,28},{8,16},{12,20},{16,8},{20,12},{24,0},{28,4},{1,25},{... | collective-permute-start | bytes 786440 | tf_op jit(solution)/shard_map/ppermute | solution.py:152
  54.7 4.0 %collective-permute-start.16 = (f32[512,128]{1,0:T(8,128)S(1)}, f32[512,128]{1,0:T(8,128)S(1)}, u32[]{:S(2)}, u32[]{:S(2)}) collective-permute-start(f32[512,128]{1,0:T(8,128)S(1)} %slice.17), channel_id=1, source_target_pairs={{0,4},{4,0},{8,12},{12,8},{16,20},{20,16},{24,28},{28,24},{1,5},{5... | collective-permute-start | bytes 786440 | tf_op jit(solution)/shard_map/ppermute | solution.py:155
  54.8 8.5 %collective-permute-start.7 = (bf16[512,128]{1,0:T(8,128)(2,1)}, bf16[512,128]{1,0:T(8,128)(2,1)S(1)}, u32[]{:S(2)}, u32[]{:S(2)}) collective-permute-start(bf16[512,128]{1,0:T(8,128)(2,1)} %get-tuple-element.19), channel_id=1, source_target_pairs={{0,1},{1,2},{2,3},{3,0},{4,5},{5,6},{6,7},{7,4},{8,9},{9,10},{10,1... | collective-permute-start | bytes 393224 | tf_op jit(solution)/shard_map/ppermute | solution.py:132
  54.8 13.2 %collective-permute-start.8 = (bf16[512,128]{1,0:T(8,128)(2,1)}, bf16[512,128]{1,0:T(8,128)(2,1)S(1)}, u32[]{:S(2)}, u32[]{:S(2)}) collective-permute-start(bf16[512,128]{1,0:T(8,128)(2,1)} %get-tuple-element.20), channel_id=1, source_target_pairs={{0,2},{1,3},{2,0},{3,1},{4,6},{5,7},{6,4},{7,5},{8,10},{9,11},{10,... | collective-permute-start | bytes 393224 | tf_op jit(solution)/shard_map/ppermute | solution.py:132
  54.9 13.1 %collective-permute-start.9 = (bf16[512,128]{1,0:T(8,128)(2,1)}, bf16[512,128]{1,0:T(8,128)(2,1)S(1)}, u32[]{:S(2)}, u32[]{:S(2)}) collective-permute-start(bf16[512,128]{1,0:T(8,128)(2,1)} %get-tuple-element.21), channel_id=1, source_target_pairs={{0,3},{1,0},{2,1},{3,2},{4,7},{5,4},{6,5},{7,6},{8,11},{9,8},{10,9... | collective-permute-start | bytes 393224 | tf_op jit(solution)/shard_map/ppermute | solution.py:132
  58.7 13.3 %collective-permute-start.17 = (bf16[512,128]{1,0:T(8,128)(2,1)S(1)}, bf16[512,128]{1,0:T(8,128)(2,1)S(1)}, u32[]{:S(2)}, u32[]{:S(2)}) collective-permute-start(bf16[512,128]{1,0:T(8,128)(2,1)S(1)} %fusion.8), channel_id=1, source_target_pairs={{0,4},{4,0},{8,12},{12,8},{16,20},{20,16},{24,28},{28,24},{1,5},{5... | collective-permute-start | bytes 393224 | tf_op jit(solution)/shard_map/ppermute | solution.py:142
  69.0 7.9 %collective-permute-start.12 = (bf16[512,128]{1,0:T(8,128)(2,1)S(1)}, bf16[512,128]{1,0:T(8,128)(2,1)S(1)}, u32[]{:S(2)}, u32[]{:S(2)}) collective-permute-start(bf16[512,128]{1,0:T(8,128)(2,1)S(1)} %fusion.9.refs_0_), channel_id=1, source_target_pairs={{0,3},{1,0},{2,1},{3,2},{4,7},{5,4},{6,5},{7,6},{8,11},{9,8},{10,9... | collective-permute-start | bytes 393224 | tf_op jit(solution)/shard_map/ppermute | solution.py:125
  72.0 13.5 %collective-permute-start.20 = (bf16[1024,128]{1,0:T(8,128)(2,1)S(1)}, bf16[1024,128]{1,0:T(8,128)(2,1)S(1)}, u32[]{:S(2)}, u32[]{:S(2)}) collective-permute-start(bf16[1024,128]{1,0:T(8,128)(2,1)S(1)} %pad_maximum_fusion.1.refs_4_), channel_id=1, source_target_pairs={{0,24},{4,28},{8,16},{12,20},{16,8},{20,12},{24,0},{28,4},{1,25},{... | collective-permute-start | bytes 786440 | tf_op jit(solution)/shard_map/ppermute | solution.py:145
  74.3 11.9 %collective-permute-start.19 = (bf16[1024,128]{1,0:T(8,128)(2,1)S(1)}, bf16[1024,128]{1,0:T(8,128)(2,1)S(1)}, u32[]{:S(2)}, u32[]{:S(2)}) collective-permute-start(bf16[1024,128]{1,0:T(8,128)(2,1)S(1)} %pad_maximum_fusion.1.refs_4_), channel_id=1, source_target_pairs={{0,16},{4,20},{8,24},{12,28},{16,0},{20,4},{24,8},{28,12},{1,17},{... | collective-permute-start | bytes 786440 | tf_op jit(solution)/shard_map/ppermute | solution.py:145
  75.2 11.0 %collective-permute-start.18 = (bf16[1024,128]{1,0:T(8,128)(2,1)S(1)}, bf16[1024,128]{1,0:T(8,128)(2,1)S(1)}, u32[]{:S(2)}, u32[]{:S(2)}) collective-permute-start(bf16[1024,128]{1,0:T(8,128)(2,1)S(1)} %pad_maximum_fusion.1.refs_4_), channel_id=1, source_target_pairs={{0,8},{4,12},{8,0},{12,4},{16,24},{20,28},{24,16},{28,20},{1,9},{5... | collective-permute-start | bytes 786440 | tf_op jit(solution)/shard_map/ppermute | solution.py:145
  75.6 10.0 %collective-permute-start.11 = (bf16[512,128]{1,0:T(8,128)(2,1)S(1)}, bf16[512,128]{1,0:T(8,128)(2,1)S(1)}, u32[]{:S(2)}, u32[]{:S(2)}) collective-permute-start(bf16[512,128]{1,0:T(8,128)(2,1)S(1)} %fusion.9.refs_0_), channel_id=1, source_target_pairs={{0,2},{1,3},{2,0},{3,1},{4,6},{5,7},{6,4},{7,5},{8,10},{9,11},{10,... | collective-permute-start | bytes 393224 | tf_op jit(solution)/shard_map/ppermute | solution.py:125
  76.9 8.6 %collective-permute-start.10 = (bf16[512,128]{1,0:T(8,128)(2,1)S(1)}, bf16[512,128]{1,0:T(8,128)(2,1)S(1)}, u32[]{:S(2)}, u32[]{:S(2)}) collective-permute-start(bf16[512,128]{1,0:T(8,128)(2,1)S(1)} %fusion.9.refs_0_), channel_id=1, source_target_pairs={{0,1},{1,2},{2,3},{3,0},{4,5},{5,6},{6,7},{7,4},{8,9},{9,10},{10,1... | collective-permute-start | bytes 393224 | tf_op jit(solution)/shard_map/ppermute | solution.py:125
  86.9 33.3 %copy-start.6 = (bf16[512,128]{1,0:T(8,128)(2,1)S(1)}, bf16[512,128]{1,0:T(8,128)(2,1)}, u32[]{:S(2)}) copy-start(bf16[512,128]{1,0:T(8,128)(2,1)} %get-tuple-element.18) | copy-start | bytes 393220
  105.7 8.4 %collective-permute-start.24 = (bf16[1024,128]{1,0:T(8,128)(2,1)}, bf16[1024,128]{1,0:T(8,128)(2,1)S(1)}, u32[]{:S(2)}, u32[]{:S(2)}) collective-permute-start(bf16[1024,128]{1,0:T(8,128)(2,1)} %get-tuple-element.31), channel_id=1, source_target_pairs={{0,8},{4,12},{8,0},{12,4},{16,24},{20,28},{24,16},{28,20},{1,9},{5... | collective-permute-start | bytes 786440 | tf_op jit(solution)/shard_map/ppermute | solution.py:152
  105.7 11.2 %collective-permute-start.25 = (bf16[1024,128]{1,0:T(8,128)(2,1)}, bf16[1024,128]{1,0:T(8,128)(2,1)S(1)}, u32[]{:S(2)}, u32[]{:S(2)}) collective-permute-start(bf16[1024,128]{1,0:T(8,128)(2,1)} %get-tuple-element.32), channel_id=1, source_target_pairs={{0,16},{4,20},{8,24},{12,28},{16,0},{20,4},{24,8},{28,12},{1,17},{... | collective-permute-start | bytes 786440 | tf_op jit(solution)/shard_map/ppermute | solution.py:152
  107.4 9.5 %collective-permute-start.26 = (bf16[1024,128]{1,0:T(8,128)(2,1)}, bf16[1024,128]{1,0:T(8,128)(2,1)S(1)}, u32[]{:S(2)}, u32[]{:S(2)}) collective-permute-start(bf16[1024,128]{1,0:T(8,128)(2,1)} %get-tuple-element.33), channel_id=1, source_target_pairs={{0,24},{4,28},{8,16},{12,20},{16,8},{20,12},{24,0},{28,4},{1,25},{... | collective-permute-start | bytes 786440 | tf_op jit(solution)/shard_map/ppermute | solution.py:152
  109.2 8.9 %collective-permute-start.21 = (bf16[512,128]{1,0:T(8,128)(2,1)}, bf16[512,128]{1,0:T(8,128)(2,1)S(1)}, u32[]{:S(2)}, u32[]{:S(2)}) collective-permute-start(bf16[512,128]{1,0:T(8,128)(2,1)} %get-tuple-element.27), channel_id=1, source_target_pairs={{0,1},{1,2},{2,3},{3,0},{4,5},{5,6},{6,7},{7,4},{8,9},{9,10},{10,1... | collective-permute-start | bytes 393224 | tf_op jit(solution)/shard_map/ppermute | solution.py:132
  109.2 10.4 %collective-permute-start.22 = (bf16[512,128]{1,0:T(8,128)(2,1)}, bf16[512,128]{1,0:T(8,128)(2,1)S(1)}, u32[]{:S(2)}, u32[]{:S(2)}) collective-permute-start(bf16[512,128]{1,0:T(8,128)(2,1)} %get-tuple-element.28), channel_id=1, source_target_pairs={{0,2},{1,3},{2,0},{3,1},{4,6},{5,7},{6,4},{7,5},{8,10},{9,11},{10,... | collective-permute-start | bytes 393224 | tf_op jit(solution)/shard_map/ppermute | solution.py:132
  114.1 6.2 %collective-permute-start.23 = (bf16[512,128]{1,0:T(8,128)(2,1)}, bf16[512,128]{1,0:T(8,128)(2,1)S(1)}, u32[]{:S(2)}, u32[]{:S(2)}) collective-permute-start(bf16[512,128]{1,0:T(8,128)(2,1)} %get-tuple-element.29), channel_id=1, source_target_pairs={{0,3},{1,0},{2,1},{3,2},{4,7},{5,4},{6,5},{7,6},{8,11},{9,8},{10,9... | collective-permute-start | bytes 393224 | tf_op jit(solution)/shard_map/ppermute | solution.py:132
  118.1 4.0 %collective-permute-start.27 = (f32[512,128]{1,0:T(8,128)S(1)}, f32[512,128]{1,0:T(8,128)S(1)}, u32[]{:S(2)}, u32[]{:S(2)}) collective-permute-start(f32[512,128]{1,0:T(8,128)S(1)} %slice.19), channel_id=1, source_target_pairs={{0,4},{4,0},{8,12},{12,8},{16,20},{20,16},{24,28},{28,24},{1,5},{5... | collective-permute-start | bytes 786440 | tf_op jit(solution)/shard_map/ppermute | solution.py:155
  (15 other events, 78.8 us)

commit v13 on v11

--- a/solution.py
+++ b/solution.py
@@ -156,6 +156,23 @@
     return total[:width] + got
 
 
+def spread_pairs(pair, axis, n):
+    blocks = [pair]
+    for b in range(1, n // 2):
+        blocks.append(lax.ppermute(pair, axis, [(i, i ^ (2 * b)) for i in range(n)]))
+    return blocks
+
+
+def reduce_pairs(blocks, axis, n):
+    total = blocks[0].astype(jnp.float32)
+    for b in range(1, n // 2):
+        got = lax.ppermute(blocks[b], axis, [(i, i ^ (2 * b)) for i in range(n)])
+        total = total + got.astype(jnp.float32)
+    width = total.shape[0] // 2
+    other = lax.ppermute(total, axis, [(i, i ^ 1) for i in range(n)])
+    return total + jnp.concatenate([other[width:], other[:width]], axis=0)
+
+
 def gather_xor(x, axis, n):
     pieces = [x]
     for p in range(1, n):
@@ -201,17 +218,30 @@
         scatters = (scatter_rotated, scatter_rotated)
         splits = (n_row, n_row)
     count = tile_count[0, 0]
+    width = ctx_in.shape[0]
     emb = emb_in
     ctx = ctx_in
+    pair = None
     for iteration in range(ITERS):
+        first, last = iteration == 0, iteration == ITERS - 1
         emb_low = gather_rotated(emb.astype(jnp.bfloat16), "col", n_col)
-        first, last = iteration == 0, iteration == ITERS - 1
-        ctx_low = gathers[0 if first else 1](ctx.astype(jnp.bfloat16), "row", n_row)
+        if not paired(n_row):
+            ctx_low = gathers[0](ctx.astype(jnp.bfloat16), "row", n_row)
+        else:
+            if first:
+                partner = lax.ppermute(ctx, "row", [(i, i ^ 1) for i in range(n_row)])
+                pair = jnp.concatenate([ctx, partner], axis=0)
+            ctx_low = spread_pairs(pair.astype(jnp.bfloat16), "row", n_row)
         grad_emb, grad_ctx = tile_sweep(
             pos, neg, rows, cols, count, emb_low, ctx_low, n_col, splits[1 if last else 0]
         )
         emb = emb + 0.05 * scatter_rotated(grad_emb, "col", n_col)
-        ctx = ctx + 0.05 * scatters[1 if last else 0](grad_ctx, "row", n_row)
+        if not paired(n_row):
+            ctx = ctx + 0.05 * scatters[0](grad_ctx, "row", n_row)
+        elif last:
+            ctx = pair[:width] + 0.05 * scatter_paired(grad_ctx, "row", n_row)
+        else:
+            pair = pair + 0.05 * reduce_pairs(grad_ctx, "row", n_row)
     return (emb, ctx)
 
 

time: 116 us -> 124 us (1.069); the launches traced: 114 us -> 125 us
  waiting for transfers between devices: 27.4 us -> 45.6 us
  starting transfers between devices: 60 us -> 53 us
    ppermute x6, starting transfers between devices: 23 us -> 9.85 us  [scatter_rotated(): lax.ppermute(chunks[(n - s) % n], axis, [(i, (i + s) % n) for i in range(...]
    ppermute x11, starting transfers between devices: 10.5 us -> 20.5 us  [the longest x3 12.8 us: reduce_pairs(): got = lax.ppermute(blocks[b], axis, [(i, i ^ 2 * b) for i in range(n)])]
    ppermute x11, waiting for transfers between devices: 7.22 us -> 15.2 us  [the longest x3 11.2 us: reduce_pairs(): got = lax.ppermute(blocks[b], axis, [(i, i ^ 2 * b) for i in range(n)])]
    ppermute x6 -> x3, waiting for transfers between devices: 0.02 us -> 7 us  [scatter_paired(): got = lax.ppermute(blocks[b], axis, [(i, i ^ 2 * b) for i in range(n)])]
    ppermute x2 -> x1, starting transfers between devices: 3.38 us -> 0.07 us  [scatter_paired(): got = lax.ppermute(total[width:], axis, [(i, i ^ 1) for i in range(n)])]
    ppermute x6, waiting for transfers between devices: 6.02 us -> 8.84 us  [scatter_rotated(): lax.ppermute(chunks[(n - s) % n], axis, [(i, (i + s) % n) for i in range(...]
    ppermute x6 -> x3, starting transfers between devices: 11.9 us -> 12.1 us  [scatter_paired(): got = lax.ppermute(blocks[b], axis, [(i, i ^ 2 * b) for i in range(n)])]
  transfers between devices with their start and end apart: 31 -> 27, of which waited for: 12 -> 12; matrix products, arithmetic and copies ran while one was open for 6% -> 6% of each run, Pallas kernels for 0% -> 0%
where the time goes in v13:
time: 124 us; the launch traced here: 125 us
  starting transfers between devices  53 us (43%)
  waiting for transfers between devices  45.6 us (37%)
  Pallas kernels  14.8 us (12%)
  other arithmetic  8.03 us (6%)
  local copies, waits for them, and re-layouts  2.49 us (2%)
  between operations  1.55 us (1%)
    pallas_call x2, Pallas kernels, tile_sweep(): pl.pallas_call(functools.partial(sweep_kernel, tile, group, len(emb_piece...  14.8 us
    ppermute x6, waiting for transfers between devices, gather_rotated(): pieces.append(lax.ppermute(x, axis, [(i, (i + s) % n) for i in range(n)]))  14.6 us
    ppermute x3, starting transfers between devices, reduce_pairs(): got = lax.ppermute(blocks[b], axis, [(i, i ^ 2 * b) for i in range(n)])  12.8 us
    ppermute x3, starting transfers between devices, scatter_paired(): got = lax.ppermute(blocks[b], axis, [(i, i ^ 2 * b) for i in range(n)])  12.1 us
    ppermute x3, waiting for transfers between devices, reduce_pairs(): got = lax.ppermute(blocks[b], axis, [(i, i ^ 2 * b) for i in range(n)])  11.2 us
    ppermute x6, starting transfers between devices, gather_rotated(): pieces.append(lax.ppermute(x, axis, [(i, (i + s) % n) for i in range(n)]))  10.5 us
    ppermute x6, starting transfers between devices, scatter_rotated(): lax.ppermute(chunks[(n - s) % n], axis, [(i, (i + s) % n) for i in range(...  9.85 us
    ppermute x6, waiting for transfers between devices, scatter_rotated(): lax.ppermute(chunks[(n - s) % n], axis, [(i, (i + s) % n) for i in range(...  8.84 us
  transfers between devices with their start and end apart: 27, of which 12 were waited for; matrix products, arithmetic and copies ran while one was open for 6% of the time, Pallas kernels for 0%

profile of v13, /device:TPU:0, one launch (start us, length us, event | category | flops | bytes accessed | tf_op | source)
XLA Modules:
  0.0 125.5 jit_solution(11953084994601662767)
XLA Ops:
  2.1 4.7 %collective-permute-start.2 = (bf16[512,128]{1,0:T(8,128)(2,1)S(1)}, bf16[512,128]{1,0:T(8,128)(2,1)S(1)}, u32[]{:S(2)}, u32[]{:S(2)}) collective-permute-start(bf16[512,128]{1,0:T(8,128)(2,1)S(1)} %convert_element_type.60.refs_0_), channel_id=1, source_target_pairs={{0,3},{1,0},{2,1},{3,2},{4,7},{5,4},{6,5},{7,6},{8,11},{9,8},{10,9... | collective-permute-start | bytes 393224 | tf_op jit(solution)/shard_map/ppermute | solution.py:125
  6.8 1.0 constant_dynamic-update-slice_fusion.1
  7.8 2.5 %collective-permute-start.6 = (bf16[1024,128]{1,0:T(8,128)(2,1)S(1)}, bf16[1024,128]{1,0:T(8,128)(2,1)S(1)}, u32[]{:S(2)}, u32[]{:S(2)}) collective-permute-start(bf16[1024,128]{1,0:T(8,128)(2,1)S(1)} %convert_element_type.61.refs_4_), channel_id=1, source_target_pairs={{0,24},{4,28},{8,16},{12,20},{16,8},{20,12},{24,0},{28,4},{1,25},{... | collective-permute-start | bytes 786440 | tf_op jit(solution)/shard_map/ppermute | solution.py:162
  12.1 1.1 collective-permute-start
  13.1 1.2 fusion.4
  14.4 6.1 %collective-permute-done.1.refs_2_ = bf16[512,128]{1,0:T(8,128)(2,1)S(1)} collective-permute-done((bf16[512,128]{1,0:T(8,128)(2,1)S(1)}, bf16[512,128]{1,0:T(8,128)(2,1)S(1)}, u32[]{:S(2)}, u32[]{:S(2)}) %collective-permute-start.1) | collective-permute-done | bytes 131104 | tf_op jit(solution)/shard_map/ppermute | solution.py:125
  20.5 2.3 %collective-permute-done.5.refs_6_ = bf16[1024,128]{1,0:T(8,128)(2,1)S(1)} collective-permute-done((bf16[1024,128]{1,0:T(8,128)(2,1)S(1)}, bf16[1024,128]{1,0:T(8,128)(2,1)S(1)}, u32[]{:S(2)}, u32[]{:S(2)}) %collective-permute-start.5) | collective-permute-done | bytes 262176 | tf_op jit(solution)/shard_map/ppermute | solution.py:162
  23.7 7.4 %shard_map.86 = (bf16[512,128]{1,0:T(8,128)(2,1)}, bf16[512,128]{1,0:T(8,128)(2,1)}, bf16[512,128]{1,0:T(8,128)(2,1)}, bf16[512,128]{1,0:T(8,128)(2,1)}, bf16[10...) custom-call(s32[64]{0:T(128)} %get-tuple-element.38.rows_ref, ...), custom_call_target="tpu_custom_call" | custom-call | flops 3221225472 | bytes 21495808 | tf_op jit(solution)/shard_map/pallas_call | solution.py:107
  31.0 11.2 %collective-permute-start.13 = (bf16[1024,128]{1,0:T(8,128)(2,1)}, bf16[1024,128]{1,0:T(8,128)(2,1)S(1)}, u32[]{:S(2)}, u32[]{:S(2)}) collective-permute-start(bf16[1024,128]{1,0:T(8,128)(2,1)} %get-tuple-element.23), channel_id=1, source_target_pairs={{0,8},{4,12},{8,0},{12,4},{16,24},{20,28},{24,16},{28,20},{1,9},{5... | collective-permute-start | bytes 786440 | tf_op jit(solution)/shard_map/ppermute | solution.py:169
  42.3 1.5 %collective-permute-start.15 = (bf16[1024,128]{1,0:T(8,128)(2,1)}, bf16[1024,128]{1,0:T(8,128)(2,1)S(1)}, u32[]{:S(2)}, u32[]{:S(2)}) collective-permute-start(bf16[1024,128]{1,0:T(8,128)(2,1)} %get-tuple-element.25), channel_id=1, source_target_pairs={{0,24},{4,28},{8,16},{12,20},{16,8},{20,12},{24,0},{28,4},{1,25},{... | collective-permute-start | bytes 786440 | tf_op jit(solution)/shard_map/ppermute | solution.py:169
  43.8 5.8 %collective-permute-done.13 = bf16[1024,128]{1,0:T(8,128)(2,1)S(1)} collective-permute-done((bf16[1024,128]{1,0:T(8,128)(2,1)}, bf16[1024,128]{1,0:T(8,128)(2,1)S(1)}, u32[]{:S(2)}, u32[]{:S(2)}) %collective-permute-start.13) | collective-permute-done | bytes 262176 | tf_op jit(solution)/shard_map/ppermute | solution.py:169
  49.6 5.4 %collective-permute-done.14 = bf16[1024,128]{1,0:T(8,128)(2,1)S(1)} collective-permute-done((bf16[1024,128]{1,0:T(8,128)(2,1)}, bf16[1024,128]{1,0:T(8,128)(2,1)S(1)}, u32[]{:S(2)}, u32[]{:S(2)}) %collective-permute-start.14) | collective-permute-done | bytes 262176 | tf_op jit(solution)/shard_map/ppermute | solution.py:169
  55.0 1.1 convert_add_fusion.1
  56.3 2.0 %collective-permute-start.8 = (bf16[512,128]{1,0:T(8,128)(2,1)}, bf16[512,128]{1,0:T(8,128)(2,1)S(1)}, u32[]{:S(2)}, u32[]{:S(2)}) collective-permute-start(bf16[512,128]{1,0:T(8,128)(2,1)} %get-tuple-element.20), channel_id=1, source_target_pairs={{0,2},{1,3},{2,0},{3,1},{4,6},{5,7},{6,4},{7,5},{8,10},{9,11},{10,... | collective-permute-start | bytes 393224 | tf_op jit(solution)/shard_map/ppermute | solution.py:132
  58.3 2.8 %collective-permute-start.9 = (bf16[512,128]{1,0:T(8,128)(2,1)}, bf16[512,128]{1,0:T(8,128)(2,1)S(1)}, u32[]{:S(2)}, u32[]{:S(2)}) collective-permute-start(bf16[512,128]{1,0:T(8,128)(2,1)} %get-tuple-element.21), channel_id=1, source_target_pairs={{0,3},{1,0},{2,1},{3,2},{4,7},{5,4},{6,5},{7,6},{8,11},{9,8},{10,9... | collective-permute-start | bytes 393224 | tf_op jit(solution)/shard_map/ppermute | solution.py:132
  61.1 3.6 %collective-permute-done.7 = bf16[512,128]{1,0:T(8,128)(2,1)S(1)} collective-permute-done((bf16[512,128]{1,0:T(8,128)(2,1)}, bf16[512,128]{1,0:T(8,128)(2,1)S(1)}, u32[]{:S(2)}, u32[]{:S(2)}) %collective-permute-start.7) | collective-permute-done | bytes 131104 | tf_op jit(solution)/shard_map/ppermute | solution.py:132
  64.7 4.7 %collective-permute-done.8 = bf16[512,128]{1,0:T(8,128)(2,1)S(1)} collective-permute-done((bf16[512,128]{1,0:T(8,128)(2,1)}, bf16[512,128]{1,0:T(8,128)(2,1)S(1)}, u32[]{:S(2)}, u32[]{:S(2)}) %collective-permute-start.8) | collective-permute-done | bytes 131104 | tf_op jit(solution)/shard_map/ppermute | solution.py:132
  69.4 1.0 fusion.8.refs_0_
  70.4 4.2 %collective-permute-start.12 = (bf16[512,128]{1,0:T(8,128)(2,1)S(1)}, bf16[512,128]{1,0:T(8,128)(2,1)S(1)}, u32[]{:S(2)}, u32[]{:S(2)}) collective-permute-start(bf16[512,128]{1,0:T(8,128)(2,1)S(1)} %fusion.8.refs_0_), channel_id=1, source_target_pairs={{0,3},{1,0},{2,1},{3,2},{4,7},{5,4},{6,5},{7,6},{8,11},{9,8},{10,9... | collective-permute-start | bytes 393224 | tf_op jit(solution)/shard_map/ppermute | solution.py:125
  74.8 1.8 %collective-permute-start.19 = (bf16[1024,128]{1,0:T(8,128)(2,1)S(1)}, bf16[1024,128]{1,0:T(8,128)(2,1)S(1)}, u32[]{:S(2)}, u32[]{:S(2)}) collective-permute-start(bf16[1024,128]{1,0:T(8,128)(2,1)S(1)} %get-tuple-element.34.refs_4_), channel_id=1, source_target_pairs={{0,24},{4,28},{8,16},{12,20},{16,8},{20,12},{24,0},{28,4},{1,25},{... | collective-permute-start | bytes 786440 | tf_op jit(solution)/shard_map/ppermute | solution.py:162
  76.9 1.5 %collective-permute-start.17 = (bf16[1024,128]{1,0:T(8,128)(2,1)S(1)}, bf16[1024,128]{1,0:T(8,128)(2,1)S(1)}, u32[]{:S(2)}, u32[]{:S(2)}) collective-permute-start(bf16[1024,128]{1,0:T(8,128)(2,1)S(1)} %get-tuple-element.34.refs_4_), channel_id=1, source_target_pairs={{0,8},{4,12},{8,0},{12,4},{16,24},{20,28},{24,16},{28,20},{1,9},{5... | collective-permute-start | bytes 786440 | tf_op jit(solution)/shard_map/ppermute | solution.py:162
  79.0 8.5 %collective-permute-done.11.refs_2_ = bf16[512,128]{1,0:T(8,128)(2,1)S(1)} collective-permute-done((bf16[512,128]{1,0:T(8,128)(2,1)S(1)}, bf16[512,128]{1,0:T(8,128)(2,1)S(1)}, u32[]{:S(2)}, u32[]{:S(2)}) %collective-permute-start.11) | collective-permute-done | bytes 131104 | tf_op jit(solution)/shard_map/ppermute | solution.py:125
  87.4 1.5 %collective-permute-done.18.refs_6_ = bf16[1024,128]{1,0:T(8,128)(2,1)S(1)} collective-permute-done((bf16[1024,128]{1,0:T(8,128)(2,1)S(1)}, bf16[1024,128]{1,0:T(8,128)(2,1)S(1)}, u32[]{:S(2)}, u32[]{:S(2)}) %collective-permute-start.18) | collective-permute-done | bytes 262176 | tf_op jit(solution)/shard_map/ppermute | solution.py:162
  89.8 7.4 %shard_map.87 = (bf16[512,128]{1,0:T(8,128)(2,1)}, bf16[512,128]{1,0:T(8,128)(2,1)}, bf16[512,128]{1,0:T(8,128)(2,1)}, bf16[512,128]{1,0:T(8,128)(2,1)}, bf16[10...) custom-call(s32[64]{0:T(128)} %get-tuple-element.38.rows_ref, ...), custom_call_target="tpu_custom_call" | custom-call | flops 3221225472 | bytes 21495808 | tf_op jit(solution)/shard_map/pallas_call | solution.py:107
  97.2 10.5 %collective-permute-start.23 = (bf16[1024,128]{1,0:T(8,128)(2,1)}, bf16[1024,128]{1,0:T(8,128)(2,1)S(1)}, u32[]{:S(2)}, u32[]{:S(2)}) collective-permute-start(bf16[1024,128]{1,0:T(8,128)(2,1)} %get-tuple-element.31), channel_id=1, source_target_pairs={{0,8},{4,12},{8,0},{12,4},{16,24},{20,28},{24,16},{28,20},{1,9},{5... | collective-permute-start | bytes 786440 | tf_op jit(solution)/shard_map/ppermute | solution.py:152
  107.7 1.5 %collective-permute-start.25 = (bf16[1024,128]{1,0:T(8,128)(2,1)}, bf16[1024,128]{1,0:T(8,128)(2,1)S(1)}, u32[]{:S(2)}, u32[]{:S(2)}) collective-permute-start(bf16[1024,128]{1,0:T(8,128)(2,1)} %get-tuple-element.33), channel_id=1, source_target_pairs={{0,24},{4,28},{8,16},{12,20},{16,8},{20,12},{24,0},{28,4},{1,25},{... | collective-permute-start | bytes 786440 | tf_op jit(solution)/shard_map/ppermute | solution.py:152
  109.3 3.8 %collective-permute-start.21 = (bf16[512,128]{1,0:T(8,128)(2,1)}, bf16[512,128]{1,0:T(8,128)(2,1)S(1)}, u32[]{:S(2)}, u32[]{:S(2)}) collective-permute-start(bf16[512,128]{1,0:T(8,128)(2,1)} %get-tuple-element.28), channel_id=1, source_target_pairs={{0,2},{1,3},{2,0},{3,1},{4,6},{5,7},{6,4},{7,5},{8,10},{9,11},{10,... | collective-permute-start | bytes 393224 | tf_op jit(solution)/shard_map/ppermute | solution.py:132
  113.0 1.8 %collective-permute-done.23 = bf16[1024,128]{1,0:T(8,128)(2,1)S(1)} collective-permute-done((bf16[1024,128]{1,0:T(8,128)(2,1)}, bf16[1024,128]{1,0:T(8,128)(2,1)S(1)}, u32[]{:S(2)}, u32[]{:S(2)}) %collective-permute-start.23) | collective-permute-done | bytes 262176 | tf_op jit(solution)/shard_map/ppermute | solution.py:152
  114.8 1.2 collective-permute-start.22
  115.9 5.2 %collective-permute-done.24 = bf16[1024,128]{1,0:T(8,128)(2,1)S(1)} collective-permute-done((bf16[1024,128]{1,0:T(8,128)(2,1)}, bf16[1024,128]{1,0:T(8,128)(2,1)S(1)}, u32[]{:S(2)}, u32[]{:S(2)}) %collective-permute-start.24) | collective-permute-done | bytes 262176 | tf_op jit(solution)/shard_map/ppermute | solution.py:152
  121.2 1.1 convert_add_fusion
  122.9 1.8 %multiply_add_fusion = f32[512,128]{1,0:T(8,128)} fusion(bf16[512,128]{1,0:T(8,128)(2,1)S(1)} %collective-permute-done.22, bf16[512,128]{1,0:T(8,128)(2,1)S(1)} %collective-permute-done.21, bf16[512,128]{1,0:T(8,128)(2,1)S(1)} %collective-permute-done.20, bf16[512,128]{1,0:T(8,128)(2,1)} %get-tuple-element.26, f32[512,128]{1,0:T(8,128)S(1)} %copy-done, ...), kind=kLoop, calls=%fused_computation.8 | loop fusion | flops 1179648 | bytes 1572864 | tf_op jit(solution)/shard_map/add | solution.py:238
  (73 shorter events, 6.7 us)
Async XLA Ops:
  0.6 7.1 %collective-permute-start.3 = (f32[512,128]{1,0:T(8,128)}, f32[512,128]{1,0:T(8,128)S(1)}, u32[]{:S(2)}, u32[]{:S(2)}) collective-permute-start(f32[512,128]{1,0:T(8,128)} %param.8), channel_id=1, source_target_pairs={{0,4},{4,0},{8,12},{12,8},{16,20},{20,16},{24,28},{28,24},{1,5},{5... | collective-permute-start | bytes 786440 | tf_op jit(solution)/shard_map/ppermute | solution.py:232
  2.1 20.8 %copy-start.3 = (bf16[512,128]{1,0:T(8,128)(2,1)}, bf16[512,128]{1,0:T(8,128)(2,1)S(1)}, u32[]{:S(2)}) copy-start(bf16[512,128]{1,0:T(8,128)(2,1)S(1)} %convert_element_type.60.refs_0_) | copy-start | bytes 393220
  2.1 9.9 %collective-permute-start.2 = (bf16[512,128]{1,0:T(8,128)(2,1)S(1)}, bf16[512,128]{1,0:T(8,128)(2,1)S(1)}, u32[]{:S(2)}, u32[]{:S(2)}) collective-permute-start(bf16[512,128]{1,0:T(8,128)(2,1)S(1)} %convert_element_type.60.refs_0_), channel_id=1, source_target_pairs={{0,3},{1,0},{2,1},{3,2},{4,7},{5,4},{6,5},{7,6},{8,11},{9,8},{10,9... | collective-permute-start | bytes 393224 | tf_op jit(solution)/shard_map/ppermute | solution.py:125
  7.8 15.1 %copy-start.1 = (bf16[1024,128]{1,0:T(8,128)(2,1)}, bf16[1024,128]{1,0:T(8,128)(2,1)S(1)}, u32[]{:S(2)}) copy-start(bf16[1024,128]{1,0:T(8,128)(2,1)S(1)} %convert_element_type.61.refs_4_) | copy-start | bytes 786436
  7.8 12.7 %collective-permute-start.6 = (bf16[1024,128]{1,0:T(8,128)(2,1)S(1)}, bf16[1024,128]{1,0:T(8,128)(2,1)S(1)}, u32[]{:S(2)}, u32[]{:S(2)}) collective-permute-start(bf16[1024,128]{1,0:T(8,128)(2,1)S(1)} %convert_element_type.61.refs_4_), channel_id=1, source_target_pairs={{0,24},{4,28},{8,16},{12,20},{16,8},{20,12},{24,0},{28,4},{1,25},{... | collective-permute-start | bytes 786440 | tf_op jit(solution)/shard_map/ppermute | solution.py:162
  10.4 12.5 %collective-permute-start.5 = (bf16[1024,128]{1,0:T(8,128)(2,1)S(1)}, bf16[1024,128]{1,0:T(8,128)(2,1)S(1)}, u32[]{:S(2)}, u32[]{:S(2)}) collective-permute-start(bf16[1024,128]{1,0:T(8,128)(2,1)S(1)} %convert_element_type.61.refs_4_), channel_id=1, source_target_pairs={{0,16},{4,20},{8,24},{12,28},{16,0},{20,4},{24,8},{28,12},{1,17},{... | collective-permute-start | bytes 786440 | tf_op jit(solution)/shard_map/ppermute | solution.py:162
  10.9 12.1 %collective-permute-start.4 = (bf16[1024,128]{1,0:T(8,128)(2,1)S(1)}, bf16[1024,128]{1,0:T(8,128)(2,1)S(1)}, u32[]{:S(2)}, u32[]{:S(2)}) collective-permute-start(bf16[1024,128]{1,0:T(8,128)(2,1)S(1)} %convert_element_type.61.refs_4_), channel_id=1, source_target_pairs={{0,8},{4,12},{8,0},{12,4},{16,24},{20,28},{24,16},{28,20},{1,9},{5... | collective-permute-start | bytes 786440 | tf_op jit(solution)/shard_map/ppermute | solution.py:162
  11.4 9.1 %collective-permute-start.1 = (bf16[512,128]{1,0:T(8,128)(2,1)S(1)}, bf16[512,128]{1,0:T(8,128)(2,1)S(1)}, u32[]{:S(2)}, u32[]{:S(2)}) collective-permute-start(bf16[512,128]{1,0:T(8,128)(2,1)S(1)} %convert_element_type.60.refs_0_), channel_id=1, source_target_pairs={{0,2},{1,3},{2,0},{3,1},{4,6},{5,7},{6,4},{7,5},{8,10},{9,11},{10,... | collective-permute-start | bytes 393224 | tf_op jit(solution)/shard_map/ppermute | solution.py:125
  12.1 8.4 %collective-permute-start = (bf16[512,128]{1,0:T(8,128)(2,1)S(1)}, bf16[512,128]{1,0:T(8,128)(2,1)S(1)}, u32[]{:S(2)}, u32[]{:S(2)}) collective-permute-start(bf16[512,128]{1,0:T(8,128)(2,1)S(1)} %convert_element_type.60.refs_0_), channel_id=1, source_target_pairs={{0,1},{1,2},{2,3},{3,0},{4,5},{5,6},{6,7},{7,4},{8,9},{9,10},{10,1... | collective-permute-start | bytes 393224 | tf_op jit(solution)/shard_map/ppermute | solution.py:125
  23.7 45.8 %copy-start = (f32[512,128]{1,0:T(8,128)S(1)}, f32[512,128]{1,0:T(8,128)}, u32[]{:S(2)}) copy-start(f32[512,128]{1,0:T(8,128)} %param.7) | copy-start | bytes 786436
  31.0 18.6 %collective-permute-start.13 = (bf16[1024,128]{1,0:T(8,128)(2,1)}, bf16[1024,128]{1,0:T(8,128)(2,1)S(1)}, u32[]{:S(2)}, u32[]{:S(2)}) collective-permute-start(bf16[1024,128]{1,0:T(8,128)(2,1)} %get-tuple-element.23), channel_id=1, source_target_pairs={{0,8},{4,12},{8,0},{12,4},{16,24},{20,28},{24,16},{28,20},{1,9},{5... | collective-permute-start | bytes 786440 | tf_op jit(solution)/shard_map/ppermute | solution.py:169
  42.3 12.8 %collective-permute-start.14 = (bf16[1024,128]{1,0:T(8,128)(2,1)}, bf16[1024,128]{1,0:T(8,128)(2,1)S(1)}, u32[]{:S(2)}, u32[]{:S(2)}) collective-permute-start(bf16[1024,128]{1,0:T(8,128)(2,1)} %get-tuple-element.24), channel_id=1, source_target_pairs={{0,16},{4,20},{8,24},{12,28},{16,0},{20,4},{24,8},{28,12},{1,17},{... | collective-permute-start | bytes 786440 | tf_op jit(solution)/shard_map/ppermute | solution.py:169
  42.3 12.8 %collective-permute-start.15 = (bf16[1024,128]{1,0:T(8,128)(2,1)}, bf16[1024,128]{1,0:T(8,128)(2,1)S(1)}, u32[]{:S(2)}, u32[]{:S(2)}) collective-permute-start(bf16[1024,128]{1,0:T(8,128)(2,1)} %get-tuple-element.25), channel_id=1, source_target_pairs={{0,24},{4,28},{8,16},{12,20},{16,8},{20,12},{24,0},{28,4},{1,25},{... | collective-permute-start | bytes 786440 | tf_op jit(solution)/shard_map/ppermute | solution.py:169
  56.1 18.5 %collective-permute-start.16 = (f32[1024,128]{1,0:T(8,128)S(1)}, f32[1024,128]{1,0:T(8,128)S(1)}, u32[]{:S(2)}, u32[]{:S(2)}) collective-permute-start(f32[1024,128]{1,0:T(8,128)S(1)} %convert_add_fusion.1), channel_id=1, source_target_pairs={{0,4},{4,0},{8,12},{12,8},{16,20},{20,16},{24,28},{28,24},{1,5},{5... | collective-permute-start | bytes 1572872 | tf_op jit(solution)/shard_map/ppermute | solution.py:172
  56.2 8.5 %collective-permute-start.7 = (bf16[512,128]{1,0:T(8,128)(2,1)}, bf16[512,128]{1,0:T(8,128)(2,1)S(1)}, u32[]{:S(2)}, u32[]{:S(2)}) collective-permute-start(bf16[512,128]{1,0:T(8,128)(2,1)} %get-tuple-element.19), channel_id=1, source_target_pairs={{0,1},{1,2},{2,3},{3,0},{4,5},{5,6},{6,7},{7,4},{8,9},{9,10},{10,1... | collective-permute-start | bytes 393224 | tf_op jit(solution)/shard_map/ppermute | solution.py:132
  56.3 13.2 %collective-permute-start.8 = (bf16[512,128]{1,0:T(8,128)(2,1)}, bf16[512,128]{1,0:T(8,128)(2,1)S(1)}, u32[]{:S(2)}, u32[]{:S(2)}) collective-permute-start(bf16[512,128]{1,0:T(8,128)(2,1)} %get-tuple-element.20), channel_id=1, source_target_pairs={{0,2},{1,3},{2,0},{3,1},{4,6},{5,7},{6,4},{7,5},{8,10},{9,11},{10,... | collective-permute-start | bytes 393224 | tf_op jit(solution)/shard_map/ppermute | solution.py:132
  58.3 11.1 %collective-permute-start.9 = (bf16[512,128]{1,0:T(8,128)(2,1)}, bf16[512,128]{1,0:T(8,128)(2,1)S(1)}, u32[]{:S(2)}, u32[]{:S(2)}) collective-permute-start(bf16[512,128]{1,0:T(8,128)(2,1)} %get-tuple-element.21), channel_id=1, source_target_pairs={{0,3},{1,0},{2,1},{3,2},{4,7},{5,4},{6,5},{7,6},{8,11},{9,8},{10,9... | collective-permute-start | bytes 393224 | tf_op jit(solution)/shard_map/ppermute | solution.py:132
  70.4 18.6 %copy-start.4 = (bf16[512,128]{1,0:T(8,128)(2,1)}, bf16[512,128]{1,0:T(8,128)(2,1)S(1)}, u32[]{:S(2)}) copy-start(bf16[512,128]{1,0:T(8,128)(2,1)S(1)} %fusion.8.refs_0_) | copy-start | bytes 393220
  70.4 8.0 %collective-permute-start.12 = (bf16[512,128]{1,0:T(8,128)(2,1)S(1)}, bf16[512,128]{1,0:T(8,128)(2,1)S(1)}, u32[]{:S(2)}, u32[]{:S(2)}) collective-permute-start(bf16[512,128]{1,0:T(8,128)(2,1)S(1)} %fusion.8.refs_0_), channel_id=1, source_target_pairs={{0,3},{1,0},{2,1},{3,2},{4,7},{5,4},{6,5},{7,6},{8,11},{9,8},{10,9... | collective-permute-start | bytes 393224 | tf_op jit(solution)/shard_map/ppermute | solution.py:125
  74.8 12.6 %collective-permute-start.19 = (bf16[1024,128]{1,0:T(8,128)(2,1)S(1)}, bf16[1024,128]{1,0:T(8,128)(2,1)S(1)}, u32[]{:S(2)}, u32[]{:S(2)}) collective-permute-start(bf16[1024,128]{1,0:T(8,128)(2,1)S(1)} %get-tuple-element.34.refs_4_), channel_id=1, source_target_pairs={{0,24},{4,28},{8,16},{12,20},{16,8},{20,12},{24,0},{28,4},{1,25},{... | collective-permute-start | bytes 786440 | tf_op jit(solution)/shard_map/ppermute | solution.py:162
  76.6 12.4 %collective-permute-start.18 = (bf16[1024,128]{1,0:T(8,128)(2,1)S(1)}, bf16[1024,128]{1,0:T(8,128)(2,1)S(1)}, u32[]{:S(2)}, u32[]{:S(2)}) collective-permute-start(bf16[1024,128]{1,0:T(8,128)(2,1)S(1)} %get-tuple-element.34.refs_4_), channel_id=1, source_target_pairs={{0,16},{4,20},{8,24},{12,28},{16,0},{20,4},{24,8},{28,12},{1,17},{... | collective-permute-start | bytes 786440 | tf_op jit(solution)/shard_map/ppermute | solution.py:162
  76.9 12.1 %collective-permute-start.17 = (bf16[1024,128]{1,0:T(8,128)(2,1)S(1)}, bf16[1024,128]{1,0:T(8,128)(2,1)S(1)}, u32[]{:S(2)}, u32[]{:S(2)}) collective-permute-start(bf16[1024,128]{1,0:T(8,128)(2,1)S(1)} %get-tuple-element.34.refs_4_), channel_id=1, source_target_pairs={{0,8},{4,12},{8,0},{12,4},{16,24},{20,28},{24,16},{28,20},{1,9},{5... | collective-permute-start | bytes 786440 | tf_op jit(solution)/shard_map/ppermute | solution.py:162
  78.4 9.1 %collective-permute-start.11 = (bf16[512,128]{1,0:T(8,128)(2,1)S(1)}, bf16[512,128]{1,0:T(8,128)(2,1)S(1)}, u32[]{:S(2)}, u32[]{:S(2)}) collective-permute-start(bf16[512,128]{1,0:T(8,128)(2,1)S(1)} %fusion.8.refs_0_), channel_id=1, source_target_pairs={{0,2},{1,3},{2,0},{3,1},{4,6},{5,7},{6,4},{7,5},{8,10},{9,11},{10,... | collective-permute-start | bytes 393224 | tf_op jit(solution)/shard_map/ppermute | solution.py:125
  78.5 8.9 %collective-permute-start.10 = (bf16[512,128]{1,0:T(8,128)(2,1)S(1)}, bf16[512,128]{1,0:T(8,128)(2,1)S(1)}, u32[]{:S(2)}, u32[]{:S(2)}) collective-permute-start(bf16[512,128]{1,0:T(8,128)(2,1)S(1)} %fusion.8.refs_0_), channel_id=1, source_target_pairs={{0,1},{1,2},{2,3},{3,0},{4,5},{5,6},{6,7},{7,4},{8,9},{9,10},{10,1... | collective-permute-start | bytes 393224 | tf_op jit(solution)/shard_map/ppermute | solution.py:125
  89.8 33.2 %copy-start.5 = (bf16[512,128]{1,0:T(8,128)(2,1)S(1)}, bf16[512,128]{1,0:T(8,128)(2,1)}, u32[]{:S(2)}) copy-start(bf16[512,128]{1,0:T(8,128)(2,1)} %get-tuple-element.18) | copy-start | bytes 393220
  97.2 17.6 %collective-permute-start.23 = (bf16[1024,128]{1,0:T(8,128)(2,1)}, bf16[1024,128]{1,0:T(8,128)(2,1)S(1)}, u32[]{:S(2)}, u32[]{:S(2)}) collective-permute-start(bf16[1024,128]{1,0:T(8,128)(2,1)} %get-tuple-element.31), channel_id=1, source_target_pairs={{0,8},{4,12},{8,0},{12,4},{16,24},{20,28},{24,16},{28,20},{1,9},{5... | collective-permute-start | bytes 786440 | tf_op jit(solution)/shard_map/ppermute | solution.py:152
  107.7 13.5 %collective-permute-start.24 = (bf16[1024,128]{1,0:T(8,128)(2,1)}, bf16[1024,128]{1,0:T(8,128)(2,1)S(1)}, u32[]{:S(2)}, u32[]{:S(2)}) collective-permute-start(bf16[1024,128]{1,0:T(8,128)(2,1)} %get-tuple-element.32), channel_id=1, source_target_pairs={{0,16},{4,20},{8,24},{12,28},{16,0},{20,4},{24,8},{28,12},{1,17},{... | collective-permute-start | bytes 786440 | tf_op jit(solution)/shard_map/ppermute | solution.py:152
  107.7 13.5 %collective-permute-start.25 = (bf16[1024,128]{1,0:T(8,128)(2,1)}, bf16[1024,128]{1,0:T(8,128)(2,1)S(1)}, u32[]{:S(2)}, u32[]{:S(2)}) collective-permute-start(bf16[1024,128]{1,0:T(8,128)(2,1)} %get-tuple-element.33), channel_id=1, source_target_pairs={{0,24},{4,28},{8,16},{12,20},{16,8},{20,12},{24,0},{28,4},{1,25},{... | collective-permute-start | bytes 786440 | tf_op jit(solution)/shard_map/ppermute | solution.py:152
  109.3 13.1 %collective-permute-start.20 = (bf16[512,128]{1,0:T(8,128)(2,1)}, bf16[512,128]{1,0:T(8,128)(2,1)S(1)}, u32[]{:S(2)}, u32[]{:S(2)}) collective-permute-start(bf16[512,128]{1,0:T(8,128)(2,1)} %get-tuple-element.27), channel_id=1, source_target_pairs={{0,1},{1,2},{2,3},{3,0},{4,5},{5,6},{6,7},{7,4},{8,9},{9,10},{10,1... | collective-permute-start | bytes 393224 | tf_op jit(solution)/shard_map/ppermute | solution.py:132
  109.3 13.6 %collective-permute-start.21 = (bf16[512,128]{1,0:T(8,128)(2,1)}, bf16[512,128]{1,0:T(8,128)(2,1)S(1)}, u32[]{:S(2)}, u32[]{:S(2)}) collective-permute-start(bf16[512,128]{1,0:T(8,128)(2,1)} %get-tuple-element.28), channel_id=1, source_target_pairs={{0,2},{1,3},{2,0},{3,1},{4,6},{5,7},{6,4},{7,5},{8,10},{9,11},{10,... | collective-permute-start | bytes 393224 | tf_op jit(solution)/shard_map/ppermute | solution.py:132
  114.8 8.2 %collective-permute-start.22 = (bf16[512,128]{1,0:T(8,128)(2,1)}, bf16[512,128]{1,0:T(8,128)(2,1)S(1)}, u32[]{:S(2)}, u32[]{:S(2)}) collective-permute-start(bf16[512,128]{1,0:T(8,128)(2,1)} %get-tuple-element.29), channel_id=1, source_target_pairs={{0,3},{1,0},{2,1},{3,2},{4,7},{5,4},{6,5},{7,6},{8,11},{9,8},{10,9... | collective-permute-start | bytes 393224 | tf_op jit(solution)/shard_map/ppermute | solution.py:132
  122.3 2.4 %collective-permute-start.26 = (f32[512,128]{1,0:T(8,128)S(1)}, f32[512,128]{1,0:T(8,128)S(1)}, u32[]{:S(2)}, u32[]{:S(2)}) collective-permute-start(f32[512,128]{1,0:T(8,128)S(1)} %slice.24), channel_id=1, source_target_pairs={{0,4},{4,0},{8,12},{12,8},{16,20},{20,16},{24,28},{28,24},{1,5},{5... | collective-permute-start | bytes 786440 | tf_op jit(solution)/shard_map/ppermute | solution.py:155
  (13 other events, 50.7 us)

commit v14 on v12

--- a/solution.py
+++ b/solution.py
@@ -192,7 +192,7 @@
     rows = rotate_index(tile_row[0, 0], me_col, n_col, per_run)
     if paired(n_row):
         cols = pair_index(tile_col[0, 0], me_row, per_run)
-        gathers = (gather_paired, gather_paired)
+        gathers = (gather_xor, gather_xor)
         scatters = (scatter_paired, scatter_paired)
         splits = (n_row // 2, n_row // 2)
     else:

time: 121 us -> 125 us (1.033); the launches traced: 123 us -> 123 us
  starting transfers between devices: 28.8 us -> 52.4 us
  Pallas kernels: 37.5 us -> 21.9 us
  waiting for transfers between devices: 44.6 us -> 36.8 us
    pallas_call x2, Pallas kernels: 37.5 us -> 21.9 us  [tile_sweep(): pl.pallas_call(functools.partial(sweep_kernel, tile, group, len(emb_piece...]
    ppermute x6, starting transfers between devices: 7 us -> 18.4 us  [scatter_paired(): got = lax.ppermute(blocks[b], axis, [(i, i ^ 2 * b) for i in range(n)])]
    ppermute x6, waiting for transfers between devices: 11.3 us -> 0.02 us  [scatter_rotated(): lax.ppermute(chunks[(n - s) % n], axis, [(i, (i + s) % n) for i in range(...]
    ppermute x8 -> x14, waiting for transfers between devices: 2.96 us -> 12.1 us  [gather_xor(): pieces.append(lax.ppermute(x, axis, [(i, i ^ p) for i in range(n)]))]
    ppermute x6, starting transfers between devices: 3.93 us -> 11.5 us  [scatter_rotated(): lax.ppermute(chunks[(n - s) % n], axis, [(i, (i + s) % n) for i in range(...]
    ppermute x6, waiting for transfers between devices: 15.4 us -> 11.5 us  [scatter_paired(): got = lax.ppermute(blocks[b], axis, [(i, i ^ 2 * b) for i in range(n)])]
    ppermute x8 -> x14, starting transfers between devices: 7.7 us -> 10.7 us  [gather_xor(): pieces.append(lax.ppermute(x, axis, [(i, i ^ p) for i in range(n)]))]
    ppermute x6, waiting for transfers between devices: 14.9 us -> 13.3 us  [gather_rotated(): pieces.append(lax.ppermute(x, axis, [(i, (i + s) % n) for i in range(n)]))]
  transfers between devices with their start and end apart: 28 -> 34, of which waited for: 14 -> 11; matrix products, arithmetic and copies ran while one was open for 5% -> 6% of each run, Pallas kernels for 0% -> 0%
where the time goes in v14:
time: 125 us; the launch traced here: 123 us
  starting transfers between devices  52.4 us (42%)
  waiting for transfers between devices  36.8 us (29%)
  Pallas kernels  21.9 us (18%)
  other arithmetic  9.02 us (7%)
  between operations  1.68 us (1%)
  local copies, waits for them, and re-layouts  1.33 us (1%)
    pallas_call x2, Pallas kernels, tile_sweep(): pl.pallas_call(functools.partial(sweep_kernel, tile, group, len(emb_piece...  21.9 us
    ppermute x6, starting transfers between devices, scatter_paired(): got = lax.ppermute(blocks[b], axis, [(i, i ^ 2 * b) for i in range(n)])  18.4 us
    ppermute x6, waiting for transfers between devices, gather_rotated(): pieces.append(lax.ppermute(x, axis, [(i, (i + s) % n) for i in range(n)]))  13.3 us
    ppermute x14, waiting for transfers between devices, gather_xor(): pieces.append(lax.ppermute(x, axis, [(i, i ^ p) for i in range(n)]))  12.1 us
    ppermute x6, starting transfers between devices, gather_rotated(): pieces.append(lax.ppermute(x, axis, [(i, (i + s) % n) for i in range(n)]))  11.7 us
    ppermute x6, starting transfers between devices, scatter_rotated(): lax.ppermute(chunks[(n - s) % n], axis, [(i, (i + s) % n) for i in range(...  11.5 us
    ppermute x6, waiting for transfers between devices, scatter_paired(): got = lax.ppermute(blocks[b], axis, [(i, i ^ 2 * b) for i in range(n)])  11.5 us
    ppermute x14, starting transfers between devices, gather_xor(): pieces.append(lax.ppermute(x, axis, [(i, i ^ p) for i in range(n)]))  10.7 us
  transfers between devices with their start and end apart: 34, of which 11 were waited for; matrix products, arithmetic and copies ran while one was open for 6% of the time, Pallas kernels for 0%

profile of v14, /device:TPU:0, one launch (start us, length us, event | category | flops | bytes accessed | tf_op | source)
XLA Modules:
  0.0 123.1 jit_solution(10393168800755138181)
XLA Ops:
  1.6 5.1 %collective-permute-start.2 = (bf16[512,128]{1,0:T(8,128)(2,1)S(1)}, bf16[512,128]{1,0:T(8,128)(2,1)S(1)}, u32[]{:S(2)}, u32[]{:S(2)}) collective-permute-start(bf16[512,128]{1,0:T(8,128)(2,1)S(1)} %convert_element_type.60.refs_0_), channel_id=1, source_target_pairs={{0,3},{1,0},{2,1},{3,2},{4,7},{5,4},{6,5},{7,6},{8,11},{9,8},{10,9... | collective-permute-start | bytes 393224 | tf_op jit(solution)/shard_map/ppermute | solution.py:125
  6.7 1.0 collective-permute-start
  8.7 1.1 collective-permute-start.9
  9.8 1.5 %collective-permute-start.8 = (bf16[512,128]{1,0:T(8,128)(2,1)S(1)}, bf16[512,128]{1,0:T(8,128)(2,1)S(1)}, u32[]{:S(2)}, u32[]{:S(2)}) collective-permute-start(bf16[512,128]{1,0:T(8,128)(2,1)S(1)} %convert_element_type.61.refs_4_), channel_id=1, source_target_pairs={{0,24},{4,28},{8,16},{12,20},{16,8},{20,12},{24,0},{28,4},{1,25},{... | collective-permute-start | bytes 393224 | tf_op jit(solution)/shard_map/ppermute | solution.py:162
  12.0 1.4 %collective-permute-start.7 = (bf16[512,128]{1,0:T(8,128)(2,1)S(1)}, bf16[512,128]{1,0:T(8,128)(2,1)S(1)}, u32[]{:S(2)}, u32[]{:S(2)}) collective-permute-start(bf16[512,128]{1,0:T(8,128)(2,1)S(1)} %convert_element_type.61.refs_4_), channel_id=1, source_target_pairs={{0,20},{4,16},{8,28},{12,24},{16,4},{20,0},{24,12},{28,8},{1,21},{... | collective-permute-start | bytes 393224 | tf_op jit(solution)/shard_map/ppermute | solution.py:162
  13.4 4.5 %collective-permute-done.1.refs_2_ = bf16[512,128]{1,0:T(8,128)(2,1)S(1)} collective-permute-done((bf16[512,128]{1,0:T(8,128)(2,1)S(1)}, bf16[512,128]{1,0:T(8,128)(2,1)S(1)}, u32[]{:S(2)}, u32[]{:S(2)}) %collective-permute-start.1) | collective-permute-done | bytes 131104 | tf_op jit(solution)/shard_map/ppermute | solution.py:125
  17.9 1.5 %collective-permute-start.6 = (bf16[512,128]{1,0:T(8,128)(2,1)S(1)}, bf16[512,128]{1,0:T(8,128)(2,1)S(1)}, u32[]{:S(2)}, u32[]{:S(2)}) collective-permute-start(bf16[512,128]{1,0:T(8,128)(2,1)S(1)} %convert_element_type.61.refs_4_), channel_id=1, source_target_pairs={{0,16},{4,20},{8,24},{12,28},{16,0},{20,4},{24,8},{28,12},{1,17},{... | collective-permute-start | bytes 393224 | tf_op jit(solution)/shard_map/ppermute | solution.py:162
  19.6 1.4 %collective-permute-start.4 = (bf16[512,128]{1,0:T(8,128)(2,1)S(1)}, bf16[512,128]{1,0:T(8,128)(2,1)S(1)}, u32[]{:S(2)}, u32[]{:S(2)}) collective-permute-start(bf16[512,128]{1,0:T(8,128)(2,1)S(1)} %convert_element_type.61.refs_4_), channel_id=1, source_target_pairs={{0,8},{4,12},{8,0},{12,4},{16,24},{20,28},{24,16},{28,20},{1,9},{5... | collective-permute-start | bytes 393224 | tf_op jit(solution)/shard_map/ppermute | solution.py:162
  21.3 1.3 %fusion.4 = (s32[64]{0:T(128)}, s32[64]{0:T(128)}) fusion(s32[1,1,64]{2,1,0:T(1,128)} %param.11, s32[]{:T(128)S(6)} %axis_index.22, s32[1,1,64]{2,1,0:T(1,128)} %param.12, s32[]{:T(128)S(6)} %axis_index.25), kind=kLoop, calls=%fused_computation.23 | loop fusion | flops 3520 | bytes 1032 | tf_op jit(solution)/shard_map/add | solution.py:180
  22.6 1.3 %collective-permute-done.6.refs_8_ = bf16[512,128]{1,0:T(8,128)(2,1)S(1)} collective-permute-done((bf16[512,128]{1,0:T(8,128)(2,1)S(1)}, bf16[512,128]{1,0:T(8,128)(2,1)S(1)}, u32[]{:S(2)}, u32[]{:S(2)}) %collective-permute-start.6) | collective-permute-done | bytes 131104 | tf_op jit(solution)/shard_map/ppermute | solution.py:162
  23.9 1.3 %collective-permute-done.5.refs_7_ = bf16[512,128]{1,0:T(8,128)(2,1)S(1)} collective-permute-done((bf16[512,128]{1,0:T(8,128)(2,1)S(1)}, bf16[512,128]{1,0:T(8,128)(2,1)S(1)}, u32[]{:S(2)}, u32[]{:S(2)}) %collective-permute-start.5) | collective-permute-done | bytes 131104 | tf_op jit(solution)/shard_map/ppermute | solution.py:162
  25.2 2.9 %collective-permute-done.4.refs_6_ = bf16[512,128]{1,0:T(8,128)(2,1)S(1)} collective-permute-done((bf16[512,128]{1,0:T(8,128)(2,1)S(1)}, bf16[512,128]{1,0:T(8,128)(2,1)S(1)}, u32[]{:S(2)}, u32[]{:S(2)}) %collective-permute-start.4) | collective-permute-done | bytes 131104 | tf_op jit(solution)/shard_map/ppermute | solution.py:162
  28.7 11.0 %shard_map.86 = (bf16[512,128]{1,0:T(8,128)(2,1)}, bf16[512,128]{1,0:T(8,128)(2,1)}, bf16[512,128]{1,0:T(8,128)(2,1)}, bf16[512,128]{1,0:T(8,128)(2,1)}, bf16[10...) custom-call(s32[64]{0:T(128)} %get-tuple-element.34.rows_ref, ...), custom_call_target="tpu_custom_call" | custom-call | flops 3221225472 | bytes 21495808 | tf_op jit(solution)/shard_map/pallas_call | solution.py:107
  39.8 8.3 %collective-permute-start.17 = (bf16[1024,128]{1,0:T(8,128)(2,1)}, bf16[1024,128]{1,0:T(8,128)(2,1)S(1)}, u32[]{:S(2)}, u32[]{:S(2)}) collective-permute-start(bf16[1024,128]{1,0:T(8,128)(2,1)} %get-tuple-element.24), channel_id=1, source_target_pairs={{0,16},{4,20},{8,24},{12,28},{16,0},{20,4},{24,8},{28,12},{1,17},{... | collective-permute-start | bytes 786440 | tf_op jit(solution)/shard_map/ppermute | solution.py:152
  48.1 3.7 %collective-permute-start.11 = (bf16[512,128]{1,0:T(8,128)(2,1)}, bf16[512,128]{1,0:T(8,128)(2,1)S(1)}, u32[]{:S(2)}, u32[]{:S(2)}) collective-permute-start(bf16[512,128]{1,0:T(8,128)(2,1)} %get-tuple-element.20), channel_id=1, source_target_pairs={{0,2},{1,3},{2,0},{3,1},{4,6},{5,7},{6,4},{7,5},{8,10},{9,11},{10,... | collective-permute-start | bytes 393224 | tf_op jit(solution)/shard_map/ppermute | solution.py:132
  51.8 2.9 %collective-permute-start.12 = (bf16[512,128]{1,0:T(8,128)(2,1)}, bf16[512,128]{1,0:T(8,128)(2,1)S(1)}, u32[]{:S(2)}, u32[]{:S(2)}) collective-permute-start(bf16[512,128]{1,0:T(8,128)(2,1)} %get-tuple-element.21), channel_id=1, source_target_pairs={{0,3},{1,0},{2,1},{3,2},{4,7},{5,4},{6,5},{7,6},{8,11},{9,8},{10,9... | collective-permute-start | bytes 393224 | tf_op jit(solution)/shard_map/ppermute | solution.py:132
  54.7 5.7 %collective-permute-done.17 = bf16[1024,128]{1,0:T(8,128)(2,1)S(1)} collective-permute-done((bf16[1024,128]{1,0:T(8,128)(2,1)}, bf16[1024,128]{1,0:T(8,128)(2,1)S(1)}, u32[]{:S(2)}, u32[]{:S(2)}) %collective-permute-start.17) | collective-permute-done | bytes 262176 | tf_op jit(solution)/shard_map/ppermute | solution.py:152
  60.4 1.1 convert_add_fusion.1
  62.7 4.9 %collective-permute-start.15 = (bf16[512,128]{1,0:T(8,128)(2,1)S(1)}, bf16[512,128]{1,0:T(8,128)(2,1)S(1)}, u32[]{:S(2)}, u32[]{:S(2)}) collective-permute-start(bf16[512,128]{1,0:T(8,128)(2,1)S(1)} %fusion.9.refs_0_), channel_id=1, source_target_pairs={{0,3},{1,0},{2,1},{3,2},{4,7},{5,4},{6,5},{7,6},{8,11},{9,8},{10,9... | collective-permute-start | bytes 393224 | tf_op jit(solution)/shard_map/ppermute | solution.py:125
  68.4 1.3 %collective-permute-start.25 = (bf16[512,128]{1,0:T(8,128)(2,1)S(1)}, bf16[512,128]{1,0:T(8,128)(2,1)S(1)}, u32[]{:S(2)}, u32[]{:S(2)}) collective-permute-start(bf16[512,128]{1,0:T(8,128)(2,1)S(1)} %fusion.8.refs_4_), channel_id=1, source_target_pairs={{0,24},{4,28},{8,16},{12,20},{16,8},{20,12},{24,0},{28,4},{1,25},{... | collective-permute-start | bytes 393224 | tf_op jit(solution)/shard_map/ppermute | solution.py:162
  69.7 1.9 %collective-permute-done.15.refs_3_ = bf16[512,128]{1,0:T(8,128)(2,1)S(1)} collective-permute-done((bf16[512,128]{1,0:T(8,128)(2,1)S(1)}, bf16[512,128]{1,0:T(8,128)(2,1)S(1)}, u32[]{:S(2)}, u32[]{:S(2)}) %collective-permute-start.15) | collective-permute-done | bytes 131104 | tf_op jit(solution)/shard_map/ppermute | solution.py:125
  71.5 6.9 %collective-permute-done.14.refs_2_ = bf16[512,128]{1,0:T(8,128)(2,1)S(1)} collective-permute-done((bf16[512,128]{1,0:T(8,128)(2,1)S(1)}, bf16[512,128]{1,0:T(8,128)(2,1)S(1)}, u32[]{:S(2)}, u32[]{:S(2)}) %collective-permute-start.14) | collective-permute-done | bytes 131104 | tf_op jit(solution)/shard_map/ppermute | solution.py:125
  78.5 1.4 %collective-permute-start.21 = (bf16[512,128]{1,0:T(8,128)(2,1)S(1)}, bf16[512,128]{1,0:T(8,128)(2,1)S(1)}, u32[]{:S(2)}, u32[]{:S(2)}) collective-permute-start(bf16[512,128]{1,0:T(8,128)(2,1)S(1)} %fusion.8.refs_4_), channel_id=1, source_target_pairs={{0,8},{4,12},{8,0},{12,4},{16,24},{20,28},{24,16},{28,20},{1,9},{5... | collective-permute-start | bytes 393224 | tf_op jit(solution)/shard_map/ppermute | solution.py:162
  80.4 3.0 %collective-permute-done.23.refs_8_ = bf16[512,128]{1,0:T(8,128)(2,1)S(1)} collective-permute-done((bf16[512,128]{1,0:T(8,128)(2,1)S(1)}, bf16[512,128]{1,0:T(8,128)(2,1)S(1)}, u32[]{:S(2)}, u32[]{:S(2)}) %collective-permute-start.23) | collective-permute-done | bytes 131104 | tf_op jit(solution)/shard_map/ppermute | solution.py:162
  84.3 2.7 %collective-permute-done.21.refs_6_ = bf16[512,128]{1,0:T(8,128)(2,1)S(1)} collective-permute-done((bf16[512,128]{1,0:T(8,128)(2,1)S(1)}, bf16[512,128]{1,0:T(8,128)(2,1)S(1)}, u32[]{:S(2)}, u32[]{:S(2)}) %collective-permute-start.21) | collective-permute-done | bytes 131104 | tf_op jit(solution)/shard_map/ppermute | solution.py:162
  87.7 11.0 %shard_map.87 = (bf16[512,128]{1,0:T(8,128)(2,1)}, bf16[512,128]{1,0:T(8,128)(2,1)}, bf16[512,128]{1,0:T(8,128)(2,1)}, bf16[512,128]{1,0:T(8,128)(2,1)}, bf16[10...) custom-call(s32[64]{0:T(128)} %get-tuple-element.34.rows_ref, ...), custom_call_target="tpu_custom_call" | custom-call | flops 3221225472 | bytes 21495808 | tf_op jit(solution)/shard_map/pallas_call | solution.py:107
  98.7 9.9 %collective-permute-start.31 = (bf16[1024,128]{1,0:T(8,128)(2,1)}, bf16[1024,128]{1,0:T(8,128)(2,1)S(1)}, u32[]{:S(2)}, u32[]{:S(2)}) collective-permute-start(bf16[1024,128]{1,0:T(8,128)(2,1)} %get-tuple-element.32), channel_id=1, source_target_pairs={{0,16},{4,20},{8,24},{12,28},{16,0},{20,4},{24,8},{28,12},{1,17},{... | collective-permute-start | bytes 786440 | tf_op jit(solution)/shard_map/ppermute | solution.py:152
  108.6 1.9 %collective-permute-start.28 = (bf16[512,128]{1,0:T(8,128)(2,1)}, bf16[512,128]{1,0:T(8,128)(2,1)S(1)}, u32[]{:S(2)}, u32[]{:S(2)}) collective-permute-start(bf16[512,128]{1,0:T(8,128)(2,1)} %get-tuple-element.28), channel_id=1, source_target_pairs={{0,2},{1,3},{2,0},{3,1},{4,6},{5,7},{6,4},{7,5},{8,10},{9,11},{10,... | collective-permute-start | bytes 393224 | tf_op jit(solution)/shard_map/ppermute | solution.py:132
  110.6 2.9 %collective-permute-start.29 = (bf16[512,128]{1,0:T(8,128)(2,1)}, bf16[512,128]{1,0:T(8,128)(2,1)S(1)}, u32[]{:S(2)}, u32[]{:S(2)}) collective-permute-start(bf16[512,128]{1,0:T(8,128)(2,1)} %get-tuple-element.29), channel_id=1, source_target_pairs={{0,3},{1,0},{2,1},{3,2},{4,7},{5,4},{6,5},{7,6},{8,11},{9,8},{10,9... | collective-permute-start | bytes 393224 | tf_op jit(solution)/shard_map/ppermute | solution.py:132
  113.5 5.8 %collective-permute-done.31 = bf16[1024,128]{1,0:T(8,128)(2,1)S(1)} collective-permute-done((bf16[1024,128]{1,0:T(8,128)(2,1)}, bf16[1024,128]{1,0:T(8,128)(2,1)S(1)}, u32[]{:S(2)}, u32[]{:S(2)}) %collective-permute-start.31) | collective-permute-done | bytes 262176 | tf_op jit(solution)/shard_map/ppermute | solution.py:152
  119.3 1.1 convert_add_fusion
  120.5 1.8 %multiply_add_fusion = f32[512,128]{1,0:T(8,128)} fusion(bf16[512,128]{1,0:T(8,128)(2,1)S(1)} %collective-permute-done.29, bf16[512,128]{1,0:T(8,128)(2,1)S(1)} %collective-permute-done.28, bf16[512,128]{1,0:T(8,128)(2,1)S(1)} %collective-permute-done.27, bf16[512,128]{1,0:T(8,128)(2,1)} %get-tuple-element.26, f32[512,128]{1,0:T(8,128)S(1)} %copy-done, ...), kind=kLoop, calls=%fused_computation.8 | loop fusion | flops 1179648 | bytes 1572864 | tf_op jit(solution)/shard_map/add | solution.py:213
  (103 shorter events, 8.0 us)
Async XLA Ops:
  1.6 10.3 %collective-permute-start.2 = (bf16[512,128]{1,0:T(8,128)(2,1)S(1)}, bf16[512,128]{1,0:T(8,128)(2,1)S(1)}, u32[]{:S(2)}, u32[]{:S(2)}) collective-permute-start(bf16[512,128]{1,0:T(8,128)(2,1)S(1)} %convert_element_type.60.refs_0_), channel_id=1, source_target_pairs={{0,3},{1,0},{2,1},{3,2},{4,7},{5,4},{6,5},{7,6},{8,11},{9,8},{10,9... | collective-permute-start | bytes 393224 | tf_op jit(solution)/shard_map/ppermute | solution.py:125
  6.7 11.2 %collective-permute-start.1 = (bf16[512,128]{1,0:T(8,128)(2,1)S(1)}, bf16[512,128]{1,0:T(8,128)(2,1)S(1)}, u32[]{:S(2)}, u32[]{:S(2)}) collective-permute-start(bf16[512,128]{1,0:T(8,128)(2,1)S(1)} %convert_element_type.60.refs_0_), channel_id=1, source_target_pairs={{0,2},{1,3},{2,0},{3,1},{4,6},{5,7},{6,4},{7,5},{8,10},{9,11},{10,... | collective-permute-start | bytes 393224 | tf_op jit(solution)/shard_map/ppermute | solution.py:125
  6.7 12.7 %collective-permute-start = (bf16[512,128]{1,0:T(8,128)(2,1)S(1)}, bf16[512,128]{1,0:T(8,128)(2,1)S(1)}, u32[]{:S(2)}, u32[]{:S(2)}) collective-permute-start(bf16[512,128]{1,0:T(8,128)(2,1)S(1)} %convert_element_type.60.refs_0_), channel_id=1, source_target_pairs={{0,1},{1,2},{2,3},{3,0},{4,5},{5,6},{6,7},{7,4},{8,9},{9,10},{10,1... | collective-permute-start | bytes 393224 | tf_op jit(solution)/shard_map/ppermute | solution.py:125
  8.7 10.9 %collective-permute-start.9 = (bf16[512,128]{1,0:T(8,128)(2,1)S(1)}, bf16[512,128]{1,0:T(8,128)(2,1)S(1)}, u32[]{:S(2)}, u32[]{:S(2)}) collective-permute-start(bf16[512,128]{1,0:T(8,128)(2,1)S(1)} %convert_element_type.61.refs_4_), channel_id=1, source_target_pairs={{0,28},{4,24},{8,20},{12,16},{16,12},{20,8},{24,4},{28,0},{1,29},{... | collective-permute-start | bytes 393224 | tf_op jit(solution)/shard_map/ppermute | solution.py:162
  9.8 11.2 %collective-permute-start.8 = (bf16[512,128]{1,0:T(8,128)(2,1)S(1)}, bf16[512,128]{1,0:T(8,128)(2,1)S(1)}, u32[]{:S(2)}, u32[]{:S(2)}) collective-permute-start(bf16[512,128]{1,0:T(8,128)(2,1)S(1)} %convert_element_type.61.refs_4_), channel_id=1, source_target_pairs={{0,24},{4,28},{8,16},{12,20},{16,8},{20,12},{24,0},{28,4},{1,25},{... | collective-permute-start | bytes 393224 | tf_op jit(solution)/shard_map/ppermute | solution.py:162
  12.0 10.6 %collective-permute-start.7 = (bf16[512,128]{1,0:T(8,128)(2,1)S(1)}, bf16[512,128]{1,0:T(8,128)(2,1)S(1)}, u32[]{:S(2)}, u32[]{:S(2)}) collective-permute-start(bf16[512,128]{1,0:T(8,128)(2,1)S(1)} %convert_element_type.61.refs_4_), channel_id=1, source_target_pairs={{0,20},{4,16},{8,28},{12,24},{16,4},{20,0},{24,12},{28,8},{1,21},{... | collective-permute-start | bytes 393224 | tf_op jit(solution)/shard_map/ppermute | solution.py:162
  17.9 6.0 %collective-permute-start.6 = (bf16[512,128]{1,0:T(8,128)(2,1)S(1)}, bf16[512,128]{1,0:T(8,128)(2,1)S(1)}, u32[]{:S(2)}, u32[]{:S(2)}) collective-permute-start(bf16[512,128]{1,0:T(8,128)(2,1)S(1)} %convert_element_type.61.refs_4_), channel_id=1, source_target_pairs={{0,16},{4,20},{8,24},{12,28},{16,0},{20,4},{24,8},{28,12},{1,17},{... | collective-permute-start | bytes 393224 | tf_op jit(solution)/shard_map/ppermute | solution.py:162
  19.4 5.8 %collective-permute-start.5 = (bf16[512,128]{1,0:T(8,128)(2,1)S(1)}, bf16[512,128]{1,0:T(8,128)(2,1)S(1)}, u32[]{:S(2)}, u32[]{:S(2)}) collective-permute-start(bf16[512,128]{1,0:T(8,128)(2,1)S(1)} %convert_element_type.61.refs_4_), channel_id=1, source_target_pairs={{0,12},{4,8},{8,4},{12,0},{16,28},{20,24},{24,20},{28,16},{1,13},{... | collective-permute-start | bytes 393224 | tf_op jit(solution)/shard_map/ppermute | solution.py:162
  19.6 8.4 %collective-permute-start.4 = (bf16[512,128]{1,0:T(8,128)(2,1)S(1)}, bf16[512,128]{1,0:T(8,128)(2,1)S(1)}, u32[]{:S(2)}, u32[]{:S(2)}) collective-permute-start(bf16[512,128]{1,0:T(8,128)(2,1)S(1)} %convert_element_type.61.refs_4_), channel_id=1, source_target_pairs={{0,8},{4,12},{8,0},{12,4},{16,24},{20,28},{24,16},{28,20},{1,9},{5... | collective-permute-start | bytes 393224 | tf_op jit(solution)/shard_map/ppermute | solution.py:162
  21.0 7.0 %collective-permute-start.3 = (bf16[512,128]{1,0:T(8,128)(2,1)S(1)}, bf16[512,128]{1,0:T(8,128)(2,1)S(1)}, u32[]{:S(2)}, u32[]{:S(2)}) collective-permute-start(bf16[512,128]{1,0:T(8,128)(2,1)S(1)} %convert_element_type.61.refs_4_), channel_id=1, source_target_pairs={{0,4},{4,0},{8,12},{12,8},{16,20},{20,16},{24,28},{28,24},{1,5},{5... | collective-permute-start | bytes 393224 | tf_op jit(solution)/shard_map/ppermute | solution.py:162
  39.7 12.1 %collective-permute-start.16 = (bf16[1024,128]{1,0:T(8,128)(2,1)}, bf16[1024,128]{1,0:T(8,128)(2,1)S(1)}, u32[]{:S(2)}, u32[]{:S(2)}) collective-permute-start(bf16[1024,128]{1,0:T(8,128)(2,1)} %get-tuple-element.23), channel_id=1, source_target_pairs={{0,8},{4,12},{8,0},{12,4},{16,24},{20,28},{24,16},{28,20},{1,9},{5... | collective-permute-start | bytes 786440 | tf_op jit(solution)/shard_map/ppermute | solution.py:152
  39.8 20.6 %collective-permute-start.17 = (bf16[1024,128]{1,0:T(8,128)(2,1)}, bf16[1024,128]{1,0:T(8,128)(2,1)S(1)}, u32[]{:S(2)}, u32[]{:S(2)}) collective-permute-start(bf16[1024,128]{1,0:T(8,128)(2,1)} %get-tuple-element.24), channel_id=1, source_target_pairs={{0,16},{4,20},{8,24},{12,28},{16,0},{20,4},{24,8},{28,12},{1,17},{... | collective-permute-start | bytes 786440 | tf_op jit(solution)/shard_map/ppermute | solution.py:152
  48.1 12.3 %collective-permute-start.18 = (bf16[1024,128]{1,0:T(8,128)(2,1)}, bf16[1024,128]{1,0:T(8,128)(2,1)S(1)}, u32[]{:S(2)}, u32[]{:S(2)}) collective-permute-start(bf16[1024,128]{1,0:T(8,128)(2,1)} %get-tuple-element.25), channel_id=1, source_target_pairs={{0,24},{4,28},{8,16},{12,20},{16,8},{20,12},{24,0},{28,4},{1,25},{... | collective-permute-start | bytes 786440 | tf_op jit(solution)/shard_map/ppermute | solution.py:152
  48.1 13.5 %collective-permute-start.10 = (bf16[512,128]{1,0:T(8,128)(2,1)}, bf16[512,128]{1,0:T(8,128)(2,1)S(1)}, u32[]{:S(2)}, u32[]{:S(2)}) collective-permute-start(bf16[512,128]{1,0:T(8,128)(2,1)} %get-tuple-element.19), channel_id=1, source_target_pairs={{0,1},{1,2},{2,3},{3,0},{4,5},{5,6},{6,7},{7,4},{8,9},{9,10},{10,1... | collective-permute-start | bytes 393224 | tf_op jit(solution)/shard_map/ppermute | solution.py:132
  48.1 13.5 %collective-permute-start.11 = (bf16[512,128]{1,0:T(8,128)(2,1)}, bf16[512,128]{1,0:T(8,128)(2,1)S(1)}, u32[]{:S(2)}, u32[]{:S(2)}) collective-permute-start(bf16[512,128]{1,0:T(8,128)(2,1)} %get-tuple-element.20), channel_id=1, source_target_pairs={{0,2},{1,3},{2,0},{3,1},{4,6},{5,7},{6,4},{7,5},{8,10},{9,11},{10,... | collective-permute-start | bytes 393224 | tf_op jit(solution)/shard_map/ppermute | solution.py:132
  51.8 9.8 %collective-permute-start.12 = (bf16[512,128]{1,0:T(8,128)(2,1)}, bf16[512,128]{1,0:T(8,128)(2,1)S(1)}, u32[]{:S(2)}, u32[]{:S(2)}) collective-permute-start(bf16[512,128]{1,0:T(8,128)(2,1)} %get-tuple-element.21), channel_id=1, source_target_pairs={{0,3},{1,0},{2,1},{3,2},{4,7},{5,4},{6,5},{7,6},{8,11},{9,8},{10,9... | collective-permute-start | bytes 393224 | tf_op jit(solution)/shard_map/ppermute | solution.py:132
  61.5 6.7 %collective-permute-start.19 = (f32[512,128]{1,0:T(8,128)S(1)}, f32[512,128]{1,0:T(8,128)S(1)}, u32[]{:S(2)}, u32[]{:S(2)}) collective-permute-start(f32[512,128]{1,0:T(8,128)S(1)} %slice.17), channel_id=1, source_target_pairs={{0,4},{4,0},{8,12},{12,8},{16,20},{20,16},{24,28},{28,24},{1,5},{5... | collective-permute-start | bytes 786440 | tf_op jit(solution)/shard_map/ppermute | solution.py:155
  62.7 8.9 %collective-permute-start.15 = (bf16[512,128]{1,0:T(8,128)(2,1)S(1)}, bf16[512,128]{1,0:T(8,128)(2,1)S(1)}, u32[]{:S(2)}, u32[]{:S(2)}) collective-permute-start(bf16[512,128]{1,0:T(8,128)(2,1)S(1)} %fusion.9.refs_0_), channel_id=1, source_target_pairs={{0,3},{1,0},{2,1},{3,2},{4,7},{5,4},{6,5},{7,6},{8,11},{9,8},{10,9... | collective-permute-start | bytes 393224 | tf_op jit(solution)/shard_map/ppermute | solution.py:125
  67.6 10.8 %collective-permute-start.14 = (bf16[512,128]{1,0:T(8,128)(2,1)S(1)}, bf16[512,128]{1,0:T(8,128)(2,1)S(1)}, u32[]{:S(2)}, u32[]{:S(2)}) collective-permute-start(bf16[512,128]{1,0:T(8,128)(2,1)S(1)} %fusion.9.refs_0_), channel_id=1, source_target_pairs={{0,2},{1,3},{2,0},{3,1},{4,6},{5,7},{6,4},{7,5},{8,10},{9,11},{10,... | collective-permute-start | bytes 393224 | tf_op jit(solution)/shard_map/ppermute | solution.py:125
  67.6 10.9 %collective-permute-start.13 = (bf16[512,128]{1,0:T(8,128)(2,1)S(1)}, bf16[512,128]{1,0:T(8,128)(2,1)S(1)}, u32[]{:S(2)}, u32[]{:S(2)}) collective-permute-start(bf16[512,128]{1,0:T(8,128)(2,1)S(1)} %fusion.9.refs_0_), channel_id=1, source_target_pairs={{0,1},{1,2},{2,3},{3,0},{4,5},{5,6},{6,7},{7,4},{8,9},{9,10},{10,1... | collective-permute-start | bytes 393224 | tf_op jit(solution)/shard_map/ppermute | solution.py:125
  68.3 10.2 %collective-permute-start.26 = (bf16[512,128]{1,0:T(8,128)(2,1)S(1)}, bf16[512,128]{1,0:T(8,128)(2,1)S(1)}, u32[]{:S(2)}, u32[]{:S(2)}) collective-permute-start(bf16[512,128]{1,0:T(8,128)(2,1)S(1)} %fusion.8.refs_4_), channel_id=1, source_target_pairs={{0,28},{4,24},{8,20},{12,16},{16,12},{20,8},{24,4},{28,0},{1,29},{... | collective-permute-start | bytes 393224 | tf_op jit(solution)/shard_map/ppermute | solution.py:162
  68.4 11.6 %collective-permute-start.25 = (bf16[512,128]{1,0:T(8,128)(2,1)S(1)}, bf16[512,128]{1,0:T(8,128)(2,1)S(1)}, u32[]{:S(2)}, u32[]{:S(2)}) collective-permute-start(bf16[512,128]{1,0:T(8,128)(2,1)S(1)} %fusion.8.refs_4_), channel_id=1, source_target_pairs={{0,24},{4,28},{8,16},{12,20},{16,8},{20,12},{24,0},{28,4},{1,25},{... | collective-permute-start | bytes 393224 | tf_op jit(solution)/shard_map/ppermute | solution.py:162
  71.5 8.8 %collective-permute-start.24 = (bf16[512,128]{1,0:T(8,128)(2,1)S(1)}, bf16[512,128]{1,0:T(8,128)(2,1)S(1)}, u32[]{:S(2)}, u32[]{:S(2)}) collective-permute-start(bf16[512,128]{1,0:T(8,128)(2,1)S(1)} %fusion.8.refs_4_), channel_id=1, source_target_pairs={{0,20},{4,16},{8,28},{12,24},{16,4},{20,0},{24,12},{28,8},{1,21},{... | collective-permute-start | bytes 393224 | tf_op jit(solution)/shard_map/ppermute | solution.py:162
  78.4 5.8 %collective-permute-start.22 = (bf16[512,128]{1,0:T(8,128)(2,1)S(1)}, bf16[512,128]{1,0:T(8,128)(2,1)S(1)}, u32[]{:S(2)}, u32[]{:S(2)}) collective-permute-start(bf16[512,128]{1,0:T(8,128)(2,1)S(1)} %fusion.8.refs_4_), channel_id=1, source_target_pairs={{0,12},{4,8},{8,4},{12,0},{16,28},{20,24},{24,20},{28,16},{1,13},{... | collective-permute-start | bytes 393224 | tf_op jit(solution)/shard_map/ppermute | solution.py:162
  78.5 8.4 %collective-permute-start.21 = (bf16[512,128]{1,0:T(8,128)(2,1)S(1)}, bf16[512,128]{1,0:T(8,128)(2,1)S(1)}, u32[]{:S(2)}, u32[]{:S(2)}) collective-permute-start(bf16[512,128]{1,0:T(8,128)(2,1)S(1)} %fusion.8.refs_4_), channel_id=1, source_target_pairs={{0,8},{4,12},{8,0},{12,4},{16,24},{20,28},{24,16},{28,20},{1,9},{5... | collective-permute-start | bytes 393224 | tf_op jit(solution)/shard_map/ppermute | solution.py:162
  80.0 7.0 %collective-permute-start.20 = (bf16[512,128]{1,0:T(8,128)(2,1)S(1)}, bf16[512,128]{1,0:T(8,128)(2,1)S(1)}, u32[]{:S(2)}, u32[]{:S(2)}) collective-permute-start(bf16[512,128]{1,0:T(8,128)(2,1)S(1)} %fusion.8.refs_4_), channel_id=1, source_target_pairs={{0,4},{4,0},{8,12},{12,8},{16,20},{20,16},{24,28},{28,24},{1,5},{5... | collective-permute-start | bytes 393224 | tf_op jit(solution)/shard_map/ppermute | solution.py:162
  98.6 11.9 %collective-permute-start.30 = (bf16[1024,128]{1,0:T(8,128)(2,1)}, bf16[1024,128]{1,0:T(8,128)(2,1)S(1)}, u32[]{:S(2)}, u32[]{:S(2)}) collective-permute-start(bf16[1024,128]{1,0:T(8,128)(2,1)} %get-tuple-element.31), channel_id=1, source_target_pairs={{0,8},{4,12},{8,0},{12,4},{16,24},{20,28},{24,16},{28,20},{1,9},{5... | collective-permute-start | bytes 786440 | tf_op jit(solution)/shard_map/ppermute | solution.py:152
  98.7 20.6 %collective-permute-start.31 = (bf16[1024,128]{1,0:T(8,128)(2,1)}, bf16[1024,128]{1,0:T(8,128)(2,1)S(1)}, u32[]{:S(2)}, u32[]{:S(2)}) collective-permute-start(bf16[1024,128]{1,0:T(8,128)(2,1)} %get-tuple-element.32), channel_id=1, source_target_pairs={{0,16},{4,20},{8,24},{12,28},{16,0},{20,4},{24,8},{28,12},{1,17},{... | collective-permute-start | bytes 786440 | tf_op jit(solution)/shard_map/ppermute | solution.py:152
  108.6 10.7 %collective-permute-start.32 = (bf16[1024,128]{1,0:T(8,128)(2,1)}, bf16[1024,128]{1,0:T(8,128)(2,1)S(1)}, u32[]{:S(2)}, u32[]{:S(2)}) collective-permute-start(bf16[1024,128]{1,0:T(8,128)(2,1)} %get-tuple-element.33), channel_id=1, source_target_pairs={{0,24},{4,28},{8,16},{12,20},{16,8},{20,12},{24,0},{28,4},{1,25},{... | collective-permute-start | bytes 786440 | tf_op jit(solution)/shard_map/ppermute | solution.py:152
  108.6 11.9 %collective-permute-start.27 = (bf16[512,128]{1,0:T(8,128)(2,1)}, bf16[512,128]{1,0:T(8,128)(2,1)S(1)}, u32[]{:S(2)}, u32[]{:S(2)}) collective-permute-start(bf16[512,128]{1,0:T(8,128)(2,1)} %get-tuple-element.27), channel_id=1, source_target_pairs={{0,1},{1,2},{2,3},{3,0},{4,5},{5,6},{6,7},{7,4},{8,9},{9,10},{10,1... | collective-permute-start | bytes 393224 | tf_op jit(solution)/shard_map/ppermute | solution.py:132
  108.6 11.9 %collective-permute-start.28 = (bf16[512,128]{1,0:T(8,128)(2,1)}, bf16[512,128]{1,0:T(8,128)(2,1)S(1)}, u32[]{:S(2)}, u32[]{:S(2)}) collective-permute-start(bf16[512,128]{1,0:T(8,128)(2,1)} %get-tuple-element.28), channel_id=1, source_target_pairs={{0,2},{1,3},{2,0},{3,1},{4,6},{5,7},{6,4},{7,5},{8,10},{9,11},{10,... | collective-permute-start | bytes 393224 | tf_op jit(solution)/shard_map/ppermute | solution.py:132
  110.6 9.9 %collective-permute-start.29 = (bf16[512,128]{1,0:T(8,128)(2,1)}, bf16[512,128]{1,0:T(8,128)(2,1)S(1)}, u32[]{:S(2)}, u32[]{:S(2)}) collective-permute-start(bf16[512,128]{1,0:T(8,128)(2,1)} %get-tuple-element.29), channel_id=1, source_target_pairs={{0,3},{1,0},{2,1},{3,2},{4,7},{5,4},{6,5},{7,6},{8,11},{9,8},{10,9... | collective-permute-start | bytes 393224 | tf_op jit(solution)/shard_map/ppermute | solution.py:132
  (29 other events, 328.2 us)

commit v15 on v11

--- a/solution.py
+++ b/solution.py
@@ -25,7 +25,7 @@
         at = 0
         for piece in emb_pieces:
             rows = piece.shape[0]
-            emb_ref[at : at + rows, :] = piece[...]
+            emb_ref[at : at + rows, :] = (piece[...].astype(jnp.float32) * 0.5).astype(emb_ref.dtype)
             emb_t[:, at : at + rows] = piece[...].astype(jnp.float32).T.astype(emb_t.dtype)
             at += rows
         at = 0
@@ -45,7 +45,7 @@
         score = lax.dot_general(e, c, (((1,), (1,)), ((), ())), preferred_element_type=jnp.float32)
         positive = pos_ref[j].astype(jnp.float32)
         negative = neg_ref[j].astype(jnp.float32)
-        t = jnp.tanh(score * 0.5)
+        t = jnp.tanh(score)
         coeff = (0.5 * ((positive - negative) - (positive + negative) * t)).astype(jnp.bfloat16)
         acc_e[pl.ds(r0, tile), :] += jnp.dot(coeff, c, preferred_element_type=jnp.float32)
         acc_ct[:, pl.ds(c0, tile)] += jnp.dot(

time: 116 us -> 116 us (level); the launches traced: 114 us -> 115 us
  waiting for transfers between devices: 27.4 us -> 40.1 us
  starting transfers between devices: 60 us -> 47.6 us
    ppermute x6, waiting for transfers between devices: 0.02 us -> 16.8 us  [scatter_paired(): got = lax.ppermute(blocks[b], axis, [(i, i ^ 2 * b) for i in range(n)])]
    ppermute x6, starting transfers between devices: 23 us -> 7.63 us  [scatter_rotated(): lax.ppermute(chunks[(n - s) % n], axis, [(i, (i + s) % n) for i in range(...]
    ppermute x6, waiting for transfers between devices: 6.02 us -> 0.02 us  [scatter_rotated(): lax.ppermute(chunks[(n - s) % n], axis, [(i, (i + s) % n) for i in range(...]
    ppermute x6, starting transfers between devices: 11.9 us -> 17.5 us  [scatter_paired(): got = lax.ppermute(blocks[b], axis, [(i, i ^ 2 * b) for i in range(n)])]
    ppermute x6, starting transfers between devices: 11.2 us -> 8.66 us  [gather_rotated(): pieces.append(lax.ppermute(x, axis, [(i, (i + s) % n) for i in range(n)]))]
    ppermute x2, starting transfers between devices: 3.38 us -> 1.28 us  [scatter_paired(): got = lax.ppermute(total[width:], axis, [(i, i ^ 1) for i in range(n)])]
    ppermute x7, starting transfers between devices: 6.47 us -> 8.4 us  [gather_xor(): pieces.append(lax.ppermute(x, axis, [(i, i ^ p) for i in range(n)]))]
    ppermute x7, waiting for transfers between devices: 4.88 us -> 6.56 us  [gather_xor(): pieces.append(lax.ppermute(x, axis, [(i, i ^ p) for i in range(n)]))]
  transfers between devices with their start and end apart: 31 -> 31, of which waited for: 12 -> 9; matrix products, arithmetic and copies ran while one was open for 6% -> 6% of each run, Pallas kernels for 0% -> 0%
where the time goes in v15:
time: 116 us; the launch traced here: 115 us
  starting transfers between devices  47.6 us (41%)
  waiting for transfers between devices  40.1 us (35%)
  Pallas kernels  15.7 us (14%)
  other arithmetic  9.03 us (8%)
  between operations  1.58 us (1%)
  local copies, waits for them, and re-layouts  1.38 us (1%)
    ppermute x6, starting transfers between devices, scatter_paired(): got = lax.ppermute(blocks[b], axis, [(i, i ^ 2 * b) for i in range(n)])  17.5 us
    ppermute x6, waiting for transfers between devices, scatter_paired(): got = lax.ppermute(blocks[b], axis, [(i, i ^ 2 * b) for i in range(n)])  16.8 us
    pallas_call x2, Pallas kernels, tile_sweep(): pl.pallas_call(functools.partial(sweep_kernel, tile, group, len(emb_piece...  15.7 us
    ppermute x6, waiting for transfers between devices, gather_rotated(): pieces.append(lax.ppermute(x, axis, [(i, (i + s) % n) for i in range(n)]))  14.4 us
    ppermute x6, starting transfers between devices, gather_rotated(): pieces.append(lax.ppermute(x, axis, [(i, (i + s) % n) for i in range(n)]))  8.66 us
    ppermute x7, starting transfers between devices, gather_xor(): pieces.append(lax.ppermute(x, axis, [(i, i ^ p) for i in range(n)]))  8.4 us
    ppermute x6, starting transfers between devices, scatter_rotated(): lax.ppermute(chunks[(n - s) % n], axis, [(i, (i + s) % n) for i in range(...  7.63 us
    ppermute x7, waiting for transfers between devices, gather_xor(): pieces.append(lax.ppermute(x, axis, [(i, i ^ p) for i in range(n)]))  6.56 us
  transfers between devices with their start and end apart: 31, of which 9 were waited for; matrix products, arithmetic and copies ran while one was open for 6% of the time, Pallas kernels for 0%

profile of v15, /device:TPU:0, one launch (start us, length us, event | category | flops | bytes accessed | tf_op | source)
XLA Modules:
  0.0 115.4 jit_solution(11800261735636697520)
XLA Ops:
  0.6 1.0 convert_element_type.61
  2.1 1.0 convert_element_type.60.refs_0_
  3.1 4.7 %collective-permute-start.2 = (bf16[512,128]{1,0:T(8,128)(2,1)S(1)}, bf16[512,128]{1,0:T(8,128)(2,1)S(1)}, u32[]{:S(2)}, u32[]{:S(2)}) collective-permute-start(bf16[512,128]{1,0:T(8,128)(2,1)S(1)} %convert_element_type.60.refs_0_), channel_id=1, source_target_pairs={{0,3},{1,0},{2,1},{3,2},{4,7},{5,4},{6,5},{7,6},{8,11},{9,8},{10,9... | collective-permute-start | bytes 393224 | tf_op jit(solution)/shard_map/ppermute | solution.py:125
  7.8 2.5 %collective-permute-start.6 = (bf16[1024,128]{1,0:T(8,128)(2,1)S(1)}, bf16[1024,128]{1,0:T(8,128)(2,1)S(1)}, u32[]{:S(2)}, u32[]{:S(2)}) collective-permute-start(bf16[1024,128]{1,0:T(8,128)(2,1)S(1)} %pad_maximum_fusion.refs_4_), channel_id=1, source_target_pairs={{0,24},{4,28},{8,16},{12,20},{16,8},{20,12},{24,0},{28,4},{1,25},{... | collective-permute-start | bytes 786440 | tf_op jit(solution)/shard_map/ppermute | solution.py:145
  12.0 1.1 collective-permute-start
  13.1 1.3 %fusion.4 = (s32[64]{0:T(128)}, s32[64]{0:T(128)}) fusion(s32[1,1,64]{2,1,0:T(1,128)} %param.11, s32[]{:T(128)S(6)} %axis_index.22, s32[1,1,64]{2,1,0:T(1,128)} %param.12, s32[]{:T(128)S(6)} %axis_index.25), kind=kLoop, calls=%fused_computation.24 | loop fusion | flops 3520 | bytes 1032 | tf_op jit(solution)/shard_map/add | solution.py:180
  14.4 6.2 %collective-permute-done.1.refs_2_ = bf16[512,128]{1,0:T(8,128)(2,1)S(1)} collective-permute-done((bf16[512,128]{1,0:T(8,128)(2,1)S(1)}, bf16[512,128]{1,0:T(8,128)(2,1)S(1)}, u32[]{:S(2)}, u32[]{:S(2)}) %collective-permute-start.1) | collective-permute-done | bytes 131104 | tf_op jit(solution)/shard_map/ppermute | solution.py:125
  20.6 2.2 %collective-permute-done.5.refs_6_ = bf16[1024,128]{1,0:T(8,128)(2,1)S(1)} collective-permute-done((bf16[1024,128]{1,0:T(8,128)(2,1)S(1)}, bf16[1024,128]{1,0:T(8,128)(2,1)S(1)}, u32[]{:S(2)}, u32[]{:S(2)}) %collective-permute-start.5) | collective-permute-done | bytes 262176 | tf_op jit(solution)/shard_map/ppermute | solution.py:145
  23.6 7.8 %shard_map.86 = (bf16[512,128]{1,0:T(8,128)(2,1)}, bf16[512,128]{1,0:T(8,128)(2,1)}, bf16[512,128]{1,0:T(8,128)(2,1)}, bf16[512,128]{1,0:T(8,128)(2,1)}, bf16[10...) custom-call(s32[64]{0:T(128)} %get-tuple-element.34.rows_ref, ...), custom_call_target="tpu_custom_call" | custom-call | flops 3221225472 | bytes 21495808 | tf_op jit(solution)/shard_map/pallas_call | solution.py:107
  31.4 2.8 %collective-permute-start.13 = (bf16[1024,128]{1,0:T(8,128)(2,1)}, bf16[1024,128]{1,0:T(8,128)(2,1)S(1)}, u32[]{:S(2)}, u32[]{:S(2)}) collective-permute-start(bf16[1024,128]{1,0:T(8,128)(2,1)} %get-tuple-element.23), channel_id=1, source_target_pairs={{0,8},{4,12},{8,0},{12,4},{16,24},{20,28},{24,16},{28,20},{1,9},{5... | collective-permute-start | bytes 786440 | tf_op jit(solution)/shard_map/ppermute | solution.py:152
  34.2 6.7 %collective-permute-start.14 = (bf16[1024,128]{1,0:T(8,128)(2,1)}, bf16[1024,128]{1,0:T(8,128)(2,1)S(1)}, u32[]{:S(2)}, u32[]{:S(2)}) collective-permute-start(bf16[1024,128]{1,0:T(8,128)(2,1)} %get-tuple-element.24), channel_id=1, source_target_pairs={{0,16},{4,20},{8,24},{12,28},{16,0},{20,4},{24,8},{28,12},{1,17},{... | collective-permute-start | bytes 786440 | tf_op jit(solution)/shard_map/ppermute | solution.py:152
  40.9 3.8 %collective-permute-start.9 = (bf16[512,128]{1,0:T(8,128)(2,1)}, bf16[512,128]{1,0:T(8,128)(2,1)S(1)}, u32[]{:S(2)}, u32[]{:S(2)}) collective-permute-start(bf16[512,128]{1,0:T(8,128)(2,1)} %get-tuple-element.21), channel_id=1, source_target_pairs={{0,3},{1,0},{2,1},{3,2},{4,7},{5,4},{6,5},{7,6},{8,11},{9,8},{10,9... | collective-permute-start | bytes 393224 | tf_op jit(solution)/shard_map/ppermute | solution.py:132
  44.7 8.3 %collective-permute-done.14 = bf16[1024,128]{1,0:T(8,128)(2,1)S(1)} collective-permute-done((bf16[1024,128]{1,0:T(8,128)(2,1)}, bf16[1024,128]{1,0:T(8,128)(2,1)S(1)}, u32[]{:S(2)}, u32[]{:S(2)}) %collective-permute-start.14) | collective-permute-done | bytes 262176 | tf_op jit(solution)/shard_map/ppermute | solution.py:152
  53.0 1.1 convert_add_fusion.1
  54.9 1.0 fusion.9.refs_0_
  55.9 1.4 %collective-permute-start.12 = (bf16[512,128]{1,0:T(8,128)(2,1)S(1)}, bf16[512,128]{1,0:T(8,128)(2,1)S(1)}, u32[]{:S(2)}, u32[]{:S(2)}) collective-permute-start(bf16[512,128]{1,0:T(8,128)(2,1)S(1)} %fusion.9.refs_0_), channel_id=1, source_target_pairs={{0,3},{1,0},{2,1},{3,2},{4,7},{5,4},{6,5},{7,6},{8,11},{9,8},{10,9... | collective-permute-start | bytes 393224 | tf_op jit(solution)/shard_map/ppermute | solution.py:125
  57.4 1.5 %collective-permute-start.11 = (bf16[512,128]{1,0:T(8,128)(2,1)S(1)}, bf16[512,128]{1,0:T(8,128)(2,1)S(1)}, u32[]{:S(2)}, u32[]{:S(2)}) collective-permute-start(bf16[512,128]{1,0:T(8,128)(2,1)S(1)} %fusion.9.refs_0_), channel_id=1, source_target_pairs={{0,2},{1,3},{2,0},{3,1},{4,6},{5,7},{6,4},{7,5},{8,10},{9,11},{10,... | collective-permute-start | bytes 393224 | tf_op jit(solution)/shard_map/ppermute | solution.py:125
  58.9 3.2 %collective-permute-start.23 = (bf16[512,128]{1,0:T(8,128)(2,1)S(1)}, bf16[512,128]{1,0:T(8,128)(2,1)S(1)}, u32[]{:S(2)}, u32[]{:S(2)}) collective-permute-start(bf16[512,128]{1,0:T(8,128)(2,1)S(1)} %fusion.8.refs_4_), channel_id=1, source_target_pairs={{0,28},{4,24},{8,20},{12,16},{16,12},{20,8},{24,4},{28,0},{1,29},{... | collective-permute-start | bytes 393224 | tf_op jit(solution)/shard_map/ppermute | solution.py:162
  62.1 0.9 collective-permute-start.22
  63.3 8.2 %collective-permute-done.11.refs_2_ = bf16[512,128]{1,0:T(8,128)(2,1)S(1)} collective-permute-done((bf16[512,128]{1,0:T(8,128)(2,1)S(1)}, bf16[512,128]{1,0:T(8,128)(2,1)S(1)}, u32[]{:S(2)}, u32[]{:S(2)}) %collective-permute-start.11) | collective-permute-done | bytes 131104 | tf_op jit(solution)/shard_map/ppermute | solution.py:125
  71.5 2.0 %collective-permute-start.20 = (bf16[512,128]{1,0:T(8,128)(2,1)S(1)}, bf16[512,128]{1,0:T(8,128)(2,1)S(1)}, u32[]{:S(2)}, u32[]{:S(2)}) collective-permute-start(bf16[512,128]{1,0:T(8,128)(2,1)S(1)} %fusion.8.refs_4_), channel_id=1, source_target_pairs={{0,16},{4,20},{8,24},{12,28},{16,0},{20,4},{24,8},{28,12},{1,17},{... | collective-permute-start | bytes 393224 | tf_op jit(solution)/shard_map/ppermute | solution.py:162
  73.9 1.5 %collective-permute-start.18 = (bf16[512,128]{1,0:T(8,128)(2,1)S(1)}, bf16[512,128]{1,0:T(8,128)(2,1)S(1)}, u32[]{:S(2)}, u32[]{:S(2)}) collective-permute-start(bf16[512,128]{1,0:T(8,128)(2,1)S(1)} %fusion.8.refs_4_), channel_id=1, source_target_pairs={{0,8},{4,12},{8,0},{12,4},{16,24},{20,28},{24,16},{28,20},{1,9},{5... | collective-permute-start | bytes 393224 | tf_op jit(solution)/shard_map/ppermute | solution.py:162
  75.5 1.6 %collective-permute-done.20.refs_8_ = bf16[512,128]{1,0:T(8,128)(2,1)S(1)} collective-permute-done((bf16[512,128]{1,0:T(8,128)(2,1)S(1)}, bf16[512,128]{1,0:T(8,128)(2,1)S(1)}, u32[]{:S(2)}, u32[]{:S(2)}) %collective-permute-start.20) | collective-permute-done | bytes 131104 | tf_op jit(solution)/shard_map/ppermute | solution.py:162
  77.1 1.9 %collective-permute-done.19.refs_7_ = bf16[512,128]{1,0:T(8,128)(2,1)S(1)} collective-permute-done((bf16[512,128]{1,0:T(8,128)(2,1)S(1)}, bf16[512,128]{1,0:T(8,128)(2,1)S(1)}, u32[]{:S(2)}, u32[]{:S(2)}) %collective-permute-start.19) | collective-permute-done | bytes 131104 | tf_op jit(solution)/shard_map/ppermute | solution.py:162
  79.0 3.1 %collective-permute-done.18.refs_6_ = bf16[512,128]{1,0:T(8,128)(2,1)S(1)} collective-permute-done((bf16[512,128]{1,0:T(8,128)(2,1)S(1)}, bf16[512,128]{1,0:T(8,128)(2,1)S(1)}, u32[]{:S(2)}, u32[]{:S(2)}) %collective-permute-start.18) | collective-permute-done | bytes 131104 | tf_op jit(solution)/shard_map/ppermute | solution.py:162
  82.8 7.9 %shard_map.87 = (bf16[512,128]{1,0:T(8,128)(2,1)}, bf16[512,128]{1,0:T(8,128)(2,1)}, bf16[512,128]{1,0:T(8,128)(2,1)}, bf16[512,128]{1,0:T(8,128)(2,1)}, bf16[10...) custom-call(s32[64]{0:T(128)} %get-tuple-element.34.rows_ref, ...), custom_call_target="tpu_custom_call" | custom-call | flops 3221225472 | bytes 21495808 | tf_op jit(solution)/shard_map/pallas_call | solution.py:107
  90.7 1.5 %collective-permute-start.27 = (bf16[1024,128]{1,0:T(8,128)(2,1)}, bf16[1024,128]{1,0:T(8,128)(2,1)S(1)}, u32[]{:S(2)}, u32[]{:S(2)}) collective-permute-start(bf16[1024,128]{1,0:T(8,128)(2,1)} %get-tuple-element.31), channel_id=1, source_target_pairs={{0,8},{4,12},{8,0},{12,4},{16,24},{20,28},{24,16},{28,20},{1,9},{5... | collective-permute-start | bytes 786440 | tf_op jit(solution)/shard_map/ppermute | solution.py:152
  92.2 6.5 %collective-permute-start.28 = (bf16[1024,128]{1,0:T(8,128)(2,1)}, bf16[1024,128]{1,0:T(8,128)(2,1)S(1)}, u32[]{:S(2)}, u32[]{:S(2)}) collective-permute-start(bf16[1024,128]{1,0:T(8,128)(2,1)} %get-tuple-element.32), channel_id=1, source_target_pairs={{0,16},{4,20},{8,24},{12,28},{16,0},{20,4},{24,8},{28,12},{1,17},{... | collective-permute-start | bytes 786440 | tf_op jit(solution)/shard_map/ppermute | solution.py:152
  98.8 3.8 %collective-permute-start.26 = (bf16[512,128]{1,0:T(8,128)(2,1)}, bf16[512,128]{1,0:T(8,128)(2,1)S(1)}, u32[]{:S(2)}, u32[]{:S(2)}) collective-permute-start(bf16[512,128]{1,0:T(8,128)(2,1)} %get-tuple-element.29), channel_id=1, source_target_pairs={{0,3},{1,0},{2,1},{3,2},{4,7},{5,4},{6,5},{7,6},{8,11},{9,8},{10,9... | collective-permute-start | bytes 393224 | tf_op jit(solution)/shard_map/ppermute | solution.py:132
  102.6 8.5 %collective-permute-done.28 = bf16[1024,128]{1,0:T(8,128)(2,1)S(1)} collective-permute-done((bf16[1024,128]{1,0:T(8,128)(2,1)}, bf16[1024,128]{1,0:T(8,128)(2,1)S(1)}, u32[]{:S(2)}, u32[]{:S(2)}) %collective-permute-start.28) | collective-permute-done | bytes 262176 | tf_op jit(solution)/shard_map/ppermute | solution.py:152
  111.1 1.1 convert_add_fusion
  112.8 1.8 %multiply_add_fusion = f32[512,128]{1,0:T(8,128)} fusion(bf16[512,128]{1,0:T(8,128)(2,1)S(1)} %collective-permute-done.26, bf16[512,128]{1,0:T(8,128)(2,1)S(1)} %collective-permute-done.25, bf16[512,128]{1,0:T(8,128)(2,1)S(1)} %collective-permute-done.24, bf16[512,128]{1,0:T(8,128)(2,1)} %get-tuple-element.26, f32[512,128]{1,0:T(8,128)S(1)} %copy-done, ...), kind=kLoop, calls=%fused_computation.9 | loop fusion | flops 1179648 | bytes 1572864 | tf_op jit(solution)/shard_map/add | solution.py:213
  (90 shorter events, 6.1 us)
Async XLA Ops:
  1.6 6.2 %collective-permute-start.3 = (bf16[512,128]{1,0:T(8,128)(2,1)S(1)}, bf16[512,128]{1,0:T(8,128)(2,1)S(1)}, u32[]{:S(2)}, u32[]{:S(2)}) collective-permute-start(bf16[512,128]{1,0:T(8,128)(2,1)S(1)} %convert_element_type.61), channel_id=1, source_target_pairs={{0,4},{4,0},{8,12},{12,8},{16,20},{20,16},{24,28},{28,24},{1,5},{5... | collective-permute-start | bytes 393224 | tf_op jit(solution)/shard_map/ppermute | solution.py:142
  3.1 8.9 %collective-permute-start.2 = (bf16[512,128]{1,0:T(8,128)(2,1)S(1)}, bf16[512,128]{1,0:T(8,128)(2,1)S(1)}, u32[]{:S(2)}, u32[]{:S(2)}) collective-permute-start(bf16[512,128]{1,0:T(8,128)(2,1)S(1)} %convert_element_type.60.refs_0_), channel_id=1, source_target_pairs={{0,3},{1,0},{2,1},{3,2},{4,7},{5,4},{6,5},{7,6},{8,11},{9,8},{10,9... | collective-permute-start | bytes 393224 | tf_op jit(solution)/shard_map/ppermute | solution.py:125
  7.8 12.8 %collective-permute-start.6 = (bf16[1024,128]{1,0:T(8,128)(2,1)S(1)}, bf16[1024,128]{1,0:T(8,128)(2,1)S(1)}, u32[]{:S(2)}, u32[]{:S(2)}) collective-permute-start(bf16[1024,128]{1,0:T(8,128)(2,1)S(1)} %pad_maximum_fusion.refs_4_), channel_id=1, source_target_pairs={{0,24},{4,28},{8,16},{12,20},{16,8},{20,12},{24,0},{28,4},{1,25},{... | collective-permute-start | bytes 786440 | tf_op jit(solution)/shard_map/ppermute | solution.py:145
  10.3 12.5 %collective-permute-start.5 = (bf16[1024,128]{1,0:T(8,128)(2,1)S(1)}, bf16[1024,128]{1,0:T(8,128)(2,1)S(1)}, u32[]{:S(2)}, u32[]{:S(2)}) collective-permute-start(bf16[1024,128]{1,0:T(8,128)(2,1)S(1)} %pad_maximum_fusion.refs_4_), channel_id=1, source_target_pairs={{0,16},{4,20},{8,24},{12,28},{16,0},{20,4},{24,8},{28,12},{1,17},{... | collective-permute-start | bytes 786440 | tf_op jit(solution)/shard_map/ppermute | solution.py:145
  10.8 12.1 %collective-permute-start.4 = (bf16[1024,128]{1,0:T(8,128)(2,1)S(1)}, bf16[1024,128]{1,0:T(8,128)(2,1)S(1)}, u32[]{:S(2)}, u32[]{:S(2)}) collective-permute-start(bf16[1024,128]{1,0:T(8,128)(2,1)S(1)} %pad_maximum_fusion.refs_4_), channel_id=1, source_target_pairs={{0,8},{4,12},{8,0},{12,4},{16,24},{20,28},{24,16},{28,20},{1,9},{5... | collective-permute-start | bytes 786440 | tf_op jit(solution)/shard_map/ppermute | solution.py:145
  11.4 9.2 %collective-permute-start.1 = (bf16[512,128]{1,0:T(8,128)(2,1)S(1)}, bf16[512,128]{1,0:T(8,128)(2,1)S(1)}, u32[]{:S(2)}, u32[]{:S(2)}) collective-permute-start(bf16[512,128]{1,0:T(8,128)(2,1)S(1)} %convert_element_type.60.refs_0_), channel_id=1, source_target_pairs={{0,2},{1,3},{2,0},{3,1},{4,6},{5,7},{6,4},{7,5},{8,10},{9,11},{10,... | collective-permute-start | bytes 393224 | tf_op jit(solution)/shard_map/ppermute | solution.py:125
  12.0 8.5 %collective-permute-start = (bf16[512,128]{1,0:T(8,128)(2,1)S(1)}, bf16[512,128]{1,0:T(8,128)(2,1)S(1)}, u32[]{:S(2)}, u32[]{:S(2)}) collective-permute-start(bf16[512,128]{1,0:T(8,128)(2,1)S(1)} %convert_element_type.60.refs_0_), channel_id=1, source_target_pairs={{0,1},{1,2},{2,3},{3,0},{4,5},{5,6},{6,7},{7,4},{8,9},{9,10},{10,1... | collective-permute-start | bytes 393224 | tf_op jit(solution)/shard_map/ppermute | solution.py:125
  23.6 35.2 %copy-start.1 = (f32[512,128]{1,0:T(8,128)S(1)}, f32[512,128]{1,0:T(8,128)}, u32[]{:S(2)}) copy-start(f32[512,128]{1,0:T(8,128)} %param.8) | copy-start | bytes 786436
  31.4 9.5 %collective-permute-start.13 = (bf16[1024,128]{1,0:T(8,128)(2,1)}, bf16[1024,128]{1,0:T(8,128)(2,1)S(1)}, u32[]{:S(2)}, u32[]{:S(2)}) collective-permute-start(bf16[1024,128]{1,0:T(8,128)(2,1)} %get-tuple-element.23), channel_id=1, source_target_pairs={{0,8},{4,12},{8,0},{12,4},{16,24},{20,28},{24,16},{28,20},{1,9},{5... | collective-permute-start | bytes 786440 | tf_op jit(solution)/shard_map/ppermute | solution.py:152
  34.2 18.8 %collective-permute-start.14 = (bf16[1024,128]{1,0:T(8,128)(2,1)}, bf16[1024,128]{1,0:T(8,128)(2,1)S(1)}, u32[]{:S(2)}, u32[]{:S(2)}) collective-permute-start(bf16[1024,128]{1,0:T(8,128)(2,1)} %get-tuple-element.24), channel_id=1, source_target_pairs={{0,16},{4,20},{8,24},{12,28},{16,0},{20,4},{24,8},{28,12},{1,17},{... | collective-permute-start | bytes 786440 | tf_op jit(solution)/shard_map/ppermute | solution.py:152
  40.9 12.1 %collective-permute-start.15 = (bf16[1024,128]{1,0:T(8,128)(2,1)}, bf16[1024,128]{1,0:T(8,128)(2,1)S(1)}, u32[]{:S(2)}, u32[]{:S(2)}) collective-permute-start(bf16[1024,128]{1,0:T(8,128)(2,1)} %get-tuple-element.25), channel_id=1, source_target_pairs={{0,24},{4,28},{8,16},{12,20},{16,8},{20,12},{24,0},{28,4},{1,25},{... | collective-permute-start | bytes 786440 | tf_op jit(solution)/shard_map/ppermute | solution.py:152
  40.9 14.0 %collective-permute-start.7 = (bf16[512,128]{1,0:T(8,128)(2,1)}, bf16[512,128]{1,0:T(8,128)(2,1)S(1)}, u32[]{:S(2)}, u32[]{:S(2)}) collective-permute-start(bf16[512,128]{1,0:T(8,128)(2,1)} %get-tuple-element.19), channel_id=1, source_target_pairs={{0,1},{1,2},{2,3},{3,0},{4,5},{5,6},{6,7},{7,4},{8,9},{9,10},{10,1... | collective-permute-start | bytes 393224 | tf_op jit(solution)/shard_map/ppermute | solution.py:132
  40.9 14.0 %collective-permute-start.8 = (bf16[512,128]{1,0:T(8,128)(2,1)}, bf16[512,128]{1,0:T(8,128)(2,1)S(1)}, u32[]{:S(2)}, u32[]{:S(2)}) collective-permute-start(bf16[512,128]{1,0:T(8,128)(2,1)} %get-tuple-element.20), channel_id=1, source_target_pairs={{0,2},{1,3},{2,0},{3,1},{4,6},{5,7},{6,4},{7,5},{8,10},{9,11},{10,... | collective-permute-start | bytes 393224 | tf_op jit(solution)/shard_map/ppermute | solution.py:132
  40.9 14.0 %collective-permute-start.9 = (bf16[512,128]{1,0:T(8,128)(2,1)}, bf16[512,128]{1,0:T(8,128)(2,1)S(1)}, u32[]{:S(2)}, u32[]{:S(2)}) collective-permute-start(bf16[512,128]{1,0:T(8,128)(2,1)} %get-tuple-element.21), channel_id=1, source_target_pairs={{0,3},{1,0},{2,1},{3,2},{4,7},{5,4},{6,5},{7,6},{8,11},{9,8},{10,9... | collective-permute-start | bytes 393224 | tf_op jit(solution)/shard_map/ppermute | solution.py:132
  54.1 4.7 %collective-permute-start.16 = (f32[512,128]{1,0:T(8,128)S(1)}, f32[512,128]{1,0:T(8,128)S(1)}, u32[]{:S(2)}, u32[]{:S(2)}) collective-permute-start(f32[512,128]{1,0:T(8,128)S(1)} %slice.17), channel_id=1, source_target_pairs={{0,4},{4,0},{8,12},{12,8},{16,20},{20,16},{24,28},{28,24},{1,5},{5... | collective-permute-start | bytes 786440 | tf_op jit(solution)/shard_map/ppermute | solution.py:155
  55.9 7.1 %collective-permute-start.12 = (bf16[512,128]{1,0:T(8,128)(2,1)S(1)}, bf16[512,128]{1,0:T(8,128)(2,1)S(1)}, u32[]{:S(2)}, u32[]{:S(2)}) collective-permute-start(bf16[512,128]{1,0:T(8,128)(2,1)S(1)} %fusion.9.refs_0_), channel_id=1, source_target_pairs={{0,3},{1,0},{2,1},{3,2},{4,7},{5,4},{6,5},{7,6},{8,11},{9,8},{10,9... | collective-permute-start | bytes 393224 | tf_op jit(solution)/shard_map/ppermute | solution.py:125
  57.4 14.2 %collective-permute-start.11 = (bf16[512,128]{1,0:T(8,128)(2,1)S(1)}, bf16[512,128]{1,0:T(8,128)(2,1)S(1)}, u32[]{:S(2)}, u32[]{:S(2)}) collective-permute-start(bf16[512,128]{1,0:T(8,128)(2,1)S(1)} %fusion.9.refs_0_), channel_id=1, source_target_pairs={{0,2},{1,3},{2,0},{3,1},{4,6},{5,7},{6,4},{7,5},{8,10},{9,11},{10,... | collective-permute-start | bytes 393224 | tf_op jit(solution)/shard_map/ppermute | solution.py:125
  58.8 14.6 %collective-permute-start.10 = (bf16[512,128]{1,0:T(8,128)(2,1)S(1)}, bf16[512,128]{1,0:T(8,128)(2,1)S(1)}, u32[]{:S(2)}, u32[]{:S(2)}) collective-permute-start(bf16[512,128]{1,0:T(8,128)(2,1)S(1)} %fusion.9.refs_0_), channel_id=1, source_target_pairs={{0,1},{1,2},{2,3},{3,0},{4,5},{5,6},{6,7},{7,4},{8,9},{9,10},{10,1... | collective-permute-start | bytes 393224 | tf_op jit(solution)/shard_map/ppermute | solution.py:125
  58.9 15.0 %collective-permute-start.23 = (bf16[512,128]{1,0:T(8,128)(2,1)S(1)}, bf16[512,128]{1,0:T(8,128)(2,1)S(1)}, u32[]{:S(2)}, u32[]{:S(2)}) collective-permute-start(bf16[512,128]{1,0:T(8,128)(2,1)S(1)} %fusion.8.refs_4_), channel_id=1, source_target_pairs={{0,28},{4,24},{8,20},{12,16},{16,12},{20,8},{24,4},{28,0},{1,29},{... | collective-permute-start | bytes 393224 | tf_op jit(solution)/shard_map/ppermute | solution.py:162
  62.1 13.3 %collective-permute-start.22 = (bf16[512,128]{1,0:T(8,128)(2,1)S(1)}, bf16[512,128]{1,0:T(8,128)(2,1)S(1)}, u32[]{:S(2)}, u32[]{:S(2)}) collective-permute-start(bf16[512,128]{1,0:T(8,128)(2,1)S(1)} %fusion.8.refs_4_), channel_id=1, source_target_pairs={{0,24},{4,28},{8,16},{12,20},{16,8},{20,12},{24,0},{28,4},{1,25},{... | collective-permute-start | bytes 393224 | tf_op jit(solution)/shard_map/ppermute | solution.py:162
  63.1 12.5 %collective-permute-start.21 = (bf16[512,128]{1,0:T(8,128)(2,1)S(1)}, bf16[512,128]{1,0:T(8,128)(2,1)S(1)}, u32[]{:S(2)}, u32[]{:S(2)}) collective-permute-start(bf16[512,128]{1,0:T(8,128)(2,1)S(1)} %fusion.8.refs_4_), channel_id=1, source_target_pairs={{0,20},{4,16},{8,28},{12,24},{16,4},{20,0},{24,12},{28,8},{1,21},{... | collective-permute-start | bytes 393224 | tf_op jit(solution)/shard_map/ppermute | solution.py:162
  71.5 5.6 %collective-permute-start.20 = (bf16[512,128]{1,0:T(8,128)(2,1)S(1)}, bf16[512,128]{1,0:T(8,128)(2,1)S(1)}, u32[]{:S(2)}, u32[]{:S(2)}) collective-permute-start(bf16[512,128]{1,0:T(8,128)(2,1)S(1)} %fusion.8.refs_4_), channel_id=1, source_target_pairs={{0,16},{4,20},{8,24},{12,28},{16,0},{20,4},{24,8},{28,12},{1,17},{... | collective-permute-start | bytes 393224 | tf_op jit(solution)/shard_map/ppermute | solution.py:162
  73.5 5.5 %collective-permute-start.19 = (bf16[512,128]{1,0:T(8,128)(2,1)S(1)}, bf16[512,128]{1,0:T(8,128)(2,1)S(1)}, u32[]{:S(2)}, u32[]{:S(2)}) collective-permute-start(bf16[512,128]{1,0:T(8,128)(2,1)S(1)} %fusion.8.refs_4_), channel_id=1, source_target_pairs={{0,12},{4,8},{8,4},{12,0},{16,28},{20,24},{24,20},{28,16},{1,13},{... | collective-permute-start | bytes 393224 | tf_op jit(solution)/shard_map/ppermute | solution.py:162
  73.9 8.2 %collective-permute-start.18 = (bf16[512,128]{1,0:T(8,128)(2,1)S(1)}, bf16[512,128]{1,0:T(8,128)(2,1)S(1)}, u32[]{:S(2)}, u32[]{:S(2)}) collective-permute-start(bf16[512,128]{1,0:T(8,128)(2,1)S(1)} %fusion.8.refs_4_), channel_id=1, source_target_pairs={{0,8},{4,12},{8,0},{12,4},{16,24},{20,28},{24,16},{28,20},{1,9},{5... | collective-permute-start | bytes 393224 | tf_op jit(solution)/shard_map/ppermute | solution.py:162
  75.4 6.7 %collective-permute-start.17 = (bf16[512,128]{1,0:T(8,128)(2,1)S(1)}, bf16[512,128]{1,0:T(8,128)(2,1)S(1)}, u32[]{:S(2)}, u32[]{:S(2)}) collective-permute-start(bf16[512,128]{1,0:T(8,128)(2,1)S(1)} %fusion.8.refs_4_), channel_id=1, source_target_pairs={{0,4},{4,0},{8,12},{12,8},{16,20},{20,16},{24,28},{28,24},{1,5},{5... | collective-permute-start | bytes 393224 | tf_op jit(solution)/shard_map/ppermute | solution.py:162
  90.7 8.1 %collective-permute-start.27 = (bf16[1024,128]{1,0:T(8,128)(2,1)}, bf16[1024,128]{1,0:T(8,128)(2,1)S(1)}, u32[]{:S(2)}, u32[]{:S(2)}) collective-permute-start(bf16[1024,128]{1,0:T(8,128)(2,1)} %get-tuple-element.31), channel_id=1, source_target_pairs={{0,8},{4,12},{8,0},{12,4},{16,24},{20,28},{24,16},{28,20},{1,9},{5... | collective-permute-start | bytes 786440 | tf_op jit(solution)/shard_map/ppermute | solution.py:152
  92.2 18.9 %collective-permute-start.28 = (bf16[1024,128]{1,0:T(8,128)(2,1)}, bf16[1024,128]{1,0:T(8,128)(2,1)S(1)}, u32[]{:S(2)}, u32[]{:S(2)}) collective-permute-start(bf16[1024,128]{1,0:T(8,128)(2,1)} %get-tuple-element.32), channel_id=1, source_target_pairs={{0,16},{4,20},{8,24},{12,28},{16,0},{20,4},{24,8},{28,12},{1,17},{... | collective-permute-start | bytes 786440 | tf_op jit(solution)/shard_map/ppermute | solution.py:152
  98.8 12.4 %collective-permute-start.29 = (bf16[1024,128]{1,0:T(8,128)(2,1)}, bf16[1024,128]{1,0:T(8,128)(2,1)S(1)}, u32[]{:S(2)}, u32[]{:S(2)}) collective-permute-start(bf16[1024,128]{1,0:T(8,128)(2,1)} %get-tuple-element.33), channel_id=1, source_target_pairs={{0,24},{4,28},{8,16},{12,20},{16,8},{20,12},{24,0},{28,4},{1,25},{... | collective-permute-start | bytes 786440 | tf_op jit(solution)/shard_map/ppermute | solution.py:152
  98.8 14.0 %collective-permute-start.24 = (bf16[512,128]{1,0:T(8,128)(2,1)}, bf16[512,128]{1,0:T(8,128)(2,1)S(1)}, u32[]{:S(2)}, u32[]{:S(2)}) collective-permute-start(bf16[512,128]{1,0:T(8,128)(2,1)} %get-tuple-element.27), channel_id=1, source_target_pairs={{0,1},{1,2},{2,3},{3,0},{4,5},{5,6},{6,7},{7,4},{8,9},{9,10},{10,1... | collective-permute-start | bytes 393224 | tf_op jit(solution)/shard_map/ppermute | solution.py:132
  98.8 14.0 %collective-permute-start.25 = (bf16[512,128]{1,0:T(8,128)(2,1)}, bf16[512,128]{1,0:T(8,128)(2,1)S(1)}, u32[]{:S(2)}, u32[]{:S(2)}) collective-permute-start(bf16[512,128]{1,0:T(8,128)(2,1)} %get-tuple-element.28), channel_id=1, source_target_pairs={{0,2},{1,3},{2,0},{3,1},{4,6},{5,7},{6,4},{7,5},{8,10},{9,11},{10,... | collective-permute-start | bytes 393224 | tf_op jit(solution)/shard_map/ppermute | solution.py:132
  98.8 14.0 %collective-permute-start.26 = (bf16[512,128]{1,0:T(8,128)(2,1)}, bf16[512,128]{1,0:T(8,128)(2,1)S(1)}, u32[]{:S(2)}, u32[]{:S(2)}) collective-permute-start(bf16[512,128]{1,0:T(8,128)(2,1)} %get-tuple-element.29), channel_id=1, source_target_pairs={{0,3},{1,0},{2,1},{3,2},{4,7},{5,4},{6,5},{7,6},{8,11},{9,8},{10,9... | collective-permute-start | bytes 393224 | tf_op jit(solution)/shard_map/ppermute | solution.py:132
  112.3 2.3 %collective-permute-start.30 = (f32[512,128]{1,0:T(8,128)S(1)}, f32[512,128]{1,0:T(8,128)S(1)}, u32[]{:S(2)}, u32[]{:S(2)}) collective-permute-start(f32[512,128]{1,0:T(8,128)S(1)} %slice.19), channel_id=1, source_target_pairs={{0,4},{4,0},{8,12},{12,8},{16,20},{20,16},{24,28},{28,24},{1,5},{5... | collective-permute-start | bytes 786440 | tf_op jit(solution)/shard_map/ppermute | solution.py:155
  (22 other events, 234.6 us)

commit v16 on v15

--- a/solution.py
+++ b/solution.py
@@ -25,13 +25,13 @@
         at = 0
         for piece in emb_pieces:
             rows = piece.shape[0]
-            emb_ref[at : at + rows, :] = (piece[...].astype(jnp.float32) * 0.5).astype(emb_ref.dtype)
-            emb_t[:, at : at + rows] = piece[...].astype(jnp.float32).T.astype(emb_t.dtype)
+            emb_ref[at : at + rows, :] = piece[...]
+            emb_t[:, at : at + rows] = (piece[...].astype(jnp.float32) * 0.5).T.astype(emb_t.dtype)
             at += rows
         at = 0
         for piece in ctx_pieces:
             rows = piece.shape[0]
-            ctx_ref[at : at + rows, :] = piece[...]
+            ctx_ref[at : at + rows, :] = (piece[...].astype(jnp.float32) * 0.5).astype(ctx_ref.dtype)
             at += rows
         acc_e[...] = jnp.zeros_like(acc_e)
         acc_ct[...] = jnp.zeros_like(acc_ct)
@@ -46,7 +46,7 @@
         positive = pos_ref[j].astype(jnp.float32)
         negative = neg_ref[j].astype(jnp.float32)
         t = jnp.tanh(score)
-        coeff = (0.5 * ((positive - negative) - (positive + negative) * t)).astype(jnp.bfloat16)
+        coeff = ((positive - negative) - (positive + negative) * t).astype(jnp.bfloat16)
         acc_e[pl.ds(r0, tile), :] += jnp.dot(coeff, c, preferred_element_type=jnp.float32)
         acc_ct[:, pl.ds(c0, tile)] += jnp.dot(
             emb_t[:, pl.ds(r0, tile)], coeff, preferred_element_type=jnp.float32

time: 116 us -> 121 us (1.043); the launches traced: 115 us -> 122 us
  starting transfers between devices: 47.6 us -> 54.4 us
  waiting for transfers between devices: 40.1 us -> 38.3 us
  Pallas kernels: 15.7 us -> 17.4 us
    ppermute x6, starting transfers between devices: 17.5 us -> 26.7 us  [scatter_paired(): got = lax.ppermute(blocks[b], axis, [(i, i ^ 2 * b) for i in range(n)])]
    ppermute x7, starting transfers between devices: 8.4 us -> 4.46 us  [gather_xor(): pieces.append(lax.ppermute(x, axis, [(i, i ^ p) for i in range(n)]))]
    ppermute x6, waiting for transfers between devices: 16.8 us -> 14.2 us  [scatter_paired(): got = lax.ppermute(blocks[b], axis, [(i, i ^ 2 * b) for i in range(n)])]
    pallas_call x2, Pallas kernels: 15.7 us -> 17.4 us  [tile_sweep(): pl.pallas_call(functools.partial(sweep_kernel, tile, group, len(emb_piece...]
  transfers between devices with their start and end apart: 31 -> 31, of which waited for: 9 -> 11; matrix products, arithmetic and copies ran while one was open for 6% -> 6% of each run, Pallas kernels for 0% -> 0%
where the time goes in v16:
time: 121 us; the launch traced here: 122 us
  starting transfers between devices  54.4 us (45%)
  waiting for transfers between devices  38.3 us (32%)
  Pallas kernels  17.4 us (14%)
  other arithmetic  9.03 us (7%)
  between operations  1.55 us (1%)
  local copies, waits for them, and re-layouts  1.38 us (1%)
    ppermute x6, starting transfers between devices, scatter_paired(): got = lax.ppermute(blocks[b], axis, [(i, i ^ 2 * b) for i in range(n)])  26.7 us
    pallas_call x2, Pallas kernels, tile_sweep(): pl.pallas_call(functools.partial(sweep_kernel, tile, group, len(emb_piece...  17.4 us
    ppermute x6, waiting for transfers between devices, gather_rotated(): pieces.append(lax.ppermute(x, axis, [(i, (i + s) % n) for i in range(n)]))  15 us
    ppermute x6, waiting for transfers between devices, scatter_paired(): got = lax.ppermute(blocks[b], axis, [(i, i ^ 2 * b) for i in range(n)])  14.2 us
    ppermute x6, starting transfers between devices, gather_rotated(): pieces.append(lax.ppermute(x, axis, [(i, (i + s) % n) for i in range(n)]))  9.83 us
    ppermute x6, starting transfers between devices, scatter_rotated(): lax.ppermute(chunks[(n - s) % n], axis, [(i, (i + s) % n) for i in range(...  7.65 us
    ppermute x7, waiting for transfers between devices, gather_xor(): pieces.append(lax.ppermute(x, axis, [(i, i ^ p) for i in range(n)]))  6.55 us
    ppermute x7, starting transfers between devices, gather_xor(): pieces.append(lax.ppermute(x, axis, [(i, i ^ p) for i in range(n)]))  4.46 us
  transfers between devices with their start and end apart: 31, of which 11 were waited for; matrix products, arithmetic and copies ran while one was open for 6% of the time, Pallas kernels for 0%

profile of v16, /device:TPU:0, one launch (start us, length us, event | category | flops | bytes accessed | tf_op | source)
XLA Modules:
  0.0 122.1 jit_solution(13018246058158871840)
XLA Ops:
  0.6 1.0 convert_element_type.61
  2.1 1.0 convert_element_type.60.refs_0_
  3.1 4.7 %collective-permute-start.2 = (bf16[512,128]{1,0:T(8,128)(2,1)S(1)}, bf16[512,128]{1,0:T(8,128)(2,1)S(1)}, u32[]{:S(2)}, u32[]{:S(2)}) collective-permute-start(bf16[512,128]{1,0:T(8,128)(2,1)S(1)} %convert_element_type.60.refs_0_), channel_id=1, source_target_pairs={{0,3},{1,0},{2,1},{3,2},{4,7},{5,4},{6,5},{7,6},{8,11},{9,8},{10,9... | collective-permute-start | bytes 393224 | tf_op jit(solution)/shard_map/ppermute | solution.py:125
  7.8 2.5 %collective-permute-start.6 = (bf16[1024,128]{1,0:T(8,128)(2,1)S(1)}, bf16[1024,128]{1,0:T(8,128)(2,1)S(1)}, u32[]{:S(2)}, u32[]{:S(2)}) collective-permute-start(bf16[1024,128]{1,0:T(8,128)(2,1)S(1)} %pad_maximum_fusion.refs_4_), channel_id=1, source_target_pairs={{0,24},{4,28},{8,16},{12,20},{16,8},{20,12},{24,0},{28,4},{1,25},{... | collective-permute-start | bytes 786440 | tf_op jit(solution)/shard_map/ppermute | solution.py:145
  12.0 1.1 collective-permute-start
  13.1 1.3 %fusion.4 = (s32[64]{0:T(128)}, s32[64]{0:T(128)}) fusion(s32[1,1,64]{2,1,0:T(1,128)} %param.11, s32[]{:T(128)S(6)} %axis_index.22, s32[1,1,64]{2,1,0:T(1,128)} %param.12, s32[]{:T(128)S(6)} %axis_index.25), kind=kLoop, calls=%fused_computation.24 | loop fusion | flops 3520 | bytes 1032 | tf_op jit(solution)/shard_map/add | solution.py:180
  14.4 6.2 %collective-permute-done.1.refs_2_ = bf16[512,128]{1,0:T(8,128)(2,1)S(1)} collective-permute-done((bf16[512,128]{1,0:T(8,128)(2,1)S(1)}, bf16[512,128]{1,0:T(8,128)(2,1)S(1)}, u32[]{:S(2)}, u32[]{:S(2)}) %collective-permute-start.1) | collective-permute-done | bytes 131104 | tf_op jit(solution)/shard_map/ppermute | solution.py:125
  20.6 2.2 %collective-permute-done.5.refs_6_ = bf16[1024,128]{1,0:T(8,128)(2,1)S(1)} collective-permute-done((bf16[1024,128]{1,0:T(8,128)(2,1)S(1)}, bf16[1024,128]{1,0:T(8,128)(2,1)S(1)}, u32[]{:S(2)}, u32[]{:S(2)}) %collective-permute-start.5) | collective-permute-done | bytes 262176 | tf_op jit(solution)/shard_map/ppermute | solution.py:145
  23.6 8.7 %shard_map.86 = (bf16[512,128]{1,0:T(8,128)(2,1)}, bf16[512,128]{1,0:T(8,128)(2,1)}, bf16[512,128]{1,0:T(8,128)(2,1)}, bf16[512,128]{1,0:T(8,128)(2,1)}, bf16[10...) custom-call(s32[64]{0:T(128)} %get-tuple-element.34.rows_ref, ...), custom_call_target="tpu_custom_call" | custom-call | flops 3221225472 | bytes 21495808 | tf_op jit(solution)/shard_map/pallas_call | solution.py:107
  32.3 1.5 %collective-permute-start.13 = (bf16[1024,128]{1,0:T(8,128)(2,1)}, bf16[1024,128]{1,0:T(8,128)(2,1)S(1)}, u32[]{:S(2)}, u32[]{:S(2)}) collective-permute-start(bf16[1024,128]{1,0:T(8,128)(2,1)} %get-tuple-element.23), channel_id=1, source_target_pairs={{0,8},{4,12},{8,0},{12,4},{16,24},{20,28},{24,16},{28,20},{1,9},{5... | collective-permute-start | bytes 786440 | tf_op jit(solution)/shard_map/ppermute | solution.py:152
  33.9 10.3 %collective-permute-start.14 = (bf16[1024,128]{1,0:T(8,128)(2,1)}, bf16[1024,128]{1,0:T(8,128)(2,1)S(1)}, u32[]{:S(2)}, u32[]{:S(2)}) collective-permute-start(bf16[1024,128]{1,0:T(8,128)(2,1)} %get-tuple-element.24), channel_id=1, source_target_pairs={{0,16},{4,20},{8,24},{12,28},{16,0},{20,4},{24,8},{28,12},{1,17},{... | collective-permute-start | bytes 786440 | tf_op jit(solution)/shard_map/ppermute | solution.py:152
  44.1 1.4 %collective-permute-start.15 = (bf16[1024,128]{1,0:T(8,128)(2,1)}, bf16[1024,128]{1,0:T(8,128)(2,1)S(1)}, u32[]{:S(2)}, u32[]{:S(2)}) collective-permute-start(bf16[1024,128]{1,0:T(8,128)(2,1)} %get-tuple-element.25), channel_id=1, source_target_pairs={{0,24},{4,28},{8,16},{12,20},{16,8},{20,12},{24,0},{28,4},{1,25},{... | collective-permute-start | bytes 786440 | tf_op jit(solution)/shard_map/ppermute | solution.py:152
  45.5 3.8 %collective-permute-start.9 = (bf16[512,128]{1,0:T(8,128)(2,1)}, bf16[512,128]{1,0:T(8,128)(2,1)S(1)}, u32[]{:S(2)}, u32[]{:S(2)}) collective-permute-start(bf16[512,128]{1,0:T(8,128)(2,1)} %get-tuple-element.21), channel_id=1, source_target_pairs={{0,3},{1,0},{2,1},{3,2},{4,7},{5,4},{6,5},{7,6},{8,11},{9,8},{10,9... | collective-permute-start | bytes 393224 | tf_op jit(solution)/shard_map/ppermute | solution.py:132
  49.4 7.0 %collective-permute-done.14 = bf16[1024,128]{1,0:T(8,128)(2,1)S(1)} collective-permute-done((bf16[1024,128]{1,0:T(8,128)(2,1)}, bf16[1024,128]{1,0:T(8,128)(2,1)S(1)}, u32[]{:S(2)}, u32[]{:S(2)}) %collective-permute-start.14) | collective-permute-done | bytes 262176 | tf_op jit(solution)/shard_map/ppermute | solution.py:152
  56.3 1.1 convert_add_fusion.1
  57.5 1.0 collective-permute-start.16
  58.6 1.0 fusion.9.refs_0_
  59.6 2.8 %collective-permute-start.12 = (bf16[512,128]{1,0:T(8,128)(2,1)S(1)}, bf16[512,128]{1,0:T(8,128)(2,1)S(1)}, u32[]{:S(2)}, u32[]{:S(2)}) collective-permute-start(bf16[512,128]{1,0:T(8,128)(2,1)S(1)} %fusion.9.refs_0_), channel_id=1, source_target_pairs={{0,3},{1,0},{2,1},{3,2},{4,7},{5,4},{6,5},{7,6},{8,11},{9,8},{10,9... | collective-permute-start | bytes 393224 | tf_op jit(solution)/shard_map/ppermute | solution.py:125
  62.4 1.3 %collective-permute-start.11 = (bf16[512,128]{1,0:T(8,128)(2,1)S(1)}, bf16[512,128]{1,0:T(8,128)(2,1)S(1)}, u32[]{:S(2)}, u32[]{:S(2)}) collective-permute-start(bf16[512,128]{1,0:T(8,128)(2,1)S(1)} %fusion.9.refs_0_), channel_id=1, source_target_pairs={{0,2},{1,3},{2,0},{3,1},{4,6},{5,7},{6,4},{7,5},{8,10},{9,11},{10,... | collective-permute-start | bytes 393224 | tf_op jit(solution)/shard_map/ppermute | solution.py:125
  63.9 1.5 %collective-permute-start.22 = (bf16[512,128]{1,0:T(8,128)(2,1)S(1)}, bf16[512,128]{1,0:T(8,128)(2,1)S(1)}, u32[]{:S(2)}, u32[]{:S(2)}) collective-permute-start(bf16[512,128]{1,0:T(8,128)(2,1)S(1)} %fusion.8.refs_4_), channel_id=1, source_target_pairs={{0,24},{4,28},{8,16},{12,20},{16,8},{20,12},{24,0},{28,4},{1,25},{... | collective-permute-start | bytes 393224 | tf_op jit(solution)/shard_map/ppermute | solution.py:162
  65.3 1.0 collective-permute-done.12.refs_3_
  67.0 7.8 %collective-permute-done.11.refs_2_ = bf16[512,128]{1,0:T(8,128)(2,1)S(1)} collective-permute-done((bf16[512,128]{1,0:T(8,128)(2,1)S(1)}, bf16[512,128]{1,0:T(8,128)(2,1)S(1)}, u32[]{:S(2)}, u32[]{:S(2)}) %collective-permute-start.11) | collective-permute-done | bytes 131104 | tf_op jit(solution)/shard_map/ppermute | solution.py:125
  75.8 1.2 collective-permute-start.18
  77.1 2.7 %collective-permute-done.20.refs_8_ = bf16[512,128]{1,0:T(8,128)(2,1)S(1)} collective-permute-done((bf16[512,128]{1,0:T(8,128)(2,1)S(1)}, bf16[512,128]{1,0:T(8,128)(2,1)S(1)}, u32[]{:S(2)}, u32[]{:S(2)}) %collective-permute-start.20) | collective-permute-done | bytes 131104 | tf_op jit(solution)/shard_map/ppermute | solution.py:162
  80.5 3.1 %collective-permute-done.18.refs_6_ = bf16[512,128]{1,0:T(8,128)(2,1)S(1)} collective-permute-done((bf16[512,128]{1,0:T(8,128)(2,1)S(1)}, bf16[512,128]{1,0:T(8,128)(2,1)S(1)}, u32[]{:S(2)}, u32[]{:S(2)}) %collective-permute-start.18) | collective-permute-done | bytes 131104 | tf_op jit(solution)/shard_map/ppermute | solution.py:162
  84.3 8.7 %shard_map.87 = (bf16[512,128]{1,0:T(8,128)(2,1)}, bf16[512,128]{1,0:T(8,128)(2,1)}, bf16[512,128]{1,0:T(8,128)(2,1)}, bf16[512,128]{1,0:T(8,128)(2,1)}, bf16[10...) custom-call(s32[64]{0:T(128)} %get-tuple-element.34.rows_ref, ...), custom_call_target="tpu_custom_call" | custom-call | flops 3221225472 | bytes 21495808 | tf_op jit(solution)/shard_map/pallas_call | solution.py:107
  93.9 11.3 %collective-permute-start.28 = (bf16[1024,128]{1,0:T(8,128)(2,1)}, bf16[1024,128]{1,0:T(8,128)(2,1)S(1)}, u32[]{:S(2)}, u32[]{:S(2)}) collective-permute-start(bf16[1024,128]{1,0:T(8,128)(2,1)} %get-tuple-element.32), channel_id=1, source_target_pairs={{0,16},{4,20},{8,24},{12,28},{16,0},{20,4},{24,8},{28,12},{1,17},{... | collective-permute-start | bytes 786440 | tf_op jit(solution)/shard_map/ppermute | solution.py:152
  105.2 1.4 %collective-permute-start.29 = (bf16[1024,128]{1,0:T(8,128)(2,1)}, bf16[1024,128]{1,0:T(8,128)(2,1)S(1)}, u32[]{:S(2)}, u32[]{:S(2)}) collective-permute-start(bf16[1024,128]{1,0:T(8,128)(2,1)} %get-tuple-element.33), channel_id=1, source_target_pairs={{0,24},{4,28},{8,16},{12,20},{16,8},{20,12},{24,0},{28,4},{1,25},{... | collective-permute-start | bytes 786440 | tf_op jit(solution)/shard_map/ppermute | solution.py:152
  106.6 3.8 %collective-permute-start.26 = (bf16[512,128]{1,0:T(8,128)(2,1)}, bf16[512,128]{1,0:T(8,128)(2,1)S(1)}, u32[]{:S(2)}, u32[]{:S(2)}) collective-permute-start(bf16[512,128]{1,0:T(8,128)(2,1)} %get-tuple-element.29), channel_id=1, source_target_pairs={{0,3},{1,0},{2,1},{3,2},{4,7},{5,4},{6,5},{7,6},{8,11},{9,8},{10,9... | collective-permute-start | bytes 393224 | tf_op jit(solution)/shard_map/ppermute | solution.py:132
  110.4 7.2 %collective-permute-done.28 = bf16[1024,128]{1,0:T(8,128)(2,1)S(1)} collective-permute-done((bf16[1024,128]{1,0:T(8,128)(2,1)}, bf16[1024,128]{1,0:T(8,128)(2,1)S(1)}, u32[]{:S(2)}, u32[]{:S(2)}) %collective-permute-start.28) | collective-permute-done | bytes 262176 | tf_op jit(solution)/shard_map/ppermute | solution.py:152
  117.6 1.1 convert_add_fusion
  119.5 1.8 %multiply_add_fusion = f32[512,128]{1,0:T(8,128)} fusion(bf16[512,128]{1,0:T(8,128)(2,1)S(1)} %collective-permute-done.26, bf16[512,128]{1,0:T(8,128)(2,1)S(1)} %collective-permute-done.25, bf16[512,128]{1,0:T(8,128)(2,1)S(1)} %collective-permute-done.24, bf16[512,128]{1,0:T(8,128)(2,1)} %get-tuple-element.26, f32[512,128]{1,0:T(8,128)S(1)} %copy-done, ...), kind=kLoop, calls=%fused_computation.9 | loop fusion | flops 1179648 | bytes 1572864 | tf_op jit(solution)/shard_map/add | solution.py:213
  (90 shorter events, 8.3 us)
Async XLA Ops:
  1.6 6.2 %collective-permute-start.3 = (bf16[512,128]{1,0:T(8,128)(2,1)S(1)}, bf16[512,128]{1,0:T(8,128)(2,1)S(1)}, u32[]{:S(2)}, u32[]{:S(2)}) collective-permute-start(bf16[512,128]{1,0:T(8,128)(2,1)S(1)} %convert_element_type.61), channel_id=1, source_target_pairs={{0,4},{4,0},{8,12},{12,8},{16,20},{20,16},{24,28},{28,24},{1,5},{5... | collective-permute-start | bytes 393224 | tf_op jit(solution)/shard_map/ppermute | solution.py:142
  3.1 8.9 %collective-permute-start.2 = (bf16[512,128]{1,0:T(8,128)(2,1)S(1)}, bf16[512,128]{1,0:T(8,128)(2,1)S(1)}, u32[]{:S(2)}, u32[]{:S(2)}) collective-permute-start(bf16[512,128]{1,0:T(8,128)(2,1)S(1)} %convert_element_type.60.refs_0_), channel_id=1, source_target_pairs={{0,3},{1,0},{2,1},{3,2},{4,7},{5,4},{6,5},{7,6},{8,11},{9,8},{10,9... | collective-permute-start | bytes 393224 | tf_op jit(solution)/shard_map/ppermute | solution.py:125
  7.8 12.8 %collective-permute-start.6 = (bf16[1024,128]{1,0:T(8,128)(2,1)S(1)}, bf16[1024,128]{1,0:T(8,128)(2,1)S(1)}, u32[]{:S(2)}, u32[]{:S(2)}) collective-permute-start(bf16[1024,128]{1,0:T(8,128)(2,1)S(1)} %pad_maximum_fusion.refs_4_), channel_id=1, source_target_pairs={{0,24},{4,28},{8,16},{12,20},{16,8},{20,12},{24,0},{28,4},{1,25},{... | collective-permute-start | bytes 786440 | tf_op jit(solution)/shard_map/ppermute | solution.py:145
  10.3 12.5 %collective-permute-start.5 = (bf16[1024,128]{1,0:T(8,128)(2,1)S(1)}, bf16[1024,128]{1,0:T(8,128)(2,1)S(1)}, u32[]{:S(2)}, u32[]{:S(2)}) collective-permute-start(bf16[1024,128]{1,0:T(8,128)(2,1)S(1)} %pad_maximum_fusion.refs_4_), channel_id=1, source_target_pairs={{0,16},{4,20},{8,24},{12,28},{16,0},{20,4},{24,8},{28,12},{1,17},{... | collective-permute-start | bytes 786440 | tf_op jit(solution)/shard_map/ppermute | solution.py:145
  10.8 12.1 %collective-permute-start.4 = (bf16[1024,128]{1,0:T(8,128)(2,1)S(1)}, bf16[1024,128]{1,0:T(8,128)(2,1)S(1)}, u32[]{:S(2)}, u32[]{:S(2)}) collective-permute-start(bf16[1024,128]{1,0:T(8,128)(2,1)S(1)} %pad_maximum_fusion.refs_4_), channel_id=1, source_target_pairs={{0,8},{4,12},{8,0},{12,4},{16,24},{20,28},{24,16},{28,20},{1,9},{5... | collective-permute-start | bytes 786440 | tf_op jit(solution)/shard_map/ppermute | solution.py:145
  11.4 9.2 %collective-permute-start.1 = (bf16[512,128]{1,0:T(8,128)(2,1)S(1)}, bf16[512,128]{1,0:T(8,128)(2,1)S(1)}, u32[]{:S(2)}, u32[]{:S(2)}) collective-permute-start(bf16[512,128]{1,0:T(8,128)(2,1)S(1)} %convert_element_type.60.refs_0_), channel_id=1, source_target_pairs={{0,2},{1,3},{2,0},{3,1},{4,6},{5,7},{6,4},{7,5},{8,10},{9,11},{10,... | collective-permute-start | bytes 393224 | tf_op jit(solution)/shard_map/ppermute | solution.py:125
  12.0 8.5 %collective-permute-start = (bf16[512,128]{1,0:T(8,128)(2,1)S(1)}, bf16[512,128]{1,0:T(8,128)(2,1)S(1)}, u32[]{:S(2)}, u32[]{:S(2)}) collective-permute-start(bf16[512,128]{1,0:T(8,128)(2,1)S(1)} %convert_element_type.60.refs_0_), channel_id=1, source_target_pairs={{0,1},{1,2},{2,3},{3,0},{4,5},{5,6},{6,7},{7,4},{8,9},{9,10},{10,1... | collective-permute-start | bytes 393224 | tf_op jit(solution)/shard_map/ppermute | solution.py:125
  23.6 40.1 %copy-start.1 = (f32[512,128]{1,0:T(8,128)S(1)}, f32[512,128]{1,0:T(8,128)}, u32[]{:S(2)}) copy-start(f32[512,128]{1,0:T(8,128)} %param.8) | copy-start | bytes 786436
  32.3 13.2 %collective-permute-start.13 = (bf16[1024,128]{1,0:T(8,128)(2,1)}, bf16[1024,128]{1,0:T(8,128)(2,1)S(1)}, u32[]{:S(2)}, u32[]{:S(2)}) collective-permute-start(bf16[1024,128]{1,0:T(8,128)(2,1)} %get-tuple-element.23), channel_id=1, source_target_pairs={{0,8},{4,12},{8,0},{12,4},{16,24},{20,28},{24,16},{28,20},{1,9},{5... | collective-permute-start | bytes 786440 | tf_op jit(solution)/shard_map/ppermute | solution.py:152
  33.9 22.5 %collective-permute-start.14 = (bf16[1024,128]{1,0:T(8,128)(2,1)}, bf16[1024,128]{1,0:T(8,128)(2,1)S(1)}, u32[]{:S(2)}, u32[]{:S(2)}) collective-permute-start(bf16[1024,128]{1,0:T(8,128)(2,1)} %get-tuple-element.24), channel_id=1, source_target_pairs={{0,16},{4,20},{8,24},{12,28},{16,0},{20,4},{24,8},{28,12},{1,17},{... | collective-permute-start | bytes 786440 | tf_op jit(solution)/shard_map/ppermute | solution.py:152
  44.1 12.2 %collective-permute-start.15 = (bf16[1024,128]{1,0:T(8,128)(2,1)}, bf16[1024,128]{1,0:T(8,128)(2,1)S(1)}, u32[]{:S(2)}, u32[]{:S(2)}) collective-permute-start(bf16[1024,128]{1,0:T(8,128)(2,1)} %get-tuple-element.25), channel_id=1, source_target_pairs={{0,24},{4,28},{8,16},{12,20},{16,8},{20,12},{24,0},{28,4},{1,25},{... | collective-permute-start | bytes 786440 | tf_op jit(solution)/shard_map/ppermute | solution.py:152
  45.5 12.9 %collective-permute-start.7 = (bf16[512,128]{1,0:T(8,128)(2,1)}, bf16[512,128]{1,0:T(8,128)(2,1)S(1)}, u32[]{:S(2)}, u32[]{:S(2)}) collective-permute-start(bf16[512,128]{1,0:T(8,128)(2,1)} %get-tuple-element.19), channel_id=1, source_target_pairs={{0,1},{1,2},{2,3},{3,0},{4,5},{5,6},{6,7},{7,4},{8,9},{9,10},{10,1... | collective-permute-start | bytes 393224 | tf_op jit(solution)/shard_map/ppermute | solution.py:132
  45.5 13.1 %collective-permute-start.8 = (bf16[512,128]{1,0:T(8,128)(2,1)}, bf16[512,128]{1,0:T(8,128)(2,1)S(1)}, u32[]{:S(2)}, u32[]{:S(2)}) collective-permute-start(bf16[512,128]{1,0:T(8,128)(2,1)} %get-tuple-element.20), channel_id=1, source_target_pairs={{0,2},{1,3},{2,0},{3,1},{4,6},{5,7},{6,4},{7,5},{8,10},{9,11},{10,... | collective-permute-start | bytes 393224 | tf_op jit(solution)/shard_map/ppermute | solution.py:132
  45.5 13.1 %collective-permute-start.9 = (bf16[512,128]{1,0:T(8,128)(2,1)}, bf16[512,128]{1,0:T(8,128)(2,1)S(1)}, u32[]{:S(2)}, u32[]{:S(2)}) collective-permute-start(bf16[512,128]{1,0:T(8,128)(2,1)} %get-tuple-element.21), channel_id=1, source_target_pairs={{0,3},{1,0},{2,1},{3,2},{4,7},{5,4},{6,5},{7,6},{8,11},{9,8},{10,9... | collective-permute-start | bytes 393224 | tf_op jit(solution)/shard_map/ppermute | solution.py:132
  57.5 6.3 %collective-permute-start.16 = (f32[512,128]{1,0:T(8,128)S(1)}, f32[512,128]{1,0:T(8,128)S(1)}, u32[]{:S(2)}, u32[]{:S(2)}) collective-permute-start(f32[512,128]{1,0:T(8,128)S(1)} %slice.17), channel_id=1, source_target_pairs={{0,4},{4,0},{8,12},{12,8},{16,20},{20,16},{24,28},{28,24},{1,5},{5... | collective-permute-start | bytes 786440 | tf_op jit(solution)/shard_map/ppermute | solution.py:155
  59.6 6.7 %collective-permute-start.12 = (bf16[512,128]{1,0:T(8,128)(2,1)S(1)}, bf16[512,128]{1,0:T(8,128)(2,1)S(1)}, u32[]{:S(2)}, u32[]{:S(2)}) collective-permute-start(bf16[512,128]{1,0:T(8,128)(2,1)S(1)} %fusion.9.refs_0_), channel_id=1, source_target_pairs={{0,3},{1,0},{2,1},{3,2},{4,7},{5,4},{6,5},{7,6},{8,11},{9,8},{10,9... | collective-permute-start | bytes 393224 | tf_op jit(solution)/shard_map/ppermute | solution.py:125
  62.4 12.4 %collective-permute-start.11 = (bf16[512,128]{1,0:T(8,128)(2,1)S(1)}, bf16[512,128]{1,0:T(8,128)(2,1)S(1)}, u32[]{:S(2)}, u32[]{:S(2)}) collective-permute-start(bf16[512,128]{1,0:T(8,128)(2,1)S(1)} %fusion.9.refs_0_), channel_id=1, source_target_pairs={{0,2},{1,3},{2,0},{3,1},{4,6},{5,7},{6,4},{7,5},{8,10},{9,11},{10,... | collective-permute-start | bytes 393224 | tf_op jit(solution)/shard_map/ppermute | solution.py:125
  63.7 11.3 %collective-permute-start.10 = (bf16[512,128]{1,0:T(8,128)(2,1)S(1)}, bf16[512,128]{1,0:T(8,128)(2,1)S(1)}, u32[]{:S(2)}, u32[]{:S(2)}) collective-permute-start(bf16[512,128]{1,0:T(8,128)(2,1)S(1)} %fusion.9.refs_0_), channel_id=1, source_target_pairs={{0,1},{1,2},{2,3},{3,0},{4,5},{5,6},{6,7},{7,4},{8,9},{9,10},{10,1... | collective-permute-start | bytes 393224 | tf_op jit(solution)/shard_map/ppermute | solution.py:125
  63.8 12.0 %collective-permute-start.23 = (bf16[512,128]{1,0:T(8,128)(2,1)S(1)}, bf16[512,128]{1,0:T(8,128)(2,1)S(1)}, u32[]{:S(2)}, u32[]{:S(2)}) collective-permute-start(bf16[512,128]{1,0:T(8,128)(2,1)S(1)} %fusion.8.refs_4_), channel_id=1, source_target_pairs={{0,28},{4,24},{8,20},{12,16},{16,12},{20,8},{24,4},{28,0},{1,29},{... | collective-permute-start | bytes 393224 | tf_op jit(solution)/shard_map/ppermute | solution.py:162
  63.9 13.1 %collective-permute-start.22 = (bf16[512,128]{1,0:T(8,128)(2,1)S(1)}, bf16[512,128]{1,0:T(8,128)(2,1)S(1)}, u32[]{:S(2)}, u32[]{:S(2)}) collective-permute-start(bf16[512,128]{1,0:T(8,128)(2,1)S(1)} %fusion.8.refs_4_), channel_id=1, source_target_pairs={{0,24},{4,28},{8,16},{12,20},{16,8},{20,12},{24,0},{28,4},{1,25},{... | collective-permute-start | bytes 393224 | tf_op jit(solution)/shard_map/ppermute | solution.py:162
  66.3 10.7 %collective-permute-start.21 = (bf16[512,128]{1,0:T(8,128)(2,1)S(1)}, bf16[512,128]{1,0:T(8,128)(2,1)S(1)}, u32[]{:S(2)}, u32[]{:S(2)}) collective-permute-start(bf16[512,128]{1,0:T(8,128)(2,1)S(1)} %fusion.8.refs_4_), channel_id=1, source_target_pairs={{0,20},{4,16},{8,28},{12,24},{16,4},{20,0},{24,12},{28,8},{1,21},{... | collective-permute-start | bytes 393224 | tf_op jit(solution)/shard_map/ppermute | solution.py:162
  74.8 5.0 %collective-permute-start.20 = (bf16[512,128]{1,0:T(8,128)(2,1)S(1)}, bf16[512,128]{1,0:T(8,128)(2,1)S(1)}, u32[]{:S(2)}, u32[]{:S(2)}) collective-permute-start(bf16[512,128]{1,0:T(8,128)(2,1)S(1)} %fusion.8.refs_4_), channel_id=1, source_target_pairs={{0,16},{4,20},{8,24},{12,28},{16,0},{20,4},{24,8},{28,12},{1,17},{... | collective-permute-start | bytes 393224 | tf_op jit(solution)/shard_map/ppermute | solution.py:162
  75.0 5.5 %collective-permute-start.19 = (bf16[512,128]{1,0:T(8,128)(2,1)S(1)}, bf16[512,128]{1,0:T(8,128)(2,1)S(1)}, u32[]{:S(2)}, u32[]{:S(2)}) collective-permute-start(bf16[512,128]{1,0:T(8,128)(2,1)S(1)} %fusion.8.refs_4_), channel_id=1, source_target_pairs={{0,12},{4,8},{8,4},{12,0},{16,28},{20,24},{24,20},{28,16},{1,13},{... | collective-permute-start | bytes 393224 | tf_op jit(solution)/shard_map/ppermute | solution.py:162
  75.8 7.9 %collective-permute-start.18 = (bf16[512,128]{1,0:T(8,128)(2,1)S(1)}, bf16[512,128]{1,0:T(8,128)(2,1)S(1)}, u32[]{:S(2)}, u32[]{:S(2)}) collective-permute-start(bf16[512,128]{1,0:T(8,128)(2,1)S(1)} %fusion.8.refs_4_), channel_id=1, source_target_pairs={{0,8},{4,12},{8,0},{12,4},{16,24},{20,28},{24,16},{28,20},{1,9},{5... | collective-permute-start | bytes 393224 | tf_op jit(solution)/shard_map/ppermute | solution.py:162
  77.0 6.7 %collective-permute-start.17 = (bf16[512,128]{1,0:T(8,128)(2,1)S(1)}, bf16[512,128]{1,0:T(8,128)(2,1)S(1)}, u32[]{:S(2)}, u32[]{:S(2)}) collective-permute-start(bf16[512,128]{1,0:T(8,128)(2,1)S(1)} %fusion.8.refs_4_), channel_id=1, source_target_pairs={{0,4},{4,0},{8,12},{12,8},{16,20},{20,16},{24,28},{28,24},{1,5},{5... | collective-permute-start | bytes 393224 | tf_op jit(solution)/shard_map/ppermute | solution.py:162
  93.0 13.6 %collective-permute-start.27 = (bf16[1024,128]{1,0:T(8,128)(2,1)}, bf16[1024,128]{1,0:T(8,128)(2,1)S(1)}, u32[]{:S(2)}, u32[]{:S(2)}) collective-permute-start(bf16[1024,128]{1,0:T(8,128)(2,1)} %get-tuple-element.31), channel_id=1, source_target_pairs={{0,8},{4,12},{8,0},{12,4},{16,24},{20,28},{24,16},{28,20},{1,9},{5... | collective-permute-start | bytes 786440 | tf_op jit(solution)/shard_map/ppermute | solution.py:152
  93.9 23.7 %collective-permute-start.28 = (bf16[1024,128]{1,0:T(8,128)(2,1)}, bf16[1024,128]{1,0:T(8,128)(2,1)S(1)}, u32[]{:S(2)}, u32[]{:S(2)}) collective-permute-start(bf16[1024,128]{1,0:T(8,128)(2,1)} %get-tuple-element.32), channel_id=1, source_target_pairs={{0,16},{4,20},{8,24},{12,28},{16,0},{20,4},{24,8},{28,12},{1,17},{... | collective-permute-start | bytes 786440 | tf_op jit(solution)/shard_map/ppermute | solution.py:152
  105.2 12.4 %collective-permute-start.29 = (bf16[1024,128]{1,0:T(8,128)(2,1)}, bf16[1024,128]{1,0:T(8,128)(2,1)S(1)}, u32[]{:S(2)}, u32[]{:S(2)}) collective-permute-start(bf16[1024,128]{1,0:T(8,128)(2,1)} %get-tuple-element.33), channel_id=1, source_target_pairs={{0,24},{4,28},{8,16},{12,20},{16,8},{20,12},{24,0},{28,4},{1,25},{... | collective-permute-start | bytes 786440 | tf_op jit(solution)/shard_map/ppermute | solution.py:152
  106.6 12.9 %collective-permute-start.24 = (bf16[512,128]{1,0:T(8,128)(2,1)}, bf16[512,128]{1,0:T(8,128)(2,1)S(1)}, u32[]{:S(2)}, u32[]{:S(2)}) collective-permute-start(bf16[512,128]{1,0:T(8,128)(2,1)} %get-tuple-element.27), channel_id=1, source_target_pairs={{0,1},{1,2},{2,3},{3,0},{4,5},{5,6},{6,7},{7,4},{8,9},{9,10},{10,1... | collective-permute-start | bytes 393224 | tf_op jit(solution)/shard_map/ppermute | solution.py:132
  106.6 12.9 %collective-permute-start.25 = (bf16[512,128]{1,0:T(8,128)(2,1)}, bf16[512,128]{1,0:T(8,128)(2,1)S(1)}, u32[]{:S(2)}, u32[]{:S(2)}) collective-permute-start(bf16[512,128]{1,0:T(8,128)(2,1)} %get-tuple-element.28), channel_id=1, source_target_pairs={{0,2},{1,3},{2,0},{3,1},{4,6},{5,7},{6,4},{7,5},{8,10},{9,11},{10,... | collective-permute-start | bytes 393224 | tf_op jit(solution)/shard_map/ppermute | solution.py:132
  106.6 12.9 %collective-permute-start.26 = (bf16[512,128]{1,0:T(8,128)(2,1)}, bf16[512,128]{1,0:T(8,128)(2,1)S(1)}, u32[]{:S(2)}, u32[]{:S(2)}) collective-permute-start(bf16[512,128]{1,0:T(8,128)(2,1)} %get-tuple-element.29), channel_id=1, source_target_pairs={{0,3},{1,0},{2,1},{3,2},{4,7},{5,4},{6,5},{7,6},{8,11},{9,8},{10,9... | collective-permute-start | bytes 393224 | tf_op jit(solution)/shard_map/ppermute | solution.py:132
  118.8 2.5 %collective-permute-start.30 = (f32[512,128]{1,0:T(8,128)S(1)}, f32[512,128]{1,0:T(8,128)S(1)}, u32[]{:S(2)}, u32[]{:S(2)}) collective-permute-start(f32[512,128]{1,0:T(8,128)S(1)} %slice.19), channel_id=1, source_target_pairs={{0,4},{4,0},{8,12},{12,8},{16,20},{20,16},{24,28},{28,24},{1,5},{5... | collective-permute-start | bytes 786440 | tf_op jit(solution)/shard_map/ppermute | solution.py:155
  (22 other events, 233.1 us)
